TPU v7x, 32 devices: a whole 2x2x4 slice. The times are simulated.
32 devices in a mesh: req: 8 (over y, x, core), hid: 4 (over z).
Axes of the slice: x: 2, y: 2, z: 4, core: 2. Of those that a mesh axis runs over, the one named last changes fastest.
Arguments:
- hidden_in: bfloat16 [2048, 1024], P('req', 'hid'), may hold values from -6 to 6
- segments: int32 [8, 256], P('req'), may hold values from 0 to 7, never falling along the last dimension, each value on 1 to 128 neighbouring positions
- prefix_group: int32 [8, 8], P('req'), may hold values from 0 to 15
- prefix_cache: bfloat16 [16, 1024, 8, 128], P('req', None, 'hid'), may hold values from -400 to 400
- page_table: int32 [8, 2], P('req'), may hold values from 0 to 1, each once within a row
- norm_gain: float32 [1024], replicated, may hold values from 0.1 to 1.9
- w_query: bfloat16 [1024, 1024], P(None, 'hid'), may hold values from -0.1875 to 0.1875
- w_keyval: bfloat16 [1024, 1024], P(None, 'hid'), may hold values from -0.1875 to 0.1875
- w_out: bfloat16 [1024, 1024], P('hid'), may hold values from -0.1875 to 0.1875
- moe_gain: float32 [1024], replicated, may hold values from 0.1 to 1.9
- routes: int32 [2048, 8], P('req'), may hold values from 0 to 15, all different within a row; in each aligned block of 256 rows (0 to 255, 256 to 511, ...) at most 256 rows name the same one
- gates: float32 [2048, 8], P('req'), may hold values from 0.05 to 0.5
- w_gate_up: bfloat16 [16, 2, 1024, 512], P('req', None, None, 'hid'), may hold values from -0.1875 to 0.1875
- w_down: bfloat16 [16, 512, 1024], P('req', 'hid'), may hold values from -0.25 to 0.25
Outputs:
- hidden_out: bfloat16 [2048, 1024], P('req', 'hid')
- kv_pages: bfloat16 [16, 128, 8, 128], P('req', None, 'hid')
Inputs may be any that keep to these rules, and one draw needn't show every extreme that they name: `routes`: within the 256 rows of one row of the stream no expert is named by more than 256 tokens. `page_table`: each row is a permutation of 0 to 1. `segments`: segment numbers of a row never fall; each of the 8 documents has 1 to 128 tokens.
All inputs are finite; a program needn't handle non-finite values.
Results may differ from a plain program's by a relative error of at most 0.013.
Values may be sent and summed in bfloat16 or wider, within the bound.
No kernel may reach another device: no remote copies, remote signals or barrier semaphores. Data moves between devices by JAX's collectives and lax.ppermute only.
A program may use at most 128 MiB of HBM per device.

v0:
```python
import jax
import jax.numpy as jnp
from jax import lax
from jax.sharding import PartitionSpec as P
from jax.experimental import pallas as pl
from jax.experimental.pallas import tpu as pltpu

PAGE = 128


EPSILON = 1e-06
THETA = 10000.0


def rms_scale(row_data, gain_row):
    floats = row_data.astype(jnp.float32)
    mean_square = jnp.mean(floats * floats, axis=-1, keepdims=True)
    return (floats * lax.rsqrt(mean_square + EPSILON) * gain_row).astype(jnp.bfloat16)


def rotate(features, positions):
    half_dim = features.shape[-1] // 2
    frequency = THETA ** (-2.0 * jnp.arange(half_dim, dtype=jnp.float32) / features.shape[-1])
    angles = positions.astype(jnp.float32)[:, None] * frequency[None, :]
    cosine = jnp.cos(angles)[:, None, :]
    sine_part = jnp.sin(angles)[:, None, :]
    front_half = features[..., :half_dim]
    second = features[..., half_dim:]
    return jnp.concatenate(
        [front_half * cosine - second * sine_part, second * cosine + front_half * sine_part],
        axis=-1,
    )


def positions_of(segment_row, offset):
    earlier = jnp.sum((segment_row[None, :] < segment_row[:, None]).astype(jnp.int32), axis=1)
    token_index = jnp.arange(segment_row.shape[0], dtype=jnp.int32)
    return token_index - earlier + offset


def slots_of(route_rows, experts):
    flat_routes = route_rows.reshape(-1)
    onehot = (flat_routes[:, None] == jnp.arange(experts, dtype=jnp.int32)[None, :]).astype(
        jnp.int32
    )
    before = jnp.cumsum(onehot, axis=0) - onehot
    return (flat_routes, jnp.sum(before * onehot, axis=1))


def expert_rows(received, gate_up, down_proj):
    local_experts = down_proj.shape[0]
    slot_count = received.shape[1]
    model_width = received.shape[2]
    grouped = received.reshape(-1, local_experts, slot_count, model_width)
    gate_proj = jnp.einsum(
        "recd,edf->recf", grouped, gate_up[:, 0], preferred_element_type=jnp.float32
    )
    up_proj = jnp.einsum(
        "recd,edf->recf", grouped, gate_up[:, 1], preferred_element_type=jnp.float32
    )
    hidden = (jax.nn.silu(gate_proj) * up_proj).astype(jnp.bfloat16)
    produced = jnp.einsum("recf,efd->recd", hidden, down_proj, preferred_element_type=jnp.float32)
    return produced.reshape(-1, slot_count, model_width)


def shifted_copies(block, axis_name):
    count = lax.axis_size(axis_name)
    copies = [block]
    for shift in range(1, count):
        pairs = [(index, (index + shift) % count) for index in range(count)]
        copies.append(lax.ppermute(block, axis_name, pairs))
    return copies


def gather_in_order(block, axis_name, axis):
    count = lax.axis_size(axis_name)
    copies = jnp.stack(shifted_copies(block, axis_name))
    order = (lax.axis_index(axis_name) - jnp.arange(count, dtype=jnp.int32)) % count
    picked = jnp.take(copies, order, axis=0)
    return jnp.concatenate([picked[index] for index in range(count)], axis=axis)


def attention_body(group_ref, bound_ref, q_ref, k_ref, v_ref, segq_ref, segk_ref, prefix_ref, out_ref):
    block = pl.program_id(1)
    seg = pl.program_id(2)
    seg_count = pl.num_programs(2)
    rows = q_ref.shape[2]
    tokens = k_ref.shape[1]
    head_dim = q_ref.shape[3]

    @pl.when(seg == 0)
    def _():
        out_ref[...] = jnp.zeros_like(out_ref)

    first = bound_ref[seg]
    last = bound_ref[seg + seg_count]
    active = (first < (block + 1) * rows) & (last > block * rows)

    @pl.when(active)
    def _():
        seg_q = segq_ref[...]
        seg_k = segk_ref[...]
        t_idx = block * rows + lax.broadcasted_iota(jnp.int32, (rows, tokens), 0)
        u_idx = lax.broadcasted_iota(jnp.int32, (rows, tokens), 1)
        visible = (seg_q == seg_k) & (u_idx <= t_idx)
        keys = k_ref[0]
        values = v_ref[0]
        prefix = prefix_ref[0, 0]
        prefix_keys = prefix[:, :head_dim]
        prefix_values = prefix[:, head_dim:]
        scale = head_dim ** (-0.5)
        mine = seg_q == seg
        contract = (((1,), (1,)), ((), ()))
        for group in range(q_ref.shape[1]):
            query = q_ref[0, group]
            local = lax.dot_general(query, keys, contract, preferred_element_type=jnp.float32) * scale
            local = jnp.where(visible, local, -jnp.inf)
            cached = (
                lax.dot_general(query, prefix_keys, contract, preferred_element_type=jnp.float32)
                * scale
            )
            top = jnp.maximum(
                jnp.max(local, axis=1, keepdims=True), jnp.max(cached, axis=1, keepdims=True)
            )
            local_num = jnp.exp(local - top)
            cached_num = jnp.exp(cached - top)
            total = jnp.sum(local_num, axis=1, keepdims=True) + jnp.sum(
                cached_num, axis=1, keepdims=True
            )
            summed = jnp.dot(
                local_num.astype(jnp.bfloat16), values, preferred_element_type=jnp.float32
            ) + jnp.dot(
                cached_num.astype(jnp.bfloat16), prefix_values, preferred_element_type=jnp.float32
            )
            out_ref[0, group] = jnp.where(mine, summed / total, out_ref[0, group])


def attend(grouped_query, key_rows, value_rows, segment_row, group_row, prefix_heads, interpret=False):
    tok_count, kv_heads, q_groups, head_dim = grouped_query.shape
    seg_count = group_row.shape[0]
    prefix_len = prefix_heads.shape[2]
    rows = min(128, tok_count)
    labels = jnp.arange(seg_count, dtype=jnp.int32)
    first = jnp.sum((segment_row[None, :] < labels[:, None]).astype(jnp.int32), axis=1)
    last = jnp.sum((segment_row[None, :] <= labels[:, None]).astype(jnp.int32), axis=1)
    bounds = jnp.concatenate([first, last])
    query_heads = grouped_query.transpose(1, 2, 0, 3)
    key_heads = key_rows.transpose(1, 0, 2)
    value_heads = value_rows.transpose(1, 0, 2)
    seg_col = segment_row.reshape(tok_count, 1)
    seg_line = segment_row.reshape(1, tok_count)
    grid_spec = pltpu.PrefetchScalarGridSpec(
        num_scalar_prefetch=2,
        grid=(kv_heads, tok_count // rows, seg_count),
        in_specs=[
            pl.BlockSpec((1, q_groups, rows, head_dim), lambda h, b, s, gr, bd: (h, 0, b, 0)),
            pl.BlockSpec((1, tok_count, head_dim), lambda h, b, s, gr, bd: (h, 0, 0)),
            pl.BlockSpec((1, tok_count, head_dim), lambda h, b, s, gr, bd: (h, 0, 0)),
            pl.BlockSpec((rows, 1), lambda h, b, s, gr, bd: (b, 0)),
            pl.BlockSpec((1, tok_count), lambda h, b, s, gr, bd: (0, 0)),
            pl.BlockSpec(
                (1, 1, prefix_len, 2 * head_dim), lambda h, b, s, gr, bd: (gr[s], h, 0, 0)
            ),
        ],
        out_specs=pl.BlockSpec((1, q_groups, rows, head_dim), lambda h, b, s, gr, bd: (h, 0, b, 0)),
    )
    out = pl.pallas_call(
        attention_body,
        grid_spec=grid_spec,
        out_shape=jax.ShapeDtypeStruct((kv_heads, q_groups, tok_count, head_dim), jnp.float32),
        compiler_params=pltpu.CompilerParams(
            dimension_semantics=("arbitrary", "arbitrary", "arbitrary")
        ),
        interpret=interpret,
    )(group_row, bounds, query_heads, key_heads, value_heads, seg_col, seg_line, prefix_heads)
    return out.transpose(2, 0, 1, 3).reshape(tok_count, -1).astype(jnp.bfloat16)


def shards(
    hidden_in,
    segments,
    prefix_group,
    prefix_cache,
    page_table,
    norm_gain,
    w_query,
    w_keyval,
    w_out,
    moe_gain,
    routes,
    gates,
    w_gate_up,
    w_down,
):
    req_count = lax.axis_size("req")
    whole = gather_in_order(hidden_in, "hid", 1)
    tok_count = whole.shape[0]
    model_width = whole.shape[1]
    segment_row = segments[0]
    prefix_len = prefix_cache.shape[1]
    kv_heads = prefix_cache.shape[2]
    head_dim = prefix_cache.shape[3] // 2
    score_scale = head_dim ** (-0.5)
    normed = rms_scale(whole, norm_gain)
    position = positions_of(segment_row, prefix_len)
    projected = jnp.dot(normed, w_query, preferred_element_type=jnp.float32).reshape(
        tok_count, -1, head_dim
    )
    queries = rotate(projected, position).astype(jnp.bfloat16)
    queries, w_gate_up, w_down = lax.optimization_barrier((queries, w_gate_up, w_down))
    q_groups = queries.shape[1] // kv_heads
    grouped_query = queries.reshape(tok_count, kv_heads, q_groups, head_dim)
    key_value = jnp.dot(normed, w_keyval, preferred_element_type=jnp.float32).reshape(
        tok_count, kv_heads, 2 * head_dim
    )
    key_rows = rotate(key_value[..., :head_dim], position).astype(jnp.bfloat16)
    value_rows = key_value[..., head_dim:].astype(jnp.bfloat16)
    pages = jnp.concatenate([key_rows, value_rows], axis=-1).reshape(
        -1, PAGE, kv_heads, 2 * head_dim
    )
    kv_pages = jnp.zeros_like(pages).at[page_table[0]].set(pages)
    gathered = lax.all_gather(prefix_cache, "req", axis=0, tiled=True)
    attention = attend(
        grouped_query, key_rows, value_rows, segment_row, prefix_group[0],
        gathered.transpose(0, 2, 1, 3),
    )
    share_width = hidden_in.shape[1]
    whole_attention = jnp.concatenate(shifted_copies(attention, "hid"), axis=1)
    whole_w_out = jnp.concatenate(shifted_copies(w_out, "hid"), axis=0)
    projected_out = jnp.dot(whole_attention, whole_w_out, preferred_element_type=jnp.float32)
    middle = (whole.astype(jnp.float32) + projected_out).astype(jnp.bfloat16)
    middle_share = lax.dynamic_slice_in_dim(
        middle, lax.axis_index("hid") * share_width, share_width, 1
    )
    normed_moe = rms_scale(middle, moe_gain)
    all_gate_up = lax.all_gather(w_gate_up, "req", axis=0, tiled=True)
    all_down = lax.all_gather(w_down, "req", axis=0, tiled=True)
    experts = all_down.shape[0]
    expert_ids = jnp.arange(experts, dtype=jnp.int32)
    combine = jnp.sum(
        jnp.where(routes[:, :, None] == expert_ids[None, None, :], gates[:, :, None], 0.0), axis=1
    )
    gate_proj = jnp.einsum(
        "td,edf->tef", normed_moe, all_gate_up[:, 0], preferred_element_type=jnp.float32
    )
    up_proj = jnp.einsum(
        "td,edf->tef", normed_moe, all_gate_up[:, 1], preferred_element_type=jnp.float32
    )
    hidden = (jax.nn.silu(gate_proj) * up_proj * combine[:, :, None]).astype(jnp.bfloat16)
    partial_out = jnp.einsum(
        "tef,efd->td", hidden, all_down, preferred_element_type=jnp.float32
    )
    hid_count = lax.axis_size("hid")
    hid_index = lax.axis_index("hid")
    expert_sum = lax.dynamic_slice_in_dim(partial_out, hid_index * share_width, share_width, 1)
    for shift in range(1, hid_count):
        block = (hid_index + shift) % hid_count
        outgoing = lax.dynamic_slice_in_dim(partial_out, block * share_width, share_width, 1)
        pairs = [(index, (index + shift) % hid_count) for index in range(hid_count)]
        incoming = lax.ppermute(outgoing.astype(jnp.bfloat16), "hid", pairs)
        expert_sum = expert_sum + incoming.astype(jnp.float32)
    hidden_out = (middle_share.astype(jnp.float32) + expert_sum).astype(jnp.bfloat16)
    return (hidden_out, kv_pages)


def solution(mesh):
    in_specs = (
        P("req", "hid"),
        P("req", None),
        P("req", None),
        P("req", None, "hid", None),
        P("req", None),
        P(),
        P(None, "hid"),
        P(None, "hid"),
        P("hid", None),
        P(),
        P("req", None),
        P("req", None),
        P("req", None, None, "hid"),
        P("req", "hid", None),
    )
    out_specs = (P("req", "hid"), P("req", None, "hid", None))
    return jax.shard_map(shards, mesh=mesh, in_specs=in_specs, out_specs=out_specs, check_vma=False)
```

profile of v0, /device:TPU:0, one launch (start us, length us, event | category | flops | bytes accessed | tf_op | source)
XLA Modules:
  0.0 189.7 jit_solution(2377654442598821371)
XLA Ops:
  7.2 2.4 %copy.55 = bf16[2,1024,2,128]{3,1,2,0:T(8,128)(2,1)} copy(bf16[2,1024,2,128]{3,2,1,0:T(2,128)(2,1)} %param.17) | data formatting | bytes 2097152 | tf_op args[3]
  9.7 3.1 %collective-permute-start = (bf16[256,256]{1,0:T(8,128)(2,1)}, bf16[256,256]{1,0:T(8,128)(2,1)S(1)}, u32[]{:S(2)}, u32[]{:S(2)}) collective-permute-start(bf16[256,256]{1,0:T(8,128)(2,1)} %param.14), channel_id=1, source_target_pairs={{0,1},{1,2},{2,3},{3,0},{4,5},{5,6},{6,7},{7,4},{8,9},{9,10},{10,1... | collective-permute-start | bytes 393224 | tf_op jit(solution)/shard_map/ppermute | solution.py:71
  12.8 2.6 %collective-permute-start.1 = (bf16[256,256]{1,0:T(8,128)(2,1)}, bf16[256,256]{1,0:T(8,128)(2,1)S(1)}, u32[]{:S(2)}, u32[]{:S(2)}) collective-permute-start(bf16[256,256]{1,0:T(8,128)(2,1)} %param.14), channel_id=1, source_target_pairs={{0,2},{1,3},{2,0},{3,1},{4,6},{5,7},{6,4},{7,5},{8,10},{9,11},{10,... | collective-permute-start | bytes 393224 | tf_op jit(solution)/shard_map/ppermute | solution.py:71
  15.4 1.3 collective-permute-start.2
  16.8 0.9 convert_reduce_fusion
  17.7 0.5 multiply_cosine_fusion
  18.3 1.2 collective-permute-done
  19.5 4.8 %collective-permute-done.1 = bf16[256,256]{1,0:T(8,128)(2,1)S(1)} collective-permute-done((bf16[256,256]{1,0:T(8,128)(2,1)}, bf16[256,256]{1,0:T(8,128)(2,1)S(1)}, u32[]{:S(2)}, u32[]{:S(2)}) %collective-permute-start.1) | collective-permute-done | bytes 131104 | tf_op jit(solution)/shard_map/ppermute | solution.py:71
  24.3 1.0 pad_maximum_fusion
  25.2 0.6 gather_fusion
  26.0 0.2 fusion.18
  26.2 0.4 fusion.36
  26.7 0.2 copy.61
  26.9 0.2 copy.62
  27.1 0.1 subtract_convert_fusion
  27.3 0.8 pad_maximum_fusion.2
  28.1 1.1 copy.58
  29.3 0.7 all-gather.8.cloned.1.call-update
  29.9 3.3 %collective-permute-start.6 = (bf16[256,1024]{1,0:T(8,128)(2,1)}, bf16[256,1024]{1,0:T(8,128)(2,1)S(1)}, u32[]{:S(2)}, u32[]{:S(2)}) collective-permute-start(bf16[256,1024]{1,0:T(8,128)(2,1)} %param.22), channel_id=1, source_target_pairs={{0,1},{1,2},{2,3},{3,0},{4,5},{5,6},{6,7},{7,4},{8,9},{9,10},{10,1... | collective-permute-start | bytes 1572872 | tf_op jit(solution)/shard_map/ppermute | solution.py:71
  33.3 1.6 collective-permute-start.7
  34.9 0.8 collective-permute-start.8
  35.7 0.8 copy.56.segq_ref
  36.5 0.2 convert_reduce_fusion.2
  36.7 0.6 pad_add_fusion.bound_ref
  37.3 0.4 fusion.34
  38.1 0.8 copy.65
  38.9 0.8 maximum_bitcast_fusion.k_ref
  39.6 27.3 %all-gather.4.cloned.1.call-done = bf16[16,1024,2,128]{3,1,2,0:T(8,128)(2,1)} async-done(((bf16[2,1024,2,128]{3,1,2,0:T(8,128)(2,1)}), bf16[16,1024,2,128]{3,1,2,0:T(8,128)(2,1)}) %all-gather.4.cloned.1.call-update) | async-done | bytes 8388624 | tf_op jit(solution)/shard_map/all_gather | solution.py:222
  66.9 32.2 %shard_map.149 = f32[2,2,256,64]{3,2,1,0:T(8,128)} custom-call(s32[8]{0:T(128)} %bitcast.72, s32[16]{0:T(128)} %pad_add_fusion.bound_ref, bf16[2,2,256,64]{3,2,1,0:T(8,128)(2,1)} %bitcast.56, bf16[2,256,64]{2,1,0:T(8,128)(2,1)} %maximum_bitcast_fusion.k_ref, bf16[2,256,64]{2,1,0:T(8,128)(2,1)} %bitcast.55, s32[256,1]{1,0:T(8,128)} %copy.56.segq_ref, ...), custom_call_target="tpu_custom_call" | custom-call | tf_op jit(solution)/shard_map/pallas_call | solution.py:167
  99.1 1.1 convert_bitcast_fusion
  100.3 1.5 collective-permute-start.3
  101.8 2.4 %collective-permute-start.4 = (bf16[256,256]{0,1:T(8,128)(2,1)S(1)}, bf16[256,256]{0,1:T(8,128)(2,1)S(1)}, u32[]{:S(2)}, u32[]{:S(2)}) collective-permute-start(bf16[256,256]{0,1:T(8,128)(2,1)S(1)} %bitcast.62), channel_id=1, source_target_pairs={{0,2},{1,3},{2,0},{3,1},{4,6},{5,7},{6,4},{7,5},{8,10},{9,11},{10,... | collective-permute-start | bytes 393224 | tf_op jit(solution)/shard_map/ppermute | solution.py:71
  104.3 1.4 collective-permute-start.5
  105.8 2.9 %collective-permute-done.3 = bf16[256,256]{0,1:T(8,128)(2,1)S(1)} collective-permute-done((bf16[256,256]{0,1:T(8,128)(2,1)S(1)}, bf16[256,256]{0,1:T(8,128)(2,1)S(1)}, u32[]{:S(2)}, u32[]{:S(2)}) %collective-permute-start.3) | collective-permute-done | bytes 131104 | tf_op jit(solution)/shard_map/ppermute | solution.py:71
  108.6 4.5 %collective-permute-done.4 = bf16[256,256]{0,1:T(8,128)(2,1)S(1)} collective-permute-done((bf16[256,256]{0,1:T(8,128)(2,1)S(1)}, bf16[256,256]{0,1:T(8,128)(2,1)S(1)}, u32[]{:S(2)}, u32[]{:S(2)}) %collective-permute-start.4) | collective-permute-done | bytes 131104 | tf_op jit(solution)/shard_map/ppermute | solution.py:71
  113.2 2.4 %fusion.15 = (f32[256]{0:T(256)S(1)}, bf16[256,1024]{1,0:T(8,128)(2,1)S(1)}) fusion(bf16[256,1024]{1,0:T(8,128)(2,1)} %collective-permute-done.8, bf16[256,1024]{1,0:T(8,128)(2,1)} %collective-permute-done.7, bf16[256,1024]{1,0:T(8,128)(2,1)} %copy-done.8, bf16[256,1024]{1,0:T(8,128)(2,1)} %param.22, bf16[256,256]{0,1:T(8,128)(2,1)S(1)} %collective-permute-done.5, ...), kind=kOutput, calls=%fused_computation.22 | convolution fusion | flops 550764288 | bytes 3671040 | tf_op jit(solution)/shard_map/dot_general | solution.py:230
  115.6 7.5 %all-gather.6.cloned.1.call-done = bf16[16,2,1024,128]{3,2,0,1:T(8,128)(2,1)} async-done(((bf16[2,2,1024,128]{3,2,0,1:T(8,128)(2,1)}), bf16[16,2,1024,128]{3,2,0,1:T(8,128)(2,1)}) %all-gather.6.cloned.1.call-update) | async-done | bytes 8388624 | tf_op jit(solution)/shard_map/all_gather | solution.py:236
  123.1 4.9 %fusion.1 = f32[256,16,128]{2,0,1:T(8,128)} fusion(bf16[16,2,1024,128]{3,2,0,1:T(8,128)(2,1)} %all-gather.6.cloned.1.call-done, bf16[256,1024]{1,0:T(8,128)(2,1)S(1)} %get-tuple-element.36, f32[1024]{0:T(1024)S(1)} %copy-done.10, f32[256]{0:T(256)S(1)} %add_rsqrt_fusion), kind=kOutput, calls=%fused_computation.5 | convolution fusion | flops 1074790400 | bytes 6820864 | tf_op jit(solution)/shard_map/td,edf->tef/dot_general | solution.py:243
  128.0 33.6 %all-gather.8.cloned.1.call-done = bf16[16,128,1024]{2,1,0:T(8,128)(2,1)} async-done(((bf16[2,128,1024]{2,1,0:T(8,128)(2,1)}), bf16[16,128,1024]{2,1,0:T(8,128)(2,1)}) %all-gather.8.cloned.1.call-update) | async-done | bytes 4194320 | tf_op jit(solution)/shard_map/all_gather | solution.py:237
  161.6 6.5 %convolution_bitcast_fusion = f32[256,1024]{1,0:T(8,128)S(1)} fusion(bf16[16,128,1024]{2,1,0:T(8,128)(2,1)} %all-gather.8.cloned.1.call-done, f32[256,16,128]{2,0,1:T(8,128)} %fusion.1, bf16[16,2,1024,128]{3,2,0,1:T(8,128)(2,1)} %all-gather.6.cloned.1.call-done, f32[256,16]{0,1:T(8,128)S(1)} %select_reduce_fusion, ...), kind=kOutput, calls=%fused_computation.18 | convolution fusion | flops 2152202240 | bytes 12080128 | tf_op jit(solution)/shard_map/tef,efd->td/dot_general | solution.py:250
  168.2 2.5 %collective-permute-start.10 = (bf16[256,256]{1,0:T(8,128)(2,1)S(1)}, bf16[256,256]{1,0:T(8,128)(2,1)S(1)}, u32[]{:S(2)}, u32[]{:S(2)}) collective-permute-start(bf16[256,256]{1,0:T(8,128)(2,1)S(1)} %get-tuple-element.22), channel_id=1, source_target_pairs={{0,2},{1,3},{2,0},{3,1},{4,6},{5,7},{6,4},{7,5},{8,10},{9,11},{10,... | collective-permute-start | bytes 393224 | tf_op jit(solution)/shard_map/ppermute | solution.py:260
  170.7 1.4 collective-permute-start.11
  172.1 0.6 collective-permute-start.9
  172.9 0.6 scatter_fusion
  173.5 0.8 copy.60
  174.3 4.5 %collective-permute-done.10 = bf16[256,256]{1,0:T(8,128)(2,1)S(1)} collective-permute-done((bf16[256,256]{1,0:T(8,128)(2,1)S(1)}, bf16[256,256]{1,0:T(8,128)(2,1)S(1)}, u32[]{:S(2)}, u32[]{:S(2)}) %collective-permute-start.10) | collective-permute-done | bytes 131104 | tf_op jit(solution)/shard_map/ppermute | solution.py:260
  178.8 2.7 %collective-permute-done.9 = bf16[256,256]{1,0:T(8,128)(2,1)S(1)} collective-permute-done((bf16[256,256]{1,0:T(8,128)(2,1)S(1)}, bf16[256,256]{1,0:T(8,128)(2,1)S(1)}, u32[]{:S(2)}, u32[]{:S(2)}) %collective-permute-start.9) | collective-permute-done | bytes 131104 | tf_op jit(solution)/shard_map/ppermute | solution.py:260
  181.5 1.6 add_convert_fusion.1
  (57 shorter events, 1.2 us)
Async XLA Ops:
  7.2 19.0 %copy-start = (bf16[1024,256]{1,0:T(8,128)(2,1)S(1)}, bf16[1024,256]{1,0:T(8,128)(2,1)}, u32[]{:S(2)}) copy-start(bf16[1024,256]{1,0:T(8,128)(2,1)} %param.20) | copy-start | bytes 1572868
  7.2 19.0 %copy-start.9 = (f32[1024]{0:T(1024)S(1)}, f32[1024]{0:T(1024)}, u32[]{:S(2)}) copy-start(f32[1024]{0:T(1024)} %param.19) | copy-start | bytes 12292
  7.2 59.7 %all-gather.4.cloned.1.call-start = ((), (), s32[]{:S(2)}) async-start(), calls=%async_computation | async-start | bytes 9437184 | tf_op jit(solution)/shard_map/all_gather | solution.py:222
  9.7 113.4 %all-gather.6.cloned.1.call-start = ((), (), s32[]{:S(2)}) async-start(), calls=%async_computation.1 | async-start | bytes 9437184 | tf_op jit(solution)/shard_map/all_gather | solution.py:236
  9.7 9.8 %collective-permute-start = (bf16[256,256]{1,0:T(8,128)(2,1)}, bf16[256,256]{1,0:T(8,128)(2,1)S(1)}, u32[]{:S(2)}, u32[]{:S(2)}) collective-permute-start(bf16[256,256]{1,0:T(8,128)(2,1)} %param.14), channel_id=1, source_target_pairs={{0,1},{1,2},{2,3},{3,0},{4,5},{5,6},{6,7},{7,4},{8,9},{9,10},{10,1... | collective-permute-start | bytes 393224 | tf_op jit(solution)/shard_map/ppermute | solution.py:71
  12.8 11.4 %collective-permute-start.1 = (bf16[256,256]{1,0:T(8,128)(2,1)}, bf16[256,256]{1,0:T(8,128)(2,1)S(1)}, u32[]{:S(2)}, u32[]{:S(2)}) collective-permute-start(bf16[256,256]{1,0:T(8,128)(2,1)} %param.14), channel_id=1, source_target_pairs={{0,2},{1,3},{2,0},{3,1},{4,6},{5,7},{6,4},{7,5},{8,10},{9,11},{10,... | collective-permute-start | bytes 393224 | tf_op jit(solution)/shard_map/ppermute | solution.py:71
  15.4 8.9 %collective-permute-start.2 = (bf16[256,256]{1,0:T(8,128)(2,1)}, bf16[256,256]{1,0:T(8,128)(2,1)S(1)}, u32[]{:S(2)}, u32[]{:S(2)}) collective-permute-start(bf16[256,256]{1,0:T(8,128)(2,1)} %param.14), channel_id=1, source_target_pairs={{0,3},{1,0},{2,1},{3,2},{4,7},{5,4},{6,5},{7,6},{8,11},{9,8},{10,9... | collective-permute-start | bytes 393224 | tf_op jit(solution)/shard_map/ppermute | solution.py:71
  26.0 2.1 %copy-start.2 = (bf16[2,2,1024,128]{3,2,1,0:T(8,128)(2,1)S(1)}, bf16[2,2,1024,128]{3,2,1,0:T(8,128)(2,1)}, u32[]{:S(2)}) copy-start(bf16[2,2,1024,128]{3,2,1,0:T(8,128)(2,1)} %param.26) | copy-start | bytes 3145732
  26.7 9.0 %copy-start.4 = (s32[1,256]{1,0:T(1,128)S(1)}, s32[1,256]{1,0:T(1,128)}, u32[]{:S(2)}) copy-start(s32[1,256]{1,0:T(1,128)} %segk_ref.1) | copy-start | bytes 3076
  27.3 10.0 %copy-start.7 = (bf16[1024,256]{1,0:T(8,128)(2,1)S(1)}, bf16[1024,256]{1,0:T(8,128)(2,1)}, u32[]{:S(2)}) copy-start(bf16[1024,256]{1,0:T(8,128)(2,1)} %param.21) | copy-start | bytes 1572868
  29.2 132.4 %all-gather.8.cloned.1.call-start = ((), (), s32[]{:S(2)}) async-start(), calls=%async_computation.2 | async-start | bytes 4718592 | tf_op jit(solution)/shard_map/all_gather | solution.py:237
  29.9 74.3 %collective-permute-start.6 = (bf16[256,1024]{1,0:T(8,128)(2,1)}, bf16[256,1024]{1,0:T(8,128)(2,1)S(1)}, u32[]{:S(2)}, u32[]{:S(2)}) collective-permute-start(bf16[256,1024]{1,0:T(8,128)(2,1)} %param.22), channel_id=1, source_target_pairs={{0,1},{1,2},{2,3},{3,0},{4,5},{5,6},{6,7},{7,4},{8,9},{9,10},{10,1... | collective-permute-start | bytes 1572872 | tf_op jit(solution)/shard_map/ppermute | solution.py:71
  33.3 72.5 %collective-permute-start.7 = (bf16[256,1024]{1,0:T(8,128)(2,1)}, bf16[256,1024]{1,0:T(8,128)(2,1)}, u32[]{:S(2)}, u32[]{:S(2)}) collective-permute-start(bf16[256,1024]{1,0:T(8,128)(2,1)} %param.22), channel_id=1, source_target_pairs={{0,2},{1,3},{2,0},{3,1},{4,6},{5,7},{6,4},{7,5},{8,10},{9,11},{10,... | collective-permute-start | bytes 1572872 | tf_op jit(solution)/shard_map/ppermute | solution.py:71
  34.9 70.8 %collective-permute-start.8 = (bf16[256,1024]{1,0:T(8,128)(2,1)}, bf16[256,1024]{1,0:T(8,128)(2,1)}, u32[]{:S(2)}, u32[]{:S(2)}) collective-permute-start(bf16[256,1024]{1,0:T(8,128)(2,1)} %param.22), channel_id=1, source_target_pairs={{0,3},{1,0},{2,1},{3,2},{4,7},{5,4},{6,5},{7,6},{8,11},{9,8},{10,9... | collective-permute-start | bytes 1572872 | tf_op jit(solution)/shard_map/ppermute | solution.py:71
  66.9 38.8 %copy-start.5 = (f32[256,8]{0,1:T(8,128)S(1)}, f32[256,8]{0,1:T(8,128)}, u32[]{:S(2)}) copy-start(f32[256,8]{0,1:T(8,128)} %param.25) | copy-start | bytes 24580
  66.9 38.8 %copy-start.6 = (s32[256,8]{0,1:T(8,128)S(1)}, s32[256,8]{0,1:T(8,128)}, u32[]{:S(2)}) copy-start(s32[256,8]{0,1:T(8,128)} %param.24) | copy-start | bytes 24580
  100.3 8.3 %collective-permute-start.3 = (bf16[256,256]{0,1:T(8,128)(2,1)S(1)}, bf16[256,256]{0,1:T(8,128)(2,1)S(1)}, u32[]{:S(2)}, u32[]{:S(2)}) collective-permute-start(bf16[256,256]{0,1:T(8,128)(2,1)S(1)} %bitcast.61), channel_id=1, source_target_pairs={{0,1},{1,2},{2,3},{3,0},{4,5},{5,6},{6,7},{7,4},{8,9},{9,10},{10,1... | collective-permute-start | bytes 393224 | tf_op jit(solution)/shard_map/ppermute | solution.py:71
  101.8 11.3 %collective-permute-start.4 = (bf16[256,256]{0,1:T(8,128)(2,1)S(1)}, bf16[256,256]{0,1:T(8,128)(2,1)S(1)}, u32[]{:S(2)}, u32[]{:S(2)}) collective-permute-start(bf16[256,256]{0,1:T(8,128)(2,1)S(1)} %bitcast.62), channel_id=1, source_target_pairs={{0,2},{1,3},{2,0},{3,1},{4,6},{5,7},{6,4},{7,5},{8,10},{9,11},{10,... | collective-permute-start | bytes 393224 | tf_op jit(solution)/shard_map/ppermute | solution.py:71
  104.3 8.9 %copy-start.8 = (bf16[256,1024]{1,0:T(8,128)(2,1)}, bf16[256,1024]{1,0:T(8,128)(2,1)S(1)}, u32[]{:S(2)}) copy-start(bf16[256,1024]{1,0:T(8,128)(2,1)S(1)} %collective-permute-done.6) | copy-start | bytes 1572868
  104.3 8.9 %collective-permute-start.5 = (bf16[256,256]{0,1:T(8,128)(2,1)S(1)}, bf16[256,256]{0,1:T(8,128)(2,1)S(1)}, u32[]{:S(2)}, u32[]{:S(2)}) collective-permute-start(bf16[256,256]{0,1:T(8,128)(2,1)S(1)} %bitcast.63), channel_id=1, source_target_pairs={{0,3},{1,0},{2,1},{3,2},{4,7},{5,4},{6,5},{7,6},{8,11},{9,8},{10,9... | collective-permute-start | bytes 393224 | tf_op jit(solution)/shard_map/ppermute | solution.py:71
  105.7 17.4 %copy-start.10 = (f32[1024]{0:T(1024)S(1)}, f32[1024]{0:T(1024)}, u32[]{:S(2)}) copy-start(f32[1024]{0:T(1024)} %param.23) | copy-start | bytes 12292
  115.6 46.0 %copy-start.3 = (bf16[256,1024]{1,0:T(8,128)(2,1)}, bf16[256,1024]{1,0:T(8,128)(2,1)S(1)}, u32[]{:S(2)}) copy-start(bf16[256,1024]{1,0:T(8,128)(2,1)S(1)} %get-tuple-element.36) | copy-start | bytes 1572868
  128.0 44.7 %copy-start.11 = (s32[1,2]{1,0:T(1,128)S(1)}, s32[1,2]{1,0:T(1,128)}, u32[]{:S(2)}) copy-start(s32[1,2]{1,0:T(1,128)} %param.18) | copy-start | bytes 28
  128.0 44.7 %copy-start.1 = (bf16[256,2,64]{2,0,1:T(8,128)(2,1)S(1)}, bf16[256,2,64]{2,0,1:T(8,128)(2,1)}, u32[]{:S(2)}) copy-start(bf16[256,2,64]{2,0,1:T(8,128)(2,1)} %copy.65) | copy-start | bytes 196612
  168.2 10.6 %collective-permute-start.10 = (bf16[256,256]{1,0:T(8,128)(2,1)S(1)}, bf16[256,256]{1,0:T(8,128)(2,1)S(1)}, u32[]{:S(2)}, u32[]{:S(2)}) collective-permute-start(bf16[256,256]{1,0:T(8,128)(2,1)S(1)} %get-tuple-element.22), channel_id=1, source_target_pairs={{0,2},{1,3},{2,0},{3,1},{4,6},{5,7},{6,4},{7,5},{8,10},{9,11},{10,... | collective-permute-start | bytes 393224 | tf_op jit(solution)/shard_map/ppermute | solution.py:260
  170.7 8.1 %collective-permute-start.11 = (bf16[256,256]{1,0:T(8,128)(2,1)S(1)}, bf16[256,256]{1,0:T(8,128)(2,1)S(1)}, u32[]{:S(2)}, u32[]{:S(2)}) collective-permute-start(bf16[256,256]{1,0:T(8,128)(2,1)S(1)} %get-tuple-element.21), channel_id=1, source_target_pairs={{0,3},{1,0},{2,1},{3,2},{4,7},{5,4},{6,5},{7,6},{8,11},{9,8},{10,9... | collective-permute-start | bytes 393224 | tf_op jit(solution)/shard_map/ppermute | solution.py:260
  172.1 9.4 %collective-permute-start.9 = (bf16[256,256]{1,0:T(8,128)(2,1)S(1)}, bf16[256,256]{1,0:T(8,128)(2,1)S(1)}, u32[]{:S(2)}, u32[]{:S(2)}) collective-permute-start(bf16[256,256]{1,0:T(8,128)(2,1)S(1)} %get-tuple-element.20), channel_id=1, source_target_pairs={{0,1},{1,2},{2,3},{3,0},{4,5},{5,6},{6,7},{7,4},{8,9},{9,10},{10,1... | collective-permute-start | bytes 393224 | tf_op jit(solution)/shard_map/ppermute | solution.py:260
Sparse Core Ops, SparseCore 0:
  9.9 56.9 all-gather.3
  68.8 54.2 all-gather.5
  125.0 36.5 all-gather.7
where the time goes:
time: 191 us; the launch traced here: 190 us
  waiting for transfers between devices  89.6 us (47%)
  Pallas kernels  32.2 us (17%)
  starting transfers between devices  22.8 us (12%)
  matrix products  14.7 us (8%)
  between operations  14 us (7%)
  other arithmetic  8.25 us (4%)
  local copies, waits for them, and re-layouts  8.04 us (4%)
    all_gather x1, waiting for transfers between devices, shards(): all_down = lax.all_gather(w_down, 'req', axis=0, tiled=True)  33.6 us
    pallas_call x1, Pallas kernels, attend(): pl.pallas_call(attention_body, grid_spec=grid_spec, out_shape=jax.ShapeDt...  32.2 us
    all_gather x1, waiting for transfers between devices, shards(): gathered = lax.all_gather(prefix_cache, 'req', axis=0, tiled=True)  27.3 us
    ppermute x9, starting transfers between devices, shifted_copies(): copies.append(lax.ppermute(block, axis_name, pairs))  18.2 us
    ppermute x9, waiting for transfers between devices, shifted_copies(): copies.append(lax.ppermute(block, axis_name, pairs))  13.4 us
    all_gather x1, waiting for transfers between devices, shards(): all_gate_up = lax.all_gather(w_gate_up, 'req', axis=0, tiled=True)  7.5 us
    ppermute x3, waiting for transfers between devices, shards(): incoming = lax.ppermute(outgoing.astype(jnp.bfloat16), 'hid', pairs)  7.17 us
    dot_general x1, matrix products, shards(): jnp.einsum('tef,efd->td', hidden, all_down, preferred_element_type=jnp.fl...  6.49 us
  transfers between devices with their start and end apart: 15, of which 9 were waited for; matrix products, arithmetic and copies ran while one was open for 11% of the time, Pallas kernels for 17%

commit v1 on v0

--- a/solution.py
+++ b/solution.py
@@ -1,3 +1,5 @@
+import functools
+
 import jax
 import jax.numpy as jnp
 from jax import lax
@@ -174,6 +176,100 @@
         interpret=interpret,
     )(group_row, bounds, query_heads, key_heads, value_heads, seg_col, seg_line, prefix_heads)
     return out.transpose(2, 0, 1, 3).reshape(tok_count, -1).astype(jnp.bfloat16)
+
+
+def owner_body(local_groups, me_ref, group_ref, bound_ref, q_ref, segq_ref, prefix_ref, o_ref, lse_ref):
+    row = pl.program_id(1)
+    block = pl.program_id(2)
+    seg = pl.program_id(3)
+    seg_count = pl.num_programs(3)
+    rows = q_ref.shape[2]
+    head_dim = q_ref.shape[3]
+
+    @pl.when(seg == 0)
+    def _():
+        o_ref[...] = jnp.zeros_like(o_ref)
+        lse_ref[...] = jnp.zeros_like(lse_ref)
+
+    group = group_ref[row * seg_count + seg]
+    first = bound_ref[row * 2 * seg_count + seg]
+    last = bound_ref[row * 2 * seg_count + seg_count + seg]
+    active = (
+        (group // local_groups == me_ref[0]) & (first < (block + 1) * rows) & (last > block * rows)
+    )
+
+    @pl.when(active)
+    def _():
+        prefix = prefix_ref[0, 0]
+        prefix_keys = prefix[:, :head_dim]
+        prefix_values = prefix[:, head_dim:]
+        mine = segq_ref[...] == seg
+        contract = (((1,), (1,)), ((), ()))
+        for q_group in range(q_ref.shape[1]):
+            scores = (
+                lax.dot_general(
+                    q_ref[0, q_group], prefix_keys, contract, preferred_element_type=jnp.float32
+                )
+                * head_dim ** (-0.5)
+            )
+            top = jnp.max(scores, axis=1, keepdims=True)
+            numerators = jnp.exp(scores - top)
+            total = jnp.sum(numerators, axis=1, keepdims=True)
+            summed = jnp.dot(
+                numerators.astype(jnp.bfloat16), prefix_values, preferred_element_type=jnp.float32
+            )
+            o_ref[0, q_group] = jnp.where(mine, summed / total, o_ref[0, q_group])
+            lse_ref[0, q_group] = jnp.where(mine, top + jnp.log(total), lse_ref[0, q_group])
+
+
+def prefix_partials(query_all, segments_all, groups_all, prefix_local, me):
+    kv_heads, q_groups, all_tokens, head_dim = query_all.shape
+    row_count, tok_count = segments_all.shape
+    seg_count = groups_all.shape[1]
+    prefix_len = prefix_local.shape[2]
+    rows = min(128, tok_count)
+    blocks = tok_count // rows
+    local_groups = prefix_local.shape[0]
+    labels = jnp.arange(seg_count, dtype=jnp.int32)
+    first = jnp.sum((segments_all[:, None, :] < labels[None, :, None]).astype(jnp.int32), axis=2)
+    last = jnp.sum((segments_all[:, None, :] <= labels[None, :, None]).astype(jnp.int32), axis=2)
+    bounds = jnp.concatenate([first, last], axis=1).reshape(-1)
+    seg_col = segments_all.reshape(all_tokens, 1)
+    grid_spec = pltpu.PrefetchScalarGridSpec(
+        num_scalar_prefetch=3,
+        grid=(kv_heads, row_count, blocks, seg_count),
+        in_specs=[
+            pl.BlockSpec(
+                (1, q_groups, rows, head_dim),
+                lambda h, r, b, s, me, gr, bd: (h, 0, r * blocks + b, 0),
+            ),
+            pl.BlockSpec((rows, 1), lambda h, r, b, s, me, gr, bd: (r * blocks + b, 0)),
+            pl.BlockSpec(
+                (1, 1, prefix_len, 2 * head_dim),
+                lambda h, r, b, s, me, gr, bd: (gr[r * seg_count + s] % local_groups, h, 0, 0),
+            ),
+        ],
+        out_specs=[
+            pl.BlockSpec(
+                (1, q_groups, rows, head_dim),
+                lambda h, r, b, s, me, gr, bd: (h, 0, r * blocks + b, 0),
+            ),
+            pl.BlockSpec(
+                (1, q_groups, rows, 1), lambda h, r, b, s, me, gr, bd: (h, 0, r * blocks + b, 0)
+            ),
+        ],
+    )
+    return pl.pallas_call(
+        functools.partial(owner_body, local_groups),
+        grid_spec=grid_spec,
+        out_shape=(
+            jax.ShapeDtypeStruct((kv_heads, q_groups, all_tokens, head_dim), jnp.float32),
+            jax.ShapeDtypeStruct((kv_heads, q_groups, all_tokens, 1), jnp.float32),
+        ),
+        compiler_params=pltpu.CompilerParams(
+            dimension_semantics=("arbitrary", "arbitrary", "arbitrary", "arbitrary")
+        ),
+    )(me.reshape(1), groups_all.reshape(-1), bounds, query_all, seg_col, prefix_local)
 
 
 def shards(
@@ -207,7 +303,6 @@
         tok_count, -1, head_dim
     )
     queries = rotate(projected, position).astype(jnp.bfloat16)
-    queries, w_gate_up, w_down = lax.optimization_barrier((queries, w_gate_up, w_down))
     q_groups = queries.shape[1] // kv_heads
     grouped_query = queries.reshape(tok_count, kv_heads, q_groups, head_dim)
     key_value = jnp.dot(normed, w_keyval, preferred_element_type=jnp.float32).reshape(
@@ -219,11 +314,45 @@
         -1, PAGE, kv_heads, 2 * head_dim
     )
     kv_pages = jnp.zeros_like(pages).at[page_table[0]].set(pages)
-    gathered = lax.all_gather(prefix_cache, "req", axis=0, tiled=True)
-    attention = attend(
-        grouped_query, key_rows, value_rows, segment_row, prefix_group[0],
-        gathered.transpose(0, 2, 1, 3),
-    )
+    query_heads = grouped_query.transpose(1, 2, 0, 3)
+    query_all = lax.all_gather(query_heads, "req", axis=2, tiled=True)
+    segments_all = lax.all_gather(segments, "req", axis=0, tiled=True)
+    groups_all = lax.all_gather(prefix_group, "req", axis=0, tiled=True)
+    query_all, w_gate_up, w_down = lax.optimization_barrier((query_all, w_gate_up, w_down))
+    cached_out, cached_lse = prefix_partials(
+        query_all, segments_all, groups_all, prefix_cache.transpose(0, 2, 1, 3),
+        lax.axis_index("req"),
+    )
+    row_split = (kv_heads, q_groups, req_count, tok_count)
+    cached_out = lax.all_to_all(
+        cached_out.astype(jnp.bfloat16).reshape(row_split + (head_dim,)),
+        "req", split_axis=2, concat_axis=2, tiled=True,
+    )
+    cached_lse = lax.all_to_all(
+        cached_lse.reshape(row_split + (1,)), "req", split_axis=2, concat_axis=2, tiled=True
+    )
+    cached_out = jnp.sum(cached_out.astype(jnp.float32), axis=2)
+    cached_lse = jnp.sum(cached_lse, axis=2)
+    token_index = jnp.arange(tok_count, dtype=jnp.int32)
+    visible = (segment_row[None, :] == segment_row[:, None]) & (
+        token_index[None, :] <= token_index[:, None]
+    )
+    local_scores = (
+        jnp.einsum("tkgd,skd->kgts", grouped_query, key_rows, preferred_element_type=jnp.float32)
+        * score_scale
+    )
+    local_scores = jnp.where(visible[None, None], local_scores, -jnp.inf)
+    local_max = jnp.max(local_scores, axis=-1, keepdims=True)
+    local_num = jnp.exp(local_scores - local_max)
+    local_total = jnp.sum(local_num, axis=-1, keepdims=True)
+    local_out = jnp.einsum(
+        "kgts,skd->kgtd", local_num.astype(jnp.bfloat16), value_rows,
+        preferred_element_type=jnp.float32,
+    ) / local_total
+    local_lse = local_max + jnp.log(local_total)
+    joint_lse = jnp.logaddexp(local_lse, cached_lse)
+    merged = jnp.exp(local_lse - joint_lse) * local_out + jnp.exp(cached_lse - joint_lse) * cached_out
+    attention = merged.transpose(2, 0, 1, 3).reshape(tok_count, -1).astype(jnp.bfloat16)
     share_width = hidden_in.shape[1]
     whole_attention = jnp.concatenate(shifted_copies(attention, "hid"), axis=1)
     whole_w_out = jnp.concatenate(shifted_copies(w_out, "hid"), axis=0)

time: 191 us -> 291 us (1.52); the launches traced: 190 us -> 285 us
  Pallas kernels: 32.2 us -> 112 us
  waiting for transfers between devices: 89.6 us -> 59.3 us
  blocking collectives: 0 us -> 16.9 us
  starting transfers between devices: 22.8 us -> 37.4 us
  other arithmetic: 8.25 us -> 14.6 us
  local copies, waits for them, and re-layouts: 8.04 us -> 12.3 us
  matrix products: 14.7 us -> 18.3 us
    pallas_call x1, Pallas kernels: 32.2 us -> 112 us  [prefix_partials(): pl.pallas_call(functools.partial(owner_body, local_groups), grid_spec=gri...]
    all_gather x1, waiting for transfers between devices: 33.6 us -> 0.01 us  [shards(): all_down = lax.all_gather(w_down, 'req', axis=0, tiled=True)]
    all_gather x0 -> x2, blocking collectives: none -> 16.9 us  [the longest x1 9.04 us: shards(): segments_all = lax.all_gather(segments, 'req', axis=0, tiled=True)]
    all_to_all x0 -> x2, starting transfers between devices: none -> 16.5 us  [the longest x1 12.3 us: shards(): lax.all_to_all(cached_lse.reshape(row_split + (1,)), 'req', split_axis=2,...]
    all_to_all x0 -> x2, waiting for transfers between devices: none -> 10.9 us  [the longest x1 10.8 us: shards(): lax.all_to_all(cached_out.astype(jnp.bfloat16).reshape(row_split + (head_...]
    all_gather x1, waiting for transfers between devices: 7.5 us -> 0.02 us  [shards(): all_gate_up = lax.all_gather(w_gate_up, 'req', axis=0, tiled=True)]
    reshape x0 -> x6, local copies, waits for them, and re-layouts: none -> 4.91 us  [the longest x1 1.61 us: shards(): cached_out.astype(jnp.bfloat16).reshape(row_split + (head_dim,))]
    pallas_call x0 -> x1, other arithmetic: none -> 3.36 us  [prefix_partials(): pl.pallas_call(functools.partial(owner_body, local_groups), grid_spec=gri...]
  transfers between devices with their start and end apart: 15 -> 17, of which waited for: 9 -> 9; matrix products, arithmetic and copies ran while one was open for 11% -> 11% of each run, Pallas kernels for 17% -> 39%
where the time goes in v1:
time: 291 us; the launch traced here: 285 us
  Pallas kernels  112 us (38%)
  waiting for transfers between devices  59.3 us (20%)
  starting transfers between devices  37.4 us (13%)
  matrix products  18.3 us (6%)
  blocking collectives  16.9 us (6%)
  other arithmetic  14.6 us (5%)
  between operations  14.3 us (5%)
  local copies, waits for them, and re-layouts  12.3 us (4%)
    pallas_call x1, Pallas kernels, prefix_partials(): pl.pallas_call(functools.partial(owner_body, local_groups), grid_spec=gri...  112 us
    all_gather x1, waiting for transfers between devices, shards(): query_all = lax.all_gather(query_heads, 'req', axis=2, tiled=True)  29.9 us
    ppermute x9, starting transfers between devices, shifted_copies(): copies.append(lax.ppermute(block, axis_name, pairs))  16.3 us
    ppermute x9, waiting for transfers between devices, shifted_copies(): copies.append(lax.ppermute(block, axis_name, pairs))  12.4 us
    all_to_all x1, starting transfers between devices, shards(): lax.all_to_all(cached_lse.reshape(row_split + (1,)), 'req', split_axis=2,...  12.3 us
    all_to_all x1, waiting for transfers between devices, shards(): lax.all_to_all(cached_out.astype(jnp.bfloat16).reshape(row_split + (head_...  10.8 us
    all_gather x1, blocking collectives, shards(): segments_all = lax.all_gather(segments, 'req', axis=0, tiled=True)  9.04 us
    all_gather x1, blocking collectives, shards(): groups_all = lax.all_gather(prefix_group, 'req', axis=0, tiled=True)  7.88 us
  transfers between devices with their start and end apart: 17, of which 9 were waited for; matrix products, arithmetic and copies ran while one was open for 11% of the time, Pallas kernels for 39%

profile of v1, /device:TPU:0, one launch (start us, length us, event | category | flops | bytes accessed | tf_op | source)
XLA Modules:
  0.0 285.3 jit_solution(12826788206549652019)
XLA Ops:
  7.2 3.1 %collective-permute-start = (bf16[256,256]{1,0:T(8,128)(2,1)}, bf16[256,256]{1,0:T(8,128)(2,1)S(1)}, u32[]{:S(2)}, u32[]{:S(2)}) collective-permute-start(bf16[256,256]{1,0:T(8,128)(2,1)} %param.14), channel_id=1, source_target_pairs={{0,1},{1,2},{2,3},{3,0},{4,5},{5,6},{6,7},{7,4},{8,9},{9,10},{10,1... | collective-permute-start | bytes 393224 | tf_op jit(solution)/shard_map/ppermute | solution.py:73
  10.3 2.6 collective-permute-start.1
  12.9 1.3 collective-permute-start.2
  14.3 0.9 convert_reduce_fusion.1
  15.6 1.4 collective-permute-done
  17.0 4.8 %collective-permute-done.1 = bf16[256,256]{1,0:T(8,128)(2,1)S(1)} collective-permute-done((bf16[256,256]{1,0:T(8,128)(2,1)}, bf16[256,256]{1,0:T(8,128)(2,1)S(1)}, u32[]{:S(2)}, u32[]{:S(2)}) %collective-permute-start.1) | collective-permute-done | bytes 131104 | tf_op jit(solution)/shard_map/ppermute | solution.py:73
  21.8 1.0 pad_maximum_fusion
  24.9 0.8 fusion.52
  25.8 29.9 %all-gather.6.cloned.1.call-done.q_ref = bf16[2,2,2048,64]{3,2,1,0:T(8,128)(2,1)} async-done(((bf16[2,2,256,64]{3,2,1,0:T(8,128)(2,1)}), bf16[2,2,2048,64]{3,2,1,0:T(8,128)(2,1)}) %all-gather.6.cloned.1.call-update) | async-done | bytes 1048592 | tf_op jit(solution)/shard_map/all_gather | solution.py:318
  55.7 1.0 copy.70
  56.8 0.7 all-gather.10.cloned.1.call-update
  57.5 1.5 collective-permute-start.6
  59.0 2.4 collective-permute-start.7
  61.4 1.4 collective-permute-start.8
  62.9 9.0 %all-gather.1 = s32[8,1,256]{2,1,0:T(1,128)S(1)} all-gather(s32[1,1,256]{2,1,0:T(1,128)S(1)} %bitcast.140), channel_id=1, replica_groups=mesh['req'=8,'hid'=4] {'req'}, dimensions={0}, use_global_device_ids=true | all-gather | bytes 9216 | tf_op jit(solution)/shard_map/all_gather | solution.py:319
  73.0 1.4 copy.64.segq_ref
  74.4 1.2 copy.83
  75.6 7.9 %all-gather = s32[8,1,8]{2,1,0:T(1,128)S(1)} all-gather(s32[1,1,8]{2,1,0:T(1,128)S(1)} %bitcast.143), channel_id=1, replica_groups=mesh['req'=8,'hid'=4] {'req'}, dimensions={0}, use_global_device_ids=true | all-gather | bytes 288 | tf_op jit(solution)/shard_map/all_gather | solution.py:320
  84.0 0.7 reduce.5
  85.3 112.3 %shard_map.152 = (f32[2,2,2048,64]{3,2,1,0:T(8,128)}, f32[2,2,2048,1]{3,2,1,0:T(8,128)}) custom-call(s32[1]{0:T(128)} %bitcast.19.me_ref, s32[64]{0:T(128)} %reshape.297.group_ref, s32[128]{0:T(128)} %reshape.298.bound_ref, bf16[2,2,2048,64]{3,2,1,0:T(8,128)(2,1)} %all-gather.6.cloned.1.call-done.q_ref, s32[2048,1]{1,0:T(8,128)} %copy.64.segq_ref, ...), custom_call_target="tpu_custom_call" | custom-call | tf_op jit(solution)/shard_map/pallas_call | solution.py:262
  197.6 3.4 %reduce.2 = f32[2,2,2048]{2,1,0:T(2,128)S(1)} reduce(f32[2,2,2048,1]{3,2,1,0:T(8,128)} %get-tuple-element.8, f32[]{:T(128)} %constant.97), dimensions={3}, to_apply=%get-tuple-element.8.reduce_sub_computation | reduce | bytes 65540 | tf_op jit(solution)/shard_map/pallas_call | solution.py:262
  201.0 0.6 copy.65
  201.6 12.3 %all-to-all-start = ((f32[2,2,8,256,1]{3,1,0,4,2:T(2,128)}), f32[2,2,8,256,1]{3,1,0,4,2:T(2,128)}, u32[]{:S(2)}, u32[]{:S(2)}) async-start(f32[2,2,8,256,1]{3,1,0,4,2:T(2,128)} %copy.65), calls=%async_computation | async-start | bytes 65536 | tf_op jit(solution)/shard_map/all_to_all | solution.py:331
  213.9 0.7 fusion.44
  214.7 2.5 convert_element_type.86
  217.2 1.6 copy.67
  218.9 4.2 %all-to-all-start.1 = ((bf16[2,2,8,256,64]{3,4,1,0,2:T(8,128)(2,1)}), bf16[2,2,8,256,64]{3,4,1,0,2:T(8,128)(2,1)S(1)}, u32[]{:S(2)}, u32[]{:S(2)}) async-start(bf16[2,2,8,256,64]{3,4,1,0,2:T(8,128)(2,1)} %copy.67), calls=%async_computation.1 | async-start | bytes 2097152 | tf_op jit(solution)/shard_map/all_to_all | solution.py:327
  223.1 1.6 fusion.47
  225.4 1.3 fusion.70
  226.9 0.8 reduce_sum.93
  227.7 10.8 %all-to-all-done.1 = bf16[2,2,8,256,64]{3,4,1,0,2:T(8,128)(2,1)S(1)} async-done(((bf16[2,2,8,256,64]{3,4,1,0,2:T(8,128)(2,1)}), bf16[2,2,8,256,64]{3,4,1,0,2:T(8,128)(2,1)S(1)}, u32[]{:S(2)}, u32[]{:S(2)}) %all-to-all-start.1) | async-done | bytes 1048608 | tf_op jit(solution)/shard_map/all_to_all | solution.py:327
  238.6 1.2 fusion.20
  239.8 0.8 collective-permute-start.3
  240.9 2.8 collective-permute-start.5
  243.7 0.7 select_reduce_fusion
  244.5 2.7 collective-permute-done.3
  247.1 3.6 %collective-permute-done.4 = bf16[256,256]{0,1:T(8,128)(2,1)S(1)} collective-permute-done((bf16[256,256]{0,1:T(8,128)(2,1)S(1)}, bf16[256,256]{0,1:T(8,128)(2,1)S(1)}, u32[]{:S(2)}, u32[]{:S(2)}) %collective-permute-start.4) | collective-permute-done | bytes 131104 | tf_op jit(solution)/shard_map/ppermute | solution.py:73
  250.8 2.4 fusion.21
  253.2 5.0 %fusion.1 = f32[256,16,128]{2,0,1:T(8,128)} fusion(bf16[16,2,1024,128]{3,2,0,1:T(8,128)(2,1)} %all-gather.8.cloned.1.call-done, bf16[256,1024]{1,0:T(8,128)(2,1)S(1)} %get-tuple-element.42, f32[1024]{0:T(1024)S(1)} %copy-done.23, f32[256]{0:T(256)S(1)} %add_rsqrt_fusion), kind=kOutput, calls=%fused_computation.5 | convolution fusion | flops 1074790400 | bytes 6820864 | tf_op jit(solution)/shard_map/td,edf->tef/dot_general | solution.py:372
  258.2 6.5 %convolution_bitcast_fusion = f32[256,1024]{1,0:T(8,128)S(1)} fusion(bf16[16,128,1024]{2,1,0:T(8,128)(2,1)} %all-gather.10.cloned.1.call-done, f32[256,16,128]{2,0,1:T(8,128)} %fusion.1, bf16[16,2,1024,128]{3,2,0,1:T(8,128)(2,1)} %all-gather.8.cloned.1.call-done, f32[256,16]{0,1:T(8,128)S(1)} %select_reduce_fusion, ...), kind=kOutput, calls=%fused_computation.19 | convolution fusion | flops 2152202240 | bytes 12080128 | tf_op jit(solution)/shard_map/tef,efd->td/dot_general | solution.py:379
  264.8 1.1 collective-permute-start.10
  265.9 3.4 %collective-permute-start.11 = (bf16[256,256]{1,0:T(8,128)(2,1)S(1)}, bf16[256,256]{1,0:T(8,128)(2,1)S(1)}, u32[]{:S(2)}, u32[]{:S(2)}) collective-permute-start(bf16[256,256]{1,0:T(8,128)(2,1)S(1)} %get-tuple-element.25), channel_id=1, source_target_pairs={{0,3},{1,0},{2,1},{3,2},{4,7},{5,4},{6,5},{7,6},{8,11},{9,8},{10,9... | collective-permute-start | bytes 393224 | tf_op jit(solution)/shard_map/ppermute | solution.py:389
  269.2 0.9 slice.78
  270.4 0.6 scatter_fusion
  271.0 0.8 copy.72
  271.8 3.4 %collective-permute-done.10 = bf16[256,256]{1,0:T(8,128)(2,1)S(1)} collective-permute-done((bf16[256,256]{1,0:T(8,128)(2,1)S(1)}, bf16[256,256]{1,0:T(8,128)(2,1)S(1)}, u32[]{:S(2)}, u32[]{:S(2)}) %collective-permute-start.10) | collective-permute-done | bytes 131104 | tf_op jit(solution)/shard_map/ppermute | solution.py:389
  275.2 2.0 collective-permute-done.9
  277.2 1.6 add_convert_fusion.1
  (102 shorter events, 6.5 us)
Async XLA Ops:
  7.2 16.6 %copy-start = (bf16[1024,256]{1,0:T(8,128)(2,1)S(1)}, bf16[1024,256]{1,0:T(8,128)(2,1)}, u32[]{:S(2)}) copy-start(bf16[1024,256]{1,0:T(8,128)(2,1)} %param.20) | copy-start | bytes 1572868
  7.2 16.6 %copy-start.21 = (f32[1024]{0:T(1024)S(1)}, f32[1024]{0:T(1024)}, u32[]{:S(2)}) copy-start(f32[1024]{0:T(1024)} %param.19) | copy-start | bytes 12292
  7.2 48.5 %all-gather.6.cloned.1.call-start = ((), (), s32[]{:S(2)}) async-start(), calls=%async_computation.2 | async-start | bytes 2359296 | tf_op jit(solution)/shard_map/all_gather | solution.py:318
  7.2 9.8 %collective-permute-start = (bf16[256,256]{1,0:T(8,128)(2,1)}, bf16[256,256]{1,0:T(8,128)(2,1)S(1)}, u32[]{:S(2)}, u32[]{:S(2)}) collective-permute-start(bf16[256,256]{1,0:T(8,128)(2,1)} %param.14), channel_id=1, source_target_pairs={{0,1},{1,2},{2,3},{3,0},{4,5},{5,6},{6,7},{7,4},{8,9},{9,10},{10,1... | collective-permute-start | bytes 393224 | tf_op jit(solution)/shard_map/ppermute | solution.py:73
  10.3 11.4 %collective-permute-start.1 = (bf16[256,256]{1,0:T(8,128)(2,1)}, bf16[256,256]{1,0:T(8,128)(2,1)S(1)}, u32[]{:S(2)}, u32[]{:S(2)}) collective-permute-start(bf16[256,256]{1,0:T(8,128)(2,1)} %param.14), channel_id=1, source_target_pairs={{0,2},{1,3},{2,0},{3,1},{4,6},{5,7},{6,4},{7,5},{8,10},{9,11},{10,... | collective-permute-start | bytes 393224 | tf_op jit(solution)/shard_map/ppermute | solution.py:73
  12.9 8.9 %collective-permute-start.2 = (bf16[256,256]{1,0:T(8,128)(2,1)}, bf16[256,256]{1,0:T(8,128)(2,1)S(1)}, u32[]{:S(2)}, u32[]{:S(2)}) collective-permute-start(bf16[256,256]{1,0:T(8,128)(2,1)} %param.14), channel_id=1, source_target_pairs={{0,3},{1,0},{2,1},{3,2},{4,7},{5,4},{6,5},{7,6},{8,11},{9,8},{10,9... | collective-permute-start | bytes 393224 | tf_op jit(solution)/shard_map/ppermute | solution.py:73
  15.4 6.4 %copy-start.8 = (f32[256,32]{0,1:T(8,128)}, f32[256,32]{0,1:T(8,128)S(1)}, u32[]{:S(2)}) copy-start(f32[256,32]{0,1:T(8,128)S(1)} %get-tuple-element.37) | copy-start | bytes 98308
  15.4 6.4 %copy-start.10 = (f32[256,32]{0,1:T(8,128)}, f32[256,32]{0,1:T(8,128)S(1)}, u32[]{:S(2)}) copy-start(f32[256,32]{0,1:T(8,128)S(1)} %get-tuple-element.38) | copy-start | bytes 98308
  23.5 0.7 copy-start.3
  23.5 0.7 copy-start.5
  23.6 0.9 copy-start.7
  23.6 32.1 %copy-start.1 = (bf16[2,2,1024,128]{3,2,1,0:T(8,128)(2,1)S(1)}, bf16[2,2,1024,128]{3,2,1,0:T(8,128)(2,1)}, u32[]{:S(2)}) copy-start(bf16[2,2,1024,128]{3,2,1,0:T(8,128)(2,1)} %param.26) | copy-start | bytes 3145732
  24.3 38.6 %copy-start.18 = (s32[1,256]{1,0:T(1,128)S(1)}, s32[1,256]{1,0:T(1,128)}, u32[]{:S(2)}) copy-start(s32[1,256]{1,0:T(1,128)} %param.15) | copy-start | bytes 3076
  24.9 49.5 %copy-start.2 = (bf16[2,1024,2,128]{3,2,1,0:T(2,128)(2,1)S(1)}, bf16[2,1024,2,128]{3,2,1,0:T(2,128)(2,1)}, u32[]{:S(2)}) copy-start(bf16[2,1024,2,128]{3,2,1,0:T(2,128)(2,1)} %param.17) | copy-start | bytes 3145732
  24.9 50.7 %copy-start.20 = (s32[1,8]{1,0:T(1,128)S(1)}, s32[1,8]{1,0:T(1,128)}, u32[]{:S(2)}) copy-start(s32[1,8]{1,0:T(1,128)} %param.16) | copy-start | bytes 100
  25.8 227.4 %all-gather.8.cloned.1.call-start = ((), (), s32[]{:S(2)}) async-start(), calls=%async_computation.3 | async-start | bytes 9437184 | tf_op jit(solution)/shard_map/all_gather | solution.py:365
  56.7 201.4 %all-gather.10.cloned.1.call-start = ((), (), s32[]{:S(2)}) async-start(), calls=%async_computation.4 | async-start | bytes 4718592 | tf_op jit(solution)/shard_map/all_gather | solution.py:366
  57.5 183.4 %collective-permute-start.6 = (bf16[256,1024]{1,0:T(8,128)(2,1)}, bf16[256,1024]{1,0:T(8,128)(2,1)}, u32[]{:S(2)}, u32[]{:S(2)}) collective-permute-start(bf16[256,1024]{1,0:T(8,128)(2,1)} %param.22), channel_id=1, source_target_pairs={{0,1},{1,2},{2,3},{3,0},{4,5},{5,6},{6,7},{7,4},{8,9},{9,10},{10,1... | collective-permute-start | bytes 1572872 | tf_op jit(solution)/shard_map/ppermute | solution.py:73
  59.0 185.4 %collective-permute-start.7 = (bf16[256,1024]{1,0:T(8,128)(2,1)}, bf16[256,1024]{1,0:T(8,128)(2,1)}, u32[]{:S(2)}, u32[]{:S(2)}) collective-permute-start(bf16[256,1024]{1,0:T(8,128)(2,1)} %param.22), channel_id=1, source_target_pairs={{0,2},{1,3},{2,0},{3,1},{4,6},{5,7},{6,4},{7,5},{8,10},{9,11},{10,... | collective-permute-start | bytes 1572872 | tf_op jit(solution)/shard_map/ppermute | solution.py:73
  61.4 183.0 %collective-permute-start.8 = (bf16[256,1024]{1,0:T(8,128)(2,1)}, bf16[256,1024]{1,0:T(8,128)(2,1)}, u32[]{:S(2)}, u32[]{:S(2)}) collective-permute-start(bf16[256,1024]{1,0:T(8,128)(2,1)} %param.22), channel_id=1, source_target_pairs={{0,3},{1,0},{2,1},{3,2},{4,7},{5,4},{6,5},{7,6},{8,11},{9,8},{10,9... | collective-permute-start | bytes 1572872 | tf_op jit(solution)/shard_map/ppermute | solution.py:73
  201.6 17.3 %all-to-all-start = ((f32[2,2,8,256,1]{3,1,0,4,2:T(2,128)}), f32[2,2,8,256,1]{3,1,0,4,2:T(2,128)}, u32[]{:S(2)}, u32[]{:S(2)}) async-start(f32[2,2,8,256,1]{3,1,0,4,2:T(2,128)} %copy.65), calls=%async_computation | async-start | bytes 65536 | tf_op jit(solution)/shard_map/all_to_all | solution.py:331
  217.1 6.0 %copy-start.4 = (bf16[256,256]{1,0:T(8,128)(2,1)S(1)}, bf16[256,256]{1,0:T(8,128)(2,1)}, u32[]{:S(2)}) copy-start(bf16[256,256]{1,0:T(8,128)(2,1)} %copy-done.3) | copy-start | bytes 393220
  217.1 6.0 %copy-start.6 = (bf16[256,256]{1,0:T(8,128)(2,1)S(1)}, bf16[256,256]{1,0:T(8,128)(2,1)}, u32[]{:S(2)}) copy-start(bf16[256,256]{1,0:T(8,128)(2,1)} %copy-done.5) | copy-start | bytes 393220
  217.1 6.0 %copy-start.22 = (f32[1024]{0:T(1024)S(1)}, f32[1024]{0:T(1024)}, u32[]{:S(2)}) copy-start(f32[1024]{0:T(1024)} %param.19) | copy-start | bytes 12292
  218.8 6.0 %copy-start.9 = (f32[256,32]{0,1:T(8,128)S(1)}, f32[256,32]{0,1:T(8,128)}, u32[]{:S(2)}) copy-start(f32[256,32]{0,1:T(8,128)} %copy-done.8) | copy-start | bytes 98308
  218.8 6.0 %copy-start.11 = (f32[256,32]{0,1:T(8,128)S(1)}, f32[256,32]{0,1:T(8,128)}, u32[]{:S(2)}) copy-start(f32[256,32]{0,1:T(8,128)} %copy-done.10) | copy-start | bytes 98308
  218.9 19.6 %all-to-all-start.1 = ((bf16[2,2,8,256,64]{3,4,1,0,2:T(8,128)(2,1)}), bf16[2,2,8,256,64]{3,4,1,0,2:T(8,128)(2,1)S(1)}, u32[]{:S(2)}, u32[]{:S(2)}) async-start(bf16[2,2,8,256,64]{3,4,1,0,2:T(8,128)(2,1)} %copy.67), calls=%async_computation.1 | async-start | bytes 2097152 | tf_op jit(solution)/shard_map/all_to_all | solution.py:327
  223.1 20.6 %copy-start.19 = (f32[256,8]{0,1:T(8,128)S(1)}, f32[256,8]{0,1:T(8,128)}, u32[]{:S(2)}) copy-start(f32[256,8]{0,1:T(8,128)} %param.25) | copy-start | bytes 24580
  224.7 0.7 copy-start.16
  224.8 1.9 copy-start.12
  224.8 1.9 copy-start.14
  239.8 7.3 %collective-permute-start.3 = (bf16[256,256]{0,1:T(8,128)(2,1)S(1)}, bf16[256,256]{0,1:T(8,128)(2,1)S(1)}, u32[]{:S(2)}, u32[]{:S(2)}) collective-permute-start(bf16[256,256]{0,1:T(8,128)(2,1)S(1)} %bitcast.144), channel_id=1, source_target_pairs={{0,1},{1,2},{2,3},{3,0},{4,5},{5,6},{6,7},{7,4},{8,9},{9,10},{10,1... | collective-permute-start | bytes 393224 | tf_op jit(solution)/shard_map/ppermute | solution.py:73
  240.7 10.1 %collective-permute-start.4 = (bf16[256,256]{0,1:T(8,128)(2,1)S(1)}, bf16[256,256]{0,1:T(8,128)(2,1)S(1)}, u32[]{:S(2)}, u32[]{:S(2)}) collective-permute-start(bf16[256,256]{0,1:T(8,128)(2,1)S(1)} %bitcast.145), channel_id=1, source_target_pairs={{0,2},{1,3},{2,0},{3,1},{4,6},{5,7},{6,4},{7,5},{8,10},{9,11},{10,... | collective-permute-start | bytes 393224 | tf_op jit(solution)/shard_map/ppermute | solution.py:73
  240.9 9.9 %collective-permute-start.5 = (bf16[256,256]{0,1:T(8,128)(2,1)S(1)}, bf16[256,256]{0,1:T(8,128)(2,1)S(1)}, u32[]{:S(2)}, u32[]{:S(2)}) collective-permute-start(bf16[256,256]{0,1:T(8,128)(2,1)S(1)} %bitcast.146), channel_id=1, source_target_pairs={{0,3},{1,0},{2,1},{3,2},{4,7},{5,4},{6,5},{7,6},{8,11},{9,8},{10,9... | collective-permute-start | bytes 393224 | tf_op jit(solution)/shard_map/ppermute | solution.py:73
  244.4 8.7 %copy-start.23 = (f32[1024]{0:T(1024)S(1)}, f32[1024]{0:T(1024)}, u32[]{:S(2)}) copy-start(f32[1024]{0:T(1024)} %param.23) | copy-start | bytes 12292
  253.1 5.1 %copy-start.17 = (bf16[256,1024]{1,0:T(8,128)(2,1)}, bf16[256,1024]{1,0:T(8,128)(2,1)S(1)}, u32[]{:S(2)}) copy-start(bf16[256,1024]{1,0:T(8,128)(2,1)S(1)} %get-tuple-element.42) | copy-start | bytes 1572868
  258.2 11.1 %copy-start.24 = (s32[1,2]{1,0:T(1,128)S(1)}, s32[1,2]{1,0:T(1,128)}, u32[]{:S(2)}) copy-start(s32[1,2]{1,0:T(1,128)} %param.18) | copy-start | bytes 28
  258.2 12.0 %copy-start.13 = (bf16[256,2,32]{0,2,1:T(8,128)(2,1)S(1)}, bf16[256,2,32]{0,2,1:T(8,128)(2,1)}, u32[]{:S(2)}) copy-start(bf16[256,2,32]{0,2,1:T(8,128)(2,1)} %copy-done.12) | copy-start | bytes 98308
  258.2 12.0 %copy-start.15 = (bf16[256,2,32]{0,2,1:T(8,128)(2,1)S(1)}, bf16[256,2,32]{0,2,1:T(8,128)(2,1)}, u32[]{:S(2)}) copy-start(bf16[256,2,32]{0,2,1:T(8,128)(2,1)} %copy-done.14) | copy-start | bytes 98308
  264.8 10.4 %collective-permute-start.10 = (bf16[256,256]{1,0:T(8,128)(2,1)S(1)}, bf16[256,256]{1,0:T(8,128)(2,1)S(1)}, u32[]{:S(2)}, u32[]{:S(2)}) collective-permute-start(bf16[256,256]{1,0:T(8,128)(2,1)S(1)} %get-tuple-element.26), channel_id=1, source_target_pairs={{0,2},{1,3},{2,0},{3,1},{4,6},{5,7},{6,4},{7,5},{8,10},{9,11},{10,... | collective-permute-start | bytes 393224 | tf_op jit(solution)/shard_map/ppermute | solution.py:389
  265.9 9.3 %collective-permute-start.11 = (bf16[256,256]{1,0:T(8,128)(2,1)S(1)}, bf16[256,256]{1,0:T(8,128)(2,1)S(1)}, u32[]{:S(2)}, u32[]{:S(2)}) collective-permute-start(bf16[256,256]{1,0:T(8,128)(2,1)S(1)} %get-tuple-element.25), channel_id=1, source_target_pairs={{0,3},{1,0},{2,1},{3,2},{4,7},{5,4},{6,5},{7,6},{8,11},{9,8},{10,9... | collective-permute-start | bytes 393224 | tf_op jit(solution)/shard_map/ppermute | solution.py:389
  269.2 7.9 %collective-permute-start.9 = (bf16[256,256]{1,0:T(8,128)(2,1)S(1)}, bf16[256,256]{1,0:T(8,128)(2,1)S(1)}, u32[]{:S(2)}, u32[]{:S(2)}) collective-permute-start(bf16[256,256]{1,0:T(8,128)(2,1)S(1)} %get-tuple-element.24), channel_id=1, source_target_pairs={{0,1},{1,2},{2,3},{3,0},{4,5},{5,6},{6,7},{7,4},{8,9},{9,10},{10,1... | collective-permute-start | bytes 393224 | tf_op jit(solution)/shard_map/ppermute | solution.py:389
Sparse Core Ops, SparseCore 0:
  25.9 29.7 all-gather.5
  57.6 54.2 all-gather.7
  113.8 36.5 all-gather.9

commit v2 on v1

--- a/solution.py
+++ b/solution.py
@@ -178,55 +178,54 @@
     return out.transpose(2, 0, 1, 3).reshape(tok_count, -1).astype(jnp.bfloat16)
 
 
-def owner_body(local_groups, me_ref, group_ref, bound_ref, q_ref, segq_ref, prefix_ref, o_ref, lse_ref):
+def owner_body(local_groups, seg_count, me_ref, group_ref, bound_ref, q_ref, segq_ref, prefix_ref, o_ref, lse_ref):
+    head = pl.program_id(0)
     row = pl.program_id(1)
     block = pl.program_id(2)
-    seg = pl.program_id(3)
-    seg_count = pl.num_programs(3)
     rows = q_ref.shape[2]
     head_dim = q_ref.shape[3]
-
-    @pl.when(seg == 0)
-    def _():
-        o_ref[...] = jnp.zeros_like(o_ref)
-        lse_ref[...] = jnp.zeros_like(lse_ref)
-
-    group = group_ref[row * seg_count + seg]
-    first = bound_ref[row * 2 * seg_count + seg]
-    last = bound_ref[row * 2 * seg_count + seg_count + seg]
-    active = (
-        (group // local_groups == me_ref[0]) & (first < (block + 1) * rows) & (last > block * rows)
-    )
-
-    @pl.when(active)
-    def _():
-        prefix = prefix_ref[0, 0]
-        prefix_keys = prefix[:, :head_dim]
-        prefix_values = prefix[:, head_dim:]
-        mine = segq_ref[...] == seg
-        contract = (((1,), (1,)), ((), ()))
-        for q_group in range(q_ref.shape[1]):
-            scores = (
-                lax.dot_general(
-                    q_ref[0, q_group], prefix_keys, contract, preferred_element_type=jnp.float32
+    o_ref[...] = jnp.zeros_like(o_ref)
+    lse_ref[...] = jnp.zeros_like(lse_ref)
+    contract = (((1,), (1,)), ((), ()))
+    for seg in range(seg_count):
+        group = group_ref[row * seg_count + seg]
+        first = bound_ref[row * 2 * seg_count + seg]
+        last = bound_ref[row * 2 * seg_count + seg_count + seg]
+        active = (
+            (group // local_groups == me_ref[0])
+            & (first < (block + 1) * rows)
+            & (last > block * rows)
+        )
+
+        @pl.when(active)
+        def _():
+            prefix = prefix_ref[group % local_groups, head]
+            prefix_keys = prefix[:, :head_dim]
+            prefix_values = prefix[:, head_dim:]
+            mine = segq_ref[...] == seg
+            for q_group in range(q_ref.shape[1]):
+                scores = (
+                    lax.dot_general(
+                        q_ref[0, q_group], prefix_keys, contract,
+                        preferred_element_type=jnp.float32,
+                    )
+                    * head_dim ** (-0.5)
                 )
-                * head_dim ** (-0.5)
-            )
-            top = jnp.max(scores, axis=1, keepdims=True)
-            numerators = jnp.exp(scores - top)
-            total = jnp.sum(numerators, axis=1, keepdims=True)
-            summed = jnp.dot(
-                numerators.astype(jnp.bfloat16), prefix_values, preferred_element_type=jnp.float32
-            )
-            o_ref[0, q_group] = jnp.where(mine, summed / total, o_ref[0, q_group])
-            lse_ref[0, q_group] = jnp.where(mine, top + jnp.log(total), lse_ref[0, q_group])
+                top = jnp.max(scores, axis=1, keepdims=True)
+                numerators = jnp.exp(scores - top)
+                total = jnp.sum(numerators, axis=1, keepdims=True)
+                summed = jnp.dot(
+                    numerators.astype(jnp.bfloat16), prefix_values,
+                    preferred_element_type=jnp.float32,
+                )
+                o_ref[0, q_group] = jnp.where(mine, summed / total, o_ref[0, q_group])
+                lse_ref[0, q_group] = jnp.where(mine, top + jnp.log(total), lse_ref[0, q_group])
 
 
 def prefix_partials(query_all, segments_all, groups_all, prefix_local, me):
     kv_heads, q_groups, all_tokens, head_dim = query_all.shape
     row_count, tok_count = segments_all.shape
     seg_count = groups_all.shape[1]
-    prefix_len = prefix_local.shape[2]
     rows = min(128, tok_count)
     blocks = tok_count // rows
     local_groups = prefix_local.shape[0]
@@ -237,37 +236,32 @@
     seg_col = segments_all.reshape(all_tokens, 1)
     grid_spec = pltpu.PrefetchScalarGridSpec(
         num_scalar_prefetch=3,
-        grid=(kv_heads, row_count, blocks, seg_count),
+        grid=(kv_heads, row_count, blocks),
         in_specs=[
             pl.BlockSpec(
-                (1, q_groups, rows, head_dim),
-                lambda h, r, b, s, me, gr, bd: (h, 0, r * blocks + b, 0),
+                (1, q_groups, rows, head_dim), lambda h, r, b, me, gr, bd: (h, 0, r * blocks + b, 0)
             ),
-            pl.BlockSpec((rows, 1), lambda h, r, b, s, me, gr, bd: (r * blocks + b, 0)),
-            pl.BlockSpec(
-                (1, 1, prefix_len, 2 * head_dim),
-                lambda h, r, b, s, me, gr, bd: (gr[r * seg_count + s] % local_groups, h, 0, 0),
-            ),
+            pl.BlockSpec((rows, 1), lambda h, r, b, me, gr, bd: (r * blocks + b, 0)),
+            pl.BlockSpec(prefix_local.shape, lambda h, r, b, me, gr, bd: (0, 0, 0, 0)),
         ],
         out_specs=[
             pl.BlockSpec(
-                (1, q_groups, rows, head_dim),
-                lambda h, r, b, s, me, gr, bd: (h, 0, r * blocks + b, 0),
+                (1, q_groups, rows, head_dim), lambda h, r, b, me, gr, bd: (h, 0, r * blocks + b, 0)
             ),
             pl.BlockSpec(
-                (1, q_groups, rows, 1), lambda h, r, b, s, me, gr, bd: (h, 0, r * blocks + b, 0)
+                (1, q_groups, rows, 1), lambda h, r, b, me, gr, bd: (h, 0, r * blocks + b, 0)
             ),
         ],
     )
     return pl.pallas_call(
-        functools.partial(owner_body, local_groups),
+        functools.partial(owner_body, local_groups, seg_count),
         grid_spec=grid_spec,
         out_shape=(
             jax.ShapeDtypeStruct((kv_heads, q_groups, all_tokens, head_dim), jnp.float32),
             jax.ShapeDtypeStruct((kv_heads, q_groups, all_tokens, 1), jnp.float32),
         ),
         compiler_params=pltpu.CompilerParams(
-            dimension_semantics=("arbitrary", "arbitrary", "arbitrary", "arbitrary")
+            dimension_semantics=("arbitrary", "arbitrary", "arbitrary")
         ),
     )(me.reshape(1), groups_all.reshape(-1), bounds, query_all, seg_col, prefix_local)
 
@@ -314,10 +308,12 @@
         -1, PAGE, kv_heads, 2 * head_dim
     )
     kv_pages = jnp.zeros_like(pages).at[page_table[0]].set(pages)
-    query_heads = grouped_query.transpose(1, 2, 0, 3)
-    query_all = lax.all_gather(query_heads, "req", axis=2, tiled=True)
-    segments_all = lax.all_gather(segments, "req", axis=0, tiled=True)
-    groups_all = lax.all_gather(prefix_group, "req", axis=0, tiled=True)
+    query_all = lax.all_gather(grouped_query, "req", axis=0, tiled=True).transpose(1, 2, 0, 3)
+    row_tables = lax.all_gather(
+        jnp.concatenate([segments, prefix_group], axis=1), "req", axis=0, tiled=True
+    )
+    segments_all = row_tables[:, : segments.shape[1]]
+    groups_all = row_tables[:, segments.shape[1] :]
     query_all, w_gate_up, w_down = lax.optimization_barrier((query_all, w_gate_up, w_down))
     cached_out, cached_lse = prefix_partials(
         query_all, segments_all, groups_all, prefix_cache.transpose(0, 2, 1, 3),

time: 291 us -> 206 us (0.71); the launches traced: 285 us -> 204 us
  Pallas kernels: 112 us -> 39.3 us
  waiting for transfers between devices: 59.3 us -> 69 us
  starting transfers between devices: 37.4 us -> 29.2 us
  blocking collectives: 16.9 us -> 9.05 us
    pallas_call x1, Pallas kernels: 112 us -> 39.3 us  [prefix_partials(): pl.pallas_call(functools.partial(owner_body, local_groups, seg_count), gr...]
    all_to_all x1, waiting for transfers between devices: 10.8 us -> 21.2 us  [shards(): lax.all_to_all(cached_out.astype(jnp.bfloat16).reshape(row_split + (head_...]
    all_gather x2 -> x1, blocking collectives: 16.9 us -> 9.05 us  [shards(): lax.all_gather(jnp.concatenate([segments, prefix_group], axis=1), 'req',...]
    all_to_all x1, starting transfers between devices: 12.3 us -> 4.59 us  [shards(): lax.all_to_all(cached_lse.reshape(row_split + (1,)), 'req', split_axis=2,...]
  transfers between devices with their start and end apart: 17 -> 17, of which waited for: 9 -> 9; matrix products, arithmetic and copies ran while one was open for 11% -> 14% of each run, Pallas kernels for 39% -> 19%
where the time goes in v2:
time: 206 us; the launch traced here: 204 us
  waiting for transfers between devices  69 us (33%)
  Pallas kernels  39.3 us (19%)
  starting transfers between devices  29.2 us (14%)
  matrix products  18.2 us (9%)
  between operations  14.2 us (7%)
  other arithmetic  13.2 us (6%)
  local copies, waits for them, and re-layouts  11.9 us (6%)
  blocking collectives  9.05 us (4%)
    pallas_call x1, Pallas kernels, prefix_partials(): pl.pallas_call(functools.partial(owner_body, local_groups, seg_count), gr...  39.3 us
    all_gather x1, waiting for transfers between devices, shards(): lax.all_gather(grouped_query, 'req', axis=0, tiled=True)  29.9 us
    all_to_all x1, waiting for transfers between devices, shards(): lax.all_to_all(cached_out.astype(jnp.bfloat16).reshape(row_split + (head_...  21.2 us
    ppermute x9, starting transfers between devices, shifted_copies(): copies.append(lax.ppermute(block, axis_name, pairs))  16.3 us
    ppermute x9, waiting for transfers between devices, shifted_copies(): copies.append(lax.ppermute(block, axis_name, pairs))  12 us
    all_gather x1, blocking collectives, shards(): lax.all_gather(jnp.concatenate([segments, prefix_group], axis=1), 'req',...  9.05 us
    dot_general x1, matrix products, shards(): jnp.einsum('tef,efd->td', hidden, all_down, preferred_element_type=jnp.fl...  6.5 us
    dot_general x1, matrix products, shards(): jnp.einsum('td,edf->tef', normed_moe, all_gate_up[:, 0], preferred_elemen...  4.98 us
  transfers between devices with their start and end apart: 17, of which 9 were waited for; matrix products, arithmetic and copies ran while one was open for 14% of the time, Pallas kernels for 19%

profile of v2, /device:TPU:0, one launch (start us, length us, event | category | flops | bytes accessed | tf_op | source)
XLA Modules:
  0.0 204.0 jit_solution(5659283616674720865)
XLA Ops:
  7.2 3.1 %collective-permute-start = (bf16[256,256]{1,0:T(8,128)(2,1)}, bf16[256,256]{1,0:T(8,128)(2,1)S(1)}, u32[]{:S(2)}, u32[]{:S(2)}) collective-permute-start(bf16[256,256]{1,0:T(8,128)(2,1)} %param.14), channel_id=1, source_target_pairs={{0,1},{1,2},{2,3},{3,0},{4,5},{5,6},{6,7},{7,4},{8,9},{9,10},{10,1... | collective-permute-start | bytes 393224 | tf_op jit(solution)/shard_map/ppermute | solution.py:73
  10.3 2.6 %collective-permute-start.1 = (bf16[256,256]{1,0:T(8,128)(2,1)}, bf16[256,256]{1,0:T(8,128)(2,1)S(1)}, u32[]{:S(2)}, u32[]{:S(2)}) collective-permute-start(bf16[256,256]{1,0:T(8,128)(2,1)} %param.14), channel_id=1, source_target_pairs={{0,2},{1,3},{2,0},{3,1},{4,6},{5,7},{6,4},{7,5},{8,10},{9,11},{10,... | collective-permute-start | bytes 393224 | tf_op jit(solution)/shard_map/ppermute | solution.py:73
  12.9 1.3 collective-permute-start.2
  14.3 0.9 convert_reduce_fusion.1
  15.6 1.4 collective-permute-done
  17.0 4.8 %collective-permute-done.1 = bf16[256,256]{1,0:T(8,128)(2,1)S(1)} collective-permute-done((bf16[256,256]{1,0:T(8,128)(2,1)}, bf16[256,256]{1,0:T(8,128)(2,1)S(1)}, u32[]{:S(2)}, u32[]{:S(2)}) %collective-permute-start.1) | collective-permute-done | bytes 131104 | tf_op jit(solution)/shard_map/ppermute | solution.py:73
  21.8 1.0 pad_maximum_fusion
  22.8 0.6 gather_fusion
  24.9 0.9 pad_maximum_fusion.2
  25.9 29.9 %all-gather.5.cloned.1.call-done = bf16[2048,2,2,64]{3,0,2,1:T(8,128)(2,1)} async-done(((bf16[256,2,2,64]{3,0,2,1:T(8,128)(2,1)}), bf16[2048,2,2,64]{3,0,2,1:T(8,128)(2,1)}) %all-gather.5.cloned.1.call-update) | async-done | bytes 1048592 | tf_op jit(solution)/shard_map/all_gather | solution.py:311
  55.8 1.0 copy.70
  56.9 0.7 all-gather.9.cloned.1.call-update
  57.6 1.5 collective-permute-start.6
  59.1 2.4 %collective-permute-start.7 = (bf16[256,1024]{1,0:T(8,128)(2,1)}, bf16[256,1024]{1,0:T(8,128)(2,1)}, u32[]{:S(2)}, u32[]{:S(2)}) collective-permute-start(bf16[256,1024]{1,0:T(8,128)(2,1)} %param.22), channel_id=1, source_target_pairs={{0,2},{1,3},{2,0},{3,1},{4,6},{5,7},{6,4},{7,5},{8,10},{9,11},{10,... | collective-permute-start | bytes 1572872 | tf_op jit(solution)/shard_map/ppermute | solution.py:73
  61.5 1.4 collective-permute-start.8
  63.0 9.0 %all-gather = s32[8,1,264]{2,1,0:T(1,128)S(1)} all-gather(s32[1,1,264]{2,1,0:T(1,128)S(1)} %add_bitcast_fusion), channel_id=1, replica_groups=mesh['req'=8,'hid'=4] {'req'}, dimensions={0}, use_global_device_ids=true | all-gather | bytes 9504 | tf_op jit(solution)/shard_map/all_gather | solution.py:312
  72.4 0.7 reshape.298.bound_ref
  73.1 1.4 copy.82
  74.6 0.6 reshape.297.group_ref
  75.1 1.2 copy.85
  76.3 39.3 %shard_map.152 = (f32[2,2,2048,64]{3,2,1,0:T(8,128)}, f32[2,2,2048,1]{3,2,1,0:T(8,128)}) custom-call(s32[1]{0:T(128)} %bitcast.19.me_ref, s32[64]{0:T(128)} %reshape.297.group_ref, s32[128]{0:T(128)} %reshape.298.bound_ref, bf16[2,2,2048,64]{3,2,1,0:T(8,128)(2,1)} %bitcast.130, s32[2048,1]{1,0:T(8,128)} %bitcast.128, bf16[2,2,1024,128]{3,2,1,0:T(8,128)(2,1)} %bitcast.129), custom_call_target="tpu_custom_call" | custom-call | tf_op jit(solution)/shard_map/pallas_call | solution.py:256
  115.6 3.4 %reduce.1 = f32[2,2,2048]{2,1,0:T(2,128)S(1)} reduce(f32[2,2,2048,1]{3,2,1,0:T(8,128)} %get-tuple-element.8, f32[]{:T(128)} %constant.96), dimensions={3}, to_apply=%get-tuple-element.8.reduce_sub_computation | reduce | bytes 65540 | tf_op jit(solution)/shard_map/pallas_call | solution.py:256
  119.0 0.6 copy.65
  119.7 4.6 %all-to-all-start = ((f32[2,2,8,256,1]{3,1,0,4,2:T(2,128)}), f32[2,2,8,256,1]{3,1,0,4,2:T(2,128)S(1)}, u32[]{:S(2)}, u32[]{:S(2)}) async-start(f32[2,2,8,256,1]{3,1,0,4,2:T(2,128)} %copy.65), calls=%async_computation | async-start | bytes 65536 | tf_op jit(solution)/shard_map/all_to_all | solution.py:327
  124.2 0.7 fusion.44
  125.0 2.5 %convert_element_type.86 = bf16[2,2,2048,64]{3,2,1,0:T(8,128)(2,1)S(1)} convert(f32[2,2,2048,64]{3,2,1,0:T(8,128)} %get-tuple-element.9) | non-fusion elementwise | flops 524288 | bytes 3145728 | tf_op jit(solution)/shard_map/convert_element_type | solution.py:324
  127.5 1.6 copy.67
  129.5 3.8 %all-to-all-start.1 = ((bf16[2,2,8,256,64]{3,4,1,0,2:T(8,128)(2,1)}), bf16[2,2,8,256,64]{3,4,1,0,2:T(8,128)(2,1)S(1)}, u32[]{:S(2)}, u32[]{:S(2)}) async-start(bf16[2,2,8,256,64]{3,4,1,0,2:T(8,128)(2,1)} %copy.67), calls=%async_computation.1 | async-start | bytes 2097152 | tf_op jit(solution)/shard_map/all_to_all | solution.py:323
  133.3 1.5 fusion.47
  134.9 0.6 copy-done.8
  135.5 1.2 fusion.69
  136.9 0.8 reduce_sum.93
  137.8 21.2 %all-to-all-done.1 = bf16[2,2,8,256,64]{3,4,1,0,2:T(8,128)(2,1)S(1)} async-done(((bf16[2,2,8,256,64]{3,4,1,0,2:T(8,128)(2,1)}), bf16[2,2,8,256,64]{3,4,1,0,2:T(8,128)(2,1)S(1)}, u32[]{:S(2)}, u32[]{:S(2)}) %all-to-all-start.1) | async-done | bytes 1048608 | tf_op jit(solution)/shard_map/all_to_all | solution.py:323
  159.1 1.2 fusion.20
  160.5 3.7 %collective-permute-start.5 = (bf16[256,256]{0,1:T(8,128)(2,1)S(1)}, bf16[256,256]{0,1:T(8,128)(2,1)S(1)}, u32[]{:S(2)}, u32[]{:S(2)}) collective-permute-start(bf16[256,256]{0,1:T(8,128)(2,1)S(1)} %bitcast.149), channel_id=1, source_target_pairs={{0,3},{1,0},{2,1},{3,2},{4,7},{5,4},{6,5},{7,6},{8,11},{9,8},{10,9... | collective-permute-start | bytes 393224 | tf_op jit(solution)/shard_map/ppermute | solution.py:73
  164.3 3.1 %collective-permute-done.3 = bf16[256,256]{0,1:T(8,128)(2,1)S(1)} collective-permute-done((bf16[256,256]{0,1:T(8,128)(2,1)S(1)}, bf16[256,256]{0,1:T(8,128)(2,1)S(1)}, u32[]{:S(2)}, u32[]{:S(2)}) %collective-permute-start.3) | collective-permute-done | bytes 131104 | tf_op jit(solution)/shard_map/ppermute | solution.py:73
  167.4 2.8 %collective-permute-done.4 = bf16[256,256]{0,1:T(8,128)(2,1)S(1)} collective-permute-done((bf16[256,256]{0,1:T(8,128)(2,1)S(1)}, bf16[256,256]{0,1:T(8,128)(2,1)S(1)}, u32[]{:S(2)}, u32[]{:S(2)}) %collective-permute-start.4) | collective-permute-done | bytes 131104 | tf_op jit(solution)/shard_map/ppermute | solution.py:73
  170.2 2.4 %fusion.21 = (f32[256]{0:T(256)S(1)}, bf16[256,1024]{1,0:T(8,128)(2,1)S(1)}) fusion(bf16[256,1024]{1,0:T(8,128)(2,1)} %collective-permute-done.8, bf16[256,1024]{1,0:T(8,128)(2,1)} %collective-permute-done.7, bf16[256,1024]{1,0:T(8,128)(2,1)} %collective-permute-done.6, bf16[256,1024]{1,0:T(8,128)(2,1)} %param.22, ...), kind=kOutput, calls=%fused_computation.31 | convolution fusion | flops 550764288 | bytes 3671040 | tf_op jit(solution)/shard_map/dot_general | solution.py:355
  172.6 5.0 %fusion.1 = f32[256,16,128]{2,0,1:T(8,128)} fusion(bf16[16,2,1024,128]{3,2,0,1:T(8,128)(2,1)} %all-gather.7.cloned.1.call-done, bf16[256,1024]{1,0:T(8,128)(2,1)S(1)} %get-tuple-element.44, f32[1024]{0:T(1024)S(1)} %copy-done.19, f32[256]{0:T(256)S(1)} %add_rsqrt_fusion), kind=kOutput, calls=%fused_computation.5 | convolution fusion | flops 1074790400 | bytes 6820864 | tf_op jit(solution)/shard_map/td,edf->tef/dot_general | solution.py:368
  177.6 6.5 %convolution_bitcast_fusion = f32[256,1024]{1,0:T(8,128)S(1)} fusion(bf16[16,128,1024]{2,1,0:T(8,128)(2,1)} %all-gather.9.cloned.1.call-done, f32[256,16,128]{2,0,1:T(8,128)} %fusion.1, bf16[16,2,1024,128]{3,2,0,1:T(8,128)(2,1)} %all-gather.7.cloned.1.call-done, f32[256,16]{0,1:T(8,128)S(1)} %select_reduce_fusion, ...), kind=kOutput, calls=%fused_computation.19 | convolution fusion | flops 2152202240 | bytes 12080128 | tf_op jit(solution)/shard_map/tef,efd->td/dot_general | solution.py:375
  184.2 1.0 collective-permute-start.10
  185.2 3.4 %collective-permute-start.11 = (bf16[256,256]{1,0:T(8,128)(2,1)S(1)}, bf16[256,256]{1,0:T(8,128)(2,1)S(1)}, u32[]{:S(2)}, u32[]{:S(2)}) collective-permute-start(bf16[256,256]{1,0:T(8,128)(2,1)S(1)} %get-tuple-element.25), channel_id=1, source_target_pairs={{0,3},{1,0},{2,1},{3,2},{4,7},{5,4},{6,5},{7,6},{8,11},{9,8},{10,9... | collective-permute-start | bytes 393224 | tf_op jit(solution)/shard_map/ppermute | solution.py:385
  188.6 0.9 slice.89
  189.7 0.6 scatter_fusion
  190.3 0.8 copy.72
  191.1 3.1 %collective-permute-done.10 = bf16[256,256]{1,0:T(8,128)(2,1)S(1)} collective-permute-done((bf16[256,256]{1,0:T(8,128)(2,1)S(1)}, bf16[256,256]{1,0:T(8,128)(2,1)S(1)}, u32[]{:S(2)}, u32[]{:S(2)}) %collective-permute-start.10) | collective-permute-done | bytes 131104 | tf_op jit(solution)/shard_map/ppermute | solution.py:385
  194.2 1.7 collective-permute-done.9
  195.9 1.6 add_convert_fusion.1
  (95 shorter events, 3.8 us)
Async XLA Ops:
  7.2 16.6 %copy-start = (bf16[1024,256]{1,0:T(8,128)(2,1)S(1)}, bf16[1024,256]{1,0:T(8,128)(2,1)}, u32[]{:S(2)}) copy-start(bf16[1024,256]{1,0:T(8,128)(2,1)} %param.20) | copy-start | bytes 1572868
  7.2 16.6 %copy-start.17 = (f32[1024]{0:T(1024)S(1)}, f32[1024]{0:T(1024)}, u32[]{:S(2)}) copy-start(f32[1024]{0:T(1024)} %param.19) | copy-start | bytes 12292
  7.2 48.6 %all-gather.5.cloned.1.call-start = ((), (), s32[]{:S(2)}) async-start(), calls=%async_computation.2 | async-start | bytes 2359296 | tf_op jit(solution)/shard_map/all_gather | solution.py:311
  7.2 9.8 %collective-permute-start = (bf16[256,256]{1,0:T(8,128)(2,1)}, bf16[256,256]{1,0:T(8,128)(2,1)S(1)}, u32[]{:S(2)}, u32[]{:S(2)}) collective-permute-start(bf16[256,256]{1,0:T(8,128)(2,1)} %param.14), channel_id=1, source_target_pairs={{0,1},{1,2},{2,3},{3,0},{4,5},{5,6},{6,7},{7,4},{8,9},{9,10},{10,1... | collective-permute-start | bytes 393224 | tf_op jit(solution)/shard_map/ppermute | solution.py:73
  10.3 11.4 %collective-permute-start.1 = (bf16[256,256]{1,0:T(8,128)(2,1)}, bf16[256,256]{1,0:T(8,128)(2,1)S(1)}, u32[]{:S(2)}, u32[]{:S(2)}) collective-permute-start(bf16[256,256]{1,0:T(8,128)(2,1)} %param.14), channel_id=1, source_target_pairs={{0,2},{1,3},{2,0},{3,1},{4,6},{5,7},{6,4},{7,5},{8,10},{9,11},{10,... | collective-permute-start | bytes 393224 | tf_op jit(solution)/shard_map/ppermute | solution.py:73
  12.9 8.9 %collective-permute-start.2 = (bf16[256,256]{1,0:T(8,128)(2,1)}, bf16[256,256]{1,0:T(8,128)(2,1)S(1)}, u32[]{:S(2)}, u32[]{:S(2)}) collective-permute-start(bf16[256,256]{1,0:T(8,128)(2,1)} %param.14), channel_id=1, source_target_pairs={{0,3},{1,0},{2,1},{3,2},{4,7},{5,4},{6,5},{7,6},{8,11},{9,8},{10,9... | collective-permute-start | bytes 393224 | tf_op jit(solution)/shard_map/ppermute | solution.py:73
  15.4 6.4 %copy-start.4 = (f32[256,32]{0,1:T(8,128)}, f32[256,32]{0,1:T(8,128)S(1)}, u32[]{:S(2)}) copy-start(f32[256,32]{0,1:T(8,128)S(1)} %get-tuple-element.39) | copy-start | bytes 98308
  15.4 6.4 %copy-start.6 = (f32[256,32]{0,1:T(8,128)}, f32[256,32]{0,1:T(8,128)S(1)}, u32[]{:S(2)}) copy-start(f32[256,32]{0,1:T(8,128)S(1)} %get-tuple-element.40) | copy-start | bytes 98308
  23.5 32.2 %copy-start.2 = (bf16[2,2,1024,128]{3,2,1,0:T(8,128)(2,1)S(1)}, bf16[2,2,1024,128]{3,2,1,0:T(8,128)(2,1)}, u32[]{:S(2)}) copy-start(bf16[2,2,1024,128]{3,2,1,0:T(8,128)(2,1)} %param.26) | copy-start | bytes 3145732
  23.8 0.6 copy-start.14
  24.3 38.6 %copy-start.11 = (s32[1,256]{1,0:T(1,128)S(1)}, s32[1,256]{1,0:T(1,128)}, u32[]{:S(2)}) copy-start(s32[1,256]{1,0:T(1,128)} %param.15) | copy-start | bytes 3076
  24.3 38.6 %copy-start.16 = (s32[1,8]{1,0:T(1,128)S(1)}, s32[1,8]{1,0:T(1,128)}, u32[]{:S(2)}) copy-start(s32[1,8]{1,0:T(1,128)} %param.16) | copy-start | bytes 100
  24.9 50.2 %copy-start.3 = (bf16[2,1024,2,128]{3,2,1,0:T(2,128)(2,1)S(1)}, bf16[2,1024,2,128]{3,2,1,0:T(2,128)(2,1)}, u32[]{:S(2)}) copy-start(bf16[2,1024,2,128]{3,2,1,0:T(2,128)(2,1)} %param.17) | copy-start | bytes 3145732
  25.8 146.8 %all-gather.7.cloned.1.call-start = ((), (), s32[]{:S(2)}) async-start(), calls=%async_computation.3 | async-start | bytes 9437184 | tf_op jit(solution)/shard_map/all_gather | solution.py:361
  56.8 120.8 %all-gather.9.cloned.1.call-start = ((), (), s32[]{:S(2)}) async-start(), calls=%async_computation.4 | async-start | bytes 4718592 | tf_op jit(solution)/shard_map/all_gather | solution.py:362
  57.6 102.9 %collective-permute-start.6 = (bf16[256,1024]{1,0:T(8,128)(2,1)}, bf16[256,1024]{1,0:T(8,128)(2,1)}, u32[]{:S(2)}, u32[]{:S(2)}) collective-permute-start(bf16[256,1024]{1,0:T(8,128)(2,1)} %param.22), channel_id=1, source_target_pairs={{0,1},{1,2},{2,3},{3,0},{4,5},{5,6},{6,7},{7,4},{8,9},{9,10},{10,1... | collective-permute-start | bytes 1572872 | tf_op jit(solution)/shard_map/ppermute | solution.py:73
  59.1 105.2 %collective-permute-start.7 = (bf16[256,1024]{1,0:T(8,128)(2,1)}, bf16[256,1024]{1,0:T(8,128)(2,1)}, u32[]{:S(2)}, u32[]{:S(2)}) collective-permute-start(bf16[256,1024]{1,0:T(8,128)(2,1)} %param.22), channel_id=1, source_target_pairs={{0,2},{1,3},{2,0},{3,1},{4,6},{5,7},{6,4},{7,5},{8,10},{9,11},{10,... | collective-permute-start | bytes 1572872 | tf_op jit(solution)/shard_map/ppermute | solution.py:73
  61.5 102.8 %collective-permute-start.8 = (bf16[256,1024]{1,0:T(8,128)(2,1)}, bf16[256,1024]{1,0:T(8,128)(2,1)}, u32[]{:S(2)}, u32[]{:S(2)}) collective-permute-start(bf16[256,1024]{1,0:T(8,128)(2,1)} %param.22), channel_id=1, source_target_pairs={{0,3},{1,0},{2,1},{3,2},{4,7},{5,4},{6,5},{7,6},{8,11},{9,8},{10,9... | collective-permute-start | bytes 1572872 | tf_op jit(solution)/shard_map/ppermute | solution.py:73
  119.7 9.8 %all-to-all-start = ((f32[2,2,8,256,1]{3,1,0,4,2:T(2,128)}), f32[2,2,8,256,1]{3,1,0,4,2:T(2,128)S(1)}, u32[]{:S(2)}, u32[]{:S(2)}) async-start(f32[2,2,8,256,1]{3,1,0,4,2:T(2,128)} %copy.65), calls=%async_computation | async-start | bytes 65536 | tf_op jit(solution)/shard_map/all_to_all | solution.py:327
  127.4 5.9 %copy-start.15 = (f32[256]{0:T(256)S(1)}, f32[256]{0:T(256)}, u32[]{:S(2)}) copy-start(f32[256]{0:T(256)} %copy-done.14) | copy-start | bytes 3076
  127.4 5.9 %copy-start.18 = (f32[1024]{0:T(1024)S(1)}, f32[1024]{0:T(1024)}, u32[]{:S(2)}) copy-start(f32[1024]{0:T(1024)} %param.19) | copy-start | bytes 12292
  127.5 7.4 %copy-start.5 = (f32[256,32]{0,1:T(8,128)S(1)}, f32[256,32]{0,1:T(8,128)}, u32[]{:S(2)}) copy-start(f32[256,32]{0,1:T(8,128)} %copy-done.4) | copy-start | bytes 98308
  127.5 7.4 %copy-start.7 = (f32[256,32]{0,1:T(8,128)S(1)}, f32[256,32]{0,1:T(8,128)}, u32[]{:S(2)}) copy-start(f32[256,32]{0,1:T(8,128)} %copy-done.6) | copy-start | bytes 98308
  127.5 8.1 %copy-start.1 = (bf16[256,2,2,64]{3,0,2,1:T(8,128)(2,1)S(1)}, bf16[256,2,2,64]{3,0,2,1:T(8,128)(2,1)}, u32[]{:S(2)}) copy-start(bf16[256,2,2,64]{3,0,2,1:T(8,128)(2,1)} %pad_maximum_fusion.2) | copy-start | bytes 393220
  129.5 5.4 %copy-start.9 = (f32[2,2,8,256,1]{3,1,0,4,2:T(2,128)}, f32[2,2,8,256,1]{3,1,0,4,2:T(2,128)S(1)}, u32[]{:S(2)}) copy-start(f32[2,2,8,256,1]{3,1,0,4,2:T(2,128)S(1)} %all-to-all-done) | copy-start | bytes 98308
  129.5 29.5 %all-to-all-start.1 = ((bf16[2,2,8,256,64]{3,4,1,0,2:T(8,128)(2,1)}), bf16[2,2,8,256,64]{3,4,1,0,2:T(8,128)(2,1)S(1)}, u32[]{:S(2)}, u32[]{:S(2)}) async-start(bf16[2,2,8,256,64]{3,4,1,0,2:T(8,128)(2,1)} %copy.67), calls=%async_computation.1 | async-start | bytes 2097152 | tf_op jit(solution)/shard_map/all_to_all | solution.py:323
  133.3 30.9 %copy-start.12 = (f32[256,8]{0,1:T(8,128)S(1)}, f32[256,8]{0,1:T(8,128)}, u32[]{:S(2)}) copy-start(f32[256,8]{0,1:T(8,128)} %param.25) | copy-start | bytes 24580
  133.3 30.9 %copy-start.13 = (s32[256,8]{0,1:T(8,128)S(1)}, s32[256,8]{0,1:T(8,128)}, u32[]{:S(2)}) copy-start(s32[256,8]{0,1:T(8,128)} %param.24) | copy-start | bytes 24580
  134.9 0.7 copy-start.8
  160.3 7.0 %collective-permute-start.3 = (bf16[256,256]{0,1:T(8,128)(2,1)S(1)}, bf16[256,256]{0,1:T(8,128)(2,1)S(1)}, u32[]{:S(2)}, u32[]{:S(2)}) collective-permute-start(bf16[256,256]{0,1:T(8,128)(2,1)S(1)} %bitcast.147), channel_id=1, source_target_pairs={{0,1},{1,2},{2,3},{3,0},{4,5},{5,6},{6,7},{7,4},{8,9},{9,10},{10,1... | collective-permute-start | bytes 393224 | tf_op jit(solution)/shard_map/ppermute | solution.py:73
  160.4 9.8 %collective-permute-start.4 = (bf16[256,256]{0,1:T(8,128)(2,1)S(1)}, bf16[256,256]{0,1:T(8,128)(2,1)S(1)}, u32[]{:S(2)}, u32[]{:S(2)}) collective-permute-start(bf16[256,256]{0,1:T(8,128)(2,1)S(1)} %bitcast.148), channel_id=1, source_target_pairs={{0,2},{1,3},{2,0},{3,1},{4,6},{5,7},{6,4},{7,5},{8,10},{9,11},{10,... | collective-permute-start | bytes 393224 | tf_op jit(solution)/shard_map/ppermute | solution.py:73
  160.5 9.7 %collective-permute-start.5 = (bf16[256,256]{0,1:T(8,128)(2,1)S(1)}, bf16[256,256]{0,1:T(8,128)(2,1)S(1)}, u32[]{:S(2)}, u32[]{:S(2)}) collective-permute-start(bf16[256,256]{0,1:T(8,128)(2,1)S(1)} %bitcast.149), channel_id=1, source_target_pairs={{0,3},{1,0},{2,1},{3,2},{4,7},{5,4},{6,5},{7,6},{8,11},{9,8},{10,9... | collective-permute-start | bytes 393224 | tf_op jit(solution)/shard_map/ppermute | solution.py:73
  164.3 8.3 %copy-start.19 = (f32[1024]{0:T(1024)S(1)}, f32[1024]{0:T(1024)}, u32[]{:S(2)}) copy-start(f32[1024]{0:T(1024)} %param.23) | copy-start | bytes 12292
  172.5 5.0 %copy-start.10 = (bf16[256,1024]{1,0:T(8,128)(2,1)}, bf16[256,1024]{1,0:T(8,128)(2,1)S(1)}, u32[]{:S(2)}) copy-start(bf16[256,1024]{1,0:T(8,128)(2,1)S(1)} %get-tuple-element.44) | copy-start | bytes 1572868
  177.6 11.0 %copy-start.20 = (s32[1,2]{1,0:T(1,128)S(1)}, s32[1,2]{1,0:T(1,128)}, u32[]{:S(2)}) copy-start(s32[1,2]{1,0:T(1,128)} %param.18) | copy-start | bytes 28
  184.2 10.0 %collective-permute-start.10 = (bf16[256,256]{1,0:T(8,128)(2,1)S(1)}, bf16[256,256]{1,0:T(8,128)(2,1)S(1)}, u32[]{:S(2)}, u32[]{:S(2)}) collective-permute-start(bf16[256,256]{1,0:T(8,128)(2,1)S(1)} %get-tuple-element.26), channel_id=1, source_target_pairs={{0,2},{1,3},{2,0},{3,1},{4,6},{5,7},{6,4},{7,5},{8,10},{9,11},{10,... | collective-permute-start | bytes 393224 | tf_op jit(solution)/shard_map/ppermute | solution.py:385
  185.2 9.0 %collective-permute-start.11 = (bf16[256,256]{1,0:T(8,128)(2,1)S(1)}, bf16[256,256]{1,0:T(8,128)(2,1)S(1)}, u32[]{:S(2)}, u32[]{:S(2)}) collective-permute-start(bf16[256,256]{1,0:T(8,128)(2,1)S(1)} %get-tuple-element.25), channel_id=1, source_target_pairs={{0,3},{1,0},{2,1},{3,2},{4,7},{5,4},{6,5},{7,6},{8,11},{9,8},{10,9... | collective-permute-start | bytes 393224 | tf_op jit(solution)/shard_map/ppermute | solution.py:385
  188.6 7.3 %collective-permute-start.9 = (bf16[256,256]{1,0:T(8,128)(2,1)S(1)}, bf16[256,256]{1,0:T(8,128)(2,1)S(1)}, u32[]{:S(2)}, u32[]{:S(2)}) collective-permute-start(bf16[256,256]{1,0:T(8,128)(2,1)S(1)} %get-tuple-element.24), channel_id=1, source_target_pairs={{0,1},{1,2},{2,3},{3,0},{4,5},{5,6},{6,7},{7,4},{8,9},{9,10},{10,1... | collective-permute-start | bytes 393224 | tf_op jit(solution)/shard_map/ppermute | solution.py:385
Sparse Core Ops, SparseCore 0:
  25.9 29.7 all-gather.4
  57.7 54.2 all-gather.6
  113.8 46.7 all-gather.8

commit v3 on v2

--- a/solution.py
+++ b/solution.py
@@ -308,13 +308,12 @@
         -1, PAGE, kv_heads, 2 * head_dim
     )
     kv_pages = jnp.zeros_like(pages).at[page_table[0]].set(pages)
-    query_all = lax.all_gather(grouped_query, "req", axis=0, tiled=True).transpose(1, 2, 0, 3)
+    query_all = gather_in_order(grouped_query, "req", 0).transpose(1, 2, 0, 3)
     row_tables = lax.all_gather(
         jnp.concatenate([segments, prefix_group], axis=1), "req", axis=0, tiled=True
     )
     segments_all = row_tables[:, : segments.shape[1]]
     groups_all = row_tables[:, segments.shape[1] :]
-    query_all, w_gate_up, w_down = lax.optimization_barrier((query_all, w_gate_up, w_down))
     cached_out, cached_lse = prefix_partials(
         query_all, segments_all, groups_all, prefix_cache.transpose(0, 2, 1, 3),
         lax.axis_index("req"),

time: 206 us -> 207 us (level)
  the two profiles are of different devices: /device:TPU:0 before, /device:TPU:11 now
where the time goes in v3:
time: 207 us; the launch traced here: 204 us
  waiting for transfers between devices  63.4 us (31%)
  starting transfers between devices  40.5 us (20%)
  Pallas kernels  32.2 us (16%)
  local copies, waits for them, and re-layouts  15.6 us (8%)
  matrix products  15.2 us (7%)
  between operations  14.7 us (7%)
  other arithmetic  11.6 us (6%)
  blocking collectives  11.2 us (5%)
    ppermute x16, waiting for transfers between devices, shifted_copies(): copies.append(lax.ppermute(block, axis_name, pairs))  42.8 us
    pallas_call x1, Pallas kernels, prefix_partials(): pl.pallas_call(functools.partial(owner_body, local_groups, seg_count), gr...  32.2 us
    ppermute x16, starting transfers between devices, shifted_copies(): copies.append(lax.ppermute(block, axis_name, pairs))  20.8 us
    all_to_all x1, starting transfers between devices, shards(): lax.all_to_all(cached_lse.reshape(row_split + (1,)), 'req', split_axis=2,...  11.6 us
    all_to_all x1, waiting for transfers between devices, shards(): lax.all_to_all(cached_out.astype(jnp.bfloat16).reshape(row_split + (head_...  11.2 us
    all_gather x1, blocking collectives, shards(): lax.all_gather(jnp.concatenate([segments, prefix_group], axis=1), 'req',...  11.2 us
    ppermute x3, waiting for transfers between devices, shards(): incoming = lax.ppermute(outgoing.astype(jnp.bfloat16), 'hid', pairs)  9.23 us
    unnamed x60, local copies, waits for them, and re-layouts  8.16 us
  transfers between devices with their start and end apart: 23, of which 12 were waited for; matrix products, arithmetic and copies ran while one was open for 15% of the time, Pallas kernels for 16%

profile of v3, /device:TPU:11, one launch (start us, length us, event | category | flops | bytes accessed | tf_op | source)
XLA Modules:
  0.0 204.4 jit_solution(12007746386223407478)
XLA Ops:
  7.3 2.3 %copy.53 = bf16[2,2,1024,128]{3,2,0,1:T(8,128)(2,1)} copy(bf16[2,2,1024,128]{3,2,1,0:T(8,128)(2,1)} %param.26) | data formatting | bytes 2097152 | tf_op args[12]
  9.7 1.3 collective-permute-start
  11.0 1.1 collective-permute-start.1
  12.1 1.4 collective-permute-start.2
  13.6 3.1 %collective-permute-start.14 = (bf16[256,1024]{1,0:T(8,128)(2,1)}, bf16[256,1024]{1,0:T(8,128)(2,1)}, u32[]{:S(2)}, u32[]{:S(2)}) collective-permute-start(bf16[256,1024]{1,0:T(8,128)(2,1)} %param.22), channel_id=1, source_target_pairs={{0,2},{1,3},{2,0},{3,1},{4,6},{5,7},{6,4},{7,5},{8,10},{9,11},{10,... | collective-permute-start | bytes 1572872 | tf_op jit(solution)/shard_map/ppermute | solution.py:73
  16.9 11.2 %all-gather = s32[8,1,264]{2,1,0:T(1,128)S(1)} all-gather(s32[1,1,264]{2,1,0:T(1,128)S(1)} %add_bitcast_fusion), channel_id=1, replica_groups=mesh['req'=8,'hid'=4] {'req'}, dimensions={0}, use_global_device_ids=true | all-gather | bytes 9504 | tf_op jit(solution)/shard_map/all_gather | solution.py:312
  28.8 18.2 %collective-permute-done.2 = bf16[256,256]{1,0:T(8,128)(2,1)S(1)} collective-permute-done((bf16[256,256]{1,0:T(8,128)(2,1)S(1)}, bf16[256,256]{1,0:T(8,128)(2,1)S(1)}, u32[]{:S(2)}, u32[]{:S(2)}) %collective-permute-start.2) | collective-permute-done | bytes 131104 | tf_op jit(solution)/shard_map/ppermute | solution.py:73
  48.6 1.6 collective-permute-start.3
  50.2 0.6 reshape.383.bound_ref
  50.9 1.4 copy.62
  52.9 1.2 copy.65
  54.1 1.2 collective-permute-start.4
  55.4 2.2 %collective-permute-start.5 = (bf16[256,2,2,64]{0,3,2,1:T(8,128)(2,1)S(1)}, bf16[256,2,2,64]{0,3,2,1:T(8,128)(2,1)S(1)}, u32[]{:S(2)}, u32[]{:S(2)}) collective-permute-start(bf16[256,2,2,64]{0,3,2,1:T(8,128)(2,1)S(1)} %pad_maximum_fusion.2), channel_id=1, source_target_pairs={{0,12},{4,16},{8,20},{12,24},{16,28},{20,0},{24,4},{28,8},{1,13},{... | collective-permute-start | bytes 393224 | tf_op jit(solution)/shard_map/ppermute | solution.py:73
  57.6 5.0 %collective-permute-done.4 = bf16[256,2,2,64]{0,3,2,1:T(8,128)(2,1)S(1)} collective-permute-done((bf16[256,2,2,64]{0,3,2,1:T(8,128)(2,1)S(1)}, bf16[256,2,2,64]{0,3,2,1:T(8,128)(2,1)S(1)}, u32[]{:S(2)}, u32[]{:S(2)}) %collective-permute-start.4) | collective-permute-done | bytes 131104 | tf_op jit(solution)/shard_map/ppermute | solution.py:73
  62.9 3.4 %collective-permute-done.5 = bf16[256,2,2,64]{0,3,2,1:T(8,128)(2,1)S(1)} collective-permute-done((bf16[256,2,2,64]{0,3,2,1:T(8,128)(2,1)S(1)}, bf16[256,2,2,64]{0,3,2,1:T(8,128)(2,1)S(1)}, u32[]{:S(2)}, u32[]{:S(2)}) %collective-permute-start.5) | collective-permute-done | bytes 131104 | tf_op jit(solution)/shard_map/ppermute | solution.py:73
  66.3 1.7 collective-permute-start.7
  68.2 5.2 %collective-permute-start.8 = (bf16[256,2,2,64]{0,3,2,1:T(8,128)(2,1)S(1)}, bf16[256,2,2,64]{0,3,2,1:T(8,128)(2,1)S(1)}, u32[]{:S(2)}, u32[]{:S(2)}) collective-permute-start(bf16[256,2,2,64]{0,3,2,1:T(8,128)(2,1)S(1)} %pad_maximum_fusion.2), channel_id=1, source_target_pairs={{0,24},{4,28},{8,0},{12,4},{16,8},{20,12},{24,16},{28,20},{1,25},{... | collective-permute-start | bytes 393224 | tf_op jit(solution)/shard_map/ppermute | solution.py:73
  73.5 4.4 %collective-permute-done.8 = bf16[256,2,2,64]{0,3,2,1:T(8,128)(2,1)S(1)} collective-permute-done((bf16[256,2,2,64]{0,3,2,1:T(8,128)(2,1)S(1)}, bf16[256,2,2,64]{0,3,2,1:T(8,128)(2,1)S(1)}, u32[]{:S(2)}, u32[]{:S(2)}) %collective-permute-start.8) | collective-permute-done | bytes 131104 | tf_op jit(solution)/shard_map/ppermute | solution.py:73
  78.0 1.1 collective-permute-done.9
  79.1 0.6 gather_fusion.1
  79.8 1.8 copy.45
  81.5 1.9 broadcast_select_fusion
  83.7 1.3 copy-done.1
  85.1 32.2 %shard_map.152 = (f32[2,2,2048,64]{3,2,1,0:T(8,128)}, f32[2,2,2048,1]{3,2,1,0:T(8,128)}) custom-call(s32[1]{0:T(128)} %bitcast.19.me_ref, s32[64]{0:T(128)} %reshape.382.group_ref, s32[128]{0:T(128)} %reshape.383.bound_ref, bf16[2,2,2048,64]{3,2,1,0:T(8,128)(2,1)} %bitcast.179, s32[2048,1]{1,0:T(8,128)} %bitcast.177, bf16[2,2,1024,128]{3,2,1,0:T(8,128)(2,1)} %bitcast.178), custom_call_target="tpu_custom_call" | custom-call | tf_op jit(solution)/shard_map/pallas_call | solution.py:256
  117.3 3.4 %reduce.1 = f32[2,2,2048]{2,1,0:T(2,128)S(1)} reduce(f32[2,2,2048,1]{3,2,1,0:T(8,128)} %get-tuple-element.4, f32[]{:T(128)} %constant.124), dimensions={3}, to_apply=%get-tuple-element.4.reduce_sub_computation | reduce | bytes 65540 | tf_op jit(solution)/shard_map/pallas_call | solution.py:256
  120.7 0.6 copy.48
  121.3 11.6 %all-to-all-start = ((f32[2,2,8,256,1]{3,1,0,4,2:T(2,128)}), f32[2,2,8,256,1]{3,1,0,4,2:T(2,128)S(1)}, u32[]{:S(2)}, u32[]{:S(2)}) async-start(f32[2,2,8,256,1]{3,1,0,4,2:T(2,128)} %copy.48), calls=%async_computation | async-start | bytes 65536 | tf_op jit(solution)/shard_map/all_to_all | solution.py:326
  132.9 0.7 fusion.52
  133.6 2.5 %convert_element_type.93 = bf16[2,2,2048,64]{3,2,1,0:T(8,128)(2,1)S(1)} convert(f32[2,2,2048,64]{3,2,1,0:T(8,128)} %get-tuple-element.5) | non-fusion elementwise | flops 524288 | bytes 3145728 | tf_op jit(solution)/shard_map/convert_element_type | solution.py:323
  136.1 1.6 copy.50
  137.7 4.3 %all-to-all-start.1 = ((bf16[2,2,8,256,64]{3,4,1,0,2:T(8,128)(2,1)}), bf16[2,2,8,256,64]{3,4,1,0,2:T(8,128)(2,1)S(1)}, u32[]{:S(2)}, u32[]{:S(2)}) async-start(bf16[2,2,8,256,64]{3,4,1,0,2:T(8,128)(2,1)} %copy.50), calls=%async_computation.1 | async-start | bytes 2097152 | tf_op jit(solution)/shard_map/all_to_all | solution.py:322
  142.5 0.6 copy-done.3
  143.8 0.8 reduce_sum.93
  144.6 11.2 %all-to-all-done.1 = bf16[2,2,8,256,64]{3,4,1,0,2:T(8,128)(2,1)S(1)} async-done(((bf16[2,2,8,256,64]{3,4,1,0,2:T(8,128)(2,1)}), bf16[2,2,8,256,64]{3,4,1,0,2:T(8,128)(2,1)S(1)}, u32[]{:S(2)}, u32[]{:S(2)}) %all-to-all-start.1) | async-done | bytes 1048608 | tf_op jit(solution)/shard_map/all_to_all | solution.py:322
  156.4 1.4 collective-permute-start.12
  157.9 3.1 %collective-permute-done.10 = bf16[256,256]{0,1:T(8,128)(2,1)S(1)} collective-permute-done((bf16[256,256]{0,1:T(8,128)(2,1)S(1)}, bf16[256,256]{0,1:T(8,128)(2,1)S(1)}, u32[]{:S(2)}, u32[]{:S(2)}) %collective-permute-start.10) | collective-permute-done | bytes 131104 | tf_op jit(solution)/shard_map/ppermute | solution.py:73
  160.9 6.5 %collective-permute-done.11 = bf16[256,256]{0,1:T(8,128)(2,1)S(1)} collective-permute-done((bf16[256,256]{0,1:T(8,128)(2,1)S(1)}, bf16[256,256]{0,1:T(8,128)(2,1)S(1)}, u32[]{:S(2)}, u32[]{:S(2)}) %collective-permute-start.11) | collective-permute-done | bytes 131104 | tf_op jit(solution)/shard_map/ppermute | solution.py:73
  167.5 0.9 collective-permute-done.12
  168.3 2.4 %fusion.21 = (f32[256]{0:T(256)S(1)}, bf16[256,1024]{1,0:T(8,128)(2,1)S(1)}) fusion(bf16[256,1024]{1,0:T(8,128)(2,1)} %collective-permute-done.15, bf16[256,1024]{1,0:T(8,128)(2,1)} %collective-permute-done.14, bf16[256,1024]{1,0:T(8,128)(2,1)} %collective-permute-done.13, bf16[256,1024]{1,0:T(8,128)(2,1)} %param.22, ...), kind=kOutput, calls=%fused_computation.33 | convolution fusion | flops 550764288 | bytes 3671040 | tf_op jit(solution)/shard_map/dot_general | solution.py:354
  170.8 4.8 %fusion.1 = f32[256,16,128]{2,0,1:T(8,128)} fusion(bf16[16,2,1024,128]{3,2,0,1:T(8,128)(2,1)} %all-gather.4.cloned.1.call-done, bf16[256,1024]{1,0:T(8,128)(2,1)S(1)} %get-tuple-element.36, f32[1024]{0:T(1024)S(1)} %copy-done.18, f32[256]{0:T(256)S(1)} %add_rsqrt_fusion), kind=kOutput, calls=%fused_computation.6 | convolution fusion | flops 1074790400 | bytes 6820864 | tf_op jit(solution)/shard_map/td,edf->tef/dot_general | solution.py:367
  175.6 6.5 %convolution_bitcast_fusion = f32[256,1024]{1,0:T(8,128)S(1)} fusion(bf16[16,128,1024]{2,1,0:T(8,128)(2,1)} %all-gather.6.cloned.1.call-done, f32[256,16,128]{2,0,1:T(8,128)} %fusion.1, bf16[16,2,1024,128]{3,2,0,1:T(8,128)(2,1)} %all-gather.4.cloned.1.call-done, f32[256,16]{0,1:T(8,128)S(1)} %select_reduce_fusion, ...), kind=kOutput, calls=%fused_computation.21 | convolution fusion | flops 2152202240 | bytes 12080128 | tf_op jit(solution)/shard_map/tef,efd->td/dot_general | solution.py:374
  182.3 2.3 %collective-permute-start.17 = (bf16[256,256]{1,0:T(8,128)(2,1)S(1)}, bf16[256,256]{1,0:T(8,128)(2,1)S(1)}, u32[]{:S(2)}, u32[]{:S(2)}) collective-permute-start(bf16[256,256]{1,0:T(8,128)(2,1)S(1)} %get-tuple-element.18), channel_id=1, source_target_pairs={{0,2},{1,3},{2,0},{3,1},{4,6},{5,7},{6,4},{7,5},{8,10},{9,11},{10,... | collective-permute-start | bytes 393224 | tf_op jit(solution)/shard_map/ppermute | solution.py:384
  184.5 1.4 collective-permute-start.18
  186.2 0.6 scatter_fusion
  186.8 0.8 copy.55
  187.6 5.5 %collective-permute-done.17 = bf16[256,256]{1,0:T(8,128)(2,1)S(1)} collective-permute-done((bf16[256,256]{1,0:T(8,128)(2,1)S(1)}, bf16[256,256]{1,0:T(8,128)(2,1)S(1)}, u32[]{:S(2)}, u32[]{:S(2)}) %collective-permute-start.17) | collective-permute-done | bytes 131104 | tf_op jit(solution)/shard_map/ppermute | solution.py:384
  193.1 3.8 %collective-permute-done.18 = bf16[256,256]{1,0:T(8,128)(2,1)S(1)} collective-permute-done((bf16[256,256]{1,0:T(8,128)(2,1)S(1)}, bf16[256,256]{1,0:T(8,128)(2,1)S(1)}, u32[]{:S(2)}, u32[]{:S(2)}) %collective-permute-start.18) | collective-permute-done | bytes 131104 | tf_op jit(solution)/shard_map/ppermute | solution.py:384
  196.8 0.8 add_convert_fusion
  (121 shorter events, 6.2 us)
Async XLA Ops:
  7.2 40.9 %copy-start = (bf16[1024,256]{1,0:T(8,128)(2,1)S(1)}, bf16[1024,256]{1,0:T(8,128)(2,1)}, u32[]{:S(2)}) copy-start(bf16[1024,256]{1,0:T(8,128)(2,1)} %param.20) | copy-start | bytes 1572868
  7.2 2.5 %copy-start.6 = (bf16[256,256]{1,0:T(8,128)(2,1)S(1)}, bf16[256,256]{1,0:T(8,128)(2,1)}, u32[]{:S(2)}) copy-start(bf16[256,256]{1,0:T(8,128)(2,1)} %param.14) | copy-start | bytes 393220
  7.2 9.5 %copy-start.12 = (s32[1,256]{1,0:T(1,128)S(1)}, s32[1,256]{1,0:T(1,128)}, u32[]{:S(2)}) copy-start(s32[1,256]{1,0:T(1,128)} %param.15) | copy-start | bytes 3076
  7.2 9.7 %copy-start.15 = (s32[1,8]{1,0:T(1,128)S(1)}, s32[1,8]{1,0:T(1,128)}, u32[]{:S(2)}) copy-start(s32[1,8]{1,0:T(1,128)} %param.16) | copy-start | bytes 100
  7.2 163.5 %all-gather.4.cloned.1.call-start = ((), (), s32[]{:S(2)}) async-start(), calls=%async_computation.2 | async-start | bytes 9437184 | tf_op jit(solution)/shard_map/all_gather | solution.py:360
  9.6 166.0 %all-gather.6.cloned.1.call-start = ((), (), s32[]{:S(2)}) async-start(), calls=%async_computation.3 | async-start | bytes 4718592 | tf_op jit(solution)/shard_map/all_gather | solution.py:361
  9.7 19.1 %collective-permute-start = (bf16[256,256]{1,0:T(8,128)(2,1)S(1)}, bf16[256,256]{1,0:T(8,128)(2,1)S(1)}, u32[]{:S(2)}, u32[]{:S(2)}) collective-permute-start(bf16[256,256]{1,0:T(8,128)(2,1)S(1)} %copy-done.6), channel_id=1, source_target_pairs={{0,1},{1,2},{2,3},{3,0},{4,5},{5,6},{6,7},{7,4},{8,9},{9,10},{10,1... | collective-permute-start | bytes 393224 | tf_op jit(solution)/shard_map/ppermute | solution.py:73
  11.0 17.7 %collective-permute-start.1 = (bf16[256,256]{1,0:T(8,128)(2,1)S(1)}, bf16[256,256]{1,0:T(8,128)(2,1)S(1)}, u32[]{:S(2)}, u32[]{:S(2)}) collective-permute-start(bf16[256,256]{1,0:T(8,128)(2,1)S(1)} %copy-done.6), channel_id=1, source_target_pairs={{0,2},{1,3},{2,0},{3,1},{4,6},{5,7},{6,4},{7,5},{8,10},{9,11},{10,... | collective-permute-start | bytes 393224 | tf_op jit(solution)/shard_map/ppermute | solution.py:73
  12.1 34.9 %collective-permute-start.2 = (bf16[256,256]{1,0:T(8,128)(2,1)S(1)}, bf16[256,256]{1,0:T(8,128)(2,1)S(1)}, u32[]{:S(2)}, u32[]{:S(2)}) collective-permute-start(bf16[256,256]{1,0:T(8,128)(2,1)S(1)} %copy-done.6), channel_id=1, source_target_pairs={{0,3},{1,0},{2,1},{3,2},{4,7},{5,4},{6,5},{7,6},{8,11},{9,8},{10,9... | collective-permute-start | bytes 393224 | tf_op jit(solution)/shard_map/ppermute | solution.py:73
  13.5 142.9 %collective-permute-start.13 = (bf16[256,1024]{1,0:T(8,128)(2,1)}, bf16[256,1024]{1,0:T(8,128)(2,1)}, u32[]{:S(2)}, u32[]{:S(2)}) collective-permute-start(bf16[256,1024]{1,0:T(8,128)(2,1)} %param.22), channel_id=1, source_target_pairs={{0,1},{1,2},{2,3},{3,0},{4,5},{5,6},{6,7},{7,4},{8,9},{9,10},{10,1... | collective-permute-start | bytes 1572872 | tf_op jit(solution)/shard_map/ppermute | solution.py:73
  13.6 144.3 %collective-permute-start.14 = (bf16[256,1024]{1,0:T(8,128)(2,1)}, bf16[256,1024]{1,0:T(8,128)(2,1)}, u32[]{:S(2)}, u32[]{:S(2)}) collective-permute-start(bf16[256,1024]{1,0:T(8,128)(2,1)} %param.22), channel_id=1, source_target_pairs={{0,2},{1,3},{2,0},{3,1},{4,6},{5,7},{6,4},{7,5},{8,10},{9,11},{10,... | collective-permute-start | bytes 1572872 | tf_op jit(solution)/shard_map/ppermute | solution.py:73
  28.7 129.1 %collective-permute-start.15 = (bf16[256,1024]{1,0:T(8,128)(2,1)}, bf16[256,1024]{1,0:T(8,128)(2,1)}, u32[]{:S(2)}, u32[]{:S(2)}) collective-permute-start(bf16[256,1024]{1,0:T(8,128)(2,1)} %param.22), channel_id=1, source_target_pairs={{0,3},{1,0},{2,1},{3,2},{4,7},{5,4},{6,5},{7,6},{8,11},{9,8},{10,9... | collective-permute-start | bytes 1572872 | tf_op jit(solution)/shard_map/ppermute | solution.py:73
  47.1 1.0 copy-start.17
  48.0 4.9 %copy-start.2 = (bf16[2,1024,2,128]{3,2,1,0:T(2,128)(2,1)S(1)}, bf16[2,1024,2,128]{3,2,1,0:T(2,128)(2,1)}, u32[]{:S(2)}) copy-start(bf16[2,1024,2,128]{3,2,1,0:T(2,128)(2,1)} %param.17) | copy-start | bytes 3145732
  48.6 6.8 %collective-permute-start.3 = (bf16[256,2,2,64]{0,3,2,1:T(8,128)(2,1)S(1)}, bf16[256,2,2,64]{0,3,2,1:T(8,128)(2,1)S(1)}, u32[]{:S(2)}, u32[]{:S(2)}) collective-permute-start(bf16[256,2,2,64]{0,3,2,1:T(8,128)(2,1)S(1)} %pad_maximum_fusion.2), channel_id=1, source_target_pairs={{0,4},{4,8},{8,12},{12,16},{16,20},{20,24},{24,28},{28,0},{1,5},{5... | collective-permute-start | bytes 393224 | tf_op jit(solution)/shard_map/ppermute | solution.py:73
  54.1 8.4 %collective-permute-start.4 = (bf16[256,2,2,64]{0,3,2,1:T(8,128)(2,1)S(1)}, bf16[256,2,2,64]{0,3,2,1:T(8,128)(2,1)S(1)}, u32[]{:S(2)}, u32[]{:S(2)}) collective-permute-start(bf16[256,2,2,64]{0,3,2,1:T(8,128)(2,1)S(1)} %pad_maximum_fusion.2), channel_id=1, source_target_pairs={{0,8},{4,12},{8,16},{12,20},{16,24},{20,28},{24,0},{28,4},{1,9},{5... | collective-permute-start | bytes 393224 | tf_op jit(solution)/shard_map/ppermute | solution.py:73
  55.4 10.9 %collective-permute-start.5 = (bf16[256,2,2,64]{0,3,2,1:T(8,128)(2,1)S(1)}, bf16[256,2,2,64]{0,3,2,1:T(8,128)(2,1)S(1)}, u32[]{:S(2)}, u32[]{:S(2)}) collective-permute-start(bf16[256,2,2,64]{0,3,2,1:T(8,128)(2,1)S(1)} %pad_maximum_fusion.2), channel_id=1, source_target_pairs={{0,12},{4,16},{8,20},{12,24},{16,28},{20,0},{24,4},{28,8},{1,13},{... | collective-permute-start | bytes 393224 | tf_op jit(solution)/shard_map/ppermute | solution.py:73
  62.6 5.6 %collective-permute-start.6 = (bf16[256,2,2,64]{0,3,2,1:T(8,128)(2,1)S(1)}, bf16[256,2,2,64]{0,3,2,1:T(8,128)(2,1)S(1)}, u32[]{:S(2)}, u32[]{:S(2)}) collective-permute-start(bf16[256,2,2,64]{0,3,2,1:T(8,128)(2,1)S(1)} %pad_maximum_fusion.2), channel_id=1, source_target_pairs={{0,16},{4,20},{8,24},{12,28},{16,0},{20,4},{24,8},{28,12},{1,17},{... | collective-permute-start | bytes 393224 | tf_op jit(solution)/shard_map/ppermute | solution.py:73
  66.3 7.1 %collective-permute-start.7 = (bf16[256,2,2,64]{0,3,2,1:T(8,128)(2,1)S(1)}, bf16[256,2,2,64]{0,3,2,1:T(8,128)(2,1)S(1)}, u32[]{:S(2)}, u32[]{:S(2)}) collective-permute-start(bf16[256,2,2,64]{0,3,2,1:T(8,128)(2,1)S(1)} %pad_maximum_fusion.2), channel_id=1, source_target_pairs={{0,20},{4,24},{8,28},{12,0},{16,4},{20,8},{24,12},{28,16},{1,21},{... | collective-permute-start | bytes 393224 | tf_op jit(solution)/shard_map/ppermute | solution.py:73
  68.2 9.8 %collective-permute-start.8 = (bf16[256,2,2,64]{0,3,2,1:T(8,128)(2,1)S(1)}, bf16[256,2,2,64]{0,3,2,1:T(8,128)(2,1)S(1)}, u32[]{:S(2)}, u32[]{:S(2)}) collective-permute-start(bf16[256,2,2,64]{0,3,2,1:T(8,128)(2,1)S(1)} %pad_maximum_fusion.2), channel_id=1, source_target_pairs={{0,24},{4,28},{8,0},{12,4},{16,8},{20,12},{24,16},{28,20},{1,25},{... | collective-permute-start | bytes 393224 | tf_op jit(solution)/shard_map/ppermute | solution.py:73
  73.5 5.7 %collective-permute-start.9 = (bf16[256,2,2,64]{0,3,2,1:T(8,128)(2,1)S(1)}, bf16[256,2,2,64]{0,3,2,1:T(8,128)(2,1)S(1)}, u32[]{:S(2)}, u32[]{:S(2)}) collective-permute-start(bf16[256,2,2,64]{0,3,2,1:T(8,128)(2,1)S(1)} %pad_maximum_fusion.2), channel_id=1, source_target_pairs={{0,28},{4,0},{8,4},{12,8},{16,12},{20,16},{24,20},{28,24},{1,29},{... | collective-permute-start | bytes 393224 | tf_op jit(solution)/shard_map/ppermute | solution.py:73
  83.7 1.3 copy-start.1
  121.3 16.4 %all-to-all-start = ((f32[2,2,8,256,1]{3,1,0,4,2:T(2,128)}), f32[2,2,8,256,1]{3,1,0,4,2:T(2,128)S(1)}, u32[]{:S(2)}, u32[]{:S(2)}) async-start(f32[2,2,8,256,1]{3,1,0,4,2:T(2,128)} %copy.48), calls=%async_computation | async-start | bytes 65536 | tf_op jit(solution)/shard_map/all_to_all | solution.py:326
  137.7 4.3 %copy-start.16 = (bf16[1024,256]{1,0:T(8,128)(2,1)S(1)}, bf16[1024,256]{1,0:T(8,128)(2,1)}, u32[]{:S(2)}) copy-start(bf16[1024,256]{1,0:T(8,128)(2,1)} %param.21) | copy-start | bytes 1572868
  137.7 4.8 %copy-start.5 = (f32[2,2,8,256,1]{3,1,0,4,2:T(2,128)}, f32[2,2,8,256,1]{3,1,0,4,2:T(2,128)S(1)}, u32[]{:S(2)}) copy-start(f32[2,2,8,256,1]{3,1,0,4,2:T(2,128)S(1)} %all-to-all-done) | copy-start | bytes 98308
  137.7 18.2 %all-to-all-start.1 = ((bf16[2,2,8,256,64]{3,4,1,0,2:T(8,128)(2,1)}), bf16[2,2,8,256,64]{3,4,1,0,2:T(8,128)(2,1)S(1)}, u32[]{:S(2)}, u32[]{:S(2)}) async-start(bf16[2,2,8,256,64]{3,4,1,0,2:T(8,128)(2,1)} %copy.50), calls=%async_computation.1 | async-start | bytes 2097152 | tf_op jit(solution)/shard_map/all_to_all | solution.py:322
  142.0 1.2 copy-start.11
  142.5 0.7 copy-start.3
  142.5 1.0 copy-start.7
  142.5 1.0 copy-start.9
  143.2 12.8 %copy-start.4 = (f32[256,256]{0,1:T(8,128)S(1)}, f32[256,256]{0,1:T(8,128)}, u32[]{:S(2)}) copy-start(f32[256,256]{0,1:T(8,128)} %copy-done.3) | copy-start | bytes 786436
  143.6 14.2 %copy-start.13 = (f32[256,8]{0,1:T(8,128)S(1)}, f32[256,8]{0,1:T(8,128)}, u32[]{:S(2)}) copy-start(f32[256,8]{0,1:T(8,128)} %param.25) | copy-start | bytes 24580
  143.6 14.2 %copy-start.14 = (s32[256,8]{0,1:T(8,128)S(1)}, s32[256,8]{0,1:T(8,128)}, u32[]{:S(2)}) copy-start(s32[256,8]{0,1:T(8,128)} %param.24) | copy-start | bytes 24580
  156.3 4.7 %collective-permute-start.10 = (bf16[256,256]{0,1:T(8,128)(2,1)S(1)}, bf16[256,256]{0,1:T(8,128)(2,1)S(1)}, u32[]{:S(2)}, u32[]{:S(2)}) collective-permute-start(bf16[256,256]{0,1:T(8,128)(2,1)S(1)} %bitcast.200), channel_id=1, source_target_pairs={{0,1},{1,2},{2,3},{3,0},{4,5},{5,6},{6,7},{7,4},{8,9},{9,10},{10,1... | collective-permute-start | bytes 393224 | tf_op jit(solution)/shard_map/ppermute | solution.py:73
  156.3 11.1 %collective-permute-start.11 = (bf16[256,256]{0,1:T(8,128)(2,1)S(1)}, bf16[256,256]{0,1:T(8,128)(2,1)S(1)}, u32[]{:S(2)}, u32[]{:S(2)}) collective-permute-start(bf16[256,256]{0,1:T(8,128)(2,1)S(1)} %bitcast.201), channel_id=1, source_target_pairs={{0,2},{1,3},{2,0},{3,1},{4,6},{5,7},{6,4},{7,5},{8,10},{9,11},{10,... | collective-permute-start | bytes 393224 | tf_op jit(solution)/shard_map/ppermute | solution.py:73
  156.4 11.9 %collective-permute-start.12 = (bf16[256,256]{0,1:T(8,128)(2,1)S(1)}, bf16[256,256]{0,1:T(8,128)(2,1)S(1)}, u32[]{:S(2)}, u32[]{:S(2)}) collective-permute-start(bf16[256,256]{0,1:T(8,128)(2,1)S(1)} %bitcast.202), channel_id=1, source_target_pairs={{0,3},{1,0},{2,1},{3,2},{4,7},{5,4},{6,5},{7,6},{8,11},{9,8},{10,9... | collective-permute-start | bytes 393224 | tf_op jit(solution)/shard_map/ppermute | solution.py:73
  157.8 12.9 %copy-start.18 = (f32[1024]{0:T(1024)S(1)}, f32[1024]{0:T(1024)}, u32[]{:S(2)}) copy-start(f32[1024]{0:T(1024)} %param.23) | copy-start | bytes 12292
  175.6 10.3 %copy-start.19 = (s32[1,2]{1,0:T(1,128)S(1)}, s32[1,2]{1,0:T(1,128)}, u32[]{:S(2)}) copy-start(s32[1,2]{1,0:T(1,128)} %param.18) | copy-start | bytes 28
  175.6 10.4 %copy-start.8 = (bf16[256,2,32]{0,2,1:T(8,128)(2,1)S(1)}, bf16[256,2,32]{0,2,1:T(8,128)(2,1)}, u32[]{:S(2)}) copy-start(bf16[256,2,32]{0,2,1:T(8,128)(2,1)} %copy-done.7) | copy-start | bytes 98308
  175.6 10.4 %copy-start.10 = (bf16[256,2,32]{0,2,1:T(8,128)(2,1)S(1)}, bf16[256,2,32]{0,2,1:T(8,128)(2,1)}, u32[]{:S(2)}) copy-start(bf16[256,2,32]{0,2,1:T(8,128)(2,1)} %copy-done.9) | copy-start | bytes 98308
  182.2 5.4 %collective-permute-start.16 = (bf16[256,256]{1,0:T(8,128)(2,1)S(1)}, bf16[256,256]{1,0:T(8,128)(2,1)S(1)}, u32[]{:S(2)}, u32[]{:S(2)}) collective-permute-start(bf16[256,256]{1,0:T(8,128)(2,1)S(1)} %get-tuple-element.16), channel_id=1, source_target_pairs={{0,1},{1,2},{2,3},{3,0},{4,5},{5,6},{6,7},{7,4},{8,9},{9,10},{10,1... | collective-permute-start | bytes 393224 | tf_op jit(solution)/shard_map/ppermute | solution.py:384
  182.3 10.8 %collective-permute-start.17 = (bf16[256,256]{1,0:T(8,128)(2,1)S(1)}, bf16[256,256]{1,0:T(8,128)(2,1)S(1)}, u32[]{:S(2)}, u32[]{:S(2)}) collective-permute-start(bf16[256,256]{1,0:T(8,128)(2,1)S(1)} %get-tuple-element.18), channel_id=1, source_target_pairs={{0,2},{1,3},{2,0},{3,1},{4,6},{5,7},{6,4},{7,5},{8,10},{9,11},{10,... | collective-permute-start | bytes 393224 | tf_op jit(solution)/shard_map/ppermute | solution.py:384
  184.5 12.3 %collective-permute-start.18 = (bf16[256,256]{1,0:T(8,128)(2,1)S(1)}, bf16[256,256]{1,0:T(8,128)(2,1)S(1)}, u32[]{:S(2)}, u32[]{:S(2)}) collective-permute-start(bf16[256,256]{1,0:T(8,128)(2,1)S(1)} %get-tuple-element.17), channel_id=1, source_target_pairs={{0,3},{1,0},{2,1},{3,2},{4,7},{5,4},{6,5},{7,6},{8,11},{9,8},{10,9... | collective-permute-start | bytes 393224 | tf_op jit(solution)/shard_map/ppermute | solution.py:384
Sparse Core Ops, SparseCore 0:
  9.9 60.6 all-gather.3
  72.5 41.8 all-gather.5

commit v4 on v0

--- a/solution.py
+++ b/solution.py
@@ -78,6 +78,23 @@
     order = (lax.axis_index(axis_name) - jnp.arange(count, dtype=jnp.int32)) % count
     picked = jnp.take(copies, order, axis=0)
     return jnp.concatenate([picked[index] for index in range(count)], axis=axis)
+
+
+def chip_gather(block, axis_name):
+    count = lax.axis_size(axis_name)
+    me = lax.axis_index(axis_name)
+    if count < 2 or count & (count - 1):
+        copies = shifted_copies(block, axis_name)
+        sources = [(me - shift) % count for shift in range(count)]
+        return jnp.concatenate(copies, axis=0), sources
+    near, near_from = [block], [me]
+    for mask in range(2, count, 2):
+        near.append(lax.ppermute(block, axis_name, [(i, i ^ mask) for i in range(count)]))
+        near_from.append(jnp.bitwise_xor(me, mask))
+    stack = jnp.concatenate(near, axis=0)
+    far = lax.ppermute(stack, axis_name, [(i, i ^ 1) for i in range(count)])
+    sources = near_from + [jnp.bitwise_xor(source, 1) for source in near_from]
+    return jnp.concatenate([stack, far], axis=0), sources
 
 
 def attention_body(group_ref, bound_ref, q_ref, k_ref, v_ref, segq_ref, segk_ref, prefix_ref, out_ref):
@@ -207,7 +224,6 @@
         tok_count, -1, head_dim
     )
     queries = rotate(projected, position).astype(jnp.bfloat16)
-    queries, w_gate_up, w_down = lax.optimization_barrier((queries, w_gate_up, w_down))
     q_groups = queries.shape[1] // kv_heads
     grouped_query = queries.reshape(tok_count, kv_heads, q_groups, head_dim)
     key_value = jnp.dot(normed, w_keyval, preferred_element_type=jnp.float32).reshape(
@@ -219,9 +235,16 @@
         -1, PAGE, kv_heads, 2 * head_dim
     )
     kv_pages = jnp.zeros_like(pages).at[page_table[0]].set(pages)
-    gathered = lax.all_gather(prefix_cache, "req", axis=0, tiled=True)
+    gathered, prefix_from = chip_gather(prefix_cache, "req")
+    local_groups = prefix_cache.shape[0]
+    group_owner = prefix_group[0] // local_groups
+    owner_slot = sum(
+        jnp.where(group_owner == source, position, 0) for position, source in enumerate(prefix_from)
+    )
+    group_place = owner_slot * local_groups + prefix_group[0] % local_groups
+    gathered, w_gate_up, w_down = lax.optimization_barrier((gathered, w_gate_up, w_down))
     attention = attend(
-        grouped_query, key_rows, value_rows, segment_row, prefix_group[0],
+        grouped_query, key_rows, value_rows, segment_row, group_place,
         gathered.transpose(0, 2, 1, 3),
     )
     share_width = hidden_in.shape[1]
@@ -233,10 +256,12 @@
         middle, lax.axis_index("hid") * share_width, share_width, 1
     )
     normed_moe = rms_scale(middle, moe_gain)
-    all_gate_up = lax.all_gather(w_gate_up, "req", axis=0, tiled=True)
-    all_down = lax.all_gather(w_down, "req", axis=0, tiled=True)
-    experts = all_down.shape[0]
-    expert_ids = jnp.arange(experts, dtype=jnp.int32)
+    local_experts = w_down.shape[0]
+    all_gate_up, weight_from = chip_gather(w_gate_up, "req")
+    all_down, _ = chip_gather(w_down, "req")
+    expert_ids = jnp.concatenate(
+        [source * local_experts + jnp.arange(local_experts, dtype=jnp.int32) for source in weight_from]
+    )
     combine = jnp.sum(
         jnp.where(routes[:, :, None] == expert_ids[None, None, :], gates[:, :, None], 0.0), axis=1
     )

time: 191 us -> 250 us (1.31)
  local copies, waits for them, and re-layouts: 8.04 us -> 36.6 us
  waiting for transfers between devices: 89.6 us -> 111 us
  between operations: 14 us -> 1.24 us
  other arithmetic: 8.25 us -> 19.3 us
  starting transfers between devices: 22.8 us -> 32.8 us
    ppermute x0 -> x12, waiting for transfers between devices: none -> 95.2 us  [the longest x9 95.2 us: chip_gather(): lax.ppermute(block, axis_name, [(i, i ^ mask) for i in range(count)])]
    all_gather x3 -> x0, waiting for transfers between devices: 68.4 us -> none  [the longest x1 33.6 us: shards(): all_down = lax.all_gather(w_down, 'req', axis=0, tiled=True)]
    unnamed x31 -> x89, local copies, waits for them, and re-layouts: 4.67 us -> 21.1 us
    ppermute x0 -> x12, starting transfers between devices: none -> 11.5 us  [the longest x9 11.5 us: chip_gather(): lax.ppermute(block, axis_name, [(i, i ^ mask) for i in range(count)])]
    concatenate x0 -> x4, local copies, waits for them, and re-layouts: none -> 9.32 us  [the longest x3 9.24 us: chip_gather(): return (jnp.concatenate([stack, far], axis=0), sources)]
    concatenate x1 -> x3, other arithmetic: 0.83 us -> 9.2 us  [chip_gather(): stack = jnp.concatenate(near, axis=0)]
    ppermute x9, waiting for transfers between devices: 13.4 us -> 10.6 us  [shifted_copies(): copies.append(lax.ppermute(block, axis_name, pairs))]
  transfers between devices with their start and end apart: 15 -> 24, of which waited for: 9 -> 12; matrix products, arithmetic and copies ran while one was open for 11% -> 18% of each run, Pallas kernels for 17% -> 13%
where the time goes in v4:
time: 250 us; the launch traced here: 247 us
  waiting for transfers between devices  111 us (44%)
  local copies, waits for them, and re-layouts  36.6 us (15%)
  starting transfers between devices  32.8 us (13%)
  Pallas kernels  32.4 us (13%)
  other arithmetic  19.3 us (8%)
  matrix products  13.4 us (5%)
    ppermute x9, waiting for transfers between devices, chip_gather(): lax.ppermute(block, axis_name, [(i, i ^ mask) for i in range(count)])  95.2 us
    pallas_call x1, Pallas kernels, attend(): pl.pallas_call(attention_body, grid_spec=grid_spec, out_shape=jax.ShapeDt...  32.4 us
    unnamed x89, local copies, waits for them, and re-layouts  21.1 us
    ppermute x9, starting transfers between devices, shifted_copies(): copies.append(lax.ppermute(block, axis_name, pairs))  16.2 us
    ppermute x9, starting transfers between devices, chip_gather(): lax.ppermute(block, axis_name, [(i, i ^ mask) for i in range(count)])  11.5 us
    ppermute x9, waiting for transfers between devices, shifted_copies(): copies.append(lax.ppermute(block, axis_name, pairs))  10.6 us
    concatenate x3, local copies, waits for them, and re-layouts, chip_gather(): return (jnp.concatenate([stack, far], axis=0), sources)  9.24 us
    concatenate x3, other arithmetic, chip_gather(): stack = jnp.concatenate(near, axis=0)  9.2 us
  transfers between devices with their start and end apart: 24, of which 12 were waited for; matrix products, arithmetic and copies ran while one was open for 18% of the time, Pallas kernels for 13%

profile of v4, /device:TPU:0, one launch (start us, length us, event | category | flops | bytes accessed | tf_op | source)
XLA Modules:
  0.0 246.9 jit_solution(16471495454087124407)
XLA Ops:
  0.6 2.5 %fusion.52 = (bf16[2,1024,2,128]{3,1,2,0:T(8,128)(2,1)S(1)}, bf16[16,1024,2,128]{3,1,2,0:T(8,128)(2,1)}) fusion(bf16[2,1024,2,128]{3,2,1,0:T(2,128)(2,1)} %param.17), kind=kLoop, calls=%fused_computation.136 | loop fusion | bytes 3145728 | tf_op args[3]
  3.2 3.0 %collective-permute-start.3 = (bf16[2,1024,2,128]{3,1,2,0:T(8,128)(2,1)S(1)}, bf16[2,1024,2,128]{3,1,2,0:T(8,128)(2,1)S(1)}, u32[]{:S(2)}, u32[]{:S(2)}) collective-permute-start(bf16[2,1024,2,128]{3,1,2,0:T(8,128)(2,1)S(1)} %get-tuple-element.23), channel_id=1, source_target_pairs={{0,8},{4,12},{8,0},{12,4},{16,24},{20,28},{24,16},{28,20},{1,9},{5... | collective-permute-start | bytes 3145736 | tf_op jit(solution)/shard_map/ppermute | solution.py:92
  6.1 1.5 collective-permute-start.4
  7.7 22.5 %collective-permute-done.3 = bf16[2,1024,2,128]{3,1,2,0:T(8,128)(2,1)S(1)} collective-permute-done((bf16[2,1024,2,128]{3,1,2,0:T(8,128)(2,1)S(1)}, bf16[2,1024,2,128]{3,1,2,0:T(8,128)(2,1)S(1)}, u32[]{:S(2)}, u32[]{:S(2)}) %collective-permute-start.3) | collective-permute-done | bytes 1048608 | tf_op jit(solution)/shard_map/ppermute | solution.py:92
  30.1 23.1 %collective-permute-done.4 = bf16[2,1024,2,128]{3,1,2,0:T(8,128)(2,1)S(1)} collective-permute-done((bf16[2,1024,2,128]{3,1,2,0:T(8,128)(2,1)S(1)}, bf16[2,1024,2,128]{3,1,2,0:T(8,128)(2,1)S(1)}, u32[]{:S(2)}, u32[]{:S(2)}) %collective-permute-start.4) | collective-permute-done | bytes 1048608 | tf_op jit(solution)/shard_map/ppermute | solution.py:92
  53.2 2.3 pad_maximum_fusion
  55.6 1.6 collective-permute-start
  57.2 2.6 %collective-permute-start.1 = (bf16[256,256]{1,0:T(8,128)(2,1)S(1)}, bf16[256,256]{1,0:T(8,128)(2,1)S(1)}, u32[]{:S(2)}, u32[]{:S(2)}) collective-permute-start(bf16[256,256]{1,0:T(8,128)(2,1)S(1)} %copy-done.20), channel_id=1, source_target_pairs={{0,2},{1,3},{2,0},{3,1},{4,6},{5,7},{6,4},{7,5},{8,10},{9,11},{10,... | collective-permute-start | bytes 393224 | tf_op jit(solution)/shard_map/ppermute | solution.py:71
  62.7 1.1 constant_dynamic-update-slice_fusion.1
  63.8 4.6 %constant_dynamic-update-slice_fusion = bf16[16,1024,2,128]{3,1,2,0:T(8,128)(2,1)} fusion(bf16[16,1024,2,128]{3,1,2,0:T(8,128)(2,1)} %constant_dynamic-update-slice_fusion.1, bf16[8,1024,2,128]{3,1,2,0:T(8,128)(2,1)} %collective-permute-done.6), kind=kLoop, calls=%fused_computation.65 | loop fusion | bytes 8388608 | tf_op jit(solution)/shard_map/concatenate | solution.py:97
  68.4 1.2 fusion.51
  69.6 1.2 collective-permute-start.13
  71.7 1.4 collective-permute-start.15
  73.9 2.8 %collective-permute-start.2 = (bf16[256,256]{1,0:T(8,128)(2,1)S(1)}, bf16[256,256]{1,0:T(8,128)(2,1)S(1)}, u32[]{:S(2)}, u32[]{:S(2)}) collective-permute-start(bf16[256,256]{1,0:T(8,128)(2,1)S(1)} %copy-done.20), channel_id=1, source_target_pairs={{0,3},{1,0},{2,1},{3,2},{4,7},{5,4},{6,5},{7,6},{8,11},{9,8},{10,9... | collective-permute-start | bytes 393224 | tf_op jit(solution)/shard_map/ppermute | solution.py:71
  78.3 2.1 collective-permute-done.2
  82.2 1.4 gather_fusion
  83.6 1.2 broadcast_select_fusion
  84.7 10.9 %collective-permute-done.13 = bf16[2,2,1024,128]{3,2,0,1:T(8,128)(2,1)S(1)} collective-permute-done((bf16[2,2,1024,128]{3,2,0,1:T(8,128)(2,1)S(1)}, bf16[2,2,1024,128]{3,2,0,1:T(8,128)(2,1)S(1)}, u32[]{:S(2)}, u32[]{:S(2)}) %collective-permute-start.13) | collective-permute-done | bytes 1048608 | tf_op jit(solution)/shard_map/ppermute | solution.py:92
  95.7 20.7 %collective-permute-done.14 = bf16[2,2,1024,128]{3,2,0,1:T(8,128)(2,1)} collective-permute-done((bf16[2,2,1024,128]{3,2,0,1:T(8,128)(2,1)S(1)}, bf16[2,2,1024,128]{3,2,0,1:T(8,128)(2,1)}, u32[]{:S(2)}, u32[]{:S(2)}) %collective-permute-start.14) | collective-permute-done | bytes 1048608 | tf_op jit(solution)/shard_map/ppermute | solution.py:92
  116.4 1.7 collective-permute-done.15
  118.1 4.1 %pad_maximum_fusion.1 = bf16[8,2,1024,128]{3,2,0,1:T(8,128)(2,1)} fusion(bf16[2,2,1024,128]{3,2,0,1:T(8,128)(2,1)} %collective-permute-done.15, bf16[2,2,1024,128]{3,2,0,1:T(8,128)(2,1)} %collective-permute-done.14, bf16[2,2,1024,128]{3,2,0,1:T(8,128)(2,1)S(1)} %collective-permute-done.13, bf16[2,2,1024,128]{3,2,0,1:T(8,128)(2,1)S(1)} %get-tuple-element.21), kind=kLoop, calls=%fused_computation.7 | loop fusion | flops 6291456 | bytes 8388608 | tf_op jit(solution)/shard_map/concatenate | solution.py:94
  123.4 1.1 fusion.33
  125.4 1.5 collective-permute-start.18
  126.9 1.1 collective-permute-start.19
  132.1 7.3 %collective-permute-done.17 = bf16[2,128,1024]{2,1,0:T(8,128)(2,1)S(1)} collective-permute-done((bf16[2,128,1024]{2,1,0:T(8,128)(2,1)S(1)}, bf16[2,128,1024]{2,1,0:T(8,128)(2,1)S(1)}, u32[]{:S(2)}, u32[]{:S(2)}) %collective-permute-start.17) | collective-permute-done | bytes 524320 | tf_op jit(solution)/shard_map/ppermute | solution.py:92
  139.4 2.0 collective-permute-start.11
  141.4 8.9 %collective-permute-done.18 = bf16[2,128,1024]{2,1,0:T(8,128)(2,1)} collective-permute-done((bf16[2,128,1024]{2,1,0:T(8,128)(2,1)S(1)}, bf16[2,128,1024]{2,1,0:T(8,128)(2,1)}, u32[]{:S(2)}, u32[]{:S(2)}) %collective-permute-start.18) | collective-permute-done | bytes 524320 | tf_op jit(solution)/shard_map/ppermute | solution.py:92
  150.3 3.0 %collective-permute-start.12 = (bf16[256,1024]{1,0:T(8,128)(2,1)}, bf16[256,1024]{1,0:T(8,128)(2,1)}, u32[]{:S(2)}, u32[]{:S(2)}) collective-permute-start(bf16[256,1024]{1,0:T(8,128)(2,1)} %param.22), channel_id=1, source_target_pairs={{0,3},{1,0},{2,1},{3,2},{4,7},{5,4},{6,5},{7,6},{8,11},{9,8},{10,9... | collective-permute-start | bytes 1572872 | tf_op jit(solution)/shard_map/ppermute | solution.py:71
  153.4 2.8 %pad_maximum_fusion.2 = bf16[8,128,1024]{2,1,0:T(8,128)(2,1)} fusion(bf16[2,128,1024]{2,1,0:T(8,128)(2,1)} %collective-permute-done.19, bf16[2,128,1024]{2,1,0:T(8,128)(2,1)} %collective-permute-done.18, bf16[2,128,1024]{2,1,0:T(8,128)(2,1)S(1)} %collective-permute-done.17, bf16[2,128,1024]{2,1,0:T(8,128)(2,1)S(1)} %copy-done.4), kind=kLoop, calls=%fused_computation.16 | loop fusion | flops 3145728 | bytes 4194304 | tf_op jit(solution)/shard_map/concatenate | solution.py:94
  159.6 32.4 %shard_map.149 = f32[2,2,256,64]{3,2,1,0:T(8,128)} custom-call(s32[8]{0:T(128)} %fusion.37.group_ref, s32[16]{0:T(128)} %pad_add_fusion.bound_ref, bf16[2,2,256,64]{3,2,1,0:T(8,128)(2,1)} %maximum_bitcast_fusion.q_ref, bf16[2,256,64]{2,1,0:T(8,128)(2,1)} %maximum_bitcast_fusion.1.k_ref, bf16[2,256,64]{2,1,0:T(8,128)(2,1)} %bitcast.68, ...), custom_call_target="tpu_custom_call" | custom-call | tf_op jit(solution)/shard_map/pallas_call | solution.py:184
  194.3 3.0 %collective-permute-start.9 = (bf16[256,256]{0,1:T(8,128)(2,1)S(1)}, bf16[256,256]{0,1:T(8,128)(2,1)}, u32[]{:S(2)}, u32[]{:S(2)}) collective-permute-start(bf16[256,256]{0,1:T(8,128)(2,1)S(1)} %bitcast.79), channel_id=1, source_target_pairs={{0,3},{1,0},{2,1},{3,2},{4,7},{5,4},{6,5},{7,6},{8,11},{9,8},{10,9... | collective-permute-start | bytes 393224 | tf_op jit(solution)/shard_map/ppermute | solution.py:71
  197.5 4.0 %collective-permute-done.7 = bf16[256,256]{0,1:T(8,128)(2,1)S(1)} collective-permute-done((bf16[256,256]{0,1:T(8,128)(2,1)S(1)}, bf16[256,256]{0,1:T(8,128)(2,1)S(1)}, u32[]{:S(2)}, u32[]{:S(2)}) %collective-permute-start.7) | collective-permute-done | bytes 131104 | tf_op jit(solution)/shard_map/ppermute | solution.py:71
  201.5 4.5 %collective-permute-done.8 = bf16[256,256]{0,1:T(8,128)(2,1)S(1)} collective-permute-done((bf16[256,256]{0,1:T(8,128)(2,1)S(1)}, bf16[256,256]{0,1:T(8,128)(2,1)S(1)}, u32[]{:S(2)}, u32[]{:S(2)}) %collective-permute-start.8) | collective-permute-done | bytes 131104 | tf_op jit(solution)/shard_map/ppermute | solution.py:71
  206.0 2.4 fusion.15
  208.5 1.2 constant_dynamic-update-slice_fusion.12
  211.0 1.4 constant_dynamic-update-slice_fusion.7
  212.4 1.4 constant_dynamic-update-slice_fusion.6
  213.8 1.8 constant_dynamic-update-slice_fusion.10
  215.5 2.1 copy-done.24
  217.6 2.9 %constant_dynamic-update-slice_fusion.5 = bf16[16,2,1024,128]{3,2,0,1:T(8,128)(2,1)S(1)} fusion(bf16[16,2,1024,128]{3,2,0,1:T(8,128)(2,1)S(1)} %constant_dynamic-update-slice_fusion.6, bf16[8,2,1024,128]{3,2,0,1:T(8,128)(2,1)} %collective-permute-done.16), kind=kLoop, calls=%fused_computation.70 | loop fusion | bytes 8388608 | tf_op jit(solution)/shard_map/concatenate | solution.py:97
  220.5 3.3 %copy-done.19 = bf16[16,2,1024,128]{3,2,0,1:T(8,128)(2,1)} copy-done((bf16[16,2,1024,128]{3,2,0,1:T(8,128)(2,1)}, bf16[16,2,1024,128]{3,2,0,1:T(8,128)(2,1)S(1)}, u32[]{:S(2)}) %copy-start.19) | copy-done | bytes 8388632
  223.8 2.7 %fusion = f32[256,16,128]{2,0,1:T(8,128)} fusion(bf16[16,2,1024,128]{3,2,0,1:T(8,128)(2,1)S(1)} %constant_dynamic-update-slice_fusion.5, bf16[256,1024]{1,0:T(8,128)(2,1)S(1)} %get-tuple-element.38, f32[1024]{0:T(1024)S(1)} %copy-done.32, f32[256]{0:T(256)S(1)} %add_rsqrt_fusion), kind=kOutput, calls=%fused_computation.3 | convolution fusion | flops 1074790400 | bytes 6820864 | tf_op jit(solution)/shard_map/td,edf->tef/dot_general | solution.py:271
  226.4 6.8 %convolution_bitcast_fusion = f32[256,1024]{1,0:T(8,128)S(1)} fusion(bf16[16,128,1024]{2,1,0:T(8,128)(2,1)} %copy-done.24, f32[256,16,128]{2,0,1:T(8,128)} %fusion, f32[256,16]{0,1:T(8,128)S(1)} %select_reduce_fusion, bf16[16,2,1024,128]{3,2,0,1:T(8,128)(2,1)} %copy-done.19, bf16[256,1024]{1,0:T(8,128)(2,1)} %copy-done.25, f32[1024]{0:T(1024)S(1)} %copy-done.32, ...), kind=kOutput, calls=%fused_computation.21 | convolution fusion | flops 2152202240 | bytes 12080128 | tf_op jit(solution)/shard_map/tef,efd->td/dot_general | solution.py:275
  233.3 2.6 %collective-permute-start.21 = (bf16[256,256]{1,0:T(8,128)(2,1)S(1)}, bf16[256,256]{1,0:T(8,128)(2,1)S(1)}, u32[]{:S(2)}, u32[]{:S(2)}) collective-permute-start(bf16[256,256]{1,0:T(8,128)(2,1)S(1)} %get-tuple-element.18), channel_id=1, source_target_pairs={{0,1},{1,2},{2,3},{3,0},{4,5},{5,6},{6,7},{7,4},{8,9},{9,10},{10,1... | collective-permute-start | bytes 393224 | tf_op jit(solution)/shard_map/ppermute | solution.py:285
  236.2 2.1 collective-permute-start.23
  240.0 1.6 collective-permute-done.21
  241.5 3.7 %collective-permute-done.22 = bf16[256,256]{1,0:T(8,128)(2,1)S(1)} collective-permute-done((bf16[256,256]{1,0:T(8,128)(2,1)S(1)}, bf16[256,256]{1,0:T(8,128)(2,1)S(1)}, u32[]{:S(2)}, u32[]{:S(2)}) %collective-permute-start.22) | collective-permute-done | bytes 131104 | tf_op jit(solution)/shard_map/ppermute | solution.py:285
  245.2 1.6 add_convert_fusion.1
  (143 shorter events, 22.8 us)
Async XLA Ops:
  0.6 121.9 %copy-start = (bf16[1024,256]{1,0:T(8,128)(2,1)S(1)}, bf16[1024,256]{1,0:T(8,128)(2,1)}, u32[]{:S(2)}) copy-start(bf16[1024,256]{1,0:T(8,128)(2,1)} %param.20) | copy-start | bytes 1572868
  3.2 52.4 %copy-start.20 = (bf16[256,256]{1,0:T(8,128)(2,1)S(1)}, bf16[256,256]{1,0:T(8,128)(2,1)}, u32[]{:S(2)}) copy-start(bf16[256,256]{1,0:T(8,128)(2,1)} %param.14) | copy-start | bytes 393220
  3.2 56.7 %copy-start.26 = (s32[1,256]{1,0:T(1,128)S(1)}, s32[1,256]{1,0:T(1,128)}, u32[]{:S(2)}) copy-start(s32[1,256]{1,0:T(1,128)} %segk_ref.1) | copy-start | bytes 3076
  3.2 27.0 %collective-permute-start.3 = (bf16[2,1024,2,128]{3,1,2,0:T(8,128)(2,1)S(1)}, bf16[2,1024,2,128]{3,1,2,0:T(8,128)(2,1)S(1)}, u32[]{:S(2)}, u32[]{:S(2)}) collective-permute-start(bf16[2,1024,2,128]{3,1,2,0:T(8,128)(2,1)S(1)} %get-tuple-element.23), channel_id=1, source_target_pairs={{0,8},{4,12},{8,0},{12,4},{16,24},{20,28},{24,16},{28,20},{1,9},{5... | collective-permute-start | bytes 3145736 | tf_op jit(solution)/shard_map/ppermute | solution.py:92
  6.1 47.1 %collective-permute-start.4 = (bf16[2,1024,2,128]{3,1,2,0:T(8,128)(2,1)S(1)}, bf16[2,1024,2,128]{3,1,2,0:T(8,128)(2,1)S(1)}, u32[]{:S(2)}, u32[]{:S(2)}) collective-permute-start(bf16[2,1024,2,128]{3,1,2,0:T(8,128)(2,1)S(1)} %get-tuple-element.23), channel_id=1, source_target_pairs={{0,16},{4,20},{8,24},{12,28},{16,0},{20,4},{24,8},{28,12},{1,17},{... | collective-permute-start | bytes 3145736 | tf_op jit(solution)/shard_map/ppermute | solution.py:92
  7.6 45.6 %collective-permute-start.5 = (bf16[2,1024,2,128]{3,1,2,0:T(8,128)(2,1)S(1)}, bf16[2,1024,2,128]{3,1,2,0:T(8,128)(2,1)S(1)}, u32[]{:S(2)}, u32[]{:S(2)}) collective-permute-start(bf16[2,1024,2,128]{3,1,2,0:T(8,128)(2,1)S(1)} %get-tuple-element.23), channel_id=1, source_target_pairs={{0,24},{4,28},{8,16},{12,20},{16,8},{20,12},{24,0},{28,4},{1,25},{... | collective-permute-start | bytes 3145736 | tf_op jit(solution)/shard_map/ppermute | solution.py:92
  55.6 8.2 %collective-permute-start.6 = (bf16[8,1024,2,128]{3,1,2,0:T(8,128)(2,1)}, bf16[8,1024,2,128]{3,1,2,0:T(8,128)(2,1)}, u32[]{:S(2)}, u32[]{:S(2)}) collective-permute-start(bf16[8,1024,2,128]{3,1,2,0:T(8,128)(2,1)} %pad_maximum_fusion), channel_id=1, source_target_pairs={{0,4},{4,0},{8,12},{12,8},{16,20},{20,16},{24,28},{28,24},{1,5},{5... | collective-permute-start | bytes 12582920 | tf_op jit(solution)/shard_map/ppermute | solution.py:95
  55.6 18.3 %collective-permute-start = (bf16[256,256]{1,0:T(8,128)(2,1)S(1)}, bf16[256,256]{1,0:T(8,128)(2,1)S(1)}, u32[]{:S(2)}, u32[]{:S(2)}) collective-permute-start(bf16[256,256]{1,0:T(8,128)(2,1)S(1)} %copy-done.20), channel_id=1, source_target_pairs={{0,1},{1,2},{2,3},{3,0},{4,5},{5,6},{6,7},{7,4},{8,9},{9,10},{10,1... | collective-permute-start | bytes 393224 | tf_op jit(solution)/shard_map/ppermute | solution.py:71
  57.2 21.0 %collective-permute-start.1 = (bf16[256,256]{1,0:T(8,128)(2,1)S(1)}, bf16[256,256]{1,0:T(8,128)(2,1)S(1)}, u32[]{:S(2)}, u32[]{:S(2)}) collective-permute-start(bf16[256,256]{1,0:T(8,128)(2,1)S(1)} %copy-done.20), channel_id=1, source_target_pairs={{0,2},{1,3},{2,0},{3,1},{4,6},{5,7},{6,4},{7,5},{8,10},{9,11},{10,... | collective-permute-start | bytes 393224 | tf_op jit(solution)/shard_map/ppermute | solution.py:71
  63.8 9.3 %copy-start.29 = (s32[1,8]{1,0:T(1,128)S(1)}, s32[1,8]{1,0:T(1,128)}, u32[]{:S(2)}) copy-start(s32[1,8]{1,0:T(1,128)} %param.16) | copy-start | bytes 100
  69.6 26.0 %collective-permute-start.13 = (bf16[2,2,1024,128]{3,2,0,1:T(8,128)(2,1)S(1)}, bf16[2,2,1024,128]{3,2,0,1:T(8,128)(2,1)S(1)}, u32[]{:S(2)}, u32[]{:S(2)}) collective-permute-start(bf16[2,2,1024,128]{3,2,0,1:T(8,128)(2,1)S(1)} %get-tuple-element.21), channel_id=1, source_target_pairs={{0,8},{4,12},{8,0},{12,4},{16,24},{20,28},{24,16},{28,20},{1,9},{5... | collective-permute-start | bytes 3145736 | tf_op jit(solution)/shard_map/ppermute | solution.py:92
  70.9 45.5 %collective-permute-start.14 = (bf16[2,2,1024,128]{3,2,0,1:T(8,128)(2,1)S(1)}, bf16[2,2,1024,128]{3,2,0,1:T(8,128)(2,1)}, u32[]{:S(2)}, u32[]{:S(2)}) collective-permute-start(bf16[2,2,1024,128]{3,2,0,1:T(8,128)(2,1)S(1)} %get-tuple-element.21), channel_id=1, source_target_pairs={{0,16},{4,20},{8,24},{12,28},{16,0},{20,4},{24,8},{28,12},{1,17},{... | collective-permute-start | bytes 3145736 | tf_op jit(solution)/shard_map/ppermute | solution.py:92
  71.7 46.4 %collective-permute-start.15 = (bf16[2,2,1024,128]{3,2,0,1:T(8,128)(2,1)S(1)}, bf16[2,2,1024,128]{3,2,0,1:T(8,128)(2,1)}, u32[]{:S(2)}, u32[]{:S(2)}) collective-permute-start(bf16[2,2,1024,128]{3,2,0,1:T(8,128)(2,1)S(1)} %get-tuple-element.21), channel_id=1, source_target_pairs={{0,24},{4,28},{8,16},{12,20},{16,8},{20,12},{24,0},{28,4},{1,25},{... | collective-permute-start | bytes 3145736 | tf_op jit(solution)/shard_map/ppermute | solution.py:92
  73.9 6.6 %copy-start.21 = (bf16[256,256]{1,0:T(8,128)(2,1)}, bf16[256,256]{1,0:T(8,128)(2,1)S(1)}, u32[]{:S(2)}) copy-start(bf16[256,256]{1,0:T(8,128)(2,1)S(1)} %collective-permute-done) | copy-start | bytes 393220
  73.9 6.6 %collective-permute-start.2 = (bf16[256,256]{1,0:T(8,128)(2,1)S(1)}, bf16[256,256]{1,0:T(8,128)(2,1)S(1)}, u32[]{:S(2)}, u32[]{:S(2)}) collective-permute-start(bf16[256,256]{1,0:T(8,128)(2,1)S(1)} %copy-done.20), channel_id=1, source_target_pairs={{0,3},{1,0},{2,1},{3,2},{4,7},{5,4},{6,5},{7,6},{8,11},{9,8},{10,9... | collective-permute-start | bytes 393224 | tf_op jit(solution)/shard_map/ppermute | solution.py:71
  78.3 114.9 %collective-permute-start.10 = (bf16[256,1024]{1,0:T(8,128)(2,1)}, bf16[256,1024]{1,0:T(8,128)(2,1)}, u32[]{:S(2)}, u32[]{:S(2)}) collective-permute-start(bf16[256,1024]{1,0:T(8,128)(2,1)} %param.22), channel_id=1, source_target_pairs={{0,1},{1,2},{2,3},{3,0},{4,5},{5,6},{6,7},{7,4},{8,9},{9,10},{10,1... | collective-permute-start | bytes 1572872 | tf_op jit(solution)/shard_map/ppermute | solution.py:71
  84.7 37.8 %copy-start.31 = (f32[1024]{0:T(1024)S(1)}, f32[1024]{0:T(1024)}, u32[]{:S(2)}) copy-start(f32[1024]{0:T(1024)} %param.19) | copy-start | bytes 12292
  122.2 95.4 %collective-permute-start.16 = (bf16[8,2,1024,128]{3,2,0,1:T(8,128)(2,1)}, bf16[8,2,1024,128]{3,2,0,1:T(8,128)(2,1)}, u32[]{:S(2)}, u32[]{:S(2)}) collective-permute-start(bf16[8,2,1024,128]{3,2,0,1:T(8,128)(2,1)} %pad_maximum_fusion.1), channel_id=1, source_target_pairs={{0,4},{4,0},{8,12},{12,8},{16,20},{20,16},{24,28},{28,24},{1,5},{5... | collective-permute-start | bytes 12582920 | tf_op jit(solution)/shard_map/ppermute | solution.py:95
  122.3 5.8 %copy-start.11 = (bf16[256,256]{1,0:T(8,128)(2,1)}, bf16[256,256]{1,0:T(8,128)(2,1)S(1)}, u32[]{:S(2)}) copy-start(bf16[256,256]{1,0:T(8,128)(2,1)S(1)} %get-tuple-element.27) | copy-start | bytes 393220
  124.6 14.8 %collective-permute-start.17 = (bf16[2,128,1024]{2,1,0:T(8,128)(2,1)S(1)}, bf16[2,128,1024]{2,1,0:T(8,128)(2,1)S(1)}, u32[]{:S(2)}, u32[]{:S(2)}) collective-permute-start(bf16[2,128,1024]{2,1,0:T(8,128)(2,1)S(1)} %copy-done.4), channel_id=1, source_target_pairs={{0,8},{4,12},{8,0},{12,4},{16,24},{20,28},{24,16},{28,20},{1,9},{5... | collective-permute-start | bytes 1572872 | tf_op jit(solution)/shard_map/ppermute | solution.py:92
  125.4 24.9 %collective-permute-start.18 = (bf16[2,128,1024]{2,1,0:T(8,128)(2,1)S(1)}, bf16[2,128,1024]{2,1,0:T(8,128)(2,1)}, u32[]{:S(2)}, u32[]{:S(2)}) collective-permute-start(bf16[2,128,1024]{2,1,0:T(8,128)(2,1)S(1)} %copy-done.4), channel_id=1, source_target_pairs={{0,16},{4,20},{8,24},{12,28},{16,0},{20,4},{24,8},{28,12},{1,17},{... | collective-permute-start | bytes 1572872 | tf_op jit(solution)/shard_map/ppermute | solution.py:92
  126.9 26.4 %collective-permute-start.19 = (bf16[2,128,1024]{2,1,0:T(8,128)(2,1)S(1)}, bf16[2,128,1024]{2,1,0:T(8,128)(2,1)}, u32[]{:S(2)}, u32[]{:S(2)}) collective-permute-start(bf16[2,128,1024]{2,1,0:T(8,128)(2,1)S(1)} %copy-done.4), channel_id=1, source_target_pairs={{0,24},{4,28},{8,16},{12,20},{16,8},{20,12},{24,0},{28,4},{1,25},{... | collective-permute-start | bytes 1572872 | tf_op jit(solution)/shard_map/ppermute | solution.py:92
  131.1 25.0 %copy-start.9 = (f32[256,2,32]{2,0,1:T(8,128)S(1)}, f32[256,2,32]{2,0,1:T(8,128)}, u32[]{:S(2)}) copy-start(f32[256,2,32]{2,0,1:T(8,128)} %copy.74) | copy-start | bytes 196612
  131.1 25.0 %copy-start.10 = (f32[256,2,32]{2,0,1:T(8,128)S(1)}, f32[256,2,32]{2,0,1:T(8,128)}, u32[]{:S(2)}) copy-start(f32[256,2,32]{2,0,1:T(8,128)} %copy.75) | copy-start | bytes 196612
  132.1 26.6 %copy-start.7 = (bf16[256,4,32]{2,0,1:T(8,128)(2,1)S(1)}, bf16[256,4,32]{2,0,1:T(8,128)(2,1)}, u32[]{:S(2)}) copy-start(bf16[256,4,32]{2,0,1:T(8,128)(2,1)} %get-tuple-element.16) | copy-start | bytes 196612
  132.1 26.6 %copy-start.8 = (bf16[256,4,32]{2,0,1:T(8,128)(2,1)S(1)}, bf16[256,4,32]{2,0,1:T(8,128)(2,1)}, u32[]{:S(2)}) copy-start(bf16[256,4,32]{2,0,1:T(8,128)(2,1)} %get-tuple-element.17) | copy-start | bytes 196612
  139.4 53.9 %collective-permute-start.11 = (bf16[256,1024]{1,0:T(8,128)(2,1)}, bf16[256,1024]{1,0:T(8,128)(2,1)}, u32[]{:S(2)}, u32[]{:S(2)}) collective-permute-start(bf16[256,1024]{1,0:T(8,128)(2,1)} %param.22), channel_id=1, source_target_pairs={{0,2},{1,3},{2,0},{3,1},{4,6},{5,7},{6,4},{7,5},{8,10},{9,11},{10,... | collective-permute-start | bytes 1572872 | tf_op jit(solution)/shard_map/ppermute | solution.py:71
  150.3 43.9 %collective-permute-start.12 = (bf16[256,1024]{1,0:T(8,128)(2,1)}, bf16[256,1024]{1,0:T(8,128)(2,1)}, u32[]{:S(2)}, u32[]{:S(2)}) collective-permute-start(bf16[256,1024]{1,0:T(8,128)(2,1)} %param.22), channel_id=1, source_target_pairs={{0,3},{1,0},{2,1},{3,2},{4,7},{5,4},{6,5},{7,6},{8,11},{9,8},{10,9... | collective-permute-start | bytes 1572872 | tf_op jit(solution)/shard_map/ppermute | solution.py:71
  156.2 57.6 %collective-permute-start.20 = (bf16[8,128,1024]{2,1,0:T(8,128)(2,1)}, bf16[8,128,1024]{2,1,0:T(8,128)(2,1)}, u32[]{:S(2)}, u32[]{:S(2)}) collective-permute-start(bf16[8,128,1024]{2,1,0:T(8,128)(2,1)} %pad_maximum_fusion.2), channel_id=1, source_target_pairs={{0,4},{4,0},{8,12},{12,8},{16,20},{20,16},{24,28},{28,24},{1,5},{5... | collective-permute-start | bytes 6291464 | tf_op jit(solution)/shard_map/ppermute | solution.py:95
  159.5 37.8 %copy-start.27 = (f32[256,8]{0,1:T(8,128)S(1)}, f32[256,8]{0,1:T(8,128)}, u32[]{:S(2)}) copy-start(f32[256,8]{0,1:T(8,128)} %param.25) | copy-start | bytes 24580
  159.5 37.8 %copy-start.28 = (s32[256,8]{0,1:T(8,128)S(1)}, s32[256,8]{0,1:T(8,128)}, u32[]{:S(2)}) copy-start(s32[256,8]{0,1:T(8,128)} %param.24) | copy-start | bytes 24580
  159.5 46.5 %copy-start.12 = (bf16[256,256]{1,0:T(8,128)(2,1)S(1)}, bf16[256,256]{1,0:T(8,128)(2,1)}, u32[]{:S(2)}) copy-start(bf16[256,256]{1,0:T(8,128)(2,1)} %copy-done.11) | copy-start | bytes 393220
  159.5 46.5 %copy-start.14 = (bf16[256,256]{1,0:T(8,128)(2,1)S(1)}, bf16[256,256]{1,0:T(8,128)(2,1)}, u32[]{:S(2)}) copy-start(bf16[256,256]{1,0:T(8,128)(2,1)} %copy-done.13) | copy-start | bytes 393220
  159.5 46.5 %copy-start.16 = (bf16[256,256]{1,0:T(8,128)(2,1)S(1)}, bf16[256,256]{1,0:T(8,128)(2,1)}, u32[]{:S(2)}) copy-start(bf16[256,256]{1,0:T(8,128)(2,1)} %copy-done.15) | copy-start | bytes 393220
  159.6 46.5 %copy-start.18 = (bf16[256,256]{1,0:T(8,128)(2,1)S(1)}, bf16[256,256]{1,0:T(8,128)(2,1)}, u32[]{:S(2)}) copy-start(bf16[256,256]{1,0:T(8,128)(2,1)} %copy-done.17) | copy-start | bytes 393220
  193.2 8.3 %collective-permute-start.7 = (bf16[256,256]{0,1:T(8,128)(2,1)S(1)}, bf16[256,256]{0,1:T(8,128)(2,1)S(1)}, u32[]{:S(2)}, u32[]{:S(2)}) collective-permute-start(bf16[256,256]{0,1:T(8,128)(2,1)S(1)} %bitcast.77), channel_id=1, source_target_pairs={{0,1},{1,2},{2,3},{3,0},{4,5},{5,6},{6,7},{7,4},{8,9},{9,10},{10,1... | collective-permute-start | bytes 393224 | tf_op jit(solution)/shard_map/ppermute | solution.py:71
  193.3 12.7 %collective-permute-start.8 = (bf16[256,256]{0,1:T(8,128)(2,1)S(1)}, bf16[256,256]{0,1:T(8,128)(2,1)S(1)}, u32[]{:S(2)}, u32[]{:S(2)}) collective-permute-start(bf16[256,256]{0,1:T(8,128)(2,1)S(1)} %bitcast.78), channel_id=1, source_target_pairs={{0,2},{1,3},{2,0},{3,1},{4,6},{5,7},{6,4},{7,5},{8,10},{9,11},{10,... | collective-permute-start | bytes 393224 | tf_op jit(solution)/shard_map/ppermute | solution.py:71
  194.3 11.7 %collective-permute-start.9 = (bf16[256,256]{0,1:T(8,128)(2,1)S(1)}, bf16[256,256]{0,1:T(8,128)(2,1)}, u32[]{:S(2)}, u32[]{:S(2)}) collective-permute-start(bf16[256,256]{0,1:T(8,128)(2,1)S(1)} %bitcast.79), channel_id=1, source_target_pairs={{0,3},{1,0},{2,1},{3,2},{4,7},{5,4},{6,5},{7,6},{8,11},{9,8},{10,9... | collective-permute-start | bytes 393224 | tf_op jit(solution)/shard_map/ppermute | solution.py:71
  197.5 13.4 %slice-start = ((s8[8388608]{0:T(1024)(128)(4,1)}), s8[4194304]{0:T(1024)(128)(4,1)S(1)}, s32[]{:S(2)}) async-start(s8[8388608]{0:T(1024)(128)(4,1)} %bitcast.75), calls=%async_computation | async-start | bytes 8388608
  197.5 13.3 %slice-start.1 = ((s8[8388608]{0:T(1024)(128)(4,1)}), s8[4194304]{0:T(1024)(128)(4,1)S(1)}, s32[]{:S(2)}) async-start(s8[8388608]{0:T(1024)(128)(4,1)} %bitcast.75), calls=%async_computation.1 | async-start | bytes 8388608
  208.5 12.0 %copy-start.25 = (bf16[256,1024]{1,0:T(8,128)(2,1)}, bf16[256,1024]{1,0:T(8,128)(2,1)S(1)}, u32[]{:S(2)}) copy-start(bf16[256,1024]{1,0:T(8,128)(2,1)S(1)} %get-tuple-element.38) | copy-start | bytes 1572868
  217.6 6.2 %copy-start.32 = (f32[1024]{0:T(1024)S(1)}, f32[1024]{0:T(1024)}, u32[]{:S(2)}) copy-start(f32[1024]{0:T(1024)} %param.23) | copy-start | bytes 12292
  226.4 11.9 %copy-start.33 = (s32[1,2]{1,0:T(1,128)S(1)}, s32[1,2]{1,0:T(1,128)}, u32[]{:S(2)}) copy-start(s32[1,2]{1,0:T(1,128)} %param.18) | copy-start | bytes 28
  226.4 11.9 %copy-start.5 = (bf16[256,2,64]{2,0,1:T(8,128)(2,1)S(1)}, bf16[256,2,64]{2,0,1:T(8,128)(2,1)}, u32[]{:S(2)}) copy-start(bf16[256,2,64]{2,0,1:T(8,128)(2,1)} %copy.76) | copy-start | bytes 196612
  226.4 20.4 %copy-start.1 = (bf16[1024,256]{1,0:T(8,128)(2,1)S(1)}, bf16[1024,256]{1,0:T(8,128)(2,1)}, u32[]{:S(2)}) copy-start(bf16[1024,256]{1,0:T(8,128)(2,1)} %param.20) | copy-start | bytes 1572868
  233.3 8.3 %collective-permute-start.21 = (bf16[256,256]{1,0:T(8,128)(2,1)S(1)}, bf16[256,256]{1,0:T(8,128)(2,1)S(1)}, u32[]{:S(2)}, u32[]{:S(2)}) collective-permute-start(bf16[256,256]{1,0:T(8,128)(2,1)S(1)} %get-tuple-element.18), channel_id=1, source_target_pairs={{0,1},{1,2},{2,3},{3,0},{4,5},{5,6},{6,7},{7,4},{8,9},{9,10},{10,1... | collective-permute-start | bytes 393224 | tf_op jit(solution)/shard_map/ppermute | solution.py:285
  235.9 9.3 %collective-permute-start.22 = (bf16[256,256]{1,0:T(8,128)(2,1)S(1)}, bf16[256,256]{1,0:T(8,128)(2,1)S(1)}, u32[]{:S(2)}, u32[]{:S(2)}) collective-permute-start(bf16[256,256]{1,0:T(8,128)(2,1)S(1)} %get-tuple-element.20), channel_id=1, source_target_pairs={{0,2},{1,3},{2,0},{3,1},{4,6},{5,7},{6,4},{7,5},{8,10},{9,11},{10,... | collective-permute-start | bytes 393224 | tf_op jit(solution)/shard_map/ppermute | solution.py:285
  236.2 9.0 %collective-permute-start.23 = (bf16[256,256]{1,0:T(8,128)(2,1)S(1)}, bf16[256,256]{1,0:T(8,128)(2,1)S(1)}, u32[]{:S(2)}, u32[]{:S(2)}) collective-permute-start(bf16[256,256]{1,0:T(8,128)(2,1)S(1)} %get-tuple-element.19), channel_id=1, source_target_pairs={{0,3},{1,0},{2,1},{3,2},{4,7},{5,4},{6,5},{7,6},{8,11},{9,8},{10,9... | collective-permute-start | bytes 393224 | tf_op jit(solution)/shard_map/ppermute | solution.py:285
  (12 other events, 39.2 us)

commit v5 on v0

--- a/solution.py
+++ b/solution.py
@@ -233,9 +233,15 @@
         middle, lax.axis_index("hid") * share_width, share_width, 1
     )
     normed_moe = rms_scale(middle, moe_gain)
-    all_gate_up = lax.all_gather(w_gate_up, "req", axis=0, tiled=True)
-    all_down = lax.all_gather(w_down, "req", axis=0, tiled=True)
-    experts = all_down.shape[0]
+    local_experts = w_down.shape[0]
+    gate_up_size = w_gate_up[0].size
+    packed = jnp.concatenate(
+        [w_gate_up.reshape(local_experts, -1), w_down.reshape(local_experts, -1)], axis=1
+    )
+    packed = lax.all_gather(packed, "req", axis=0, tiled=True)
+    experts = packed.shape[0]
+    all_gate_up = packed[:, :gate_up_size].reshape((experts,) + w_gate_up.shape[1:])
+    all_down = packed[:, gate_up_size:].reshape((experts,) + w_down.shape[1:])
     expert_ids = jnp.arange(experts, dtype=jnp.int32)
     combine = jnp.sum(
         jnp.where(routes[:, :, None] == expert_ids[None, None, :], gates[:, :, None], 0.0), axis=1

time: 191 us -> 215 us (1.13)
  local copies, waits for them, and re-layouts: 8.04 us -> 51.6 us
  waiting for transfers between devices: 89.6 us -> 56.7 us
  other arithmetic: 8.25 us -> 22 us
  starting transfers between devices: 22.8 us -> 19.9 us
    unnamed x31 -> x51, local copies, waits for them, and re-layouts: 4.67 us -> 49.3 us
    all_gather x2 -> x1, waiting for transfers between devices: 41.1 us -> 22.3 us  [shards(): packed = lax.all_gather(packed, 'req', axis=0, tiled=True)]
    all_gather x1, waiting for transfers between devices: 27.3 us -> 9.02 us  [shards(): gathered = lax.all_gather(prefix_cache, 'req', axis=0, tiled=True)]
    unnamed x0 -> x1, other arithmetic: none -> 14.6 us
    ppermute x9, starting transfers between devices: 18.2 us -> 15.3 us  [shifted_copies(): copies.append(lax.ppermute(block, axis_name, pairs))]
    ppermute x9, waiting for transfers between devices: 13.4 us -> 16.2 us  [shifted_copies(): copies.append(lax.ppermute(block, axis_name, pairs))]
  transfers between devices with their start and end apart: 15 -> 14, of which waited for: 9 -> 7; matrix products, arithmetic and copies ran while one was open for 11% -> 19% of each run, Pallas kernels for 17% -> 16%
where the time goes in v5:
time: 215 us; the launch traced here: 214 us
  waiting for transfers between devices  56.7 us (26%)
  local copies, waits for them, and re-layouts  51.6 us (24%)
  Pallas kernels  34 us (16%)
  other arithmetic  22 us (10%)
  starting transfers between devices  19.9 us (9%)
  matrix products  15.5 us (7%)
  between operations  14.4 us (7%)
    unnamed x51, local copies, waits for them, and re-layouts  49.3 us
    pallas_call x1, Pallas kernels, attend(): pl.pallas_call(attention_body, grid_spec=grid_spec, out_shape=jax.ShapeDt...  34 us
    all_gather x1, waiting for transfers between devices, shards(): packed = lax.all_gather(packed, 'req', axis=0, tiled=True)  22.3 us
    ppermute x9, waiting for transfers between devices, shifted_copies(): copies.append(lax.ppermute(block, axis_name, pairs))  16.2 us
    ppermute x9, starting transfers between devices, shifted_copies(): copies.append(lax.ppermute(block, axis_name, pairs))  15.3 us
    unnamed x1, other arithmetic  14.6 us
    ppermute x3, waiting for transfers between devices, shards(): incoming = lax.ppermute(outgoing.astype(jnp.bfloat16), 'hid', pairs)  9.15 us
    all_gather x1, waiting for transfers between devices, shards(): gathered = lax.all_gather(prefix_cache, 'req', axis=0, tiled=True)  9.02 us
  transfers between devices with their start and end apart: 14, of which 7 were waited for; matrix products, arithmetic and copies ran while one was open for 19% of the time, Pallas kernels for 16%

profile of v5, /device:TPU:0, one launch (start us, length us, event | category | flops | bytes accessed | tf_op | source)
XLA Modules:
  0.0 214.2 jit_solution(11979009551673030026)
XLA Ops:
  7.2 5.1 %collective-permute-start.2 = (bf16[256,256]{1,0:T(8,128)(2,1)}, bf16[256,256]{1,0:T(8,128)(2,1)S(1)}, u32[]{:S(2)}, u32[]{:S(2)}) collective-permute-start(bf16[256,256]{1,0:T(8,128)(2,1)} %param.14), channel_id=1, source_target_pairs={{0,3},{1,0},{2,1},{3,2},{4,7},{5,4},{6,5},{7,6},{8,11},{9,8},{10,9... | collective-permute-start | bytes 393224 | tf_op jit(solution)/shard_map/ppermute | solution.py:71
  12.4 1.0 collective-permute-start
  13.4 2.4 %copy.55 = bf16[2,1024,2,128]{3,1,2,0:T(8,128)(2,1)} copy(bf16[2,1024,2,128]{3,2,1,0:T(2,128)(2,1)} %param.17) | data formatting | bytes 2097152 | tf_op args[3]
  15.9 0.9 convert_reduce_fusion
  16.8 0.5 multiply_cosine_fusion
  17.4 6.4 %collective-permute-done.1 = bf16[256,256]{1,0:T(8,128)(2,1)S(1)} collective-permute-done((bf16[256,256]{1,0:T(8,128)(2,1)}, bf16[256,256]{1,0:T(8,128)(2,1)S(1)}, u32[]{:S(2)}, u32[]{:S(2)}) %collective-permute-start.1) | collective-permute-done | bytes 131104 | tf_op jit(solution)/shard_map/ppermute | solution.py:71
  23.8 1.0 pad_maximum_fusion
  24.8 0.6 gather_fusion
  25.6 0.2 fusion.18
  25.8 0.4 fusion.36
  26.3 0.2 copy.63
  26.5 0.2 copy.62
  26.9 0.9 pad_maximum_fusion.2
  27.8 0.5 copy.70
  28.3 8.9 %copy.74 = bf16[1,2,2048,128]{3,1,2,0:T(2,128)(2,1)S(1)} copy(bf16[1,2,2048,128]{3,2,1,0:T(8,128)(2,1)S(1)} %bitcast.81) | data formatting | bytes 2097152
  37.2 14.6 %maximum_bitcast_fusion = bf16[1,2,393216]{2,1,0:T(2,128)(2,1)} fusion(bf16[2,131072]{1,0:T(2,128)(2,1)S(1)} %bitcast.79, bf16[2,262144]{1,0:T(2,128)(2,1)S(1)} %bitcast.77), kind=kLoop, calls=%fused_computation.16 | loop fusion | flops 3145728 | bytes 3145728
  51.8 1.6 collective-permute-start.8
  53.4 1.2 collective-permute-start.7
  54.6 1.9 collective-permute-start.6
  56.5 0.8 copy.56.segq_ref
  57.3 0.1 convert_reduce_fusion.2
  57.5 0.6 pad_add_fusion.bound_ref
  58.1 1.6 fusion.34
  60.1 0.8 copy.68
  60.9 0.8 maximum_bitcast_fusion.1.k_ref
  61.6 9.0 %all-gather.4.cloned.1.call-done = bf16[16,1024,2,128]{3,1,2,0:T(8,128)(2,1)} async-done(((bf16[2,1024,2,128]{3,1,2,0:T(8,128)(2,1)}), bf16[16,1024,2,128]{3,1,2,0:T(8,128)(2,1)}) %all-gather.4.cloned.1.call-update) | async-done | bytes 8388624 | tf_op jit(solution)/shard_map/all_gather | solution.py:222
  70.6 34.0 %shard_map.149 = f32[2,2,256,64]{3,2,1,0:T(8,128)} custom-call(s32[8]{0:T(128)} %bitcast.99, s32[16]{0:T(128)} %pad_add_fusion.bound_ref, bf16[2,2,256,64]{3,2,1,0:T(8,128)(2,1)} %bitcast.82, bf16[2,256,64]{2,1,0:T(8,128)(2,1)} %maximum_bitcast_fusion.1.k_ref, bf16[2,256,64]{2,1,0:T(8,128)(2,1)} %bitcast.80, s32[256,1]{1,0:T(8,128)} %copy.56.segq_ref, ...), custom_call_target="tpu_custom_call" | custom-call | tf_op jit(solution)/shard_map/pallas_call | solution.py:167
  104.6 1.1 convert_bitcast_fusion
  105.8 3.4 %collective-permute-start.5 = (bf16[256,256]{0,1:T(8,128)(2,1)S(1)}, bf16[256,256]{0,1:T(8,128)(2,1)S(1)}, u32[]{:S(2)}, u32[]{:S(2)}) collective-permute-start(bf16[256,256]{0,1:T(8,128)(2,1)S(1)} %bitcast.88), channel_id=1, source_target_pairs={{0,3},{1,0},{2,1},{3,2},{4,7},{5,4},{6,5},{7,6},{8,11},{9,8},{10,9... | collective-permute-start | bytes 393224 | tf_op jit(solution)/shard_map/ppermute | solution.py:71
  109.2 1.1 collective-permute-start.3
  110.4 2.7 %collective-permute-done.5 = bf16[256,256]{0,1:T(8,128)(2,1)S(1)} collective-permute-done((bf16[256,256]{0,1:T(8,128)(2,1)S(1)}, bf16[256,256]{0,1:T(8,128)(2,1)S(1)}, u32[]{:S(2)}, u32[]{:S(2)}) %collective-permute-start.5) | collective-permute-done | bytes 131104 | tf_op jit(solution)/shard_map/ppermute | solution.py:71
  113.1 7.1 %collective-permute-done.4 = bf16[256,256]{0,1:T(8,128)(2,1)S(1)} collective-permute-done((bf16[256,256]{0,1:T(8,128)(2,1)S(1)}, bf16[256,256]{0,1:T(8,128)(2,1)S(1)}, u32[]{:S(2)}, u32[]{:S(2)}) %collective-permute-start.4) | collective-permute-done | bytes 131104 | tf_op jit(solution)/shard_map/ppermute | solution.py:71
  120.2 2.0 fusion.15
  122.3 22.3 %all-gather.6.cloned.1.call-done = bf16[8,2,393216]{2,1,0:T(2,128)(2,1)} async-done(((bf16[1,2,393216]{2,1,0:T(2,128)(2,1)}), bf16[8,2,393216]{2,1,0:T(2,128)(2,1)}) %all-gather.6.cloned.1.call-update) | async-done | bytes 12582928 | tf_op jit(solution)/shard_map/all_gather | solution.py:241
  144.6 15.6 %reshape.219 = bf16[16,393216]{1,0:T(8,128)(2,1)} reshape(bf16[8,2,393216]{2,1,0:T(2,128)(2,1)} %all-gather.6.cloned.1.call-done) | data formatting | bytes 25165824
  160.1 7.4 %slice_bitcast_fusion = bf16[2,8,2048,128]{3,1,2,0:T(8,128)(2,1)} fusion(bf16[16,393216]{1,0:T(8,128)(2,1)} %reshape.219), kind=kLoop, calls=%fused_computation.2 | loop fusion | bytes 16777216
  167.5 4.3 %copy.72 = bf16[2,8,128,1024]{3,2,1,0:T(8,128)(2,1)} copy(bf16[2,8,128,1024]{3,1,2,0:T(8,128)(2,1)S(1)} %bitcast.73) | data formatting | bytes 8388608
  171.8 8.1 %copy.71 = bf16[2,8,2048,128]{3,2,1,0:T(8,128)(2,1)} copy(bf16[2,8,2048,128]{3,1,2,0:T(8,128)(2,1)} %slice_bitcast_fusion) | data formatting | bytes 16777216
  179.9 4.8 %fusion.1 = f32[256,16,128]{2,0,1:T(8,128)} fusion(bf16[16,2,1024,128]{3,2,1,0:T(8,128)(2,1)} %bitcast.75, bf16[256,1024]{1,0:T(8,128)(2,1)S(1)} %get-tuple-element.36, f32[1024]{0:T(1024)S(1)} %copy-done.17, f32[256]{0:T(256)S(1)} %add_rsqrt_fusion), kind=kOutput, calls=%fused_computation.6 | convolution fusion | flops 1074790400 | bytes 6820864 | tf_op jit(solution)/shard_map/td,edf->tef/dot_general | solution.py:249
  184.7 6.6 %convolution_bitcast_fusion = f32[256,1024]{1,0:T(8,128)S(1)} fusion(bf16[16,128,1024]{2,1,0:T(8,128)(2,1)} %bitcast.78, f32[256,16,128]{2,0,1:T(8,128)} %fusion.1, bf16[16,2,1024,128]{3,2,1,0:T(8,128)(2,1)} %bitcast.76, f32[256,16]{0,1:T(8,128)S(1)} %select_reduce_fusion, bf16[256,1024]{1,0:T(8,128)(2,1)S(1)} %get-tuple-element.36, ...), kind=kOutput, calls=%fused_computation.20 | convolution fusion | flops 2152202240 | bytes 12080128 | tf_op jit(solution)/shard_map/tef,efd->td/dot_general | solution.py:256
  191.4 3.4 %collective-permute-start.11 = (bf16[256,256]{1,0:T(8,128)(2,1)S(1)}, bf16[256,256]{1,0:T(8,128)(2,1)S(1)}, u32[]{:S(2)}, u32[]{:S(2)}) collective-permute-start(bf16[256,256]{1,0:T(8,128)(2,1)S(1)} %get-tuple-element.21), channel_id=1, source_target_pairs={{0,3},{1,0},{2,1},{3,2},{4,7},{5,4},{6,5},{7,6},{8,11},{9,8},{10,9... | collective-permute-start | bytes 393224 | tf_op jit(solution)/shard_map/ppermute | solution.py:266
  194.8 1.1 collective-permute-start.9
  195.9 0.1 pad_maximum_fusion.3
  196.1 0.6 scatter_fusion
  196.7 0.8 copy.61
  197.5 1.2 collective-permute-done.11
  198.7 7.9 %collective-permute-done.10 = bf16[256,256]{1,0:T(8,128)(2,1)S(1)} collective-permute-done((bf16[256,256]{1,0:T(8,128)(2,1)S(1)}, bf16[256,256]{1,0:T(8,128)(2,1)S(1)}, u32[]{:S(2)}, u32[]{:S(2)}) %collective-permute-start.10) | collective-permute-done | bytes 131104 | tf_op jit(solution)/shard_map/ppermute | solution.py:266
  206.6 0.7 add_convert_fusion.1
  (76 shorter events, 1.2 us)
Async XLA Ops:
  7.2 18.6 %copy-start = (bf16[1024,256]{1,0:T(8,128)(2,1)S(1)}, bf16[1024,256]{1,0:T(8,128)(2,1)}, u32[]{:S(2)}) copy-start(bf16[1024,256]{1,0:T(8,128)(2,1)} %param.20) | copy-start | bytes 1572868
  7.2 18.6 %copy-start.16 = (f32[1024]{0:T(1024)S(1)}, f32[1024]{0:T(1024)}, u32[]{:S(2)}) copy-start(f32[1024]{0:T(1024)} %param.19) | copy-start | bytes 12292
  7.2 63.4 %all-gather.4.cloned.1.call-start = ((), (), s32[]{:S(2)}) async-start(), calls=%async_computation | async-start | bytes 9437184 | tf_op jit(solution)/shard_map/all_gather | solution.py:222
  7.2 10.1 %collective-permute-start.2 = (bf16[256,256]{1,0:T(8,128)(2,1)}, bf16[256,256]{1,0:T(8,128)(2,1)S(1)}, u32[]{:S(2)}, u32[]{:S(2)}) collective-permute-start(bf16[256,256]{1,0:T(8,128)(2,1)} %param.14), channel_id=1, source_target_pairs={{0,3},{1,0},{2,1},{3,2},{4,7},{5,4},{6,5},{7,6},{8,11},{9,8},{10,9... | collective-permute-start | bytes 393224 | tf_op jit(solution)/shard_map/ppermute | solution.py:71
  12.4 11.4 %collective-permute-start.1 = (bf16[256,256]{1,0:T(8,128)(2,1)}, bf16[256,256]{1,0:T(8,128)(2,1)S(1)}, u32[]{:S(2)}, u32[]{:S(2)}) collective-permute-start(bf16[256,256]{1,0:T(8,128)(2,1)} %param.14), channel_id=1, source_target_pairs={{0,2},{1,3},{2,0},{3,1},{4,6},{5,7},{6,4},{7,5},{8,10},{9,11},{10,... | collective-permute-start | bytes 393224 | tf_op jit(solution)/shard_map/ppermute | solution.py:71
  12.4 11.4 %collective-permute-start = (bf16[256,256]{1,0:T(8,128)(2,1)}, bf16[256,256]{1,0:T(8,128)(2,1)S(1)}, u32[]{:S(2)}, u32[]{:S(2)}) collective-permute-start(bf16[256,256]{1,0:T(8,128)(2,1)} %param.14), channel_id=1, source_target_pairs={{0,1},{1,2},{2,3},{3,0},{4,5},{5,6},{6,7},{7,4},{8,9},{9,10},{10,1... | collective-permute-start | bytes 393224 | tf_op jit(solution)/shard_map/ppermute | solution.py:71
  15.8 128.8 %all-gather.6.cloned.1.call-start = ((), (), s32[]{:S(2)}) async-start(), calls=%async_computation.1 | async-start | bytes 14155776 | tf_op jit(solution)/shard_map/all_gather | solution.py:241
  25.5 0.8 copy-start.5
  25.6 0.8 copy-start.7
  25.6 0.7 copy-start.9
  25.6 2.2 %copy-start.4 = (bf16[2,128,1024]{2,1,0:T(8,128)(2,1)S(1)}, bf16[2,128,1024]{2,1,0:T(8,128)(2,1)}, u32[]{:S(2)}) copy-start(bf16[2,128,1024]{2,1,0:T(8,128)(2,1)} %param.27) | copy-start | bytes 1572868
  25.8 2.5 %copy-start.3 = (bf16[2,2,1024,128]{3,2,1,0:T(8,128)(2,1)S(1)}, bf16[2,2,1024,128]{3,2,1,0:T(8,128)(2,1)}, u32[]{:S(2)}) copy-start(bf16[2,2,1024,128]{3,2,1,0:T(8,128)(2,1)} %param.26) | copy-start | bytes 3145732
  26.9 29.6 %copy-start.11 = (s32[1,256]{1,0:T(1,128)S(1)}, s32[1,256]{1,0:T(1,128)}, u32[]{:S(2)}) copy-start(s32[1,256]{1,0:T(1,128)} %segk_ref.1) | copy-start | bytes 3076
  27.8 30.3 %copy-start.6 = (bf16[256,256]{1,0:T(8,128)(2,1)S(1)}, bf16[256,256]{1,0:T(8,128)(2,1)}, u32[]{:S(2)}) copy-start(bf16[256,256]{1,0:T(8,128)(2,1)} %copy-done.5) | copy-start | bytes 393220
  27.8 30.3 %copy-start.8 = (bf16[256,256]{1,0:T(8,128)(2,1)S(1)}, bf16[256,256]{1,0:T(8,128)(2,1)}, u32[]{:S(2)}) copy-start(bf16[256,256]{1,0:T(8,128)(2,1)} %copy-done.7) | copy-start | bytes 393220
  27.8 30.3 %copy-start.10 = (bf16[256,256]{1,0:T(8,128)(2,1)S(1)}, bf16[256,256]{1,0:T(8,128)(2,1)}, u32[]{:S(2)}) copy-start(bf16[256,256]{1,0:T(8,128)(2,1)} %copy-done.9) | copy-start | bytes 393220
  51.8 57.4 %collective-permute-start.8 = (bf16[256,1024]{1,0:T(8,128)(2,1)}, bf16[256,1024]{1,0:T(8,128)(2,1)S(1)}, u32[]{:S(2)}, u32[]{:S(2)}) collective-permute-start(bf16[256,1024]{1,0:T(8,128)(2,1)} %param.22), channel_id=1, source_target_pairs={{0,3},{1,0},{2,1},{3,2},{4,7},{5,4},{6,5},{7,6},{8,11},{9,8},{10,9... | collective-permute-start | bytes 1572872 | tf_op jit(solution)/shard_map/ppermute | solution.py:71
  53.4 57.0 %collective-permute-start.7 = (bf16[256,1024]{1,0:T(8,128)(2,1)}, bf16[256,1024]{1,0:T(8,128)(2,1)S(1)}, u32[]{:S(2)}, u32[]{:S(2)}) collective-permute-start(bf16[256,1024]{1,0:T(8,128)(2,1)} %param.22), channel_id=1, source_target_pairs={{0,2},{1,3},{2,0},{3,1},{4,6},{5,7},{6,4},{7,5},{8,10},{9,11},{10,... | collective-permute-start | bytes 1572872 | tf_op jit(solution)/shard_map/ppermute | solution.py:71
  54.6 55.8 %collective-permute-start.6 = (bf16[256,1024]{1,0:T(8,128)(2,1)}, bf16[256,1024]{1,0:T(8,128)(2,1)}, u32[]{:S(2)}, u32[]{:S(2)}) collective-permute-start(bf16[256,1024]{1,0:T(8,128)(2,1)} %param.22), channel_id=1, source_target_pairs={{0,1},{1,2},{2,3},{3,0},{4,5},{5,6},{6,7},{7,4},{8,9},{9,10},{10,1... | collective-permute-start | bytes 1572872 | tf_op jit(solution)/shard_map/ppermute | solution.py:71
  70.6 39.7 %copy-start.12 = (f32[256,8]{0,1:T(8,128)S(1)}, f32[256,8]{0,1:T(8,128)}, u32[]{:S(2)}) copy-start(f32[256,8]{0,1:T(8,128)} %param.25) | copy-start | bytes 24580
  70.6 39.7 %copy-start.13 = (s32[256,8]{0,1:T(8,128)S(1)}, s32[256,8]{0,1:T(8,128)}, u32[]{:S(2)}) copy-start(s32[256,8]{0,1:T(8,128)} %param.24) | copy-start | bytes 24580
  70.6 49.6 %copy-start.14 = (bf16[256,1024]{1,0:T(8,128)(2,1)S(1)}, bf16[256,1024]{1,0:T(8,128)(2,1)}, u32[]{:S(2)}) copy-start(bf16[256,1024]{1,0:T(8,128)(2,1)} %param.22) | copy-start | bytes 1572868
  105.8 7.3 %collective-permute-start.5 = (bf16[256,256]{0,1:T(8,128)(2,1)S(1)}, bf16[256,256]{0,1:T(8,128)(2,1)S(1)}, u32[]{:S(2)}, u32[]{:S(2)}) collective-permute-start(bf16[256,256]{0,1:T(8,128)(2,1)S(1)} %bitcast.88), channel_id=1, source_target_pairs={{0,3},{1,0},{2,1},{3,2},{4,7},{5,4},{6,5},{7,6},{8,11},{9,8},{10,9... | collective-permute-start | bytes 393224 | tf_op jit(solution)/shard_map/ppermute | solution.py:71
  109.2 11.0 %collective-permute-start.4 = (bf16[256,256]{0,1:T(8,128)(2,1)S(1)}, bf16[256,256]{0,1:T(8,128)(2,1)S(1)}, u32[]{:S(2)}, u32[]{:S(2)}) collective-permute-start(bf16[256,256]{0,1:T(8,128)(2,1)S(1)} %bitcast.89), channel_id=1, source_target_pairs={{0,2},{1,3},{2,0},{3,1},{4,6},{5,7},{6,4},{7,5},{8,10},{9,11},{10,... | collective-permute-start | bytes 393224 | tf_op jit(solution)/shard_map/ppermute | solution.py:71
  109.2 11.0 %collective-permute-start.3 = (bf16[256,256]{0,1:T(8,128)(2,1)S(1)}, bf16[256,256]{0,1:T(8,128)(2,1)S(1)}, u32[]{:S(2)}, u32[]{:S(2)}) collective-permute-start(bf16[256,256]{0,1:T(8,128)(2,1)S(1)} %bitcast.90), channel_id=1, source_target_pairs={{0,1},{1,2},{2,3},{3,0},{4,5},{5,6},{6,7},{7,4},{8,9},{9,10},{10,1... | collective-permute-start | bytes 393224 | tf_op jit(solution)/shard_map/ppermute | solution.py:71
  110.4 9.8 %copy-start.15 = (bf16[256,1024]{1,0:T(8,128)(2,1)}, bf16[256,1024]{1,0:T(8,128)(2,1)S(1)}, u32[]{:S(2)}) copy-start(bf16[256,1024]{1,0:T(8,128)(2,1)S(1)} %collective-permute-done.7) | copy-start | bytes 1572868
  160.1 7.4 %slice-start = ((bf16[16,393216]{1,0:T(8,128)(2,1)}), bf16[16,131072]{1,0:T(8,128)(2,1)S(1)}, s32[]{:S(2)}) async-start(bf16[16,393216]{1,0:T(8,128)(2,1)} %reshape.219), calls=%async_computation.2 | async-start | bytes 8388608 | tf_op jit(solution)/shard_map/slice | solution.py:244
  171.8 8.1 %copy-start.17 = (f32[1024]{0:T(1024)S(1)}, f32[1024]{0:T(1024)}, u32[]{:S(2)}) copy-start(f32[1024]{0:T(1024)} %param.23) | copy-start | bytes 12292
  184.7 11.2 %copy-start.18 = (s32[1,2]{1,0:T(1,128)S(1)}, s32[1,2]{1,0:T(1,128)}, u32[]{:S(2)}) copy-start(s32[1,2]{1,0:T(1,128)} %param.18) | copy-start | bytes 28
  184.7 11.2 %copy-start.2 = (bf16[256,2,64]{2,0,1:T(8,128)(2,1)S(1)}, bf16[256,2,64]{2,0,1:T(8,128)(2,1)}, u32[]{:S(2)}) copy-start(bf16[256,2,64]{2,0,1:T(8,128)(2,1)} %copy.68) | copy-start | bytes 196612
  184.7 22.7 %copy-start.1 = (bf16[1024,256]{1,0:T(8,128)(2,1)S(1)}, bf16[1024,256]{1,0:T(8,128)(2,1)}, u32[]{:S(2)}) copy-start(bf16[1024,256]{1,0:T(8,128)(2,1)} %param.20) | copy-start | bytes 1572868
  191.4 7.4 %collective-permute-start.11 = (bf16[256,256]{1,0:T(8,128)(2,1)S(1)}, bf16[256,256]{1,0:T(8,128)(2,1)S(1)}, u32[]{:S(2)}, u32[]{:S(2)}) collective-permute-start(bf16[256,256]{1,0:T(8,128)(2,1)S(1)} %get-tuple-element.21), channel_id=1, source_target_pairs={{0,3},{1,0},{2,1},{3,2},{4,7},{5,4},{6,5},{7,6},{8,11},{9,8},{10,9... | collective-permute-start | bytes 393224 | tf_op jit(solution)/shard_map/ppermute | solution.py:266
  194.7 11.9 %collective-permute-start.10 = (bf16[256,256]{1,0:T(8,128)(2,1)S(1)}, bf16[256,256]{1,0:T(8,128)(2,1)S(1)}, u32[]{:S(2)}, u32[]{:S(2)}) collective-permute-start(bf16[256,256]{1,0:T(8,128)(2,1)S(1)} %get-tuple-element.22), channel_id=1, source_target_pairs={{0,2},{1,3},{2,0},{3,1},{4,6},{5,7},{6,4},{7,5},{8,10},{9,11},{10,... | collective-permute-start | bytes 393224 | tf_op jit(solution)/shard_map/ppermute | solution.py:266
  194.8 11.9 %collective-permute-start.9 = (bf16[256,256]{1,0:T(8,128)(2,1)S(1)}, bf16[256,256]{1,0:T(8,128)(2,1)S(1)}, u32[]{:S(2)}, u32[]{:S(2)}) collective-permute-start(bf16[256,256]{1,0:T(8,128)(2,1)S(1)} %get-tuple-element.20), channel_id=1, source_target_pairs={{0,1},{1,2},{2,3},{3,0},{4,5},{5,6},{6,7},{7,4},{8,9},{9,10},{10,1... | collective-permute-start | bytes 393224 | tf_op jit(solution)/shard_map/ppermute | solution.py:266
Sparse Core Ops, SparseCore 0:
  15.9 54.7 all-gather.3
  72.5 71.9 all-gather.5

commit v6 on v0

--- a/solution.py
+++ b/solution.py
@@ -233,9 +233,15 @@
         middle, lax.axis_index("hid") * share_width, share_width, 1
     )
     normed_moe = rms_scale(middle, moe_gain)
-    all_gate_up = lax.all_gather(w_gate_up, "req", axis=0, tiled=True)
-    all_down = lax.all_gather(w_down, "req", axis=0, tiled=True)
-    experts = all_down.shape[0]
+    local_experts, hidden_units, model_cols = w_down.shape
+    lane_width = w_gate_up.shape[-1]
+    down_view = w_down.reshape(local_experts, 1, -1, lane_width)
+    packed = lax.all_gather(
+        jnp.concatenate([w_gate_up, down_view], axis=1), "req", axis=0, tiled=True
+    )
+    experts = packed.shape[0]
+    all_gate_up = packed[:, :2]
+    all_down = packed[:, 2].reshape(experts, hidden_units, model_cols // lane_width, lane_width)
     expert_ids = jnp.arange(experts, dtype=jnp.int32)
     combine = jnp.sum(
         jnp.where(routes[:, :, None] == expert_ids[None, None, :], gates[:, :, None], 0.0), axis=1
@@ -248,8 +254,8 @@
     )
     hidden = (jax.nn.silu(gate_proj) * up_proj * combine[:, :, None]).astype(jnp.bfloat16)
     partial_out = jnp.einsum(
-        "tef,efd->td", hidden, all_down, preferred_element_type=jnp.float32
-    )
+        "tef,efhl->thl", hidden, all_down, preferred_element_type=jnp.float32
+    ).reshape(tok_count, model_width)
     hid_count = lax.axis_size("hid")
     hid_index = lax.axis_index("hid")
     expert_sum = lax.dynamic_slice_in_dim(partial_out, hid_index * share_width, share_width, 1)

time: 191 us -> 185 us (0.969)
  waiting for transfers between devices: 89.6 us -> 72.7 us
  local copies, waits for them, and re-layouts: 8.04 us -> 19 us
  Pallas kernels: 32.2 us -> 34.2 us
    all_gather x2 -> x1, waiting for transfers between devices: 41.1 us -> 23.6 us  [shards(): lax.all_gather(jnp.concatenate([w_gate_up, down_view], axis=1), 'req', ax...]
    dot_general x0 -> x2, local copies, waits for them, and re-layouts: none -> 11.2 us  [shards(): jnp.einsum('tef,efhl->thl', hidden, all_down, preferred_element_type=jnp....]
    pallas_call x1, Pallas kernels: 32.2 us -> 34.2 us  [attend(): pl.pallas_call(attention_body, grid_spec=grid_spec, out_shape=jax.ShapeDt...]
    unnamed x31 -> x51, local copies, waits for them, and re-layouts: 4.67 us -> 5.25 us
  transfers between devices with their start and end apart: 15 -> 14, of which waited for: 9 -> 8; matrix products, arithmetic and copies ran while one was open for 11% -> 8% of each run, Pallas kernels for 17% -> 19%
where the time goes in v6:
time: 185 us; the launch traced here: 184 us
  waiting for transfers between devices  72.7 us (39%)
  Pallas kernels  34.2 us (18%)
  starting transfers between devices  22.8 us (12%)
  local copies, waits for them, and re-layouts  19 us (10%)
  between operations  14.4 us (8%)
  matrix products  14.3 us (8%)
  other arithmetic  7.03 us (4%)
    pallas_call x1, Pallas kernels, attend(): pl.pallas_call(attention_body, grid_spec=grid_spec, out_shape=jax.ShapeDt...  34.2 us
    all_gather x1, waiting for transfers between devices, shards(): gathered = lax.all_gather(prefix_cache, 'req', axis=0, tiled=True)  28 us
    all_gather x1, waiting for transfers between devices, shards(): lax.all_gather(jnp.concatenate([w_gate_up, down_view], axis=1), 'req', ax...  23.6 us
    ppermute x9, starting transfers between devices, shifted_copies(): copies.append(lax.ppermute(block, axis_name, pairs))  18.2 us
    ppermute x9, waiting for transfers between devices, shifted_copies(): copies.append(lax.ppermute(block, axis_name, pairs))  13.9 us
    dot_general x2, local copies, waits for them, and re-layouts, shards(): jnp.einsum('tef,efhl->thl', hidden, all_down, preferred_element_type=jnp....  11.2 us
    ppermute x3, waiting for transfers between devices, shards(): incoming = lax.ppermute(outgoing.astype(jnp.bfloat16), 'hid', pairs)  7.17 us
    dot_general x1, matrix products, shards(): jnp.einsum('tef,efhl->thl', hidden, all_down, preferred_element_type=jnp....  6.49 us
  transfers between devices with their start and end apart: 14, of which 8 were waited for; matrix products, arithmetic and copies ran while one was open for 8% of the time, Pallas kernels for 19%

profile of v6, /device:TPU:0, one launch (start us, length us, event | category | flops | bytes accessed | tf_op | source)
XLA Modules:
  0.0 184.4 jit_solution(10384504043060123428)
XLA Ops:
  7.2 2.4 %copy.58 = bf16[2,1024,2,128]{3,1,2,0:T(8,128)(2,1)} copy(bf16[2,1024,2,128]{3,2,1,0:T(2,128)(2,1)} %param.17) | data formatting | bytes 2097152 | tf_op args[3]
  9.8 3.1 %collective-permute-start = (bf16[256,256]{1,0:T(8,128)(2,1)S(1)}, bf16[256,256]{1,0:T(8,128)(2,1)S(1)}, u32[]{:S(2)}, u32[]{:S(2)}) collective-permute-start(bf16[256,256]{1,0:T(8,128)(2,1)S(1)} %copy-done.13), channel_id=1, source_target_pairs={{0,1},{1,2},{2,3},{3,0},{4,5},{5,6},{6,7},{7,4},{8,9},{9,10},{10,1... | collective-permute-start | bytes 393224 | tf_op jit(solution)/shard_map/ppermute | solution.py:71
  12.9 2.6 %collective-permute-start.1 = (bf16[256,256]{1,0:T(8,128)(2,1)S(1)}, bf16[256,256]{1,0:T(8,128)(2,1)S(1)}, u32[]{:S(2)}, u32[]{:S(2)}) collective-permute-start(bf16[256,256]{1,0:T(8,128)(2,1)S(1)} %copy-done.13), channel_id=1, source_target_pairs={{0,2},{1,3},{2,0},{3,1},{4,6},{5,7},{6,4},{7,5},{8,10},{9,11},{10,... | collective-permute-start | bytes 393224 | tf_op jit(solution)/shard_map/ppermute | solution.py:71
  15.4 1.3 collective-permute-start.2
  16.8 0.2 convert_reduce_fusion
  17.0 0.5 multiply_cosine_fusion
  17.6 1.7 collective-permute-done
  19.3 4.8 %collective-permute-done.1 = bf16[256,256]{1,0:T(8,128)(2,1)S(1)} collective-permute-done((bf16[256,256]{1,0:T(8,128)(2,1)S(1)}, bf16[256,256]{1,0:T(8,128)(2,1)S(1)}, u32[]{:S(2)}, u32[]{:S(2)}) %collective-permute-start.1) | collective-permute-done | bytes 131104 | tf_op jit(solution)/shard_map/ppermute | solution.py:71
  24.2 0.6 gather_fusion
  25.0 0.2 fusion.18
  25.2 0.4 copy-done.4
  25.7 0.4 fusion.36
  26.2 0.2 copy.65
  26.4 0.2 copy.66
  26.8 0.9 pad_maximum_fusion.3
  27.6 0.2 reshape.190
  27.9 1.3 pad_maximum_fusion
  29.2 3.3 %collective-permute-start.6 = (bf16[256,1024]{1,0:T(8,128)(2,1)}, bf16[256,1024]{1,0:T(8,128)(2,1)S(1)}, u32[]{:S(2)}, u32[]{:S(2)}) collective-permute-start(bf16[256,1024]{1,0:T(8,128)(2,1)} %param.22), channel_id=1, source_target_pairs={{0,1},{1,2},{2,3},{3,0},{4,5},{5,6},{6,7},{7,4},{8,9},{9,10},{10,1... | collective-permute-start | bytes 1572872 | tf_op jit(solution)/shard_map/ppermute | solution.py:71
  32.5 1.6 collective-permute-start.7
  34.2 0.8 collective-permute-start.8
  35.0 0.8 copy.59.segq_ref
  35.8 0.2 convert_reduce_fusion.2
  35.9 0.6 pad_add_fusion.bound_ref
  36.6 0.4 fusion.34
  37.4 0.8 copy.69
  38.2 0.8 maximum_bitcast_fusion.k_ref
  38.9 28.0 %all-gather.3.cloned.1.call-done = bf16[16,1024,2,128]{3,1,2,0:T(8,128)(2,1)} async-done(((bf16[2,1024,2,128]{3,1,2,0:T(8,128)(2,1)}), bf16[16,1024,2,128]{3,1,2,0:T(8,128)(2,1)}) %all-gather.3.cloned.1.call-update) | async-done | bytes 8388624 | tf_op jit(solution)/shard_map/all_gather | solution.py:222
  66.9 34.2 %shard_map.149 = f32[2,2,256,64]{3,2,1,0:T(8,128)} custom-call(s32[8]{0:T(128)} %bitcast.78, s32[16]{0:T(128)} %pad_add_fusion.bound_ref, bf16[2,2,256,64]{3,2,1,0:T(8,128)(2,1)} %bitcast.62, bf16[2,256,64]{2,1,0:T(8,128)(2,1)} %maximum_bitcast_fusion.k_ref, bf16[2,256,64]{2,1,0:T(8,128)(2,1)} %bitcast.61, s32[256,1]{1,0:T(8,128)} %copy.59.segq_ref, ...), custom_call_target="tpu_custom_call" | custom-call | tf_op jit(solution)/shard_map/pallas_call | solution.py:167
  101.1 1.1 convert_bitcast_fusion
  102.3 1.6 collective-permute-start.3
  103.9 2.4 %collective-permute-start.4 = (bf16[256,256]{0,1:T(8,128)(2,1)S(1)}, bf16[256,256]{0,1:T(8,128)(2,1)S(1)}, u32[]{:S(2)}, u32[]{:S(2)}) collective-permute-start(bf16[256,256]{0,1:T(8,128)(2,1)S(1)} %bitcast.68), channel_id=1, source_target_pairs={{0,2},{1,3},{2,0},{3,1},{4,6},{5,7},{6,4},{7,5},{8,10},{9,11},{10,... | collective-permute-start | bytes 393224 | tf_op jit(solution)/shard_map/ppermute | solution.py:71
  106.3 1.4 collective-permute-start.5
  107.8 2.9 %collective-permute-done.3 = bf16[256,256]{0,1:T(8,128)(2,1)S(1)} collective-permute-done((bf16[256,256]{0,1:T(8,128)(2,1)S(1)}, bf16[256,256]{0,1:T(8,128)(2,1)S(1)}, u32[]{:S(2)}, u32[]{:S(2)}) %collective-permute-start.3) | collective-permute-done | bytes 131104 | tf_op jit(solution)/shard_map/ppermute | solution.py:71
  110.7 4.5 %collective-permute-done.4 = bf16[256,256]{0,1:T(8,128)(2,1)S(1)} collective-permute-done((bf16[256,256]{0,1:T(8,128)(2,1)S(1)}, bf16[256,256]{0,1:T(8,128)(2,1)S(1)}, u32[]{:S(2)}, u32[]{:S(2)}) %collective-permute-start.4) | collective-permute-done | bytes 131104 | tf_op jit(solution)/shard_map/ppermute | solution.py:71
  115.2 2.0 %fusion.15 = (f32[256]{0:T(256)S(1)}, bf16[256,1024]{1,0:T(8,128)(2,1)S(1)}) fusion(bf16[256,1024]{1,0:T(8,128)(2,1)} %collective-permute-done.8, bf16[256,1024]{1,0:T(8,128)(2,1)} %collective-permute-done.7, bf16[256,1024]{1,0:T(8,128)(2,1)S(1)} %collective-permute-done.6, bf16[256,1024]{1,0:T(8,128)(2,1)S(1)} %copy-done.18, ...), kind=kOutput, calls=%fused_computation.24 | convolution fusion | flops 550764288 | bytes 3671040 | tf_op jit(solution)/shard_map/dot_general | solution.py:230
  117.3 23.6 %all-gather.5.cloned.1.call-done = bf16[16,3,1024,128]{3,2,0,1:T(8,128)(2,1)} async-done(((bf16[2,3,1024,128]{3,2,0,1:T(8,128)(2,1)}), bf16[16,3,1024,128]{3,2,0,1:T(8,128)(2,1)}) %all-gather.5.cloned.1.call-update) | async-done | bytes 12582928 | tf_op jit(solution)/shard_map/all_gather | solution.py:239
  140.8 4.5 %slice_bitcast_fusion = bf16[8,128,16,128]{1,0,3,2:T(8,128)(2,1)} fusion(bf16[16,3,1024,128]{3,2,0,1:T(8,128)(2,1)} %all-gather.5.cloned.1.call-done), kind=kLoop, calls=%fused_computation.2 | loop fusion | bytes 8388608 | tf_op jit(solution)/shard_map/tef,efhl->thl/dot_general | solution.py:256
  145.4 6.7 %copy.62 = bf16[8,128,16,128]{3,1,0,2:T(8,128)(2,1)} copy(bf16[8,128,16,128]{1,0,3,2:T(8,128)(2,1)} %slice_bitcast_fusion) | data formatting | bytes 8388608 | tf_op jit(solution)/shard_map/tef,efhl->thl/dot_general | solution.py:256
  152.1 4.8 %fusion.1 = f32[256,16,128]{2,0,1:T(8,128)} fusion(bf16[16,3,1024,128]{3,2,0,1:T(8,128)(2,1)} %all-gather.5.cloned.1.call-done, bf16[256,1024]{1,0:T(8,128)(2,1)S(1)} %get-tuple-element.36, f32[1024]{0:T(1024)S(1)} %copy-done.20, f32[256]{0:T(256)S(1)} %add_rsqrt_fusion), kind=kOutput, calls=%fused_computation.6 | convolution fusion | flops 1074790400 | bytes 6820864 | tf_op jit(solution)/shard_map/td,edf->tef/dot_general | solution.py:249
  156.9 6.5 %convolution_bitcast_fusion = f32[256,1024]{1,0:T(8,128)S(1)} fusion(bf16[1024,16,128]{2,0,1:T(8,128)(2,1)} %bitcast.60, f32[256,16,128]{2,0,1:T(8,128)} %fusion.1, bf16[16,3,1024,128]{3,2,0,1:T(8,128)(2,1)} %all-gather.5.cloned.1.call-done, f32[256,16]{0,1:T(8,128)S(1)} %select_reduce_fusion, bf16[256,1024]{1,0:T(8,128)(2,1)S(1)} %get-tuple-element.36, ...), kind=kOutput, calls=%fused_computation.20 | convolution fusion | flops 2152202240 | bytes 12080128 | tf_op jit(solution)/shard_map/tef,efhl->thl/dot_general | solution.py:256
  163.5 2.5 %collective-permute-start.10 = (bf16[256,256]{1,0:T(8,128)(2,1)S(1)}, bf16[256,256]{1,0:T(8,128)(2,1)S(1)}, u32[]{:S(2)}, u32[]{:S(2)}) collective-permute-start(bf16[256,256]{1,0:T(8,128)(2,1)S(1)} %get-tuple-element.22), channel_id=1, source_target_pairs={{0,2},{1,3},{2,0},{3,1},{4,6},{5,7},{6,4},{7,5},{8,10},{9,11},{10,... | collective-permute-start | bytes 393224 | tf_op jit(solution)/shard_map/ppermute | solution.py:266
  166.0 1.4 collective-permute-start.11
  167.4 0.6 collective-permute-start.9
  168.2 0.6 scatter_fusion
  168.8 0.8 copy.64
  169.6 4.5 %collective-permute-done.10 = bf16[256,256]{1,0:T(8,128)(2,1)S(1)} collective-permute-done((bf16[256,256]{1,0:T(8,128)(2,1)S(1)}, bf16[256,256]{1,0:T(8,128)(2,1)S(1)}, u32[]{:S(2)}, u32[]{:S(2)}) %collective-permute-start.10) | collective-permute-done | bytes 131104 | tf_op jit(solution)/shard_map/ppermute | solution.py:266
  174.1 2.7 %collective-permute-done.9 = bf16[256,256]{1,0:T(8,128)(2,1)S(1)} collective-permute-done((bf16[256,256]{1,0:T(8,128)(2,1)S(1)}, bf16[256,256]{1,0:T(8,128)(2,1)S(1)}, u32[]{:S(2)}, u32[]{:S(2)}) %collective-permute-start.9) | collective-permute-done | bytes 131104 | tf_op jit(solution)/shard_map/ppermute | solution.py:266
  176.8 0.7 add_convert_fusion.1
  (77 shorter events, 1.5 us)
Async XLA Ops:
  7.2 18.5 %copy-start = (bf16[1024,256]{1,0:T(8,128)(2,1)S(1)}, bf16[1024,256]{1,0:T(8,128)(2,1)}, u32[]{:S(2)}) copy-start(bf16[1024,256]{1,0:T(8,128)(2,1)} %param.20) | copy-start | bytes 1572868
  7.2 2.6 %copy-start.13 = (bf16[256,256]{1,0:T(8,128)(2,1)S(1)}, bf16[256,256]{1,0:T(8,128)(2,1)}, u32[]{:S(2)}) copy-start(bf16[256,256]{1,0:T(8,128)(2,1)} %param.14) | copy-start | bytes 393220
  7.2 9.6 %copy-start.14 = (s32[1,256]{1,0:T(1,128)S(1)}, s32[1,256]{1,0:T(1,128)}, u32[]{:S(2)}) copy-start(s32[1,256]{1,0:T(1,128)} %segk_ref.1) | copy-start | bytes 3076
  7.2 59.7 %all-gather.3.cloned.1.call-start = ((), (), s32[]{:S(2)}) async-start(), calls=%async_computation | async-start | bytes 9437184 | tf_op jit(solution)/shard_map/all_gather | solution.py:222
  9.7 16.0 %copy-start.19 = (f32[1024]{0:T(1024)S(1)}, f32[1024]{0:T(1024)}, u32[]{:S(2)}) copy-start(f32[1024]{0:T(1024)} %param.19) | copy-start | bytes 12292
  9.7 131.1 %all-gather.5.cloned.1.call-start = ((), (), s32[]{:S(2)}) async-start(), calls=%async_computation.1 | async-start | bytes 14155776 | tf_op jit(solution)/shard_map/all_gather | solution.py:239
  9.8 9.6 %collective-permute-start = (bf16[256,256]{1,0:T(8,128)(2,1)S(1)}, bf16[256,256]{1,0:T(8,128)(2,1)S(1)}, u32[]{:S(2)}, u32[]{:S(2)}) collective-permute-start(bf16[256,256]{1,0:T(8,128)(2,1)S(1)} %copy-done.13), channel_id=1, source_target_pairs={{0,1},{1,2},{2,3},{3,0},{4,5},{5,6},{6,7},{7,4},{8,9},{9,10},{10,1... | collective-permute-start | bytes 393224 | tf_op jit(solution)/shard_map/ppermute | solution.py:71
  12.9 11.2 %collective-permute-start.1 = (bf16[256,256]{1,0:T(8,128)(2,1)S(1)}, bf16[256,256]{1,0:T(8,128)(2,1)S(1)}, u32[]{:S(2)}, u32[]{:S(2)}) collective-permute-start(bf16[256,256]{1,0:T(8,128)(2,1)S(1)} %copy-done.13), channel_id=1, source_target_pairs={{0,2},{1,3},{2,0},{3,1},{4,6},{5,7},{6,4},{7,5},{8,10},{9,11},{10,... | collective-permute-start | bytes 393224 | tf_op jit(solution)/shard_map/ppermute | solution.py:71
  15.4 8.6 %collective-permute-start.2 = (bf16[256,256]{1,0:T(8,128)(2,1)S(1)}, bf16[256,256]{1,0:T(8,128)(2,1)S(1)}, u32[]{:S(2)}, u32[]{:S(2)}) collective-permute-start(bf16[256,256]{1,0:T(8,128)(2,1)S(1)} %copy-done.13), channel_id=1, source_target_pairs={{0,3},{1,0},{2,1},{3,2},{4,7},{5,4},{6,5},{7,6},{8,11},{9,8},{10,9... | collective-permute-start | bytes 393224 | tf_op jit(solution)/shard_map/ppermute | solution.py:71
  24.9 0.7 copy-start.4
  24.9 0.7 copy-start.6
  24.9 0.7 copy-start.8
  25.0 0.7 copy-start.10
  25.7 1.9 %copy-start.3 = (bf16[2,128,1024]{2,1,0:T(8,128)(2,1)S(1)}, bf16[2,128,1024]{2,1,0:T(8,128)(2,1)}, u32[]{:S(2)}) copy-start(bf16[2,128,1024]{2,1,0:T(8,128)(2,1)} %param.27) | copy-start | bytes 1572868
  26.2 1.7 copy-start.2
  27.6 8.9 %copy-start.5 = (bf16[256,256]{1,0:T(8,128)(2,1)S(1)}, bf16[256,256]{1,0:T(8,128)(2,1)}, u32[]{:S(2)}) copy-start(bf16[256,256]{1,0:T(8,128)(2,1)} %copy-done.4) | copy-start | bytes 393220
  27.6 8.9 %copy-start.7 = (bf16[256,256]{1,0:T(8,128)(2,1)S(1)}, bf16[256,256]{1,0:T(8,128)(2,1)}, u32[]{:S(2)}) copy-start(bf16[256,256]{1,0:T(8,128)(2,1)} %copy-done.6) | copy-start | bytes 393220
  27.6 8.9 %copy-start.9 = (bf16[256,256]{1,0:T(8,128)(2,1)S(1)}, bf16[256,256]{1,0:T(8,128)(2,1)}, u32[]{:S(2)}) copy-start(bf16[256,256]{1,0:T(8,128)(2,1)} %copy-done.8) | copy-start | bytes 393220
  27.6 8.9 %copy-start.11 = (bf16[256,256]{1,0:T(8,128)(2,1)S(1)}, bf16[256,256]{1,0:T(8,128)(2,1)}, u32[]{:S(2)}) copy-start(bf16[256,256]{1,0:T(8,128)(2,1)} %copy-done.10) | copy-start | bytes 393220
  27.9 8.7 %copy-start.17 = (bf16[1024,256]{1,0:T(8,128)(2,1)S(1)}, bf16[1024,256]{1,0:T(8,128)(2,1)}, u32[]{:S(2)}) copy-start(bf16[1024,256]{1,0:T(8,128)(2,1)} %param.21) | copy-start | bytes 1572868
  29.2 77.1 %collective-permute-start.6 = (bf16[256,1024]{1,0:T(8,128)(2,1)}, bf16[256,1024]{1,0:T(8,128)(2,1)S(1)}, u32[]{:S(2)}, u32[]{:S(2)}) collective-permute-start(bf16[256,1024]{1,0:T(8,128)(2,1)} %param.22), channel_id=1, source_target_pairs={{0,1},{1,2},{2,3},{3,0},{4,5},{5,6},{6,7},{7,4},{8,9},{9,10},{10,1... | collective-permute-start | bytes 1572872 | tf_op jit(solution)/shard_map/ppermute | solution.py:71
  32.5 75.2 %collective-permute-start.7 = (bf16[256,1024]{1,0:T(8,128)(2,1)}, bf16[256,1024]{1,0:T(8,128)(2,1)}, u32[]{:S(2)}, u32[]{:S(2)}) collective-permute-start(bf16[256,1024]{1,0:T(8,128)(2,1)} %param.22), channel_id=1, source_target_pairs={{0,2},{1,3},{2,0},{3,1},{4,6},{5,7},{6,4},{7,5},{8,10},{9,11},{10,... | collective-permute-start | bytes 1572872 | tf_op jit(solution)/shard_map/ppermute | solution.py:71
  34.2 73.6 %collective-permute-start.8 = (bf16[256,1024]{1,0:T(8,128)(2,1)}, bf16[256,1024]{1,0:T(8,128)(2,1)}, u32[]{:S(2)}, u32[]{:S(2)}) collective-permute-start(bf16[256,1024]{1,0:T(8,128)(2,1)} %param.22), channel_id=1, source_target_pairs={{0,3},{1,0},{2,1},{3,2},{4,7},{5,4},{6,5},{7,6},{8,11},{9,8},{10,9... | collective-permute-start | bytes 1572872 | tf_op jit(solution)/shard_map/ppermute | solution.py:71
  66.9 40.8 %copy-start.15 = (f32[256,8]{0,1:T(8,128)S(1)}, f32[256,8]{0,1:T(8,128)}, u32[]{:S(2)}) copy-start(f32[256,8]{0,1:T(8,128)} %param.25) | copy-start | bytes 24580
  66.9 40.8 %copy-start.16 = (s32[256,8]{0,1:T(8,128)S(1)}, s32[256,8]{0,1:T(8,128)}, u32[]{:S(2)}) copy-start(s32[256,8]{0,1:T(8,128)} %param.24) | copy-start | bytes 24580
  66.9 48.3 %copy-start.12 = (bf16[256,256]{1,0:T(8,128)(2,1)S(1)}, bf16[256,256]{1,0:T(8,128)(2,1)}, u32[]{:S(2)}) copy-start(bf16[256,256]{1,0:T(8,128)(2,1)} %copy-done.10) | copy-start | bytes 393220
  66.9 48.3 %copy-start.18 = (bf16[256,1024]{1,0:T(8,128)(2,1)S(1)}, bf16[256,1024]{1,0:T(8,128)(2,1)}, u32[]{:S(2)}) copy-start(bf16[256,1024]{1,0:T(8,128)(2,1)} %param.22) | copy-start | bytes 1572868
  102.3 8.3 %collective-permute-start.3 = (bf16[256,256]{0,1:T(8,128)(2,1)S(1)}, bf16[256,256]{0,1:T(8,128)(2,1)S(1)}, u32[]{:S(2)}, u32[]{:S(2)}) collective-permute-start(bf16[256,256]{0,1:T(8,128)(2,1)S(1)} %bitcast.67), channel_id=1, source_target_pairs={{0,1},{1,2},{2,3},{3,0},{4,5},{5,6},{6,7},{7,4},{8,9},{9,10},{10,1... | collective-permute-start | bytes 393224 | tf_op jit(solution)/shard_map/ppermute | solution.py:71
  103.9 11.3 %collective-permute-start.4 = (bf16[256,256]{0,1:T(8,128)(2,1)S(1)}, bf16[256,256]{0,1:T(8,128)(2,1)S(1)}, u32[]{:S(2)}, u32[]{:S(2)}) collective-permute-start(bf16[256,256]{0,1:T(8,128)(2,1)S(1)} %bitcast.68), channel_id=1, source_target_pairs={{0,2},{1,3},{2,0},{3,1},{4,6},{5,7},{6,4},{7,5},{8,10},{9,11},{10,... | collective-permute-start | bytes 393224 | tf_op jit(solution)/shard_map/ppermute | solution.py:71
  106.3 8.9 %collective-permute-start.5 = (bf16[256,256]{0,1:T(8,128)(2,1)S(1)}, bf16[256,256]{0,1:T(8,128)(2,1)S(1)}, u32[]{:S(2)}, u32[]{:S(2)}) collective-permute-start(bf16[256,256]{0,1:T(8,128)(2,1)S(1)} %bitcast.69), channel_id=1, source_target_pairs={{0,3},{1,0},{2,1},{3,2},{4,7},{5,4},{6,5},{7,6},{8,11},{9,8},{10,9... | collective-permute-start | bytes 393224 | tf_op jit(solution)/shard_map/ppermute | solution.py:71
  145.4 6.7 %copy-start.20 = (f32[1024]{0:T(1024)S(1)}, f32[1024]{0:T(1024)}, u32[]{:S(2)}) copy-start(f32[1024]{0:T(1024)} %param.23) | copy-start | bytes 12292
  156.9 11.1 %copy-start.21 = (s32[1,2]{1,0:T(1,128)S(1)}, s32[1,2]{1,0:T(1,128)}, u32[]{:S(2)}) copy-start(s32[1,2]{1,0:T(1,128)} %param.18) | copy-start | bytes 28
  156.9 11.1 %copy-start.1 = (bf16[256,2,64]{2,0,1:T(8,128)(2,1)S(1)}, bf16[256,2,64]{2,0,1:T(8,128)(2,1)}, u32[]{:S(2)}) copy-start(bf16[256,2,64]{2,0,1:T(8,128)(2,1)} %copy.69) | copy-start | bytes 196612
  163.5 10.6 %collective-permute-start.10 = (bf16[256,256]{1,0:T(8,128)(2,1)S(1)}, bf16[256,256]{1,0:T(8,128)(2,1)S(1)}, u32[]{:S(2)}, u32[]{:S(2)}) collective-permute-start(bf16[256,256]{1,0:T(8,128)(2,1)S(1)} %get-tuple-element.22), channel_id=1, source_target_pairs={{0,2},{1,3},{2,0},{3,1},{4,6},{5,7},{6,4},{7,5},{8,10},{9,11},{10,... | collective-permute-start | bytes 393224 | tf_op jit(solution)/shard_map/ppermute | solution.py:266
  166.0 8.1 %collective-permute-start.11 = (bf16[256,256]{1,0:T(8,128)(2,1)S(1)}, bf16[256,256]{1,0:T(8,128)(2,1)S(1)}, u32[]{:S(2)}, u32[]{:S(2)}) collective-permute-start(bf16[256,256]{1,0:T(8,128)(2,1)S(1)} %get-tuple-element.21), channel_id=1, source_target_pairs={{0,3},{1,0},{2,1},{3,2},{4,7},{5,4},{6,5},{7,6},{8,11},{9,8},{10,9... | collective-permute-start | bytes 393224 | tf_op jit(solution)/shard_map/ppermute | solution.py:266
  167.4 9.4 %collective-permute-start.9 = (bf16[256,256]{1,0:T(8,128)(2,1)S(1)}, bf16[256,256]{1,0:T(8,128)(2,1)S(1)}, u32[]{:S(2)}, u32[]{:S(2)}) collective-permute-start(bf16[256,256]{1,0:T(8,128)(2,1)S(1)} %get-tuple-element.20), channel_id=1, source_target_pairs={{0,1},{1,2},{2,3},{3,0},{4,5},{5,6},{6,7},{7,4},{8,9},{9,10},{10,1... | collective-permute-start | bytes 393224 | tf_op jit(solution)/shard_map/ppermute | solution.py:266
Sparse Core Ops, SparseCore 0:
  9.9 56.9 all-gather.2
  68.8 71.9 all-gather.4

commit v7 on v6

--- a/solution.py
+++ b/solution.py
@@ -176,6 +176,32 @@
     return out.transpose(2, 0, 1, 3).reshape(tok_count, -1).astype(jnp.bfloat16)
 
 
+def down_body(hidden_ref, weight_ref, out_ref):
+    total = jnp.zeros(out_ref.shape[1:], jnp.float32)
+    for expert in range(hidden_ref.shape[0]):
+        total = total + jnp.dot(
+            hidden_ref[expert], weight_ref[0, expert], preferred_element_type=jnp.float32
+        )
+    out_ref[0] = total
+
+
+def down_project(hidden, packed):
+    experts, tok_count, units = hidden.shape
+    lanes = packed.shape[3]
+    col_blocks = packed.shape[2] // units
+    return pl.pallas_call(
+        down_body,
+        grid=(col_blocks,),
+        in_specs=[
+            pl.BlockSpec((experts, tok_count, units), lambda c: (0, 0, 0)),
+            pl.BlockSpec((1, experts, units, lanes), lambda c: (2, 0, c, 0)),
+        ],
+        out_specs=pl.BlockSpec((1, tok_count, lanes), lambda c: (c, 0, 0)),
+        out_shape=jax.ShapeDtypeStruct((col_blocks, tok_count, lanes), jnp.float32),
+        compiler_params=pltpu.CompilerParams(dimension_semantics=("arbitrary",)),
+    )(hidden, packed)
+
+
 def shards(
     hidden_in,
     segments,
@@ -235,27 +261,26 @@
     normed_moe = rms_scale(middle, moe_gain)
     local_experts, hidden_units, model_cols = w_down.shape
     lane_width = w_gate_up.shape[-1]
-    down_view = w_down.reshape(local_experts, 1, -1, lane_width)
-    packed = lax.all_gather(
-        jnp.concatenate([w_gate_up, down_view], axis=1), "req", axis=0, tiled=True
-    )
-    experts = packed.shape[0]
-    all_gate_up = packed[:, :2]
-    all_down = packed[:, 2].reshape(experts, hidden_units, model_cols // lane_width, lane_width)
+    down_view = (
+        w_down.reshape(local_experts, hidden_units, model_cols // lane_width, lane_width)
+        .transpose(0, 2, 1, 3)
+        .reshape(local_experts, 1, -1, lane_width)
+    )
+    packed = jnp.concatenate([w_gate_up, down_view], axis=1).transpose(1, 0, 2, 3)
+    packed = lax.all_gather(packed, "req", axis=1, tiled=True)
+    experts = packed.shape[1]
     expert_ids = jnp.arange(experts, dtype=jnp.int32)
     combine = jnp.sum(
         jnp.where(routes[:, :, None] == expert_ids[None, None, :], gates[:, :, None], 0.0), axis=1
     )
     gate_proj = jnp.einsum(
-        "td,edf->tef", normed_moe, all_gate_up[:, 0], preferred_element_type=jnp.float32
+        "td,edf->etf", normed_moe, packed[0], preferred_element_type=jnp.float32
     )
     up_proj = jnp.einsum(
-        "td,edf->tef", normed_moe, all_gate_up[:, 1], preferred_element_type=jnp.float32
-    )
-    hidden = (jax.nn.silu(gate_proj) * up_proj * combine[:, :, None]).astype(jnp.bfloat16)
-    partial_out = jnp.einsum(
-        "tef,efhl->thl", hidden, all_down, preferred_element_type=jnp.float32
-    ).reshape(tok_count, model_width)
+        "td,edf->etf", normed_moe, packed[1], preferred_element_type=jnp.float32
+    )
+    hidden = (jax.nn.silu(gate_proj) * up_proj * combine.T[:, :, None]).astype(jnp.bfloat16)
+    partial_out = down_project(hidden, packed).transpose(1, 0, 2).reshape(tok_count, model_width)
     hid_count = lax.axis_size("hid")
     hid_index = lax.axis_index("hid")
     expert_sum = lax.dynamic_slice_in_dim(partial_out, hid_index * share_width, share_width, 1)

time: 185 us -> 181 us (0.978)
  local copies, waits for them, and re-layouts: 19 us -> 9.18 us
  Pallas kernels: 34.2 us -> 41.7 us
  matrix products: 14.3 us -> 11.4 us
    dot_general x2 -> x0, local copies, waits for them, and re-layouts: 11.2 us -> none  [shards(): jnp.einsum('tef,efhl->thl', hidden, all_down, preferred_element_type=jnp....]
    pallas_call x0 -> x1, Pallas kernels: none -> 7.74 us  [down_project(): pl.pallas_call(down_body, grid=(col_blocks,), in_specs=[pl.BlockSpec((exp...]
    dot_general x2, matrix products: 11.3 us -> 8.11 us  [the longest x1 4.61 us: shards(): jnp.einsum('td,edf->etf', normed_moe, packed[1], preferred_element_type=j...]
    unnamed x51 -> x39, local copies, waits for them, and re-layouts: 5.25 us -> 5.19 us
where the time goes in v7:
time: 181 us; the launch traced here: 180 us
  waiting for transfers between devices  72.8 us (40%)
  Pallas kernels  41.7 us (23%)
  starting transfers between devices  22.9 us (13%)
  between operations  14.4 us (8%)
  matrix products  11.4 us (6%)
  local copies, waits for them, and re-layouts  9.18 us (5%)
  other arithmetic  7.96 us (4%)
    pallas_call x1, Pallas kernels, attend(): pl.pallas_call(attention_body, grid_spec=grid_spec, out_shape=jax.ShapeDt...  34 us
    all_gather x1, waiting for transfers between devices, shards(): gathered = lax.all_gather(prefix_cache, 'req', axis=0, tiled=True)  28.7 us
    all_gather x1, waiting for transfers between devices, shards(): packed = lax.all_gather(packed, 'req', axis=1, tiled=True)  22.9 us
    ppermute x9, starting transfers between devices, shifted_copies(): copies.append(lax.ppermute(block, axis_name, pairs))  18.2 us
    ppermute x9, waiting for transfers between devices, shifted_copies(): copies.append(lax.ppermute(block, axis_name, pairs))  14.4 us
    pallas_call x1, Pallas kernels, down_project(): pl.pallas_call(down_body, grid=(col_blocks,), in_specs=[pl.BlockSpec((exp...  7.74 us
    ppermute x3, waiting for transfers between devices, shards(): incoming = lax.ppermute(outgoing.astype(jnp.bfloat16), 'hid', pairs)  6.7 us
    unnamed x39, local copies, waits for them, and re-layouts  5.19 us
  transfers between devices with their start and end apart: 14, of which 8 were waited for; matrix products, arithmetic and copies ran while one was open for 8% of the time, Pallas kernels for 19%

profile of v7, /device:TPU:0, one launch (start us, length us, event | category | flops | bytes accessed | tf_op | source)
XLA Modules:
  0.0 180.3 jit_solution(14072634286744236053)
XLA Ops:
  7.2 2.4 %copy.80 = bf16[2,1024,2,128]{3,1,2,0:T(8,128)(2,1)} copy(bf16[2,1024,2,128]{3,2,1,0:T(2,128)(2,1)} %param.17) | data formatting | bytes 2097152 | tf_op args[3]
  9.7 3.1 %collective-permute-start = (bf16[256,256]{1,0:T(8,128)(2,1)S(1)}, bf16[256,256]{1,0:T(8,128)(2,1)S(1)}, u32[]{:S(2)}, u32[]{:S(2)}) collective-permute-start(bf16[256,256]{1,0:T(8,128)(2,1)S(1)} %copy-done.3), channel_id=1, source_target_pairs={{0,1},{1,2},{2,3},{3,0},{4,5},{5,6},{6,7},{7,4},{8,9},{9,10},{10,1... | collective-permute-start | bytes 393224 | tf_op jit(solution)/shard_map/ppermute | solution.py:71
  12.8 2.6 %collective-permute-start.1 = (bf16[256,256]{1,0:T(8,128)(2,1)S(1)}, bf16[256,256]{1,0:T(8,128)(2,1)S(1)}, u32[]{:S(2)}, u32[]{:S(2)}) collective-permute-start(bf16[256,256]{1,0:T(8,128)(2,1)S(1)} %copy-done.3), channel_id=1, source_target_pairs={{0,2},{1,3},{2,0},{3,1},{4,6},{5,7},{6,4},{7,5},{8,10},{9,11},{10,... | collective-permute-start | bytes 393224 | tf_op jit(solution)/shard_map/ppermute | solution.py:71
  15.4 1.3 collective-permute-start.2
  16.8 0.2 convert_reduce_fusion
  17.0 0.5 multiply_cosine_fusion
  17.6 1.7 collective-permute-done
  19.3 4.8 %collective-permute-done.1 = bf16[256,256]{1,0:T(8,128)(2,1)S(1)} collective-permute-done((bf16[256,256]{1,0:T(8,128)(2,1)S(1)}, bf16[256,256]{1,0:T(8,128)(2,1)S(1)}, u32[]{:S(2)}, u32[]{:S(2)}) %collective-permute-start.1) | collective-permute-done | bytes 131104 | tf_op jit(solution)/shard_map/ppermute | solution.py:71
  24.2 0.6 gather_fusion
  24.9 0.2 fusion.23
  25.2 0.5 fusion.38
  25.7 0.2 copy.100
  25.9 0.2 copy.101
  26.1 0.1 subtract_convert_fusion
  26.3 0.9 pad_maximum_fusion.2
  27.3 1.3 maximum_bitcast_fusion
  28.7 3.3 %collective-permute-start.6 = (bf16[256,1024]{1,0:T(8,128)(2,1)}, bf16[256,1024]{1,0:T(8,128)(2,1)}, u32[]{:S(2)}, u32[]{:S(2)}) collective-permute-start(bf16[256,1024]{1,0:T(8,128)(2,1)} %param.22), channel_id=1, source_target_pairs={{0,1},{1,2},{2,3},{3,0},{4,5},{5,6},{6,7},{7,4},{8,9},{9,10},{10,1... | collective-permute-start | bytes 1572872 | tf_op jit(solution)/shard_map/ppermute | solution.py:71
  32.0 1.6 collective-permute-start.7
  33.6 0.8 collective-permute-start.8
  34.4 0.8 copy.81.segq_ref
  35.2 0.2 convert_reduce_fusion.2
  35.4 0.6 pad_add_fusion.bound_ref
  35.9 0.4 fusion.36
  36.7 0.8 copy.108
  37.5 0.8 maximum_bitcast_fusion.1.k_ref
  38.3 28.7 %all-gather.3.cloned.1.call-done = bf16[16,1024,2,128]{3,1,2,0:T(8,128)(2,1)} async-done(((bf16[2,1024,2,128]{3,1,2,0:T(8,128)(2,1)}), bf16[16,1024,2,128]{3,1,2,0:T(8,128)(2,1)}) %all-gather.3.cloned.1.call-update) | async-done | bytes 8388624 | tf_op jit(solution)/shard_map/all_gather | solution.py:248
  67.0 34.0 %shard_map.149 = f32[2,2,256,64]{3,2,1,0:T(8,128)} custom-call(s32[8]{0:T(128)} %bitcast.103, s32[16]{0:T(128)} %pad_add_fusion.bound_ref, bf16[2,2,256,64]{3,2,1,0:T(8,128)(2,1)} %bitcast.86, bf16[2,256,64]{2,1,0:T(8,128)(2,1)} %maximum_bitcast_fusion.1.k_ref, bf16[2,256,64]{2,1,0:T(8,128)(2,1)} %bitcast.85, s32[256,1]{1,0:T(8,128)} %copy.81.segq_ref, ...), custom_call_target="tpu_custom_call" | custom-call | tf_op jit(solution)/shard_map/pallas_call | solution.py:167
  100.9 1.1 convert_bitcast_fusion
  102.1 1.6 collective-permute-start.3
  103.7 2.4 %collective-permute-start.4 = (bf16[256,256]{0,1:T(8,128)(2,1)S(1)}, bf16[256,256]{0,1:T(8,128)(2,1)S(1)}, u32[]{:S(2)}, u32[]{:S(2)}) collective-permute-start(bf16[256,256]{0,1:T(8,128)(2,1)S(1)} %bitcast.92), channel_id=1, source_target_pairs={{0,2},{1,3},{2,0},{3,1},{4,6},{5,7},{6,4},{7,5},{8,10},{9,11},{10,... | collective-permute-start | bytes 393224 | tf_op jit(solution)/shard_map/ppermute | solution.py:71
  106.1 1.4 collective-permute-start.5
  107.6 2.8 %collective-permute-done.3 = bf16[256,256]{0,1:T(8,128)(2,1)S(1)} collective-permute-done((bf16[256,256]{0,1:T(8,128)(2,1)S(1)}, bf16[256,256]{0,1:T(8,128)(2,1)S(1)}, u32[]{:S(2)}, u32[]{:S(2)}) %collective-permute-start.3) | collective-permute-done | bytes 131104 | tf_op jit(solution)/shard_map/ppermute | solution.py:71
  110.4 5.1 %collective-permute-done.4 = bf16[256,256]{0,1:T(8,128)(2,1)S(1)} collective-permute-done((bf16[256,256]{0,1:T(8,128)(2,1)S(1)}, bf16[256,256]{0,1:T(8,128)(2,1)S(1)}, u32[]{:S(2)}, u32[]{:S(2)}) %collective-permute-start.4) | collective-permute-done | bytes 131104 | tf_op jit(solution)/shard_map/ppermute | solution.py:71
  115.6 2.4 %fusion.20 = (f32[256]{0:T(256)S(1)}, bf16[256,1024]{1,0:T(8,128)(2,1)S(1)}) fusion(bf16[256,1024]{1,0:T(8,128)(2,1)} %copy-done.10, bf16[256,1024]{1,0:T(8,128)(2,1)} %collective-permute-done.7, bf16[256,1024]{1,0:T(8,128)(2,1)} %collective-permute-done.6, bf16[256,1024]{1,0:T(8,128)(2,1)} %param.22, bf16[256,256]{0,1:T(8,128)(2,1)S(1)} %collective-permute-done.5, ...), kind=kOutput, calls=%fused_computation.29 | convolution fusion | flops 550764288 | bytes 3671040 | tf_op jit(solution)/shard_map/dot_general | solution.py:256
  118.0 22.9 %all-gather.5.cloned.1.call-done.weight_ref = bf16[3,16,1024,128]{3,2,1,0:T(8,128)(2,1)} async-done(((bf16[3,2,1024,128]{3,2,1,0:T(8,128)(2,1)}), bf16[3,16,1024,128]{3,2,1,0:T(8,128)(2,1)}) %all-gather.5.cloned.1.call-update) | async-done | bytes 12582928 | tf_op jit(solution)/shard_map/all_gather | solution.py:270
  140.9 3.5 %fusion.1 = f32[16,128,256]{1,2,0:T(8,128)S(1)} fusion(bf16[3,16,1024,128]{3,2,1,0:T(8,128)(2,1)} %all-gather.5.cloned.1.call-done.weight_ref, bf16[256,1024]{1,0:T(8,128)(2,1)S(1)} %get-tuple-element.36, f32[1024]{0:T(1024)S(1)} %copy-done.12, f32[256]{0:T(256)S(1)} %add_rsqrt_fusion), kind=kOutput, calls=%fused_computation.5 | convolution fusion | flops 1074790400 | bytes 6820864 | tf_op jit(solution)/shard_map/td,edf->etf/dot_general | solution.py:276
  144.4 4.6 %fusion.11.hidden_ref = bf16[16,256,128]{2,1,0:T(8,128)(2,1)} fusion(f32[16,128,256]{1,2,0:T(8,128)S(1)} %fusion.1, bf16[3,16,1024,128]{3,2,1,0:T(8,128)(2,1)} %all-gather.5.cloned.1.call-done.weight_ref, f32[16,256]{1,0:T(8,128)S(1)} %bitcast.102, bf16[256,1024]{1,0:T(8,128)(2,1)S(1)} %get-tuple-element.36, f32[1024]{0:T(1024)S(1)} %copy-done.12, ...), kind=kOutput, calls=%fused_computation.16 | convolution fusion | flops 1078460416 | bytes 7885824 | tf_op jit(solution)/shard_map/td,edf->etf/dot_general | solution.py:279
  149.0 7.7 %shard_map.150 = f32[8,256,128]{2,1,0:T(8,128)} custom-call(bf16[16,256,128]{2,1,0:T(8,128)(2,1)} %fusion.11.hidden_ref, bf16[3,16,1024,128]{3,2,1,0:T(8,128)(2,1)} %all-gather.5.cloned.1.call-done.weight_ref), custom_call_target="tpu_custom_call" | custom-call | tf_op jit(solution)/shard_map/pallas_call | solution.py:192
  156.8 1.6 copy.89
  158.5 2.5 %collective-permute-start.10 = (bf16[256,256]{1,0:T(8,128)(2,1)S(1)}, bf16[256,256]{1,0:T(8,128)(2,1)S(1)}, u32[]{:S(2)}, u32[]{:S(2)}) collective-permute-start(bf16[256,256]{1,0:T(8,128)(2,1)S(1)} %copy.104), channel_id=1, source_target_pairs={{0,2},{1,3},{2,0},{3,1},{4,6},{5,7},{6,4},{7,5},{8,10},{9,11},{10,... | collective-permute-start | bytes 393224 | tf_op jit(solution)/shard_map/ppermute | solution.py:291
  161.1 1.5 collective-permute-start.11
  162.7 0.6 collective-permute-start.9
  163.3 0.1 pad_maximum_fusion.3
  163.5 0.6 scatter_fusion
  164.2 0.8 copy.95
  165.1 4.0 %collective-permute-done.10 = bf16[256,256]{1,0:T(8,128)(2,1)S(1)} collective-permute-done((bf16[256,256]{1,0:T(8,128)(2,1)S(1)}, bf16[256,256]{1,0:T(8,128)(2,1)S(1)}, u32[]{:S(2)}, u32[]{:S(2)}) %collective-permute-start.10) | collective-permute-done | bytes 131104 | tf_op jit(solution)/shard_map/ppermute | solution.py:291
  169.1 2.7 %collective-permute-done.9 = bf16[256,256]{1,0:T(8,128)(2,1)S(1)} collective-permute-done((bf16[256,256]{1,0:T(8,128)(2,1)S(1)}, bf16[256,256]{1,0:T(8,128)(2,1)S(1)}, u32[]{:S(2)}, u32[]{:S(2)}) %collective-permute-start.9) | collective-permute-done | bytes 131104 | tf_op jit(solution)/shard_map/ppermute | solution.py:291
  171.8 1.6 add_convert_fusion.1
  (66 shorter events, 1.7 us)
Async XLA Ops:
  7.2 20.0 %copy-start = (bf16[2,128,1024]{2,1,0:T(8,128)(2,1)S(1)}, bf16[2,128,1024]{2,1,0:T(8,128)(2,1)}, u32[]{:S(2)}) copy-start(bf16[2,128,1024]{2,1,0:T(8,128)(2,1)} %param.27) | copy-start | bytes 1572868
  7.2 2.6 %copy-start.3 = (bf16[256,256]{1,0:T(8,128)(2,1)S(1)}, bf16[256,256]{1,0:T(8,128)(2,1)}, u32[]{:S(2)}) copy-start(bf16[256,256]{1,0:T(8,128)(2,1)} %param.14) | copy-start | bytes 393220
  7.2 9.6 %copy-start.5 = (s32[1,256]{1,0:T(1,128)S(1)}, s32[1,256]{1,0:T(1,128)}, u32[]{:S(2)}) copy-start(s32[1,256]{1,0:T(1,128)} %segk_ref.1) | copy-start | bytes 3076
  7.2 59.8 %all-gather.3.cloned.1.call-start = ((), (), s32[]{:S(2)}) async-start(), calls=%async_computation | async-start | bytes 9437184 | tf_op jit(solution)/shard_map/all_gather | solution.py:248
  9.7 131.2 %all-gather.5.cloned.1.call-start = ((), (), s32[]{:S(2)}) async-start(), calls=%async_computation.1 | async-start | bytes 14155776 | tf_op jit(solution)/shard_map/all_gather | solution.py:270
  9.7 9.6 %collective-permute-start = (bf16[256,256]{1,0:T(8,128)(2,1)S(1)}, bf16[256,256]{1,0:T(8,128)(2,1)S(1)}, u32[]{:S(2)}, u32[]{:S(2)}) collective-permute-start(bf16[256,256]{1,0:T(8,128)(2,1)S(1)} %copy-done.3), channel_id=1, source_target_pairs={{0,1},{1,2},{2,3},{3,0},{4,5},{5,6},{6,7},{7,4},{8,9},{9,10},{10,1... | collective-permute-start | bytes 393224 | tf_op jit(solution)/shard_map/ppermute | solution.py:71
  12.8 11.2 %collective-permute-start.1 = (bf16[256,256]{1,0:T(8,128)(2,1)S(1)}, bf16[256,256]{1,0:T(8,128)(2,1)S(1)}, u32[]{:S(2)}, u32[]{:S(2)}) collective-permute-start(bf16[256,256]{1,0:T(8,128)(2,1)S(1)} %copy-done.3), channel_id=1, source_target_pairs={{0,2},{1,3},{2,0},{3,1},{4,6},{5,7},{6,4},{7,5},{8,10},{9,11},{10,... | collective-permute-start | bytes 393224 | tf_op jit(solution)/shard_map/ppermute | solution.py:71
  15.4 8.6 %collective-permute-start.2 = (bf16[256,256]{1,0:T(8,128)(2,1)S(1)}, bf16[256,256]{1,0:T(8,128)(2,1)S(1)}, u32[]{:S(2)}, u32[]{:S(2)}) collective-permute-start(bf16[256,256]{1,0:T(8,128)(2,1)S(1)} %copy-done.3), channel_id=1, source_target_pairs={{0,3},{1,0},{2,1},{3,2},{4,7},{5,4},{6,5},{7,6},{8,11},{9,8},{10,9... | collective-permute-start | bytes 393224 | tf_op jit(solution)/shard_map/ppermute | solution.py:71
  24.2 1.0 copy-start.8
  24.2 1.0 copy-start.11
  25.9 1.4 copy-start.2
  27.3 8.6 %copy-start.9 = (bf16[1024,256]{1,0:T(8,128)(2,1)S(1)}, bf16[1024,256]{1,0:T(8,128)(2,1)}, u32[]{:S(2)}) copy-start(bf16[1024,256]{1,0:T(8,128)(2,1)} %param.21) | copy-start | bytes 1572868
  28.7 77.4 %collective-permute-start.6 = (bf16[256,1024]{1,0:T(8,128)(2,1)}, bf16[256,1024]{1,0:T(8,128)(2,1)}, u32[]{:S(2)}, u32[]{:S(2)}) collective-permute-start(bf16[256,1024]{1,0:T(8,128)(2,1)} %param.22), channel_id=1, source_target_pairs={{0,1},{1,2},{2,3},{3,0},{4,5},{5,6},{6,7},{7,4},{8,9},{9,10},{10,1... | collective-permute-start | bytes 1572872 | tf_op jit(solution)/shard_map/ppermute | solution.py:71
  32.0 75.6 %collective-permute-start.7 = (bf16[256,1024]{1,0:T(8,128)(2,1)}, bf16[256,1024]{1,0:T(8,128)(2,1)}, u32[]{:S(2)}, u32[]{:S(2)}) collective-permute-start(bf16[256,1024]{1,0:T(8,128)(2,1)} %param.22), channel_id=1, source_target_pairs={{0,2},{1,3},{2,0},{3,1},{4,6},{5,7},{6,4},{7,5},{8,10},{9,11},{10,... | collective-permute-start | bytes 1572872 | tf_op jit(solution)/shard_map/ppermute | solution.py:71
  33.6 74.0 %collective-permute-start.8 = (bf16[256,1024]{1,0:T(8,128)(2,1)}, bf16[256,1024]{1,0:T(8,128)(2,1)S(1)}, u32[]{:S(2)}, u32[]{:S(2)}) collective-permute-start(bf16[256,1024]{1,0:T(8,128)(2,1)} %param.22), channel_id=1, source_target_pairs={{0,3},{1,0},{2,1},{3,2},{4,7},{5,4},{6,5},{7,6},{8,11},{9,8},{10,9... | collective-permute-start | bytes 1572872 | tf_op jit(solution)/shard_map/ppermute | solution.py:71
  67.0 40.6 %copy-start.13 = (s32[1,2]{1,0:T(1,128)S(1)}, s32[1,2]{1,0:T(1,128)}, u32[]{:S(2)}) copy-start(s32[1,2]{1,0:T(1,128)} %param.18) | copy-start | bytes 28
  67.0 40.6 %copy-start.6 = (f32[256,8]{0,1:T(8,128)S(1)}, f32[256,8]{0,1:T(8,128)}, u32[]{:S(2)}) copy-start(f32[256,8]{0,1:T(8,128)} %param.25) | copy-start | bytes 24580
  67.0 40.6 %copy-start.7 = (s32[256,8]{0,1:T(8,128)S(1)}, s32[256,8]{0,1:T(8,128)}, u32[]{:S(2)}) copy-start(s32[256,8]{0,1:T(8,128)} %param.24) | copy-start | bytes 24580
  102.1 8.3 %collective-permute-start.3 = (bf16[256,256]{0,1:T(8,128)(2,1)S(1)}, bf16[256,256]{0,1:T(8,128)(2,1)S(1)}, u32[]{:S(2)}, u32[]{:S(2)}) collective-permute-start(bf16[256,256]{0,1:T(8,128)(2,1)S(1)} %bitcast.91), channel_id=1, source_target_pairs={{0,1},{1,2},{2,3},{3,0},{4,5},{5,6},{6,7},{7,4},{8,9},{9,10},{10,1... | collective-permute-start | bytes 393224 | tf_op jit(solution)/shard_map/ppermute | solution.py:71
  103.7 11.9 %collective-permute-start.4 = (bf16[256,256]{0,1:T(8,128)(2,1)S(1)}, bf16[256,256]{0,1:T(8,128)(2,1)S(1)}, u32[]{:S(2)}, u32[]{:S(2)}) collective-permute-start(bf16[256,256]{0,1:T(8,128)(2,1)S(1)} %bitcast.92), channel_id=1, source_target_pairs={{0,2},{1,3},{2,0},{3,1},{4,6},{5,7},{6,4},{7,5},{8,10},{9,11},{10,... | collective-permute-start | bytes 393224 | tf_op jit(solution)/shard_map/ppermute | solution.py:71
  106.1 9.5 %collective-permute-start.5 = (bf16[256,256]{0,1:T(8,128)(2,1)S(1)}, bf16[256,256]{0,1:T(8,128)(2,1)S(1)}, u32[]{:S(2)}, u32[]{:S(2)}) collective-permute-start(bf16[256,256]{0,1:T(8,128)(2,1)S(1)} %bitcast.93), channel_id=1, source_target_pairs={{0,3},{1,0},{2,1},{3,2},{4,7},{5,4},{6,5},{7,6},{8,11},{9,8},{10,9... | collective-permute-start | bytes 393224 | tf_op jit(solution)/shard_map/ppermute | solution.py:71
  107.6 33.3 %copy-start.12 = (f32[1024]{0:T(1024)S(1)}, f32[1024]{0:T(1024)}, u32[]{:S(2)}) copy-start(f32[1024]{0:T(1024)} %param.23) | copy-start | bytes 12292
  107.6 7.9 %copy-start.10 = (bf16[256,1024]{1,0:T(8,128)(2,1)}, bf16[256,1024]{1,0:T(8,128)(2,1)S(1)}, u32[]{:S(2)}) copy-start(bf16[256,1024]{1,0:T(8,128)(2,1)S(1)} %collective-permute-done.8) | copy-start | bytes 1572868
  117.9 26.5 %copy-start.4 = (bf16[256,1024]{1,0:T(8,128)(2,1)}, bf16[256,1024]{1,0:T(8,128)(2,1)S(1)}, u32[]{:S(2)}) copy-start(bf16[256,1024]{1,0:T(8,128)(2,1)S(1)} %get-tuple-element.36) | copy-start | bytes 1572868
  156.8 6.6 %copy-start.1 = (bf16[256,2,64]{2,0,1:T(8,128)(2,1)S(1)}, bf16[256,2,64]{2,0,1:T(8,128)(2,1)}, u32[]{:S(2)}) copy-start(bf16[256,2,64]{2,0,1:T(8,128)(2,1)} %copy.108) | copy-start | bytes 196612
  158.5 10.6 %collective-permute-start.10 = (bf16[256,256]{1,0:T(8,128)(2,1)S(1)}, bf16[256,256]{1,0:T(8,128)(2,1)S(1)}, u32[]{:S(2)}, u32[]{:S(2)}) collective-permute-start(bf16[256,256]{1,0:T(8,128)(2,1)S(1)} %copy.104), channel_id=1, source_target_pairs={{0,2},{1,3},{2,0},{3,1},{4,6},{5,7},{6,4},{7,5},{8,10},{9,11},{10,... | collective-permute-start | bytes 393224 | tf_op jit(solution)/shard_map/ppermute | solution.py:291
  161.1 8.0 %collective-permute-start.11 = (bf16[256,256]{1,0:T(8,128)(2,1)S(1)}, bf16[256,256]{1,0:T(8,128)(2,1)S(1)}, u32[]{:S(2)}, u32[]{:S(2)}) collective-permute-start(bf16[256,256]{1,0:T(8,128)(2,1)S(1)} %copy.105), channel_id=1, source_target_pairs={{0,3},{1,0},{2,1},{3,2},{4,7},{5,4},{6,5},{7,6},{8,11},{9,8},{10,9... | collective-permute-start | bytes 393224 | tf_op jit(solution)/shard_map/ppermute | solution.py:291
  162.7 9.1 %collective-permute-start.9 = (bf16[256,256]{1,0:T(8,128)(2,1)S(1)}, bf16[256,256]{1,0:T(8,128)(2,1)S(1)}, u32[]{:S(2)}, u32[]{:S(2)}) collective-permute-start(bf16[256,256]{1,0:T(8,128)(2,1)S(1)} %copy.103), channel_id=1, source_target_pairs={{0,1},{1,2},{2,3},{3,0},{4,5},{5,6},{6,7},{7,4},{8,9},{9,10},{10,1... | collective-permute-start | bytes 393224 | tf_op jit(solution)/shard_map/ppermute | solution.py:291
Sparse Core Ops, SparseCore 0:
  9.9 57.0 all-gather.2
  68.9 71.9 all-gather.4

commit v8 on v7

--- a/solution.py
+++ b/solution.py
@@ -1,3 +1,5 @@
+import functools
+
 import jax
 import jax.numpy as jnp
 from jax import lax
@@ -203,6 +205,7 @@
 
 
 def shards(
+    req_axes,
     hidden_in,
     segments,
     prefix_group,
@@ -218,7 +221,7 @@
     w_gate_up,
     w_down,
 ):
-    req_count = lax.axis_size("req")
+    req_count = lax.axis_size(req_axes)
     whole = gather_in_order(hidden_in, "hid", 1)
     tok_count = whole.shape[0]
     model_width = whole.shape[1]
@@ -245,9 +248,16 @@
         -1, PAGE, kv_heads, 2 * head_dim
     )
     kv_pages = jnp.zeros_like(pages).at[page_table[0]].set(pages)
-    gathered = lax.all_gather(prefix_cache, "req", axis=0, tiled=True)
+    gathered, prefix_from = staged_gather(prefix_cache, req_axes, 0)
+    local_groups = prefix_cache.shape[0]
+    group_owner = prefix_group[0] // local_groups
+    group_place = (
+        jnp.sum(jnp.where(group_owner[:, None] == prefix_from[None, :], jnp.arange(prefix_from.shape[0])[None, :], 0), axis=1)
+        * local_groups
+        + prefix_group[0] % local_groups
+    )
     attention = attend(
-        grouped_query, key_rows, value_rows, segment_row, prefix_group[0],
+        grouped_query, key_rows, value_rows, segment_row, group_place,
         gathered.transpose(0, 2, 1, 3),
     )
     share_width = hidden_in.shape[1]
@@ -267,9 +277,10 @@
         .reshape(local_experts, 1, -1, lane_width)
     )
     packed = jnp.concatenate([w_gate_up, down_view], axis=1).transpose(1, 0, 2, 3)
-    packed = lax.all_gather(packed, "req", axis=1, tiled=True)
-    experts = packed.shape[1]
-    expert_ids = jnp.arange(experts, dtype=jnp.int32)
+    packed, weight_from = staged_gather(packed, req_axes, 1)
+    expert_ids = (
+        weight_from[:, None] * local_experts + jnp.arange(local_experts, dtype=jnp.int32)[None, :]
+    ).reshape(-1)
     combine = jnp.sum(
         jnp.where(routes[:, :, None] == expert_ids[None, None, :], gates[:, :, None], 0.0), axis=1
     )
@@ -294,22 +305,50 @@
     return (hidden_out, kv_pages)
 
 
+def staged_gather(block, req_axes, axis):
+    if isinstance(req_axes, str):
+        count = lax.axis_size(req_axes)
+        return lax.all_gather(block, req_axes, axis=axis, tiled=True), jnp.arange(count)
+    chips = lax.axis_size(req_axes[0])
+    cores = lax.axis_size(req_axes[1])
+    near = lax.all_gather(block, req_axes[0], axis=axis, tiled=True)
+    whole = lax.all_gather(near, req_axes[1], axis=axis, tiled=True)
+    order = jnp.arange(chips * cores, dtype=jnp.int32)
+    return whole, (order % chips) * cores + order // chips
+
+
+def req_layout(mesh):
+    devices = mesh.devices
+    rows = devices.shape[0]
+    if rows % 2 or devices.ndim != 2:
+        return mesh, "req"
+    for pair in range(0, rows, 2):
+        for col in range(devices.shape[1]):
+            first, second = devices[pair, col], devices[pair + 1, col]
+            same_chip = getattr(first, "coords", None) == getattr(second, "coords", None)
+            if getattr(first, "coords", None) is None or not same_chip:
+                return mesh, "req"
+    shaped = devices.reshape(rows // 2, 2, devices.shape[1])
+    return jax.sharding.Mesh(shaped, ("chip", "core", "hid")), ("chip", "core")
+
+
 def solution(mesh):
+    mesh, req_axes = req_layout(mesh)
     in_specs = (
-        P("req", "hid"),
-        P("req", None),
-        P("req", None),
-        P("req", None, "hid", None),
-        P("req", None),
+        P(req_axes, "hid"),
+        P(req_axes, None),
+        P(req_axes, None),
+        P(req_axes, None, "hid", None),
+        P(req_axes, None),
         P(),
         P(None, "hid"),
         P(None, "hid"),
         P("hid", None),
         P(),
-        P("req", None),
-        P("req", None),
-        P("req", None, None, "hid"),
-        P("req", "hid", None),
-    )
-    out_specs = (P("req", "hid"), P("req", None, "hid", None))
-    return jax.shard_map(shards, mesh=mesh, in_specs=in_specs, out_specs=out_specs, check_vma=False)
+        P(req_axes, None),
+        P(req_axes, None),
+        P(req_axes, None, None, "hid"),
+        P(req_axes, "hid", None),
+    )
+    out_specs = (P(req_axes, "hid"), P(req_axes, None, "hid", None))
+    return jax.shard_map(functools.partial(shards, req_axes), mesh=mesh, in_specs=in_specs, out_specs=out_specs, check_vma=False)

time: 181 us -> 250 us (1.38)
  waiting for transfers between devices: 72.8 us -> 140 us
    all_gather x2 -> x4, waiting for transfers between devices: 51.6 us -> 119 us  [the longest x2 108 us: staged_gather(): near = lax.all_gather(block, req_axes[0], axis=axis, tiled=True)]
    unnamed x39 -> x43, local copies, waits for them, and re-layouts: 5.19 us -> 6.19 us
  transfers between devices with their start and end apart: 14 -> 16, of which waited for: 8 -> 9; matrix products, arithmetic and copies ran while one was open for 8% -> 6% of each run, Pallas kernels for 19% -> 13%
where the time goes in v8:
time: 250 us; the launch traced here: 248 us
  waiting for transfers between devices  140 us (56%)
  Pallas kernels  39.5 us (16%)
  starting transfers between devices  24 us (10%)
  between operations  14.2 us (6%)
  matrix products  11.4 us (5%)
  local copies, waits for them, and re-layouts  10.3 us (4%)
  other arithmetic  8.82 us (4%)
    all_gather x2, waiting for transfers between devices, staged_gather(): near = lax.all_gather(block, req_axes[0], axis=axis, tiled=True)  108 us
    pallas_call x1, Pallas kernels, attend(): pl.pallas_call(attention_body, grid_spec=grid_spec, out_shape=jax.ShapeDt...  31.7 us
    ppermute x9, starting transfers between devices, shifted_copies(): copies.append(lax.ppermute(block, axis_name, pairs))  18 us
    ppermute x9, waiting for transfers between devices, shifted_copies(): copies.append(lax.ppermute(block, axis_name, pairs))  14 us
    all_gather x2, waiting for transfers between devices, staged_gather(): whole = lax.all_gather(near, req_axes[1], axis=axis, tiled=True)  10.3 us
    pallas_call x1, Pallas kernels, down_project(): pl.pallas_call(down_body, grid=(col_blocks,), in_specs=[pl.BlockSpec((exp...  7.75 us
    ppermute x3, waiting for transfers between devices, shards(): incoming = lax.ppermute(outgoing.astype(jnp.bfloat16), 'hid', pairs)  6.94 us
    unnamed x43, local copies, waits for them, and re-layouts  6.19 us
  transfers between devices with their start and end apart: 16, of which 9 were waited for; matrix products, arithmetic and copies ran while one was open for 6% of the time, Pallas kernels for 13%

profile of v8, /device:TPU:0, one launch (start us, length us, event | category | flops | bytes accessed | tf_op | source)
XLA Modules:
  0.0 247.8 jit_solution(8653166578269046021)
XLA Ops:
  7.2 2.4 copy.80
  9.7 3.1 %collective-permute-start = (bf16[256,256]{1,0:T(8,128)(2,1)S(1)}, bf16[256,256]{1,0:T(8,128)(2,1)S(1)}, u32[]{:S(2)}, u32[]{:S(2)}) collective-permute-start(bf16[256,256]{1,0:T(8,128)(2,1)S(1)} %copy-done.3), channel_id=1, source_target_pairs={{0,1},{1,2},{2,3},{3,0},{4,5},{5,6},{6,7},{7,4},{8,9},{9,10},{10,1... | collective-permute-start | bytes 393224 | tf_op jit(solution)/shard_map/ppermute | solution.py:73
  12.8 2.6 %collective-permute-start.1 = (bf16[256,256]{1,0:T(8,128)(2,1)S(1)}, bf16[256,256]{1,0:T(8,128)(2,1)S(1)}, u32[]{:S(2)}, u32[]{:S(2)}) collective-permute-start(bf16[256,256]{1,0:T(8,128)(2,1)S(1)} %copy-done.3), channel_id=1, source_target_pairs={{0,2},{1,3},{2,0},{3,1},{4,6},{5,7},{6,4},{7,5},{8,10},{9,11},{10,... | collective-permute-start | bytes 393224 | tf_op jit(solution)/shard_map/ppermute | solution.py:73
  15.4 1.3 collective-permute-start.2
  16.8 0.2 convert_reduce_fusion
  17.0 0.5 multiply_cosine_fusion
  17.6 1.7 collective-permute-done
  19.3 4.8 %collective-permute-done.1 = bf16[256,256]{1,0:T(8,128)(2,1)S(1)} collective-permute-done((bf16[256,256]{1,0:T(8,128)(2,1)S(1)}, bf16[256,256]{1,0:T(8,128)(2,1)S(1)}, u32[]{:S(2)}, u32[]{:S(2)}) %collective-permute-start.1) | collective-permute-done | bytes 131104 | tf_op jit(solution)/shard_map/ppermute | solution.py:73
  24.2 0.6 gather_fusion
  24.9 0.2 fusion.23
  25.2 0.5 fusion.38
  25.7 0.2 copy.100
  25.9 0.2 copy.101
  26.3 0.9 pad_maximum_fusion.2
  27.3 1.3 maximum_bitcast_fusion
  28.6 36.5 %all-gather.5.cloned.1.call-done = bf16[8,1024,2,128]{3,1,2,0:T(8,128)(2,1)} async-done(((bf16[2,1024,2,128]{3,1,2,0:T(8,128)(2,1)}), bf16[8,1024,2,128]{3,1,2,0:T(8,128)(2,1)}) %all-gather.5.cloned.1.call-update) | async-done | bytes 4194320 | tf_op jit(solution)/shard_map/all_gather | solution.py:314
  65.3 71.8 %all-gather.9.cloned.1.call-done = bf16[3,8,1024,128]{3,2,1,0:T(8,128)(2,1)} async-done(((bf16[3,2,1024,128]{3,2,1,0:T(8,128)(2,1)}), bf16[3,8,1024,128]{3,2,1,0:T(8,128)(2,1)}) %all-gather.9.cloned.1.call-update) | async-done | bytes 6291472 | tf_op jit(solution)/shard_map/all_gather | solution.py:314
  137.1 1.0 copy-done.10
  138.1 1.5 collective-permute-start.6
  139.6 2.4 collective-permute-start.7
  142.0 1.4 collective-permute-start.8
  143.5 0.8 copy.81.segq_ref
  144.4 0.6 pad_add_fusion.bound_ref
  145.0 0.2 select_reduce_fusion.1
  145.2 0.6 fusion.42.group_ref
  145.8 0.4 fusion.36
  146.6 0.8 copy.108
  147.4 0.8 maximum_bitcast_fusion.1.k_ref
  148.2 10.3 %all-gather.7.cloned.1.call-done = bf16[16,1024,2,128]{3,1,2,0:T(8,128)(2,1)} async-done(((bf16[8,1024,2,128]{3,1,2,0:T(8,128)(2,1)}), bf16[16,1024,2,128]{3,1,2,0:T(8,128)(2,1)}) %all-gather.7.cloned.1.call-update) | async-done | bytes 8388624 | tf_op jit(solution)/shard_map/all_gather | solution.py:315
  158.5 31.7 %shard_map.149 = f32[2,2,256,64]{3,2,1,0:T(8,128)} custom-call(s32[8]{0:T(128)} %fusion.42.group_ref, s32[16]{0:T(128)} %pad_add_fusion.bound_ref, bf16[2,2,256,64]{3,2,1,0:T(8,128)(2,1)} %bitcast.100, bf16[2,256,64]{2,1,0:T(8,128)(2,1)} %maximum_bitcast_fusion.1.k_ref, bf16[2,256,64]{2,1,0:T(8,128)(2,1)} %bitcast.99, s32[256,1]{1,0:T(8,128)} %copy.81.segq_ref, ...), custom_call_target="tpu_custom_call" | custom-call | tf_op jit(solution)/shard_map/pallas_call | solution.py:169
  190.2 1.1 convert_bitcast_fusion
  191.5 1.8 collective-permute-start.3
  193.3 2.4 collective-permute-start.4
  195.7 1.4 collective-permute-start.5
  197.3 2.4 collective-permute-done.3
  199.8 5.0 %collective-permute-done.4 = bf16[256,256]{0,1:T(8,128)(2,1)S(1)} collective-permute-done((bf16[256,256]{0,1:T(8,128)(2,1)S(1)}, bf16[256,256]{0,1:T(8,128)(2,1)S(1)}, u32[]{:S(2)}, u32[]{:S(2)}) %collective-permute-start.4) | collective-permute-done | bytes 131104 | tf_op jit(solution)/shard_map/ppermute | solution.py:73
  204.8 2.2 fusion.20
  207.1 3.6 %fusion.1 = f32[16,128,256]{1,2,0:T(8,128)S(1)} fusion(bf16[3,16,1024,128]{3,2,1,0:T(8,128)(2,1)} %all-gather.11.cloned.1.call-done.weight_ref, bf16[256,1024]{1,0:T(8,128)(2,1)S(1)} %get-tuple-element.36, f32[1024]{0:T(1024)S(1)} %copy-done.13, f32[256]{0:T(256)S(1)} %add_rsqrt_fusion), kind=kOutput, calls=%fused_computation.5 | convolution fusion | flops 1074790400 | bytes 6820864 | tf_op jit(solution)/shard_map/td,edf->etf/dot_general | solution.py:287
  210.8 4.6 %fusion.11.hidden_ref = bf16[16,256,128]{2,1,0:T(8,128)(2,1)} fusion(f32[16,128,256]{1,2,0:T(8,128)S(1)} %fusion.1, bf16[3,16,1024,128]{3,2,1,0:T(8,128)(2,1)} %all-gather.11.cloned.1.call-done.weight_ref, f32[16,256]{1,0:T(8,128)S(1)} %bitcast.116, bf16[256,1024]{1,0:T(8,128)(2,1)S(1)} %get-tuple-element.36, f32[1024]{0:T(1024)S(1)} %copy-done.13, ...), kind=kOutput, calls=%fused_computation.16 | convolution fusion | flops 1078460416 | bytes 7885824 | tf_op jit(solution)/shard_map/td,edf->etf/dot_general | solution.py:290
  215.4 7.7 %shard_map.150 = f32[8,256,128]{2,1,0:T(8,128)} custom-call(bf16[16,256,128]{2,1,0:T(8,128)(2,1)} %fusion.11.hidden_ref, bf16[3,16,1024,128]{3,2,1,0:T(8,128)(2,1)} %all-gather.11.cloned.1.call-done.weight_ref), custom_call_target="tpu_custom_call" | custom-call | tf_op jit(solution)/shard_map/pallas_call | solution.py:194
  223.1 1.6 copy.89
  224.9 2.3 collective-permute-start.10
  227.3 3.4 %collective-permute-start.11 = (bf16[256,256]{1,0:T(8,128)(2,1)S(1)}, bf16[256,256]{1,0:T(8,128)(2,1)S(1)}, u32[]{:S(2)}, u32[]{:S(2)}) collective-permute-start(bf16[256,256]{1,0:T(8,128)(2,1)S(1)} %copy.105), channel_id=1, source_target_pairs={{0,3},{1,0},{2,1},{3,2},{4,7},{5,4},{6,5},{7,6},{8,11},{9,8},{10,9... | collective-permute-start | bytes 393224 | tf_op jit(solution)/shard_map/ppermute | solution.py:302
  231.1 0.6 scatter_fusion
  231.8 0.8 copy.95
  232.7 1.9 collective-permute-done.11
  234.6 5.0 %collective-permute-done.9 = bf16[256,256]{1,0:T(8,128)(2,1)S(1)} collective-permute-done((bf16[256,256]{1,0:T(8,128)(2,1)S(1)}, bf16[256,256]{1,0:T(8,128)(2,1)S(1)}, u32[]{:S(2)}, u32[]{:S(2)}) %collective-permute-start.9) | collective-permute-done | bytes 131104 | tf_op jit(solution)/shard_map/ppermute | solution.py:302
  239.6 1.6 add_convert_fusion.1
  (82 shorter events, 2.6 us)
Async XLA Ops:
  7.2 20.0 %copy-start = (bf16[2,128,1024]{2,1,0:T(8,128)(2,1)S(1)}, bf16[2,128,1024]{2,1,0:T(8,128)(2,1)}, u32[]{:S(2)}) copy-start(bf16[2,128,1024]{2,1,0:T(8,128)(2,1)} %param.27) | copy-start | bytes 1572868
  7.2 2.6 %copy-start.3 = (bf16[256,256]{1,0:T(8,128)(2,1)S(1)}, bf16[256,256]{1,0:T(8,128)(2,1)}, u32[]{:S(2)}) copy-start(bf16[256,256]{1,0:T(8,128)(2,1)} %param.14) | copy-start | bytes 393220
  7.2 9.6 %copy-start.5 = (s32[1,256]{1,0:T(1,128)S(1)}, s32[1,256]{1,0:T(1,128)}, u32[]{:S(2)}) copy-start(s32[1,256]{1,0:T(1,128)} %segk_ref.1) | copy-start | bytes 3076
  7.2 58.0 %all-gather.5.cloned.1.call-start = ((), (), s32[]{:S(2)}) async-start(), calls=%async_computation | async-start | bytes 5242880 | tf_op jit(solution)/shard_map/all_gather | solution.py:314
  9.7 127.4 %all-gather.9.cloned.1.call-start = ((), (), s32[]{:S(2)}) async-start(), calls=%async_computation.2 | async-start | bytes 7864320 | tf_op jit(solution)/shard_map/all_gather | solution.py:314
  9.7 9.6 %collective-permute-start = (bf16[256,256]{1,0:T(8,128)(2,1)S(1)}, bf16[256,256]{1,0:T(8,128)(2,1)S(1)}, u32[]{:S(2)}, u32[]{:S(2)}) collective-permute-start(bf16[256,256]{1,0:T(8,128)(2,1)S(1)} %copy-done.3), channel_id=1, source_target_pairs={{0,1},{1,2},{2,3},{3,0},{4,5},{5,6},{6,7},{7,4},{8,9},{9,10},{10,1... | collective-permute-start | bytes 393224 | tf_op jit(solution)/shard_map/ppermute | solution.py:73
  12.8 11.2 %collective-permute-start.1 = (bf16[256,256]{1,0:T(8,128)(2,1)S(1)}, bf16[256,256]{1,0:T(8,128)(2,1)S(1)}, u32[]{:S(2)}, u32[]{:S(2)}) collective-permute-start(bf16[256,256]{1,0:T(8,128)(2,1)S(1)} %copy-done.3), channel_id=1, source_target_pairs={{0,2},{1,3},{2,0},{3,1},{4,6},{5,7},{6,4},{7,5},{8,10},{9,11},{10,... | collective-permute-start | bytes 393224 | tf_op jit(solution)/shard_map/ppermute | solution.py:73
  15.4 8.6 %collective-permute-start.2 = (bf16[256,256]{1,0:T(8,128)(2,1)S(1)}, bf16[256,256]{1,0:T(8,128)(2,1)S(1)}, u32[]{:S(2)}, u32[]{:S(2)}) collective-permute-start(bf16[256,256]{1,0:T(8,128)(2,1)S(1)} %copy-done.3), channel_id=1, source_target_pairs={{0,3},{1,0},{2,1},{3,2},{4,7},{5,4},{6,5},{7,6},{8,11},{9,8},{10,9... | collective-permute-start | bytes 393224 | tf_op jit(solution)/shard_map/ppermute | solution.py:73
  24.2 1.0 copy-start.8
  24.2 1.0 copy-start.12
  25.9 1.3 copy-start.2
  28.6 129.9 %all-gather.7.cloned.1.call-start = ((), (), s32[]{:S(2)}) async-start(), calls=%async_computation.1 | async-start | bytes 12582912 | tf_op jit(solution)/shard_map/all_gather | solution.py:315
  65.2 141.9 %all-gather.11.cloned.1.call-start = ((), (), s32[]{:S(2)}) async-start(), calls=%async_computation.3 | async-start | bytes 18874368 | tf_op jit(solution)/shard_map/all_gather | solution.py:315
  137.1 1.0 copy-start.10
  137.1 7.9 %copy-start.14 = (s32[1,8]{1,0:T(1,128)S(1)}, s32[1,8]{1,0:T(1,128)}, u32[]{:S(2)}) copy-start(s32[1,8]{1,0:T(1,128)} %param.16) | copy-start | bytes 100
  137.1 8.7 %copy-start.9 = (bf16[1024,256]{1,0:T(8,128)(2,1)S(1)}, bf16[1024,256]{1,0:T(8,128)(2,1)}, u32[]{:S(2)}) copy-start(bf16[1024,256]{1,0:T(8,128)(2,1)} %param.21) | copy-start | bytes 1572868
  138.1 57.6 %collective-permute-start.6 = (bf16[256,1024]{1,0:T(8,128)(2,1)S(1)}, bf16[256,1024]{1,0:T(8,128)(2,1)}, u32[]{:S(2)}, u32[]{:S(2)}) collective-permute-start(bf16[256,1024]{1,0:T(8,128)(2,1)S(1)} %copy-done.10), channel_id=1, source_target_pairs={{0,1},{1,2},{2,3},{3,0},{4,5},{5,6},{6,7},{7,4},{8,9},{9,10},{10,1... | collective-permute-start | bytes 1572872 | tf_op jit(solution)/shard_map/ppermute | solution.py:73
  139.6 57.7 %collective-permute-start.7 = (bf16[256,1024]{1,0:T(8,128)(2,1)S(1)}, bf16[256,1024]{1,0:T(8,128)(2,1)}, u32[]{:S(2)}, u32[]{:S(2)}) collective-permute-start(bf16[256,1024]{1,0:T(8,128)(2,1)S(1)} %copy-done.10), channel_id=1, source_target_pairs={{0,2},{1,3},{2,0},{3,1},{4,6},{5,7},{6,4},{7,5},{8,10},{9,11},{10,... | collective-permute-start | bytes 1572872 | tf_op jit(solution)/shard_map/ppermute | solution.py:73
  142.0 55.3 %collective-permute-start.8 = (bf16[256,1024]{1,0:T(8,128)(2,1)S(1)}, bf16[256,1024]{1,0:T(8,128)(2,1)}, u32[]{:S(2)}, u32[]{:S(2)}) collective-permute-start(bf16[256,1024]{1,0:T(8,128)(2,1)S(1)} %copy-done.10), channel_id=1, source_target_pairs={{0,3},{1,0},{2,1},{3,2},{4,7},{5,4},{6,5},{7,6},{8,11},{9,8},{10,9... | collective-permute-start | bytes 1572872 | tf_op jit(solution)/shard_map/ppermute | solution.py:73
  158.5 38.6 %copy-start.15 = (s32[1,2]{1,0:T(1,128)S(1)}, s32[1,2]{1,0:T(1,128)}, u32[]{:S(2)}) copy-start(s32[1,2]{1,0:T(1,128)} %param.18) | copy-start | bytes 28
  158.5 38.7 %copy-start.6 = (f32[256,8]{0,1:T(8,128)S(1)}, f32[256,8]{0,1:T(8,128)}, u32[]{:S(2)}) copy-start(f32[256,8]{0,1:T(8,128)} %param.25) | copy-start | bytes 24580
  158.5 38.7 %copy-start.7 = (s32[256,8]{0,1:T(8,128)S(1)}, s32[256,8]{0,1:T(8,128)}, u32[]{:S(2)}) copy-start(s32[256,8]{0,1:T(8,128)} %param.24) | copy-start | bytes 24580
  158.5 46.3 %copy-start.11 = (bf16[256,1024]{1,0:T(8,128)(2,1)S(1)}, bf16[256,1024]{1,0:T(8,128)(2,1)}, u32[]{:S(2)}) copy-start(bf16[256,1024]{1,0:T(8,128)(2,1)} %param.22) | copy-start | bytes 1572868
  191.5 8.3 %collective-permute-start.3 = (bf16[256,256]{0,1:T(8,128)(2,1)S(1)}, bf16[256,256]{0,1:T(8,128)(2,1)S(1)}, u32[]{:S(2)}, u32[]{:S(2)}) collective-permute-start(bf16[256,256]{0,1:T(8,128)(2,1)S(1)} %bitcast.105), channel_id=1, source_target_pairs={{0,1},{1,2},{2,3},{3,0},{4,5},{5,6},{6,7},{7,4},{8,9},{9,10},{10,1... | collective-permute-start | bytes 393224 | tf_op jit(solution)/shard_map/ppermute | solution.py:73
  193.3 11.5 %collective-permute-start.4 = (bf16[256,256]{0,1:T(8,128)(2,1)S(1)}, bf16[256,256]{0,1:T(8,128)(2,1)S(1)}, u32[]{:S(2)}, u32[]{:S(2)}) collective-permute-start(bf16[256,256]{0,1:T(8,128)(2,1)S(1)} %bitcast.106), channel_id=1, source_target_pairs={{0,2},{1,3},{2,0},{3,1},{4,6},{5,7},{6,4},{7,5},{8,10},{9,11},{10,... | collective-permute-start | bytes 393224 | tf_op jit(solution)/shard_map/ppermute | solution.py:73
  195.7 9.1 %collective-permute-start.5 = (bf16[256,256]{0,1:T(8,128)(2,1)S(1)}, bf16[256,256]{0,1:T(8,128)(2,1)S(1)}, u32[]{:S(2)}, u32[]{:S(2)}) collective-permute-start(bf16[256,256]{0,1:T(8,128)(2,1)S(1)} %bitcast.107), channel_id=1, source_target_pairs={{0,3},{1,0},{2,1},{3,2},{4,7},{5,4},{6,5},{7,6},{8,11},{9,8},{10,9... | collective-permute-start | bytes 393224 | tf_op jit(solution)/shard_map/ppermute | solution.py:73
  197.3 9.8 %copy-start.13 = (f32[1024]{0:T(1024)S(1)}, f32[1024]{0:T(1024)}, u32[]{:S(2)}) copy-start(f32[1024]{0:T(1024)} %param.23) | copy-start | bytes 12292
  207.0 3.7 %copy-start.4 = (bf16[256,1024]{1,0:T(8,128)(2,1)}, bf16[256,1024]{1,0:T(8,128)(2,1)S(1)}, u32[]{:S(2)}) copy-start(bf16[256,1024]{1,0:T(8,128)(2,1)S(1)} %get-tuple-element.36) | copy-start | bytes 1572868
  223.1 7.8 %copy-start.1 = (bf16[256,2,64]{2,0,1:T(8,128)(2,1)S(1)}, bf16[256,2,64]{2,0,1:T(8,128)(2,1)}, u32[]{:S(2)}) copy-start(bf16[256,2,64]{2,0,1:T(8,128)(2,1)} %copy.108) | copy-start | bytes 196612
  224.9 7.8 %collective-permute-start.10 = (bf16[256,256]{1,0:T(8,128)(2,1)S(1)}, bf16[256,256]{1,0:T(8,128)(2,1)S(1)}, u32[]{:S(2)}, u32[]{:S(2)}) collective-permute-start(bf16[256,256]{1,0:T(8,128)(2,1)S(1)} %copy.104), channel_id=1, source_target_pairs={{0,2},{1,3},{2,0},{3,1},{4,6},{5,7},{6,4},{7,5},{8,10},{9,11},{10,... | collective-permute-start | bytes 393224 | tf_op jit(solution)/shard_map/ppermute | solution.py:302
  227.3 7.3 %collective-permute-start.11 = (bf16[256,256]{1,0:T(8,128)(2,1)S(1)}, bf16[256,256]{1,0:T(8,128)(2,1)S(1)}, u32[]{:S(2)}, u32[]{:S(2)}) collective-permute-start(bf16[256,256]{1,0:T(8,128)(2,1)S(1)} %copy.105), channel_id=1, source_target_pairs={{0,3},{1,0},{2,1},{3,2},{4,7},{5,4},{6,5},{7,6},{8,11},{9,8},{10,9... | collective-permute-start | bytes 393224 | tf_op jit(solution)/shard_map/ppermute | solution.py:302
  230.8 8.8 %collective-permute-start.9 = (bf16[256,256]{1,0:T(8,128)(2,1)S(1)}, bf16[256,256]{1,0:T(8,128)(2,1)S(1)}, u32[]{:S(2)}, u32[]{:S(2)}) collective-permute-start(bf16[256,256]{1,0:T(8,128)(2,1)S(1)} %copy.103), channel_id=1, source_target_pairs={{0,1},{1,2},{2,3},{3,0},{4,5},{5,6},{6,7},{7,4},{8,9},{9,10},{10,1... | collective-permute-start | bytes 393224 | tf_op jit(solution)/shard_map/ppermute | solution.py:302
Sparse Core Ops, SparseCore 0:
  9.9 55.2 all-gather.4
  67.0 70.0 all-gather.8
  138.6 19.8 all-gather.6
  159.9 25.8 all-gather.10

commit v9 on v7

--- a/solution.py
+++ b/solution.py
@@ -1,3 +1,5 @@
+import functools
+
 import jax
 import jax.numpy as jnp
 from jax import lax
@@ -78,6 +80,23 @@
     order = (lax.axis_index(axis_name) - jnp.arange(count, dtype=jnp.int32)) % count
     picked = jnp.take(copies, order, axis=0)
     return jnp.concatenate([picked[index] for index in range(count)], axis=axis)
+
+
+def chip_gather(block, axis_name):
+    count = lax.axis_size(axis_name)
+    me = lax.axis_index(axis_name)
+    if count < 2 or count & (count - 1):
+        copies = shifted_copies(block, axis_name)
+        sources = [(me - shift) % count for shift in range(count)]
+        return jnp.concatenate(copies, axis=0), sources
+    near, near_from = [block], [me]
+    for mask in range(2, count, 2):
+        near.append(lax.ppermute(block, axis_name, [(i, i ^ mask) for i in range(count)]))
+        near_from.append(jnp.bitwise_xor(me, mask))
+    stack = jnp.concatenate(near, axis=0)
+    far = lax.ppermute(stack, axis_name, [(i, i ^ 1) for i in range(count)])
+    sources = near_from + [jnp.bitwise_xor(source, 1) for source in near_from]
+    return jnp.concatenate([stack, far], axis=0), sources
 
 
 def attention_body(group_ref, bound_ref, q_ref, k_ref, v_ref, segq_ref, segk_ref, prefix_ref, out_ref):
@@ -233,7 +252,6 @@
         tok_count, -1, head_dim
     )
     queries = rotate(projected, position).astype(jnp.bfloat16)
-    queries, w_gate_up, w_down = lax.optimization_barrier((queries, w_gate_up, w_down))
     q_groups = queries.shape[1] // kv_heads
     grouped_query = queries.reshape(tok_count, kv_heads, q_groups, head_dim)
     key_value = jnp.dot(normed, w_keyval, preferred_element_type=jnp.float32).reshape(
@@ -245,9 +263,15 @@
         -1, PAGE, kv_heads, 2 * head_dim
     )
     kv_pages = jnp.zeros_like(pages).at[page_table[0]].set(pages)
-    gathered = lax.all_gather(prefix_cache, "req", axis=0, tiled=True)
+    gathered, prefix_from = chip_gather(prefix_cache, "req")
+    local_groups = prefix_cache.shape[0]
+    group_owner = prefix_group[0] // local_groups
+    owner_slot = sum(
+        jnp.where(group_owner == source, position, 0) for position, source in enumerate(prefix_from)
+    )
+    group_place = owner_slot * local_groups + prefix_group[0] % local_groups
     attention = attend(
-        grouped_query, key_rows, value_rows, segment_row, prefix_group[0],
+        grouped_query, key_rows, value_rows, segment_row, group_place,
         gathered.transpose(0, 2, 1, 3),
     )
     share_width = hidden_in.shape[1]

time: 181 us -> 201 us (1.11)
  local copies, waits for them, and re-layouts: 9.18 us -> 21.3 us
  waiting for transfers between devices: 72.8 us -> 66.7 us
  other arithmetic: 7.96 us -> 14 us
  starting transfers between devices: 22.9 us -> 27.7 us
    ppermute x0 -> x4, waiting for transfers between devices: none -> 53.1 us  [the longest x3 53.1 us: chip_gather(): lax.ppermute(block, axis_name, [(i, i ^ mask) for i in range(count)])]
    all_gather x1 -> x0, waiting for transfers between devices: 28.7 us -> none  [shards(): gathered = lax.all_gather(prefix_cache, 'req', axis=0, tiled=True)]
    all_gather x1, waiting for transfers between devices: 22.9 us -> 0.02 us  [shards(): packed = lax.all_gather(packed, 'req', axis=1, tiled=True)]
    unnamed x39 -> x50, local copies, waits for them, and re-layouts: 5.19 us -> 12.2 us
    ppermute x9, waiting for transfers between devices: 14.4 us -> 8.39 us  [shifted_copies(): copies.append(lax.ppermute(block, axis_name, pairs))]
    concatenate x0 -> x1, local copies, waits for them, and re-layouts: none -> 4.54 us  [chip_gather(): return (jnp.concatenate([stack, far], axis=0), sources)]
    ppermute x0 -> x4, starting transfers between devices: none -> 4.49 us  [the longest x3 4.49 us: chip_gather(): lax.ppermute(block, axis_name, [(i, i ^ mask) for i in range(count)])]
    concatenate x1, other arithmetic: 0.9 us -> 4.1 us  [chip_gather(): stack = jnp.concatenate(near, axis=0)]
  transfers between devices with their start and end apart: 14 -> 17, of which waited for: 8 -> 6; matrix products, arithmetic and copies ran while one was open for 8% -> 17% of each run, Pallas kernels for 19% -> 17%
where the time goes in v9:
time: 201 us; the launch traced here: 199 us
  waiting for transfers between devices  66.7 us (33%)
  Pallas kernels  41.6 us (21%)
  starting transfers between devices  27.7 us (14%)
  local copies, waits for them, and re-layouts  21.3 us (11%)
  between operations  14.5 us (7%)
  other arithmetic  14 us (7%)
  matrix products  13.3 us (7%)
    ppermute x3, waiting for transfers between devices, chip_gather(): lax.ppermute(block, axis_name, [(i, i ^ mask) for i in range(count)])  53.1 us
    pallas_call x1, Pallas kernels, attend(): pl.pallas_call(attention_body, grid_spec=grid_spec, out_shape=jax.ShapeDt...  33.9 us
    ppermute x9, starting transfers between devices, shifted_copies(): copies.append(lax.ppermute(block, axis_name, pairs))  17.8 us
    unnamed x50, local copies, waits for them, and re-layouts  12.2 us
    ppermute x9, waiting for transfers between devices, shifted_copies(): copies.append(lax.ppermute(block, axis_name, pairs))  8.39 us
    pallas_call x1, Pallas kernels, down_project(): pl.pallas_call(down_body, grid=(col_blocks,), in_specs=[pl.BlockSpec((exp...  7.78 us
    ppermute x3, starting transfers between devices, shards(): incoming = lax.ppermute(outgoing.astype(jnp.bfloat16), 'hid', pairs)  5.4 us
    ppermute x3, waiting for transfers between devices, shards(): incoming = lax.ppermute(outgoing.astype(jnp.bfloat16), 'hid', pairs)  5.14 us
  transfers between devices with their start and end apart: 17, of which 6 were waited for; matrix products, arithmetic and copies ran while one was open for 17% of the time, Pallas kernels for 17%

profile of v9, /device:TPU:0, one launch (start us, length us, event | category | flops | bytes accessed | tf_op | source)
XLA Modules:
  0.0 199.1 jit_solution(15648112949826763161)
XLA Ops:
  7.2 1.0 copy-done
  8.3 2.5 %maximum_bitcast_fusion = bf16[3,2,1024,128]{3,2,1,0:T(8,128)(2,1)} fusion(bf16[2,1,1024,128]{3,2,0,1:T(8,128)(2,1)S(1)} %bitcast.97, bf16[2,2,1024,128]{3,2,1,0:T(8,128)(2,1)} %param.26), kind=kLoop, calls=%fused_computation.23 | loop fusion | flops 3145728 | bytes 3145728 | tf_op jit(solution)/shard_map/transpose | solution.py:293
  10.9 1.3 fusion.53
  12.2 3.0 %collective-permute-start.3 = (bf16[2,1024,2,128]{3,1,2,0:T(8,128)(2,1)S(1)}, bf16[2,1024,2,128]{3,1,2,0:T(8,128)(2,1)S(1)}, u32[]{:S(2)}, u32[]{:S(2)}) collective-permute-start(bf16[2,1024,2,128]{3,1,2,0:T(8,128)(2,1)S(1)} %get-tuple-element.15), channel_id=1, source_target_pairs={{0,8},{4,12},{8,0},{12,4},{16,24},{20,28},{24,16},{28,20},{1,9},{5... | collective-permute-start | bytes 3145736 | tf_op jit(solution)/shard_map/ppermute | solution.py:94
  15.2 1.5 collective-permute-start.4
  16.7 2.1 %collective-permute-start = (bf16[256,256]{1,0:T(8,128)(2,1)S(1)}, bf16[256,256]{1,0:T(8,128)(2,1)S(1)}, u32[]{:S(2)}, u32[]{:S(2)}) collective-permute-start(bf16[256,256]{1,0:T(8,128)(2,1)S(1)} %copy-done.9), channel_id=1, source_target_pairs={{0,1},{1,2},{2,3},{3,0},{4,5},{5,6},{6,7},{7,4},{8,9},{9,10},{10,1... | collective-permute-start | bytes 393224 | tf_op jit(solution)/shard_map/ppermute | solution.py:73
  18.8 2.6 %collective-permute-start.1 = (bf16[256,256]{1,0:T(8,128)(2,1)S(1)}, bf16[256,256]{1,0:T(8,128)(2,1)S(1)}, u32[]{:S(2)}, u32[]{:S(2)}) collective-permute-start(bf16[256,256]{1,0:T(8,128)(2,1)S(1)} %copy-done.9), channel_id=1, source_target_pairs={{0,2},{1,3},{2,0},{3,1},{4,6},{5,7},{6,4},{7,5},{8,10},{9,11},{10,... | collective-permute-start | bytes 393224 | tf_op jit(solution)/shard_map/ppermute | solution.py:73
  21.4 33.3 %collective-permute-done.3 = bf16[2,1024,2,128]{3,1,2,0:T(8,128)(2,1)S(1)} collective-permute-done((bf16[2,1024,2,128]{3,1,2,0:T(8,128)(2,1)S(1)}, bf16[2,1024,2,128]{3,1,2,0:T(8,128)(2,1)S(1)}, u32[]{:S(2)}, u32[]{:S(2)}) %collective-permute-start.3) | collective-permute-done | bytes 1048608 | tf_op jit(solution)/shard_map/ppermute | solution.py:94
  54.7 3.7 %collective-permute-start.2 = (bf16[256,256]{1,0:T(8,128)(2,1)S(1)}, bf16[256,256]{1,0:T(8,128)(2,1)S(1)}, u32[]{:S(2)}, u32[]{:S(2)}) collective-permute-start(bf16[256,256]{1,0:T(8,128)(2,1)S(1)} %copy-done.9), channel_id=1, source_target_pairs={{0,3},{1,0},{2,1},{3,2},{4,7},{5,4},{6,5},{7,6},{8,11},{9,8},{10,9... | collective-permute-start | bytes 393224 | tf_op jit(solution)/shard_map/ppermute | solution.py:73
  58.4 19.8 %collective-permute-done.4 = bf16[2,1024,2,128]{3,1,2,0:T(8,128)(2,1)} collective-permute-done((bf16[2,1024,2,128]{3,1,2,0:T(8,128)(2,1)S(1)}, bf16[2,1024,2,128]{3,1,2,0:T(8,128)(2,1)}, u32[]{:S(2)}, u32[]{:S(2)}) %collective-permute-start.4) | collective-permute-done | bytes 1048608 | tf_op jit(solution)/shard_map/ppermute | solution.py:94
  78.2 1.5 collective-permute-start.10
  79.7 4.1 %pad_maximum_fusion = bf16[8,1024,2,128]{3,1,2,0:T(8,128)(2,1)} fusion(bf16[2,1024,2,128]{3,1,2,0:T(8,128)(2,1)} %collective-permute-done.5, bf16[2,1024,2,128]{3,1,2,0:T(8,128)(2,1)} %collective-permute-done.4, bf16[2,1024,2,128]{3,1,2,0:T(8,128)(2,1)S(1)} %collective-permute-done.3, bf16[2,1024,2,128]{3,1,2,0:T(8,128)(2,1)S(1)} %get-tuple-element.15), kind=kLoop, calls=%fused_computation.6 | loop fusion | flops 6291456 | bytes 8388608 | tf_op jit(solution)/shard_map/concatenate | solution.py:96
  84.2 0.6 fusion.40.group_ref
  85.4 0.7 pad_add_fusion.bound_ref
  86.0 0.8 copy.70.segq_ref
  86.8 2.7 %collective-permute-start.11 = (bf16[256,1024]{1,0:T(8,128)(2,1)}, bf16[256,1024]{1,0:T(8,128)(2,1)}, u32[]{:S(2)}, u32[]{:S(2)}) collective-permute-start(bf16[256,1024]{1,0:T(8,128)(2,1)} %param.22), channel_id=1, source_target_pairs={{0,2},{1,3},{2,0},{3,1},{4,6},{5,7},{6,4},{7,5},{8,10},{9,11},{10,... | collective-permute-start | bytes 1572872 | tf_op jit(solution)/shard_map/ppermute | solution.py:73
  89.5 1.3 collective-permute-start.12
  91.9 1.5 fusion.36
  93.5 0.6 slice.58
  94.3 0.8 copy.96
  95.1 1.5 fusion.38
  97.1 1.6 copy.97
  98.7 1.0 subtract_convert_fusion.1
  99.7 0.8 maximum_bitcast_fusion.2.k_ref
  100.6 0.9 maximum_bitcast_fusion.1.q_ref
  101.5 1.0 constant_dynamic-update-slice_fusion.3
  102.5 2.3 %constant_dynamic-update-slice_fusion.2 = bf16[16,1024,2,128]{3,1,2,0:T(8,128)(2,1)} fusion(bf16[16,1024,2,128]{3,1,2,0:T(8,128)(2,1)} %constant_dynamic-update-slice_fusion.3, bf16[2,1024,2,128]{3,1,2,0:T(8,128)(2,1)} %collective-permute-done.4), kind=kLoop, calls=%fused_computation.70 | loop fusion | bytes 2097152
  104.8 2.3 %constant_dynamic-update-slice_fusion.1 = bf16[16,1024,2,128]{3,1,2,0:T(8,128)(2,1)} fusion(bf16[16,1024,2,128]{3,1,2,0:T(8,128)(2,1)} %constant_dynamic-update-slice_fusion.2, bf16[2,1024,2,128]{3,1,2,0:T(8,128)(2,1)} %collective-permute-done.5), kind=kLoop, calls=%fused_computation.69 | loop fusion | bytes 2097152
  107.1 4.5 %constant_dynamic-update-slice_fusion = bf16[16,1024,2,128]{3,1,2,0:T(8,128)(2,1)} fusion(bf16[16,1024,2,128]{3,1,2,0:T(8,128)(2,1)} %constant_dynamic-update-slice_fusion.1, bf16[8,1024,2,128]{3,1,2,0:T(8,128)(2,1)} %collective-permute-done.6), kind=kLoop, calls=%fused_computation.68 | loop fusion | bytes 8388608 | tf_op jit(solution)/shard_map/concatenate | solution.py:99
  111.7 33.9 %shard_map.149 = f32[2,2,256,64]{3,2,1,0:T(8,128)} custom-call(s32[8]{0:T(128)} %fusion.40.group_ref, s32[16]{0:T(128)} %pad_add_fusion.bound_ref, bf16[2,2,256,64]{3,2,1,0:T(8,128)(2,1)} %maximum_bitcast_fusion.1.q_ref, bf16[2,256,64]{2,1,0:T(8,128)(2,1)} %maximum_bitcast_fusion.2.k_ref, bf16[2,256,64]{2,1,0:T(8,128)(2,1)} %bitcast.98, ...), custom_call_target="tpu_custom_call" | custom-call | tf_op jit(solution)/shard_map/pallas_call | solution.py:186
  145.6 1.1 convert_bitcast_fusion
  146.8 0.7 collective-permute-start.7
  147.9 2.7 %collective-permute-start.9 = (bf16[256,256]{0,1:T(8,128)(2,1)S(1)}, bf16[256,256]{0,1:T(8,128)(2,1)S(1)}, u32[]{:S(2)}, u32[]{:S(2)}) collective-permute-start(bf16[256,256]{0,1:T(8,128)(2,1)S(1)} %bitcast.107), channel_id=1, source_target_pairs={{0,3},{1,0},{2,1},{3,2},{4,7},{5,4},{6,5},{7,6},{8,11},{9,8},{10,9... | collective-permute-start | bytes 393224 | tf_op jit(solution)/shard_map/ppermute | solution.py:73
  150.8 4.3 %collective-permute-done.7 = bf16[256,256]{0,1:T(8,128)(2,1)S(1)} collective-permute-done((bf16[256,256]{0,1:T(8,128)(2,1)S(1)}, bf16[256,256]{0,1:T(8,128)(2,1)S(1)}, u32[]{:S(2)}, u32[]{:S(2)}) %collective-permute-start.7) | collective-permute-done | bytes 131104 | tf_op jit(solution)/shard_map/ppermute | solution.py:73
  155.0 4.1 %collective-permute-done.8 = bf16[256,256]{0,1:T(8,128)(2,1)S(1)} collective-permute-done((bf16[256,256]{0,1:T(8,128)(2,1)S(1)}, bf16[256,256]{0,1:T(8,128)(2,1)S(1)}, u32[]{:S(2)}, u32[]{:S(2)}) %collective-permute-start.8) | collective-permute-done | bytes 131104 | tf_op jit(solution)/shard_map/ppermute | solution.py:73
  159.2 2.2 %fusion.20 = (f32[256]{0:T(256)S(1)}, bf16[256,1024]{1,0:T(8,128)(2,1)S(1)}) fusion(bf16[256,1024]{1,0:T(8,128)(2,1)} %collective-permute-done.12, bf16[256,1024]{1,0:T(8,128)(2,1)} %collective-permute-done.11, bf16[256,1024]{1,0:T(8,128)(2,1)} %collective-permute-done.10, bf16[256,1024]{1,0:T(8,128)(2,1)S(1)} %copy-done.14, ...), kind=kOutput, calls=%fused_computation.30 | convolution fusion | flops 550764288 | bytes 3671040 | tf_op jit(solution)/shard_map/dot_general | solution.py:280
  161.4 3.5 %fusion.1 = f32[16,128,256]{1,2,0:T(8,128)S(1)} fusion(bf16[3,16,1024,128]{3,2,1,0:T(8,128)(2,1)} %all-gather.2.cloned.1.call-done.weight_ref, bf16[256,1024]{1,0:T(8,128)(2,1)S(1)} %get-tuple-element.30, f32[1024]{0:T(1024)S(1)} %copy-done.16, f32[256]{0:T(256)S(1)} %add_rsqrt_fusion), kind=kOutput, calls=%fused_computation.5 | convolution fusion | flops 1074790400 | bytes 6820864 | tf_op jit(solution)/shard_map/td,edf->etf/dot_general | solution.py:300
  164.9 4.6 %fusion.11.hidden_ref = bf16[16,256,128]{2,1,0:T(8,128)(2,1)} fusion(f32[16,128,256]{1,2,0:T(8,128)S(1)} %fusion.1, bf16[3,16,1024,128]{3,2,1,0:T(8,128)(2,1)} %all-gather.2.cloned.1.call-done.weight_ref, f32[16,256]{1,0:T(8,128)S(1)} %bitcast.116, bf16[256,1024]{1,0:T(8,128)(2,1)S(1)} %get-tuple-element.30, f32[1024]{0:T(1024)S(1)} %copy-done.16, ...), kind=kOutput, calls=%fused_computation.17 | convolution fusion | flops 1078460416 | bytes 7885824 | tf_op jit(solution)/shard_map/td,edf->etf/dot_general | solution.py:303
  169.5 7.8 %shard_map.150 = f32[8,256,128]{2,1,0:T(8,128)} custom-call(bf16[16,256,128]{2,1,0:T(8,128)(2,1)} %fusion.11.hidden_ref, bf16[3,16,1024,128]{3,2,1,0:T(8,128)(2,1)} %all-gather.2.cloned.1.call-done.weight_ref), custom_call_target="tpu_custom_call" | custom-call | tf_op jit(solution)/shard_map/pallas_call | solution.py:211
  177.3 1.6 copy.78
  179.0 2.9 %collective-permute-start.13 = (bf16[256,256]{1,0:T(8,128)(2,1)S(1)}, bf16[256,256]{1,0:T(8,128)(2,1)S(1)}, u32[]{:S(2)}, u32[]{:S(2)}) collective-permute-start(bf16[256,256]{1,0:T(8,128)(2,1)S(1)} %copy.92), channel_id=1, source_target_pairs={{0,1},{1,2},{2,3},{3,0},{4,5},{5,6},{6,7},{7,4},{8,9},{9,10},{10,1... | collective-permute-start | bytes 393224 | tf_op jit(solution)/shard_map/ppermute | solution.py:315
  182.0 0.6 collective-permute-start.14
  182.7 1.9 collective-permute-start.15
  184.8 0.6 scatter_fusion
  185.5 0.8 copy.84
  186.4 0.7 collective-permute-done.13
  187.1 4.4 %collective-permute-done.14 = bf16[256,256]{1,0:T(8,128)(2,1)S(1)} collective-permute-done((bf16[256,256]{1,0:T(8,128)(2,1)S(1)}, bf16[256,256]{1,0:T(8,128)(2,1)S(1)}, u32[]{:S(2)}, u32[]{:S(2)}) %collective-permute-start.14) | collective-permute-done | bytes 131104 | tf_op jit(solution)/shard_map/ppermute | solution.py:315
  191.6 0.7 add_convert_fusion.1
  (85 shorter events, 4.2 us)
Async XLA Ops:
  7.2 1.0 copy-start
  7.2 3.7 %copy-start.2 = (bf16[2,1024,2,128]{3,2,1,0:T(2,128)(2,1)S(1)}, bf16[2,1024,2,128]{3,2,1,0:T(2,128)(2,1)}, u32[]{:S(2)}) copy-start(bf16[2,1024,2,128]{3,2,1,0:T(2,128)(2,1)} %param.17) | copy-start | bytes 3145732
  7.2 154.2 %all-gather.2.cloned.1.call-start = ((), (), s32[]{:S(2)}) async-start(), calls=%async_computation | async-start | bytes 14155776 | tf_op jit(solution)/shard_map/all_gather | solution.py:294
  8.3 8.4 %copy-start.9 = (bf16[256,256]{1,0:T(8,128)(2,1)S(1)}, bf16[256,256]{1,0:T(8,128)(2,1)}, u32[]{:S(2)}) copy-start(bf16[256,256]{1,0:T(8,128)(2,1)} %param.14) | copy-start | bytes 393220
  12.2 42.5 %collective-permute-start.3 = (bf16[2,1024,2,128]{3,1,2,0:T(8,128)(2,1)S(1)}, bf16[2,1024,2,128]{3,1,2,0:T(8,128)(2,1)S(1)}, u32[]{:S(2)}, u32[]{:S(2)}) collective-permute-start(bf16[2,1024,2,128]{3,1,2,0:T(8,128)(2,1)S(1)} %get-tuple-element.15), channel_id=1, source_target_pairs={{0,8},{4,12},{8,0},{12,4},{16,24},{20,28},{24,16},{28,20},{1,9},{5... | collective-permute-start | bytes 3145736 | tf_op jit(solution)/shard_map/ppermute | solution.py:94
  15.2 63.0 %collective-permute-start.4 = (bf16[2,1024,2,128]{3,1,2,0:T(8,128)(2,1)S(1)}, bf16[2,1024,2,128]{3,1,2,0:T(8,128)(2,1)}, u32[]{:S(2)}, u32[]{:S(2)}) collective-permute-start(bf16[2,1024,2,128]{3,1,2,0:T(8,128)(2,1)S(1)} %get-tuple-element.15), channel_id=1, source_target_pairs={{0,16},{4,20},{8,24},{12,28},{16,0},{20,4},{24,8},{28,12},{1,17},{... | collective-permute-start | bytes 3145736 | tf_op jit(solution)/shard_map/ppermute | solution.py:94
  16.7 63.0 %collective-permute-start.5 = (bf16[2,1024,2,128]{3,1,2,0:T(8,128)(2,1)S(1)}, bf16[2,1024,2,128]{3,1,2,0:T(8,128)(2,1)}, u32[]{:S(2)}, u32[]{:S(2)}) collective-permute-start(bf16[2,1024,2,128]{3,1,2,0:T(8,128)(2,1)S(1)} %get-tuple-element.15), channel_id=1, source_target_pairs={{0,24},{4,28},{8,16},{12,20},{16,8},{20,12},{24,0},{28,4},{1,25},{... | collective-permute-start | bytes 3145736 | tf_op jit(solution)/shard_map/ppermute | solution.py:94
  16.7 70.1 %collective-permute-start = (bf16[256,256]{1,0:T(8,128)(2,1)S(1)}, bf16[256,256]{1,0:T(8,128)(2,1)S(1)}, u32[]{:S(2)}, u32[]{:S(2)}) collective-permute-start(bf16[256,256]{1,0:T(8,128)(2,1)S(1)} %copy-done.9), channel_id=1, source_target_pairs={{0,1},{1,2},{2,3},{3,0},{4,5},{5,6},{6,7},{7,4},{8,9},{9,10},{10,1... | collective-permute-start | bytes 393224 | tf_op jit(solution)/shard_map/ppermute | solution.py:73
  18.8 70.8 %collective-permute-start.1 = (bf16[256,256]{1,0:T(8,128)(2,1)S(1)}, bf16[256,256]{1,0:T(8,128)(2,1)S(1)}, u32[]{:S(2)}, u32[]{:S(2)}) collective-permute-start(bf16[256,256]{1,0:T(8,128)(2,1)S(1)} %copy-done.9), channel_id=1, source_target_pairs={{0,2},{1,3},{2,0},{3,1},{4,6},{5,7},{6,4},{7,5},{8,10},{9,11},{10,... | collective-permute-start | bytes 393224 | tf_op jit(solution)/shard_map/ppermute | solution.py:73
  21.4 62.5 %copy-start.10 = (s32[1,256]{1,0:T(1,128)S(1)}, s32[1,256]{1,0:T(1,128)}, u32[]{:S(2)}) copy-start(s32[1,256]{1,0:T(1,128)} %segk_ref.1) | copy-start | bytes 3076
  21.4 62.8 %copy-start.13 = (s32[1,8]{1,0:T(1,128)S(1)}, s32[1,8]{1,0:T(1,128)}, u32[]{:S(2)}) copy-start(s32[1,8]{1,0:T(1,128)} %param.16) | copy-start | bytes 100
  54.7 36.1 %collective-permute-start.2 = (bf16[256,256]{1,0:T(8,128)(2,1)S(1)}, bf16[256,256]{1,0:T(8,128)(2,1)S(1)}, u32[]{:S(2)}, u32[]{:S(2)}) collective-permute-start(bf16[256,256]{1,0:T(8,128)(2,1)S(1)} %copy-done.9), channel_id=1, source_target_pairs={{0,3},{1,0},{2,1},{3,2},{4,7},{5,4},{6,5},{7,6},{8,11},{9,8},{10,9... | collective-permute-start | bytes 393224 | tf_op jit(solution)/shard_map/ppermute | solution.py:73
  78.2 69.8 %collective-permute-start.10 = (bf16[256,1024]{1,0:T(8,128)(2,1)}, bf16[256,1024]{1,0:T(8,128)(2,1)}, u32[]{:S(2)}, u32[]{:S(2)}) collective-permute-start(bf16[256,1024]{1,0:T(8,128)(2,1)} %param.22), channel_id=1, source_target_pairs={{0,1},{1,2},{2,3},{3,0},{4,5},{5,6},{6,7},{7,4},{8,9},{9,10},{10,1... | collective-permute-start | bytes 1572872 | tf_op jit(solution)/shard_map/ppermute | solution.py:73
  83.8 8.1 %copy-start.15 = (f32[1024]{0:T(1024)S(1)}, f32[1024]{0:T(1024)}, u32[]{:S(2)}) copy-start(f32[1024]{0:T(1024)} %param.19) | copy-start | bytes 12292
  83.8 23.3 %collective-permute-start.6 = (bf16[8,1024,2,128]{3,1,2,0:T(8,128)(2,1)}, bf16[8,1024,2,128]{3,1,2,0:T(8,128)(2,1)}, u32[]{:S(2)}, u32[]{:S(2)}) collective-permute-start(bf16[8,1024,2,128]{3,1,2,0:T(8,128)(2,1)} %pad_maximum_fusion), channel_id=1, source_target_pairs={{0,4},{4,0},{8,12},{12,8},{16,20},{20,16},{24,28},{28,24},{1,5},{5... | collective-permute-start | bytes 12582920 | tf_op jit(solution)/shard_map/ppermute | solution.py:97
  86.8 63.9 %collective-permute-start.11 = (bf16[256,1024]{1,0:T(8,128)(2,1)}, bf16[256,1024]{1,0:T(8,128)(2,1)}, u32[]{:S(2)}, u32[]{:S(2)}) collective-permute-start(bf16[256,1024]{1,0:T(8,128)(2,1)} %param.22), channel_id=1, source_target_pairs={{0,2},{1,3},{2,0},{3,1},{4,6},{5,7},{6,4},{7,5},{8,10},{9,11},{10,... | collective-permute-start | bytes 1572872 | tf_op jit(solution)/shard_map/ppermute | solution.py:73
  89.5 61.2 %collective-permute-start.12 = (bf16[256,1024]{1,0:T(8,128)(2,1)}, bf16[256,1024]{1,0:T(8,128)(2,1)}, u32[]{:S(2)}, u32[]{:S(2)}) collective-permute-start(bf16[256,1024]{1,0:T(8,128)(2,1)} %param.22), channel_id=1, source_target_pairs={{0,3},{1,0},{2,1},{3,2},{4,7},{5,4},{6,5},{7,6},{8,11},{9,8},{10,9... | collective-permute-start | bytes 1572872 | tf_op jit(solution)/shard_map/ppermute | solution.py:73
  91.7 4.9 %copy-start.3 = (bf16[256,256]{1,0:T(8,128)(2,1)}, bf16[256,256]{1,0:T(8,128)(2,1)S(1)}, u32[]{:S(2)}) copy-start(bf16[256,256]{1,0:T(8,128)(2,1)S(1)} %get-tuple-element.20) | copy-start | bytes 393220
  91.7 4.9 %copy-start.5 = (bf16[256,256]{1,0:T(8,128)(2,1)}, bf16[256,256]{1,0:T(8,128)(2,1)S(1)}, u32[]{:S(2)}) copy-start(bf16[256,256]{1,0:T(8,128)(2,1)S(1)} %get-tuple-element.21) | copy-start | bytes 393220
  91.7 4.9 %copy-start.7 = (bf16[256,256]{1,0:T(8,128)(2,1)}, bf16[256,256]{1,0:T(8,128)(2,1)S(1)}, u32[]{:S(2)}) copy-start(bf16[256,256]{1,0:T(8,128)(2,1)S(1)} %get-tuple-element.22) | copy-start | bytes 393220
  111.7 39.0 %copy-start.17 = (s32[1,2]{1,0:T(1,128)S(1)}, s32[1,2]{1,0:T(1,128)}, u32[]{:S(2)}) copy-start(s32[1,2]{1,0:T(1,128)} %param.18) | copy-start | bytes 28
  111.7 39.0 %copy-start.11 = (f32[256,8]{0,1:T(8,128)S(1)}, f32[256,8]{0,1:T(8,128)}, u32[]{:S(2)}) copy-start(f32[256,8]{0,1:T(8,128)} %param.25) | copy-start | bytes 24580
  111.7 39.0 %copy-start.12 = (s32[256,8]{0,1:T(8,128)S(1)}, s32[256,8]{0,1:T(8,128)}, u32[]{:S(2)}) copy-start(s32[256,8]{0,1:T(8,128)} %param.24) | copy-start | bytes 24580
  111.7 47.4 %copy-start.4 = (bf16[256,256]{1,0:T(8,128)(2,1)S(1)}, bf16[256,256]{1,0:T(8,128)(2,1)}, u32[]{:S(2)}) copy-start(bf16[256,256]{1,0:T(8,128)(2,1)} %copy-done.3) | copy-start | bytes 393220
  111.7 47.4 %copy-start.6 = (bf16[256,256]{1,0:T(8,128)(2,1)S(1)}, bf16[256,256]{1,0:T(8,128)(2,1)}, u32[]{:S(2)}) copy-start(bf16[256,256]{1,0:T(8,128)(2,1)} %copy-done.5) | copy-start | bytes 393220
  111.7 47.4 %copy-start.8 = (bf16[256,256]{1,0:T(8,128)(2,1)S(1)}, bf16[256,256]{1,0:T(8,128)(2,1)}, u32[]{:S(2)}) copy-start(bf16[256,256]{1,0:T(8,128)(2,1)} %copy-done.7) | copy-start | bytes 393220
  111.7 47.4 %copy-start.14 = (bf16[256,1024]{1,0:T(8,128)(2,1)S(1)}, bf16[256,1024]{1,0:T(8,128)(2,1)}, u32[]{:S(2)}) copy-start(bf16[256,1024]{1,0:T(8,128)(2,1)} %param.22) | copy-start | bytes 1572868
  146.8 8.2 %collective-permute-start.7 = (bf16[256,256]{0,1:T(8,128)(2,1)S(1)}, bf16[256,256]{0,1:T(8,128)(2,1)S(1)}, u32[]{:S(2)}, u32[]{:S(2)}) collective-permute-start(bf16[256,256]{0,1:T(8,128)(2,1)S(1)} %bitcast.105), channel_id=1, source_target_pairs={{0,1},{1,2},{2,3},{3,0},{4,5},{5,6},{6,7},{7,4},{8,9},{9,10},{10,1... | collective-permute-start | bytes 393224 | tf_op jit(solution)/shard_map/ppermute | solution.py:73
  147.4 11.7 %collective-permute-start.8 = (bf16[256,256]{0,1:T(8,128)(2,1)S(1)}, bf16[256,256]{0,1:T(8,128)(2,1)S(1)}, u32[]{:S(2)}, u32[]{:S(2)}) collective-permute-start(bf16[256,256]{0,1:T(8,128)(2,1)S(1)} %bitcast.106), channel_id=1, source_target_pairs={{0,2},{1,3},{2,0},{3,1},{4,6},{5,7},{6,4},{7,5},{8,10},{9,11},{10,... | collective-permute-start | bytes 393224 | tf_op jit(solution)/shard_map/ppermute | solution.py:73
  147.9 11.2 %collective-permute-start.9 = (bf16[256,256]{0,1:T(8,128)(2,1)S(1)}, bf16[256,256]{0,1:T(8,128)(2,1)S(1)}, u32[]{:S(2)}, u32[]{:S(2)}) collective-permute-start(bf16[256,256]{0,1:T(8,128)(2,1)S(1)} %bitcast.107), channel_id=1, source_target_pairs={{0,3},{1,0},{2,1},{3,2},{4,7},{5,4},{6,5},{7,6},{8,11},{9,8},{10,9... | collective-permute-start | bytes 393224 | tf_op jit(solution)/shard_map/ppermute | solution.py:73
  150.7 10.7 %copy-start.16 = (f32[1024]{0:T(1024)S(1)}, f32[1024]{0:T(1024)}, u32[]{:S(2)}) copy-start(f32[1024]{0:T(1024)} %param.23) | copy-start | bytes 12292
  169.5 15.1 %copy-start.1 = (bf16[256,2,64]{2,0,1:T(8,128)(2,1)S(1)}, bf16[256,2,64]{2,0,1:T(8,128)(2,1)}, u32[]{:S(2)}) copy-start(bf16[256,2,64]{2,0,1:T(8,128)(2,1)} %copy.97) | copy-start | bytes 196612
  179.0 8.1 %collective-permute-start.13 = (bf16[256,256]{1,0:T(8,128)(2,1)S(1)}, bf16[256,256]{1,0:T(8,128)(2,1)S(1)}, u32[]{:S(2)}, u32[]{:S(2)}) collective-permute-start(bf16[256,256]{1,0:T(8,128)(2,1)S(1)} %copy.92), channel_id=1, source_target_pairs={{0,1},{1,2},{2,3},{3,0},{4,5},{5,6},{6,7},{7,4},{8,9},{9,10},{10,1... | collective-permute-start | bytes 393224 | tf_op jit(solution)/shard_map/ppermute | solution.py:315
  182.0 9.5 %collective-permute-start.14 = (bf16[256,256]{1,0:T(8,128)(2,1)S(1)}, bf16[256,256]{1,0:T(8,128)(2,1)S(1)}, u32[]{:S(2)}, u32[]{:S(2)}) collective-permute-start(bf16[256,256]{1,0:T(8,128)(2,1)S(1)} %copy.93), channel_id=1, source_target_pairs={{0,2},{1,3},{2,0},{3,1},{4,6},{5,7},{6,4},{7,5},{8,10},{9,11},{10,... | collective-permute-start | bytes 393224 | tf_op jit(solution)/shard_map/ppermute | solution.py:315
  182.7 8.8 %collective-permute-start.15 = (bf16[256,256]{1,0:T(8,128)(2,1)S(1)}, bf16[256,256]{1,0:T(8,128)(2,1)S(1)}, u32[]{:S(2)}, u32[]{:S(2)}) collective-permute-start(bf16[256,256]{1,0:T(8,128)(2,1)S(1)} %copy.94), channel_id=1, source_target_pairs={{0,3},{1,0},{2,1},{3,2},{4,7},{5,4},{6,5},{7,6},{8,11},{9,8},{10,9... | collective-permute-start | bytes 393224 | tf_op jit(solution)/shard_map/ppermute | solution.py:315
Sparse Core Ops, SparseCore 0:
  11.0 111.8 all-gather.1

commit v10 on v7

--- a/solution.py
+++ b/solution.py
@@ -1,3 +1,5 @@
+import functools
+
 import jax
 import jax.numpy as jnp
 from jax import lax
@@ -176,30 +178,45 @@
     return out.transpose(2, 0, 1, 3).reshape(tok_count, -1).astype(jnp.bfloat16)
 
 
-def down_body(hidden_ref, weight_ref, out_ref):
+def expert_body(normed_ref, combine_ref, weight_ref, down_ref, out_ref, hidden_ref):
+    experts = hidden_ref.shape[0]
+
+    @pl.when(pl.program_id(0) == 0)
+    def _():
+        rows = normed_ref[...]
+        for expert in range(experts):
+            gate_proj = jnp.dot(rows, weight_ref[0, expert], preferred_element_type=jnp.float32)
+            up_proj = jnp.dot(rows, weight_ref[1, expert], preferred_element_type=jnp.float32)
+            activated = gate_proj / (1.0 + jnp.exp(-gate_proj))
+            hidden_ref[expert] = (activated * up_proj * combine_ref[expert]).astype(jnp.bfloat16)
+
     total = jnp.zeros(out_ref.shape[1:], jnp.float32)
-    for expert in range(hidden_ref.shape[0]):
+    for expert in range(experts):
         total = total + jnp.dot(
-            hidden_ref[expert], weight_ref[0, expert], preferred_element_type=jnp.float32
+            hidden_ref[expert], down_ref[0, expert], preferred_element_type=jnp.float32
         )
     out_ref[0] = total
 
 
-def down_project(hidden, packed):
-    experts, tok_count, units = hidden.shape
-    lanes = packed.shape[3]
+def expert_project(normed_moe, combine, packed):
+    tok_count, model_width = normed_moe.shape
+    experts, lanes = packed.shape[1], packed.shape[3]
+    units = lanes
     col_blocks = packed.shape[2] // units
     return pl.pallas_call(
-        down_body,
+        expert_body,
         grid=(col_blocks,),
         in_specs=[
-            pl.BlockSpec((experts, tok_count, units), lambda c: (0, 0, 0)),
+            pl.BlockSpec((tok_count, model_width), lambda c: (0, 0)),
+            pl.BlockSpec((experts, tok_count, 1), lambda c: (0, 0, 0)),
+            pl.BlockSpec((2, experts, model_width, lanes), lambda c: (0, 0, 0, 0)),
             pl.BlockSpec((1, experts, units, lanes), lambda c: (2, 0, c, 0)),
         ],
         out_specs=pl.BlockSpec((1, tok_count, lanes), lambda c: (c, 0, 0)),
         out_shape=jax.ShapeDtypeStruct((col_blocks, tok_count, lanes), jnp.float32),
+        scratch_shapes=[pltpu.VMEM((experts, tok_count, units), jnp.bfloat16)],
         compiler_params=pltpu.CompilerParams(dimension_semantics=("arbitrary",)),
-    )(hidden, packed)
+    )(normed_moe, combine, packed, packed)
 
 
 def shards(
@@ -273,14 +290,11 @@
     combine = jnp.sum(
         jnp.where(routes[:, :, None] == expert_ids[None, None, :], gates[:, :, None], 0.0), axis=1
     )
-    gate_proj = jnp.einsum(
-        "td,edf->etf", normed_moe, packed[0], preferred_element_type=jnp.float32
-    )
-    up_proj = jnp.einsum(
-        "td,edf->etf", normed_moe, packed[1], preferred_element_type=jnp.float32
-    )
-    hidden = (jax.nn.silu(gate_proj) * up_proj * combine.T[:, :, None]).astype(jnp.bfloat16)
-    partial_out = down_project(hidden, packed).transpose(1, 0, 2).reshape(tok_count, model_width)
+    partial_out = (
+        expert_project(normed_moe, combine.T[:, :, None], packed)
+        .transpose(1, 0, 2)
+        .reshape(tok_count, model_width)
+    )
     hid_count = lax.axis_size("hid")
     hid_index = lax.axis_index("hid")
     expert_sum = lax.dynamic_slice_in_dim(partial_out, hid_index * share_width, share_width, 1)

time: 181 us -> 181 us (level)
  matrix products: 11.4 us -> 3.26 us
  Pallas kernels: 41.7 us -> 49.1 us
  starting transfers between devices: 22.9 us -> 19.9 us
  waiting for transfers between devices: 72.8 us -> 75.3 us
    dot_general x2 -> x0, matrix products: 8.11 us -> none  [the longest x1 4.61 us: shards(): jnp.einsum('td,edf->etf', normed_moe, packed[1], preferred_element_type=j...]
    pallas_call x1, Pallas kernels: 7.74 us -> 15.2 us  [expert_project(): pl.pallas_call(expert_body, grid=(col_blocks,), in_specs=[pl.BlockSpec((t...]
    ppermute x9, waiting for transfers between devices: 14.4 us -> 18.4 us  [shifted_copies(): copies.append(lax.ppermute(block, axis_name, pairs))]
    all_gather x1, waiting for transfers between devices: 22.9 us -> 19.9 us  [shards(): packed = lax.all_gather(packed, 'req', axis=1, tiled=True)]
    ppermute x9, starting transfers between devices: 18.2 us -> 15.3 us  [shifted_copies(): copies.append(lax.ppermute(block, axis_name, pairs))]
    ppermute x3, waiting for transfers between devices: 6.7 us -> 9.14 us  [shards(): incoming = lax.ppermute(outgoing.astype(jnp.bfloat16), 'hid', pairs)]
    broadcast_in_dim x0 -> x1, local copies, waits for them, and re-layouts: none -> 2 us  [shards(): combine.T[:, :, None]]
    unnamed x39 -> x31, local copies, waits for them, and re-layouts: 5.19 us -> 4.68 us
  transfers between devices with their start and end apart: 14 -> 14, of which waited for: 8 -> 8; matrix products, arithmetic and copies ran while one was open for 8% -> 10% of each run, Pallas kernels for 19% -> 19%
where the time goes in v10:
time: 181 us; the launch traced here: 180 us
  waiting for transfers between devices  75.3 us (42%)
  Pallas kernels  49.1 us (27%)
  starting transfers between devices  19.9 us (11%)
  between operations  14.3 us (8%)
  local copies, waits for them, and re-layouts  10.4 us (6%)
  other arithmetic  8.1 us (4%)
  matrix products  3.26 us (2%)
    pallas_call x1, Pallas kernels, attend(): pl.pallas_call(attention_body, grid_spec=grid_spec, out_shape=jax.ShapeDt...  33.8 us
    all_gather x1, waiting for transfers between devices, shards(): gathered = lax.all_gather(prefix_cache, 'req', axis=0, tiled=True)  27.7 us
    all_gather x1, waiting for transfers between devices, shards(): packed = lax.all_gather(packed, 'req', axis=1, tiled=True)  19.9 us
    ppermute x9, waiting for transfers between devices, shifted_copies(): copies.append(lax.ppermute(block, axis_name, pairs))  18.4 us
    ppermute x9, starting transfers between devices, shifted_copies(): copies.append(lax.ppermute(block, axis_name, pairs))  15.3 us
    pallas_call x1, Pallas kernels, expert_project(): pl.pallas_call(expert_body, grid=(col_blocks,), in_specs=[pl.BlockSpec((t...  15.2 us
    ppermute x3, waiting for transfers between devices, shards(): incoming = lax.ppermute(outgoing.astype(jnp.bfloat16), 'hid', pairs)  9.14 us
    unnamed x31, local copies, waits for them, and re-layouts  4.68 us
  transfers between devices with their start and end apart: 14, of which 8 were waited for; matrix products, arithmetic and copies ran while one was open for 10% of the time, Pallas kernels for 19%

profile of v10, /device:TPU:0, one launch (start us, length us, event | category | flops | bytes accessed | tf_op | source)
XLA Modules:
  0.0 180.3 jit_solution(4222140514071453294)
XLA Ops:
  7.2 2.4 %copy.63 = bf16[2,1024,2,128]{3,1,2,0:T(8,128)(2,1)} copy(bf16[2,1024,2,128]{3,2,1,0:T(2,128)(2,1)} %param.17) | data formatting | bytes 2097152 | tf_op args[3]
  9.7 5.1 %collective-permute-start.2 = (bf16[256,256]{1,0:T(8,128)(2,1)S(1)}, bf16[256,256]{1,0:T(8,128)(2,1)S(1)}, u32[]{:S(2)}, u32[]{:S(2)}) collective-permute-start(bf16[256,256]{1,0:T(8,128)(2,1)S(1)} %copy-done.3), channel_id=1, source_target_pairs={{0,3},{1,0},{2,1},{3,2},{4,7},{5,4},{6,5},{7,6},{8,11},{9,8},{10,9... | collective-permute-start | bytes 393224 | tf_op jit(solution)/shard_map/ppermute | solution.py:73
  14.9 1.0 collective-permute-start
  15.9 0.2 convert_reduce_fusion
  16.1 0.5 multiply_cosine_fusion
  16.7 2.1 %collective-permute-done.2 = bf16[256,256]{1,0:T(8,128)(2,1)S(1)} collective-permute-done((bf16[256,256]{1,0:T(8,128)(2,1)S(1)}, bf16[256,256]{1,0:T(8,128)(2,1)S(1)}, u32[]{:S(2)}, u32[]{:S(2)}) %collective-permute-start.2) | collective-permute-done | bytes 131104 | tf_op jit(solution)/shard_map/ppermute | solution.py:73
  18.8 7.3 %collective-permute-done.1 = bf16[256,256]{1,0:T(8,128)(2,1)S(1)} collective-permute-done((bf16[256,256]{1,0:T(8,128)(2,1)S(1)}, bf16[256,256]{1,0:T(8,128)(2,1)S(1)}, u32[]{:S(2)}, u32[]{:S(2)}) %collective-permute-start.1) | collective-permute-done | bytes 131104 | tf_op jit(solution)/shard_map/ppermute | solution.py:73
  26.2 0.6 gather_fusion
  26.9 0.2 fusion.16
  27.1 0.5 fusion.28
  27.6 0.2 copy.73
  27.8 0.2 copy.72
  28.0 0.1 subtract_convert_fusion
  28.2 0.9 pad_maximum_fusion.2
  29.2 1.3 maximum_bitcast_fusion
  30.6 1.6 collective-permute-start.8
  32.1 1.2 collective-permute-start.7
  33.3 1.9 %collective-permute-start.6 = (bf16[256,1024]{1,0:T(8,128)(2,1)}, bf16[256,1024]{1,0:T(8,128)(2,1)}, u32[]{:S(2)}, u32[]{:S(2)}) collective-permute-start(bf16[256,1024]{1,0:T(8,128)(2,1)} %param.22), channel_id=1, source_target_pairs={{0,1},{1,2},{2,3},{3,0},{4,5},{5,6},{6,7},{7,4},{8,9},{9,10},{10,1... | collective-permute-start | bytes 1572872 | tf_op jit(solution)/shard_map/ppermute | solution.py:73
  35.3 0.8 copy.64.segq_ref
  36.0 0.2 convert_reduce_fusion.2
  36.2 0.6 pad_add_fusion.bound_ref
  36.8 0.4 fusion.26
  37.3 0.1 copy.75
  37.4 0.1 copy.74
  37.7 0.8 copy.76
  38.4 0.8 maximum_bitcast_fusion.1.k_ref
  39.2 27.7 %all-gather.3.cloned.1.call-done = bf16[16,1024,2,128]{3,1,2,0:T(8,128)(2,1)} async-done(((bf16[2,1024,2,128]{3,1,2,0:T(8,128)(2,1)}), bf16[16,1024,2,128]{3,1,2,0:T(8,128)(2,1)}) %all-gather.3.cloned.1.call-update) | async-done | bytes 8388624 | tf_op jit(solution)/shard_map/all_gather | solution.py:265
  66.9 33.8 %shard_map.149 = f32[2,2,256,64]{3,2,1,0:T(8,128)} custom-call(s32[8]{0:T(128)} %bitcast.75, s32[16]{0:T(128)} %pad_add_fusion.bound_ref, bf16[2,2,256,64]{3,2,1,0:T(8,128)(2,1)} %bitcast.58, bf16[2,256,64]{2,1,0:T(8,128)(2,1)} %maximum_bitcast_fusion.1.k_ref, bf16[2,256,64]{2,1,0:T(8,128)(2,1)} %bitcast.57, s32[256,1]{1,0:T(8,128)} %copy.64.segq_ref, ...), custom_call_target="tpu_custom_call" | custom-call | tf_op jit(solution)/shard_map/pallas_call | solution.py:169
  100.8 1.1 convert_bitcast_fusion
  101.8 0.1 copy.65
  102.0 3.3 %collective-permute-start.5 = (bf16[256,256]{0,1:T(8,128)(2,1)S(1)}, bf16[256,256]{0,1:T(8,128)(2,1)S(1)}, u32[]{:S(2)}, u32[]{:S(2)}) collective-permute-start(bf16[256,256]{0,1:T(8,128)(2,1)S(1)} %bitcast.63), channel_id=1, source_target_pairs={{0,3},{1,0},{2,1},{3,2},{4,7},{5,4},{6,5},{7,6},{8,11},{9,8},{10,9... | collective-permute-start | bytes 393224 | tf_op jit(solution)/shard_map/ppermute | solution.py:73
  105.3 1.1 collective-permute-start.3
  106.5 2.0 %copy.68.combine_ref = f32[16,256,1]{2,1,0:T(8,128)} copy(f32[16,256,1]{1,0,2:T(8,128)S(1)} %bitcast.71) | data formatting | bytes 32768 | tf_op jit(solution)/shard_map/broadcast_in_dim | solution.py:294
  108.5 0.8 collective-permute-done.5
  109.3 8.2 %collective-permute-done.4 = bf16[256,256]{0,1:T(8,128)(2,1)S(1)} collective-permute-done((bf16[256,256]{0,1:T(8,128)(2,1)S(1)}, bf16[256,256]{0,1:T(8,128)(2,1)S(1)}, u32[]{:S(2)}, u32[]{:S(2)}) %collective-permute-start.4) | collective-permute-done | bytes 131104 | tf_op jit(solution)/shard_map/ppermute | solution.py:73
  117.5 2.4 %fusion.13 = (f32[256]{0:T(256)S(1)}, bf16[256,1024]{1,0:T(8,128)(2,1)S(1)}) fusion(bf16[256,1024]{1,0:T(8,128)(2,1)} %collective-permute-done.8, bf16[256,1024]{1,0:T(8,128)(2,1)} %collective-permute-done.7, bf16[256,1024]{1,0:T(8,128)(2,1)} %collective-permute-done.6, bf16[256,1024]{1,0:T(8,128)(2,1)} %param.22, ...), kind=kOutput, calls=%fused_computation.17 | convolution fusion | flops 550764288 | bytes 3671040 | tf_op jit(solution)/shard_map/dot_general | solution.py:273
  119.9 1.0 fusion.15.normed_ref
  120.9 19.9 %all-gather.5.cloned.1.call-done.weight_ref.down_ref = bf16[3,16,1024,128]{3,2,1,0:T(8,128)(2,1)} async-done(((bf16[3,2,1024,128]{3,2,1,0:T(8,128)(2,1)}), bf16[3,16,1024,128]{3,2,1,0:T(8,128)(2,1)}) %all-gather.5.cloned.1.call-update) | async-done | bytes 12582928 | tf_op jit(solution)/shard_map/all_gather | solution.py:287
  140.8 15.2 %shard_map.150 = f32[8,256,128]{2,1,0:T(8,128)} custom-call(bf16[256,1024]{1,0:T(8,128)(2,1)} %fusion.15.normed_ref, f32[16,256,1]{2,1,0:T(8,128)} %copy.68.combine_ref, bf16[3,16,1024,128]{3,2,1,0:T(8,128)(2,1)} %all-gather.5.cloned.1.call-done.weight_ref.down_ref, bf16[3,16,1024,128]{3,2,1,0:T(8,128)(2,1)} %all-gather.5.cloned.1.call-done.weight_ref.down_ref), custom_call_target="tpu_custom_call" | custom-call | tf_op jit(solution)/shard_map/pallas_call | solution.py:206
  156.1 1.3 copy_bitcast_fusion
  157.5 3.4 %collective-permute-start.11 = (bf16[256,256]{1,0:T(8,128)(2,1)S(1)}, bf16[256,256]{1,0:T(8,128)(2,1)S(1)}, u32[]{:S(2)}, u32[]{:S(2)}) collective-permute-start(bf16[256,256]{1,0:T(8,128)(2,1)S(1)} %get-tuple-element.21), channel_id=1, source_target_pairs={{0,3},{1,0},{2,1},{3,2},{4,7},{5,4},{6,5},{7,6},{8,11},{9,8},{10,9... | collective-permute-start | bytes 393224 | tf_op jit(solution)/shard_map/ppermute | solution.py:305
  160.9 1.1 collective-permute-start.9
  162.0 0.1 pad_maximum_fusion.3
  162.2 0.6 scatter_fusion
  162.8 0.8 copy.71
  163.6 1.2 collective-permute-done.11
  164.9 7.9 %collective-permute-done.10 = bf16[256,256]{1,0:T(8,128)(2,1)S(1)} collective-permute-done((bf16[256,256]{1,0:T(8,128)(2,1)S(1)}, bf16[256,256]{1,0:T(8,128)(2,1)S(1)}, u32[]{:S(2)}, u32[]{:S(2)}) %collective-permute-start.10) | collective-permute-done | bytes 131104 | tf_op jit(solution)/shard_map/ppermute | solution.py:305
  172.8 0.7 add_convert_fusion.1
  (57 shorter events, 0.8 us)
Async XLA Ops:
  7.2 21.9 %copy-start = (bf16[2,128,1024]{2,1,0:T(8,128)(2,1)S(1)}, bf16[2,128,1024]{2,1,0:T(8,128)(2,1)}, u32[]{:S(2)}) copy-start(bf16[2,128,1024]{2,1,0:T(8,128)(2,1)} %param.27) | copy-start | bytes 1572868
  7.2 2.6 %copy-start.3 = (bf16[256,256]{1,0:T(8,128)(2,1)S(1)}, bf16[256,256]{1,0:T(8,128)(2,1)}, u32[]{:S(2)}) copy-start(bf16[256,256]{1,0:T(8,128)(2,1)} %param.14) | copy-start | bytes 393220
  7.2 8.7 %copy-start.4 = (s32[1,256]{1,0:T(1,128)S(1)}, s32[1,256]{1,0:T(1,128)}, u32[]{:S(2)}) copy-start(s32[1,256]{1,0:T(1,128)} %segk_ref.1) | copy-start | bytes 3076
  7.2 59.7 %all-gather.3.cloned.1.call-start = ((), (), s32[]{:S(2)}) async-start(), calls=%async_computation | async-start | bytes 9437184 | tf_op jit(solution)/shard_map/all_gather | solution.py:265
  9.7 17.5 %copy-start.8 = (bf16[1024,256]{1,0:T(8,128)(2,1)S(1)}, bf16[1024,256]{1,0:T(8,128)(2,1)}, u32[]{:S(2)}) copy-start(bf16[1024,256]{1,0:T(8,128)(2,1)} %param.20) | copy-start | bytes 1572868
  9.7 17.5 %copy-start.10 = (f32[1024]{0:T(1024)S(1)}, f32[1024]{0:T(1024)}, u32[]{:S(2)}) copy-start(f32[1024]{0:T(1024)} %param.19) | copy-start | bytes 12292
  9.7 131.2 %all-gather.5.cloned.1.call-start = ((), (), s32[]{:S(2)}) async-start(), calls=%async_computation.1 | async-start | bytes 14155776 | tf_op jit(solution)/shard_map/all_gather | solution.py:287
  9.7 9.0 %collective-permute-start.2 = (bf16[256,256]{1,0:T(8,128)(2,1)S(1)}, bf16[256,256]{1,0:T(8,128)(2,1)S(1)}, u32[]{:S(2)}, u32[]{:S(2)}) collective-permute-start(bf16[256,256]{1,0:T(8,128)(2,1)S(1)} %copy-done.3), channel_id=1, source_target_pairs={{0,3},{1,0},{2,1},{3,2},{4,7},{5,4},{6,5},{7,6},{8,11},{9,8},{10,9... | collective-permute-start | bytes 393224 | tf_op jit(solution)/shard_map/ppermute | solution.py:73
  14.9 11.2 %collective-permute-start.1 = (bf16[256,256]{1,0:T(8,128)(2,1)S(1)}, bf16[256,256]{1,0:T(8,128)(2,1)S(1)}, u32[]{:S(2)}, u32[]{:S(2)}) collective-permute-start(bf16[256,256]{1,0:T(8,128)(2,1)S(1)} %copy-done.3), channel_id=1, source_target_pairs={{0,2},{1,3},{2,0},{3,1},{4,6},{5,7},{6,4},{7,5},{8,10},{9,11},{10,... | collective-permute-start | bytes 393224 | tf_op jit(solution)/shard_map/ppermute | solution.py:73
  14.9 11.2 %collective-permute-start = (bf16[256,256]{1,0:T(8,128)(2,1)S(1)}, bf16[256,256]{1,0:T(8,128)(2,1)S(1)}, u32[]{:S(2)}, u32[]{:S(2)}) collective-permute-start(bf16[256,256]{1,0:T(8,128)(2,1)S(1)} %copy-done.3), channel_id=1, source_target_pairs={{0,1},{1,2},{2,3},{3,0},{4,5},{5,6},{6,7},{7,4},{8,9},{9,10},{10,1... | collective-permute-start | bytes 393224 | tf_op jit(solution)/shard_map/ppermute | solution.py:73
  27.6 1.6 copy-start.2
  29.1 7.8 %copy-start.9 = (bf16[1024,256]{1,0:T(8,128)(2,1)S(1)}, bf16[1024,256]{1,0:T(8,128)(2,1)}, u32[]{:S(2)}) copy-start(bf16[1024,256]{1,0:T(8,128)(2,1)} %param.21) | copy-start | bytes 1572868
  30.6 74.8 %collective-permute-start.8 = (bf16[256,1024]{1,0:T(8,128)(2,1)}, bf16[256,1024]{1,0:T(8,128)(2,1)}, u32[]{:S(2)}, u32[]{:S(2)}) collective-permute-start(bf16[256,1024]{1,0:T(8,128)(2,1)} %param.22), channel_id=1, source_target_pairs={{0,3},{1,0},{2,1},{3,2},{4,7},{5,4},{6,5},{7,6},{8,11},{9,8},{10,9... | collective-permute-start | bytes 1572872 | tf_op jit(solution)/shard_map/ppermute | solution.py:73
  32.1 76.3 %collective-permute-start.7 = (bf16[256,1024]{1,0:T(8,128)(2,1)}, bf16[256,1024]{1,0:T(8,128)(2,1)}, u32[]{:S(2)}, u32[]{:S(2)}) collective-permute-start(bf16[256,1024]{1,0:T(8,128)(2,1)} %param.22), channel_id=1, source_target_pairs={{0,2},{1,3},{2,0},{3,1},{4,6},{5,7},{6,4},{7,5},{8,10},{9,11},{10,... | collective-permute-start | bytes 1572872 | tf_op jit(solution)/shard_map/ppermute | solution.py:73
  33.3 75.2 %collective-permute-start.6 = (bf16[256,1024]{1,0:T(8,128)(2,1)}, bf16[256,1024]{1,0:T(8,128)(2,1)}, u32[]{:S(2)}, u32[]{:S(2)}) collective-permute-start(bf16[256,1024]{1,0:T(8,128)(2,1)} %param.22), channel_id=1, source_target_pairs={{0,1},{1,2},{2,3},{3,0},{4,5},{5,6},{6,7},{7,4},{8,9},{9,10},{10,1... | collective-permute-start | bytes 1572872 | tf_op jit(solution)/shard_map/ppermute | solution.py:73
  66.9 39.5 %copy-start.5 = (f32[256,8]{0,1:T(8,128)S(1)}, f32[256,8]{0,1:T(8,128)}, u32[]{:S(2)}) copy-start(f32[256,8]{0,1:T(8,128)} %param.25) | copy-start | bytes 24580
  66.9 39.5 %copy-start.6 = (s32[256,8]{0,1:T(8,128)S(1)}, s32[256,8]{0,1:T(8,128)}, u32[]{:S(2)}) copy-start(s32[256,8]{0,1:T(8,128)} %param.24) | copy-start | bytes 24580
  102.0 7.3 %collective-permute-start.5 = (bf16[256,256]{0,1:T(8,128)(2,1)S(1)}, bf16[256,256]{0,1:T(8,128)(2,1)S(1)}, u32[]{:S(2)}, u32[]{:S(2)}) collective-permute-start(bf16[256,256]{0,1:T(8,128)(2,1)S(1)} %bitcast.63), channel_id=1, source_target_pairs={{0,3},{1,0},{2,1},{3,2},{4,7},{5,4},{6,5},{7,6},{8,11},{9,8},{10,9... | collective-permute-start | bytes 393224 | tf_op jit(solution)/shard_map/ppermute | solution.py:73
  105.3 12.2 %collective-permute-start.4 = (bf16[256,256]{0,1:T(8,128)(2,1)S(1)}, bf16[256,256]{0,1:T(8,128)(2,1)S(1)}, u32[]{:S(2)}, u32[]{:S(2)}) collective-permute-start(bf16[256,256]{0,1:T(8,128)(2,1)S(1)} %bitcast.64), channel_id=1, source_target_pairs={{0,2},{1,3},{2,0},{3,1},{4,6},{5,7},{6,4},{7,5},{8,10},{9,11},{10,... | collective-permute-start | bytes 393224 | tf_op jit(solution)/shard_map/ppermute | solution.py:73
  105.3 12.2 %collective-permute-start.3 = (bf16[256,256]{0,1:T(8,128)(2,1)S(1)}, bf16[256,256]{0,1:T(8,128)(2,1)S(1)}, u32[]{:S(2)}, u32[]{:S(2)}) collective-permute-start(bf16[256,256]{0,1:T(8,128)(2,1)S(1)} %bitcast.65), channel_id=1, source_target_pairs={{0,1},{1,2},{2,3},{3,0},{4,5},{5,6},{6,7},{7,4},{8,9},{9,10},{10,1... | collective-permute-start | bytes 393224 | tf_op jit(solution)/shard_map/ppermute | solution.py:73
  108.5 11.4 %copy-start.7 = (f32[1024]{0:T(1024)S(1)}, f32[1024]{0:T(1024)}, u32[]{:S(2)}) copy-start(f32[1024]{0:T(1024)} %param.23) | copy-start | bytes 12292
  120.9 41.1 %copy-start.11 = (s32[1,2]{1,0:T(1,128)S(1)}, s32[1,2]{1,0:T(1,128)}, u32[]{:S(2)}) copy-start(s32[1,2]{1,0:T(1,128)} %param.18) | copy-start | bytes 28
  120.9 41.1 %copy-start.1 = (bf16[256,2,64]{2,0,1:T(8,128)(2,1)S(1)}, bf16[256,2,64]{2,0,1:T(8,128)(2,1)}, u32[]{:S(2)}) copy-start(bf16[256,2,64]{2,0,1:T(8,128)(2,1)} %copy.76) | copy-start | bytes 196612
  157.5 7.4 %collective-permute-start.11 = (bf16[256,256]{1,0:T(8,128)(2,1)S(1)}, bf16[256,256]{1,0:T(8,128)(2,1)S(1)}, u32[]{:S(2)}, u32[]{:S(2)}) collective-permute-start(bf16[256,256]{1,0:T(8,128)(2,1)S(1)} %get-tuple-element.21), channel_id=1, source_target_pairs={{0,3},{1,0},{2,1},{3,2},{4,7},{5,4},{6,5},{7,6},{8,11},{9,8},{10,9... | collective-permute-start | bytes 393224 | tf_op jit(solution)/shard_map/ppermute | solution.py:305
  160.9 11.9 %collective-permute-start.10 = (bf16[256,256]{1,0:T(8,128)(2,1)S(1)}, bf16[256,256]{1,0:T(8,128)(2,1)S(1)}, u32[]{:S(2)}, u32[]{:S(2)}) collective-permute-start(bf16[256,256]{1,0:T(8,128)(2,1)S(1)} %get-tuple-element.22), channel_id=1, source_target_pairs={{0,2},{1,3},{2,0},{3,1},{4,6},{5,7},{6,4},{7,5},{8,10},{9,11},{10,... | collective-permute-start | bytes 393224 | tf_op jit(solution)/shard_map/ppermute | solution.py:305
  160.9 11.9 %collective-permute-start.9 = (bf16[256,256]{1,0:T(8,128)(2,1)S(1)}, bf16[256,256]{1,0:T(8,128)(2,1)S(1)}, u32[]{:S(2)}, u32[]{:S(2)}) collective-permute-start(bf16[256,256]{1,0:T(8,128)(2,1)S(1)} %get-tuple-element.20), channel_id=1, source_target_pairs={{0,1},{1,2},{2,3},{3,0},{4,5},{5,6},{6,7},{7,4},{8,9},{9,10},{10,1... | collective-permute-start | bytes 393224 | tf_op jit(solution)/shard_map/ppermute | solution.py:305
Sparse Core Ops, SparseCore 0:
  9.9 56.9 all-gather.2
  68.8 71.9 all-gather.4

commit v11 on v10

--- a/solution.py
+++ b/solution.py
@@ -178,43 +178,39 @@
     return out.transpose(2, 0, 1, 3).reshape(tok_count, -1).astype(jnp.bfloat16)
 
 
-def expert_body(normed_ref, combine_ref, weight_ref, down_ref, out_ref, hidden_ref):
-    experts = hidden_ref.shape[0]
-
+def expert_body(normed_ref, combine_ref, weight_ref, down_ref, out_ref):
     @pl.when(pl.program_id(0) == 0)
     def _():
-        rows = normed_ref[...]
-        for expert in range(experts):
-            gate_proj = jnp.dot(rows, weight_ref[0, expert], preferred_element_type=jnp.float32)
-            up_proj = jnp.dot(rows, weight_ref[1, expert], preferred_element_type=jnp.float32)
-            activated = gate_proj / (1.0 + jnp.exp(-gate_proj))
-            hidden_ref[expert] = (activated * up_proj * combine_ref[expert]).astype(jnp.bfloat16)
-
-    total = jnp.zeros(out_ref.shape[1:], jnp.float32)
-    for expert in range(experts):
-        total = total + jnp.dot(
-            hidden_ref[expert], down_ref[0, expert], preferred_element_type=jnp.float32
+        out_ref[...] = jnp.zeros_like(out_ref)
+
+    rows = normed_ref[...]
+    gate_proj = jnp.dot(rows, weight_ref[0, 0], preferred_element_type=jnp.float32)
+    up_proj = jnp.dot(rows, weight_ref[1, 0], preferred_element_type=jnp.float32)
+    activated = gate_proj / (1.0 + jnp.exp(-gate_proj))
+    hidden = (activated * up_proj * combine_ref[0]).astype(jnp.bfloat16)
+    units = hidden.shape[1]
+    for col in range(out_ref.shape[0]):
+        out_ref[col] += jnp.dot(
+            hidden, down_ref[0, 0, col * units : (col + 1) * units, :],
+            preferred_element_type=jnp.float32,
         )
-    out_ref[0] = total
 
 
 def expert_project(normed_moe, combine, packed):
     tok_count, model_width = normed_moe.shape
-    experts, lanes = packed.shape[1], packed.shape[3]
-    units = lanes
-    col_blocks = packed.shape[2] // units
+    experts, rows_per, lanes = packed.shape[1], packed.shape[2], packed.shape[3]
+    col_blocks = rows_per // lanes
     return pl.pallas_call(
         expert_body,
-        grid=(col_blocks,),
+        grid=(experts,),
         in_specs=[
-            pl.BlockSpec((tok_count, model_width), lambda c: (0, 0)),
-            pl.BlockSpec((experts, tok_count, 1), lambda c: (0, 0, 0)),
-            pl.BlockSpec((2, experts, model_width, lanes), lambda c: (0, 0, 0, 0)),
-            pl.BlockSpec((1, experts, units, lanes), lambda c: (2, 0, c, 0)),
+            pl.BlockSpec((tok_count, model_width), lambda e: (0, 0)),
+            pl.BlockSpec((1, tok_count, 1), lambda e: (e, 0, 0)),
+            pl.BlockSpec((2, 1, model_width, lanes), lambda e: (0, e, 0, 0)),
+            pl.BlockSpec((1, 1, rows_per, lanes), lambda e: (2, e, 0, 0)),
         ],
-        out_specs=pl.BlockSpec((1, tok_count, lanes), lambda c: (c, 0, 0)),
+        out_specs=pl.BlockSpec((col_blocks, tok_count, lanes), lambda e: (0, 0, 0)),
         out_shape=jax.ShapeDtypeStruct((col_blocks, tok_count, lanes), jnp.float32),
-        scratch_shapes=[pltpu.VMEM((experts, tok_count, units), jnp.bfloat16)],
         compiler_params=pltpu.CompilerParams(dimension_semantics=("arbitrary",)),
     )(normed_moe, combine, packed, packed)
 

time: 181 us -> 183 us (1.011)
  Pallas kernels: 49.1 us -> 51.2 us
  transfers between devices with their start and end apart: 14 -> 14, of which waited for: 8 -> 8; matrix products, arithmetic and copies ran while one was open for 10% -> 9% of each run, Pallas kernels for 19% -> 19%
where the time goes in v11:
time: 183 us; the launch traced here: 182 us
  waiting for transfers between devices  75 us (41%)
  Pallas kernels  51.2 us (28%)
  starting transfers between devices  19.9 us (11%)
  between operations  14.3 us (8%)
  local copies, waits for them, and re-layouts  10.4 us (6%)
  other arithmetic  8.1 us (4%)
  matrix products  3.26 us (2%)
    pallas_call x1, Pallas kernels, attend(): pl.pallas_call(attention_body, grid_spec=grid_spec, out_shape=jax.ShapeDt...  34.2 us
    all_gather x1, waiting for transfers between devices, shards(): gathered = lax.all_gather(prefix_cache, 'req', axis=0, tiled=True)  27.7 us
    all_gather x1, waiting for transfers between devices, shards(): packed = lax.all_gather(packed, 'req', axis=1, tiled=True)  20 us
    ppermute x9, waiting for transfers between devices, shifted_copies(): copies.append(lax.ppermute(block, axis_name, pairs))  18.1 us
    pallas_call x1, Pallas kernels, expert_project(): pl.pallas_call(expert_body, grid=(experts,), in_specs=[pl.BlockSpec((tok_...  17.1 us
    ppermute x9, starting transfers between devices, shifted_copies(): copies.append(lax.ppermute(block, axis_name, pairs))  15.3 us
    ppermute x3, waiting for transfers between devices, shards(): incoming = lax.ppermute(outgoing.astype(jnp.bfloat16), 'hid', pairs)  9.14 us
    unnamed x31, local copies, waits for them, and re-layouts  4.68 us
  transfers between devices with their start and end apart: 14, of which 8 were waited for; matrix products, arithmetic and copies ran while one was open for 9% of the time, Pallas kernels for 19%

profile of v11, /device:TPU:0, one launch (start us, length us, event | category | flops | bytes accessed | tf_op | source)
XLA Modules:
  0.0 182.2 jit_solution(15564336164869717498)
XLA Ops:
  7.2 2.4 %copy.63 = bf16[2,1024,2,128]{3,1,2,0:T(8,128)(2,1)} copy(bf16[2,1024,2,128]{3,2,1,0:T(2,128)(2,1)} %param.17) | data formatting | bytes 2097152 | tf_op args[3]
  9.7 5.1 %collective-permute-start.2 = (bf16[256,256]{1,0:T(8,128)(2,1)S(1)}, bf16[256,256]{1,0:T(8,128)(2,1)S(1)}, u32[]{:S(2)}, u32[]{:S(2)}) collective-permute-start(bf16[256,256]{1,0:T(8,128)(2,1)S(1)} %copy-done.3), channel_id=1, source_target_pairs={{0,3},{1,0},{2,1},{3,2},{4,7},{5,4},{6,5},{7,6},{8,11},{9,8},{10,9... | collective-permute-start | bytes 393224 | tf_op jit(solution)/shard_map/ppermute | solution.py:73
  14.9 1.0 collective-permute-start
  15.9 0.2 convert_reduce_fusion
  16.1 0.5 multiply_cosine_fusion
  16.7 2.1 %collective-permute-done.2 = bf16[256,256]{1,0:T(8,128)(2,1)S(1)} collective-permute-done((bf16[256,256]{1,0:T(8,128)(2,1)S(1)}, bf16[256,256]{1,0:T(8,128)(2,1)S(1)}, u32[]{:S(2)}, u32[]{:S(2)}) %collective-permute-start.2) | collective-permute-done | bytes 131104 | tf_op jit(solution)/shard_map/ppermute | solution.py:73
  18.8 7.3 %collective-permute-done.1 = bf16[256,256]{1,0:T(8,128)(2,1)S(1)} collective-permute-done((bf16[256,256]{1,0:T(8,128)(2,1)S(1)}, bf16[256,256]{1,0:T(8,128)(2,1)S(1)}, u32[]{:S(2)}, u32[]{:S(2)}) %collective-permute-start.1) | collective-permute-done | bytes 131104 | tf_op jit(solution)/shard_map/ppermute | solution.py:73
  26.2 0.6 gather_fusion
  26.9 0.2 fusion.16
  27.1 0.5 fusion.28
  27.6 0.2 copy.73
  27.8 0.2 copy.72
  28.0 0.1 subtract_convert_fusion
  28.2 0.9 pad_maximum_fusion.2
  29.2 1.3 maximum_bitcast_fusion
  30.6 1.6 collective-permute-start.8
  32.1 1.2 collective-permute-start.7
  33.3 1.9 %collective-permute-start.6 = (bf16[256,1024]{1,0:T(8,128)(2,1)}, bf16[256,1024]{1,0:T(8,128)(2,1)}, u32[]{:S(2)}, u32[]{:S(2)}) collective-permute-start(bf16[256,1024]{1,0:T(8,128)(2,1)} %param.22), channel_id=1, source_target_pairs={{0,1},{1,2},{2,3},{3,0},{4,5},{5,6},{6,7},{7,4},{8,9},{9,10},{10,1... | collective-permute-start | bytes 1572872 | tf_op jit(solution)/shard_map/ppermute | solution.py:73
  35.3 0.8 copy.64.segq_ref
  36.0 0.2 convert_reduce_fusion.2
  36.2 0.6 pad_add_fusion.bound_ref
  36.8 0.4 fusion.26
  37.3 0.1 copy.75
  37.4 0.1 copy.74
  37.7 0.8 copy.76
  38.4 0.8 maximum_bitcast_fusion.1.k_ref
  39.2 27.7 %all-gather.3.cloned.1.call-done = bf16[16,1024,2,128]{3,1,2,0:T(8,128)(2,1)} async-done(((bf16[2,1024,2,128]{3,1,2,0:T(8,128)(2,1)}), bf16[16,1024,2,128]{3,1,2,0:T(8,128)(2,1)}) %all-gather.3.cloned.1.call-update) | async-done | bytes 8388624 | tf_op jit(solution)/shard_map/all_gather | solution.py:261
  66.9 34.2 %shard_map.149 = f32[2,2,256,64]{3,2,1,0:T(8,128)} custom-call(s32[8]{0:T(128)} %bitcast.75, s32[16]{0:T(128)} %pad_add_fusion.bound_ref, bf16[2,2,256,64]{3,2,1,0:T(8,128)(2,1)} %bitcast.58, bf16[2,256,64]{2,1,0:T(8,128)(2,1)} %maximum_bitcast_fusion.1.k_ref, bf16[2,256,64]{2,1,0:T(8,128)(2,1)} %bitcast.57, s32[256,1]{1,0:T(8,128)} %copy.64.segq_ref, ...), custom_call_target="tpu_custom_call" | custom-call | tf_op jit(solution)/shard_map/pallas_call | solution.py:169
  101.1 1.1 convert_bitcast_fusion
  102.2 0.1 copy.65
  102.3 3.4 %collective-permute-start.5 = (bf16[256,256]{0,1:T(8,128)(2,1)S(1)}, bf16[256,256]{0,1:T(8,128)(2,1)S(1)}, u32[]{:S(2)}, u32[]{:S(2)}) collective-permute-start(bf16[256,256]{0,1:T(8,128)(2,1)S(1)} %bitcast.63), channel_id=1, source_target_pairs={{0,3},{1,0},{2,1},{3,2},{4,7},{5,4},{6,5},{7,6},{8,11},{9,8},{10,9... | collective-permute-start | bytes 393224 | tf_op jit(solution)/shard_map/ppermute | solution.py:73
  105.7 1.1 collective-permute-start.3
  106.8 2.0 %copy.68.combine_ref = f32[16,256,1]{2,1,0:T(8,128)} copy(f32[16,256,1]{1,0,2:T(8,128)S(1)} %bitcast.71) | data formatting | bytes 32768 | tf_op jit(solution)/shard_map/broadcast_in_dim | solution.py:290
  108.8 0.8 collective-permute-done.5
  109.6 7.9 %collective-permute-done.4 = bf16[256,256]{0,1:T(8,128)(2,1)S(1)} collective-permute-done((bf16[256,256]{0,1:T(8,128)(2,1)S(1)}, bf16[256,256]{0,1:T(8,128)(2,1)S(1)}, u32[]{:S(2)}, u32[]{:S(2)}) %collective-permute-start.4) | collective-permute-done | bytes 131104 | tf_op jit(solution)/shard_map/ppermute | solution.py:73
  117.5 2.4 %fusion.13 = (f32[256]{0:T(256)S(1)}, bf16[256,1024]{1,0:T(8,128)(2,1)S(1)}) fusion(bf16[256,1024]{1,0:T(8,128)(2,1)} %collective-permute-done.8, bf16[256,1024]{1,0:T(8,128)(2,1)} %collective-permute-done.7, bf16[256,1024]{1,0:T(8,128)(2,1)} %collective-permute-done.6, bf16[256,1024]{1,0:T(8,128)(2,1)} %param.22, ...), kind=kOutput, calls=%fused_computation.17 | convolution fusion | flops 550764288 | bytes 3671040 | tf_op jit(solution)/shard_map/dot_general | solution.py:269
  119.9 1.0 fusion.15.normed_ref
  120.9 20.0 %all-gather.5.cloned.1.call-done.weight_ref.down_ref = bf16[3,16,1024,128]{3,2,1,0:T(8,128)(2,1)} async-done(((bf16[3,2,1024,128]{3,2,1,0:T(8,128)(2,1)}), bf16[3,16,1024,128]{3,2,1,0:T(8,128)(2,1)}) %all-gather.5.cloned.1.call-update) | async-done | bytes 12582928 | tf_op jit(solution)/shard_map/all_gather | solution.py:283
  140.9 17.1 %shard_map.150 = f32[8,256,128]{2,1,0:T(8,128)} custom-call(bf16[256,1024]{1,0:T(8,128)(2,1)} %fusion.15.normed_ref, f32[16,256,1]{2,1,0:T(8,128)} %copy.68.combine_ref, bf16[3,16,1024,128]{3,2,1,0:T(8,128)(2,1)} %all-gather.5.cloned.1.call-done.weight_ref.down_ref, bf16[3,16,1024,128]{3,2,1,0:T(8,128)(2,1)} %all-gather.5.cloned.1.call-done.weight_ref.down_ref), custom_call_target="tpu_custom_call" | custom-call | tf_op jit(solution)/shard_map/pallas_call | solution.py:203
  157.9 1.3 copy_bitcast_fusion
  159.3 3.4 %collective-permute-start.11 = (bf16[256,256]{1,0:T(8,128)(2,1)S(1)}, bf16[256,256]{1,0:T(8,128)(2,1)S(1)}, u32[]{:S(2)}, u32[]{:S(2)}) collective-permute-start(bf16[256,256]{1,0:T(8,128)(2,1)S(1)} %get-tuple-element.21), channel_id=1, source_target_pairs={{0,3},{1,0},{2,1},{3,2},{4,7},{5,4},{6,5},{7,6},{8,11},{9,8},{10,9... | collective-permute-start | bytes 393224 | tf_op jit(solution)/shard_map/ppermute | solution.py:301
  162.7 1.1 collective-permute-start.9
  163.8 0.1 pad_maximum_fusion.3
  164.0 0.6 scatter_fusion
  164.7 0.8 copy.71
  165.5 1.2 collective-permute-done.11
  166.7 7.9 %collective-permute-done.10 = bf16[256,256]{1,0:T(8,128)(2,1)S(1)} collective-permute-done((bf16[256,256]{1,0:T(8,128)(2,1)S(1)}, bf16[256,256]{1,0:T(8,128)(2,1)S(1)}, u32[]{:S(2)}, u32[]{:S(2)}) %collective-permute-start.10) | collective-permute-done | bytes 131104 | tf_op jit(solution)/shard_map/ppermute | solution.py:301
  174.6 0.7 add_convert_fusion.1
  (57 shorter events, 0.8 us)
Async XLA Ops:
  7.2 21.9 %copy-start = (bf16[2,128,1024]{2,1,0:T(8,128)(2,1)S(1)}, bf16[2,128,1024]{2,1,0:T(8,128)(2,1)}, u32[]{:S(2)}) copy-start(bf16[2,128,1024]{2,1,0:T(8,128)(2,1)} %param.27) | copy-start | bytes 1572868
  7.2 2.6 %copy-start.3 = (bf16[256,256]{1,0:T(8,128)(2,1)S(1)}, bf16[256,256]{1,0:T(8,128)(2,1)}, u32[]{:S(2)}) copy-start(bf16[256,256]{1,0:T(8,128)(2,1)} %param.14) | copy-start | bytes 393220
  7.2 8.7 %copy-start.4 = (s32[1,256]{1,0:T(1,128)S(1)}, s32[1,256]{1,0:T(1,128)}, u32[]{:S(2)}) copy-start(s32[1,256]{1,0:T(1,128)} %segk_ref.1) | copy-start | bytes 3076
  7.2 59.7 %all-gather.3.cloned.1.call-start = ((), (), s32[]{:S(2)}) async-start(), calls=%async_computation | async-start | bytes 9437184 | tf_op jit(solution)/shard_map/all_gather | solution.py:261
  9.7 17.5 %copy-start.8 = (bf16[1024,256]{1,0:T(8,128)(2,1)S(1)}, bf16[1024,256]{1,0:T(8,128)(2,1)}, u32[]{:S(2)}) copy-start(bf16[1024,256]{1,0:T(8,128)(2,1)} %param.20) | copy-start | bytes 1572868
  9.7 17.5 %copy-start.10 = (f32[1024]{0:T(1024)S(1)}, f32[1024]{0:T(1024)}, u32[]{:S(2)}) copy-start(f32[1024]{0:T(1024)} %param.19) | copy-start | bytes 12292
  9.7 131.2 %all-gather.5.cloned.1.call-start = ((), (), s32[]{:S(2)}) async-start(), calls=%async_computation.1 | async-start | bytes 14155776 | tf_op jit(solution)/shard_map/all_gather | solution.py:283
  9.7 9.0 %collective-permute-start.2 = (bf16[256,256]{1,0:T(8,128)(2,1)S(1)}, bf16[256,256]{1,0:T(8,128)(2,1)S(1)}, u32[]{:S(2)}, u32[]{:S(2)}) collective-permute-start(bf16[256,256]{1,0:T(8,128)(2,1)S(1)} %copy-done.3), channel_id=1, source_target_pairs={{0,3},{1,0},{2,1},{3,2},{4,7},{5,4},{6,5},{7,6},{8,11},{9,8},{10,9... | collective-permute-start | bytes 393224 | tf_op jit(solution)/shard_map/ppermute | solution.py:73
  14.9 11.2 %collective-permute-start.1 = (bf16[256,256]{1,0:T(8,128)(2,1)S(1)}, bf16[256,256]{1,0:T(8,128)(2,1)S(1)}, u32[]{:S(2)}, u32[]{:S(2)}) collective-permute-start(bf16[256,256]{1,0:T(8,128)(2,1)S(1)} %copy-done.3), channel_id=1, source_target_pairs={{0,2},{1,3},{2,0},{3,1},{4,6},{5,7},{6,4},{7,5},{8,10},{9,11},{10,... | collective-permute-start | bytes 393224 | tf_op jit(solution)/shard_map/ppermute | solution.py:73
  14.9 11.2 %collective-permute-start = (bf16[256,256]{1,0:T(8,128)(2,1)S(1)}, bf16[256,256]{1,0:T(8,128)(2,1)S(1)}, u32[]{:S(2)}, u32[]{:S(2)}) collective-permute-start(bf16[256,256]{1,0:T(8,128)(2,1)S(1)} %copy-done.3), channel_id=1, source_target_pairs={{0,1},{1,2},{2,3},{3,0},{4,5},{5,6},{6,7},{7,4},{8,9},{9,10},{10,1... | collective-permute-start | bytes 393224 | tf_op jit(solution)/shard_map/ppermute | solution.py:73
  27.6 1.6 copy-start.2
  29.1 7.8 %copy-start.9 = (bf16[1024,256]{1,0:T(8,128)(2,1)S(1)}, bf16[1024,256]{1,0:T(8,128)(2,1)}, u32[]{:S(2)}) copy-start(bf16[1024,256]{1,0:T(8,128)(2,1)} %param.21) | copy-start | bytes 1572868
  30.6 75.1 %collective-permute-start.8 = (bf16[256,1024]{1,0:T(8,128)(2,1)}, bf16[256,1024]{1,0:T(8,128)(2,1)}, u32[]{:S(2)}, u32[]{:S(2)}) collective-permute-start(bf16[256,1024]{1,0:T(8,128)(2,1)} %param.22), channel_id=1, source_target_pairs={{0,3},{1,0},{2,1},{3,2},{4,7},{5,4},{6,5},{7,6},{8,11},{9,8},{10,9... | collective-permute-start | bytes 1572872 | tf_op jit(solution)/shard_map/ppermute | solution.py:73
  32.1 76.7 %collective-permute-start.7 = (bf16[256,1024]{1,0:T(8,128)(2,1)}, bf16[256,1024]{1,0:T(8,128)(2,1)}, u32[]{:S(2)}, u32[]{:S(2)}) collective-permute-start(bf16[256,1024]{1,0:T(8,128)(2,1)} %param.22), channel_id=1, source_target_pairs={{0,2},{1,3},{2,0},{3,1},{4,6},{5,7},{6,4},{7,5},{8,10},{9,11},{10,... | collective-permute-start | bytes 1572872 | tf_op jit(solution)/shard_map/ppermute | solution.py:73
  33.3 75.5 %collective-permute-start.6 = (bf16[256,1024]{1,0:T(8,128)(2,1)}, bf16[256,1024]{1,0:T(8,128)(2,1)}, u32[]{:S(2)}, u32[]{:S(2)}) collective-permute-start(bf16[256,1024]{1,0:T(8,128)(2,1)} %param.22), channel_id=1, source_target_pairs={{0,1},{1,2},{2,3},{3,0},{4,5},{5,6},{6,7},{7,4},{8,9},{9,10},{10,1... | collective-permute-start | bytes 1572872 | tf_op jit(solution)/shard_map/ppermute | solution.py:73
  66.9 39.9 %copy-start.5 = (f32[256,8]{0,1:T(8,128)S(1)}, f32[256,8]{0,1:T(8,128)}, u32[]{:S(2)}) copy-start(f32[256,8]{0,1:T(8,128)} %param.25) | copy-start | bytes 24580
  66.9 39.9 %copy-start.6 = (s32[256,8]{0,1:T(8,128)S(1)}, s32[256,8]{0,1:T(8,128)}, u32[]{:S(2)}) copy-start(s32[256,8]{0,1:T(8,128)} %param.24) | copy-start | bytes 24580
  102.3 7.3 %collective-permute-start.5 = (bf16[256,256]{0,1:T(8,128)(2,1)S(1)}, bf16[256,256]{0,1:T(8,128)(2,1)S(1)}, u32[]{:S(2)}, u32[]{:S(2)}) collective-permute-start(bf16[256,256]{0,1:T(8,128)(2,1)S(1)} %bitcast.63), channel_id=1, source_target_pairs={{0,3},{1,0},{2,1},{3,2},{4,7},{5,4},{6,5},{7,6},{8,11},{9,8},{10,9... | collective-permute-start | bytes 393224 | tf_op jit(solution)/shard_map/ppermute | solution.py:73
  105.7 11.9 %collective-permute-start.4 = (bf16[256,256]{0,1:T(8,128)(2,1)S(1)}, bf16[256,256]{0,1:T(8,128)(2,1)S(1)}, u32[]{:S(2)}, u32[]{:S(2)}) collective-permute-start(bf16[256,256]{0,1:T(8,128)(2,1)S(1)} %bitcast.64), channel_id=1, source_target_pairs={{0,2},{1,3},{2,0},{3,1},{4,6},{5,7},{6,4},{7,5},{8,10},{9,11},{10,... | collective-permute-start | bytes 393224 | tf_op jit(solution)/shard_map/ppermute | solution.py:73
  105.7 11.9 %collective-permute-start.3 = (bf16[256,256]{0,1:T(8,128)(2,1)S(1)}, bf16[256,256]{0,1:T(8,128)(2,1)S(1)}, u32[]{:S(2)}, u32[]{:S(2)}) collective-permute-start(bf16[256,256]{0,1:T(8,128)(2,1)S(1)} %bitcast.65), channel_id=1, source_target_pairs={{0,1},{1,2},{2,3},{3,0},{4,5},{5,6},{6,7},{7,4},{8,9},{9,10},{10,1... | collective-permute-start | bytes 393224 | tf_op jit(solution)/shard_map/ppermute | solution.py:73
  108.8 11.1 %copy-start.7 = (f32[1024]{0:T(1024)S(1)}, f32[1024]{0:T(1024)}, u32[]{:S(2)}) copy-start(f32[1024]{0:T(1024)} %param.23) | copy-start | bytes 12292
  120.9 42.9 %copy-start.11 = (s32[1,2]{1,0:T(1,128)S(1)}, s32[1,2]{1,0:T(1,128)}, u32[]{:S(2)}) copy-start(s32[1,2]{1,0:T(1,128)} %param.18) | copy-start | bytes 28
  120.9 42.9 %copy-start.1 = (bf16[256,2,64]{2,0,1:T(8,128)(2,1)S(1)}, bf16[256,2,64]{2,0,1:T(8,128)(2,1)}, u32[]{:S(2)}) copy-start(bf16[256,2,64]{2,0,1:T(8,128)(2,1)} %copy.76) | copy-start | bytes 196612
  159.3 7.4 %collective-permute-start.11 = (bf16[256,256]{1,0:T(8,128)(2,1)S(1)}, bf16[256,256]{1,0:T(8,128)(2,1)S(1)}, u32[]{:S(2)}, u32[]{:S(2)}) collective-permute-start(bf16[256,256]{1,0:T(8,128)(2,1)S(1)} %get-tuple-element.21), channel_id=1, source_target_pairs={{0,3},{1,0},{2,1},{3,2},{4,7},{5,4},{6,5},{7,6},{8,11},{9,8},{10,9... | collective-permute-start | bytes 393224 | tf_op jit(solution)/shard_map/ppermute | solution.py:301
  162.7 11.9 %collective-permute-start.10 = (bf16[256,256]{1,0:T(8,128)(2,1)S(1)}, bf16[256,256]{1,0:T(8,128)(2,1)S(1)}, u32[]{:S(2)}, u32[]{:S(2)}) collective-permute-start(bf16[256,256]{1,0:T(8,128)(2,1)S(1)} %get-tuple-element.22), channel_id=1, source_target_pairs={{0,2},{1,3},{2,0},{3,1},{4,6},{5,7},{6,4},{7,5},{8,10},{9,11},{10,... | collective-permute-start | bytes 393224 | tf_op jit(solution)/shard_map/ppermute | solution.py:301
  162.7 11.9 %collective-permute-start.9 = (bf16[256,256]{1,0:T(8,128)(2,1)S(1)}, bf16[256,256]{1,0:T(8,128)(2,1)S(1)}, u32[]{:S(2)}, u32[]{:S(2)}) collective-permute-start(bf16[256,256]{1,0:T(8,128)(2,1)S(1)} %get-tuple-element.20), channel_id=1, source_target_pairs={{0,1},{1,2},{2,3},{3,0},{4,5},{5,6},{6,7},{7,4},{8,9},{9,10},{10,1... | collective-permute-start | bytes 393224 | tf_op jit(solution)/shard_map/ppermute | solution.py:301
Sparse Core Ops, SparseCore 0:
  9.9 56.9 all-gather.2
  68.8 72.0 all-gather.4

commit v12 on v10

--- a/solution.py
+++ b/solution.py
@@ -296,14 +296,9 @@
         .reshape(tok_count, model_width)
     )
     hid_count = lax.axis_size("hid")
-    hid_index = lax.axis_index("hid")
-    expert_sum = lax.dynamic_slice_in_dim(partial_out, hid_index * share_width, share_width, 1)
-    for shift in range(1, hid_count):
-        block = (hid_index + shift) % hid_count
-        outgoing = lax.dynamic_slice_in_dim(partial_out, block * share_width, share_width, 1)
-        pairs = [(index, (index + shift) % hid_count) for index in range(hid_count)]
-        incoming = lax.ppermute(outgoing.astype(jnp.bfloat16), "hid", pairs)
-        expert_sum = expert_sum + incoming.astype(jnp.float32)
+    pieces = partial_out.astype(jnp.bfloat16).reshape(tok_count, hid_count, share_width)
+    received = lax.all_to_all(pieces, "hid", split_axis=1, concat_axis=1, tiled=True)
+    expert_sum = jnp.sum(received.astype(jnp.float32), axis=1)
     hidden_out = (middle_share.astype(jnp.float32) + expert_sum).astype(jnp.bfloat16)
     return (hidden_out, kv_pages)
 

time: 181 us -> 186 us (1.028)
  waiting for transfers between devices: 75.3 us -> 79.2 us
    all_to_all x0 -> x1, waiting for transfers between devices: none -> 13.3 us  [shards(): lax.all_to_all(pieces, 'hid', split_axis=1, concat_axis=1, tiled=True)]
    ppermute x3 -> x0, waiting for transfers between devices: 9.14 us -> none  [shards(): incoming = lax.ppermute(outgoing.astype(jnp.bfloat16), 'hid', pairs)]
    all_to_all x0 -> x1, starting transfers between devices: none -> 4.59 us  [shards(): lax.all_to_all(pieces, 'hid', split_axis=1, concat_axis=1, tiled=True)]
    ppermute x3 -> x0, starting transfers between devices: 4.49 us -> none  [shards(): incoming = lax.ppermute(outgoing.astype(jnp.bfloat16), 'hid', pairs)]
    ppermute x9, waiting for transfers between devices: 18.4 us -> 16.2 us  [shifted_copies(): copies.append(lax.ppermute(block, axis_name, pairs))]
    all_gather x1, waiting for transfers between devices: 19.9 us -> 21.9 us  [shards(): packed = lax.all_gather(packed, 'req', axis=1, tiled=True)]
  transfers between devices with their start and end apart: 14 -> 12, of which waited for: 8 -> 7; matrix products, arithmetic and copies ran while one was open for 10% -> 9% of each run, Pallas kernels for 19% -> 18%
where the time goes in v12:
time: 186 us
  waiting for transfers between devices  79.2 us (43%)
  Pallas kernels  49.4 us (27%)
  starting transfers between devices  20 us (11%)
  between operations  14.3 us (8%)
  local copies, waits for them, and re-layouts  10.2 us (5%)
  other arithmetic  9.51 us (5%)
  matrix products  3.09 us (2%)
    pallas_call x1, Pallas kernels, attend(): pl.pallas_call(attention_body, grid_spec=grid_spec, out_shape=jax.ShapeDt...  34.2 us
    all_gather x1, waiting for transfers between devices, shards(): gathered = lax.all_gather(prefix_cache, 'req', axis=0, tiled=True)  27.7 us
    all_gather x1, waiting for transfers between devices, shards(): packed = lax.all_gather(packed, 'req', axis=1, tiled=True)  21.9 us
    ppermute x9, waiting for transfers between devices, shifted_copies(): copies.append(lax.ppermute(block, axis_name, pairs))  16.2 us
    ppermute x9, starting transfers between devices, shifted_copies(): copies.append(lax.ppermute(block, axis_name, pairs))  15.3 us
    pallas_call x1, Pallas kernels, expert_project(): pl.pallas_call(expert_body, grid=(col_blocks,), in_specs=[pl.BlockSpec((t...  15.3 us
    all_to_all x1, waiting for transfers between devices, shards(): lax.all_to_all(pieces, 'hid', split_axis=1, concat_axis=1, tiled=True)  13.3 us
    unnamed x31, local copies, waits for them, and re-layouts  4.67 us
  transfers between devices with their start and end apart: 12, of which 7 were waited for; matrix products, arithmetic and copies ran while one was open for 9% of the time, Pallas kernels for 18%

profile of v12, /device:TPU:0, one launch (start us, length us, event | category | flops | bytes accessed | tf_op | source)
XLA Modules:
  0.0 185.7 jit_solution(1799967015921220899)
XLA Ops:
  7.2 2.4 %copy.63 = bf16[2,1024,2,128]{3,1,2,0:T(8,128)(2,1)} copy(bf16[2,1024,2,128]{3,2,1,0:T(2,128)(2,1)} %param.17) | data formatting | bytes 2097152 | tf_op args[3]
  9.8 5.1 %collective-permute-start.2 = (bf16[256,256]{1,0:T(8,128)(2,1)S(1)}, bf16[256,256]{1,0:T(8,128)(2,1)S(1)}, u32[]{:S(2)}, u32[]{:S(2)}) collective-permute-start(bf16[256,256]{1,0:T(8,128)(2,1)S(1)} %copy-done.3), channel_id=1, source_target_pairs={{0,3},{1,0},{2,1},{3,2},{4,7},{5,4},{6,5},{7,6},{8,11},{9,8},{10,9... | collective-permute-start | bytes 393224 | tf_op jit(solution)/shard_map/ppermute | solution.py:73
  14.9 1.0 collective-permute-start
  15.9 0.2 convert_reduce_fusion.1
  16.1 0.5 multiply_cosine_fusion
  16.7 2.1 %collective-permute-done.2 = bf16[256,256]{1,0:T(8,128)(2,1)S(1)} collective-permute-done((bf16[256,256]{1,0:T(8,128)(2,1)S(1)}, bf16[256,256]{1,0:T(8,128)(2,1)S(1)}, u32[]{:S(2)}, u32[]{:S(2)}) %collective-permute-start.2) | collective-permute-done | bytes 131104 | tf_op jit(solution)/shard_map/ppermute | solution.py:73
  18.8 7.3 %collective-permute-done.1 = bf16[256,256]{1,0:T(8,128)(2,1)S(1)} collective-permute-done((bf16[256,256]{1,0:T(8,128)(2,1)S(1)}, bf16[256,256]{1,0:T(8,128)(2,1)S(1)}, u32[]{:S(2)}, u32[]{:S(2)}) %collective-permute-start.1) | collective-permute-done | bytes 131104 | tf_op jit(solution)/shard_map/ppermute | solution.py:73
  26.2 0.6 gather_fusion
  26.9 0.2 fusion.16
  27.1 0.5 fusion.28
  27.6 0.2 copy.74
  27.8 0.2 copy.73
  28.0 0.1 subtract_convert_fusion
  28.2 0.9 pad_maximum_fusion.2
  29.2 1.3 maximum_bitcast_fusion
  30.6 1.6 collective-permute-start.8
  32.1 1.2 collective-permute-start.7
  33.3 1.9 %collective-permute-start.6 = (bf16[256,1024]{1,0:T(8,128)(2,1)}, bf16[256,1024]{1,0:T(8,128)(2,1)}, u32[]{:S(2)}, u32[]{:S(2)}) collective-permute-start(bf16[256,1024]{1,0:T(8,128)(2,1)} %param.22), channel_id=1, source_target_pairs={{0,1},{1,2},{2,3},{3,0},{4,5},{5,6},{6,7},{7,4},{8,9},{9,10},{10,1... | collective-permute-start | bytes 1572872 | tf_op jit(solution)/shard_map/ppermute | solution.py:73
  35.3 0.8 copy.64.segq_ref
  36.1 0.1 convert_reduce_fusion.3
  36.2 0.6 pad_add_fusion.bound_ref
  36.9 0.4 fusion.26
  37.3 0.1 copy.76
  37.5 0.1 copy.75
  37.7 0.8 copy.77
  38.5 0.8 maximum_bitcast_fusion.1.k_ref
  39.2 27.7 %all-gather.3.cloned.1.call-done = bf16[16,1024,2,128]{3,1,2,0:T(8,128)(2,1)} async-done(((bf16[2,1024,2,128]{3,1,2,0:T(8,128)(2,1)}), bf16[16,1024,2,128]{3,1,2,0:T(8,128)(2,1)}) %all-gather.3.cloned.1.call-update) | async-done | bytes 8388624 | tf_op jit(solution)/shard_map/all_gather | solution.py:265
  66.9 34.2 %shard_map.149 = f32[2,2,256,64]{3,2,1,0:T(8,128)} custom-call(s32[8]{0:T(128)} %bitcast.72, s32[16]{0:T(128)} %pad_add_fusion.bound_ref, bf16[2,2,256,64]{3,2,1,0:T(8,128)(2,1)} %bitcast.55, bf16[2,256,64]{2,1,0:T(8,128)(2,1)} %maximum_bitcast_fusion.1.k_ref, bf16[2,256,64]{2,1,0:T(8,128)(2,1)} %bitcast.54, s32[256,1]{1,0:T(8,128)} %copy.64.segq_ref, ...), custom_call_target="tpu_custom_call" | custom-call | tf_op jit(solution)/shard_map/pallas_call | solution.py:169
  101.1 1.1 convert_bitcast_fusion.1
  102.2 0.1 copy.65
  102.3 3.4 %collective-permute-start.5 = (bf16[256,256]{0,1:T(8,128)(2,1)S(1)}, bf16[256,256]{0,1:T(8,128)(2,1)S(1)}, u32[]{:S(2)}, u32[]{:S(2)}) collective-permute-start(bf16[256,256]{0,1:T(8,128)(2,1)S(1)} %bitcast.60), channel_id=1, source_target_pairs={{0,3},{1,0},{2,1},{3,2},{4,7},{5,4},{6,5},{7,6},{8,11},{9,8},{10,9... | collective-permute-start | bytes 393224 | tf_op jit(solution)/shard_map/ppermute | solution.py:73
  105.7 1.1 collective-permute-start.3
  106.8 2.0 %copy.68.combine_ref = f32[16,256,1]{2,1,0:T(8,128)} copy(f32[16,256,1]{1,0,2:T(8,128)S(1)} %bitcast.68) | data formatting | bytes 32768 | tf_op jit(solution)/shard_map/broadcast_in_dim | solution.py:294
  108.8 0.3 collective-permute-done.5
  109.1 6.6 %collective-permute-done.4 = bf16[256,256]{0,1:T(8,128)(2,1)S(1)} collective-permute-done((bf16[256,256]{0,1:T(8,128)(2,1)S(1)}, bf16[256,256]{0,1:T(8,128)(2,1)S(1)}, u32[]{:S(2)}, u32[]{:S(2)}) %collective-permute-start.4) | collective-permute-done | bytes 131104 | tf_op jit(solution)/shard_map/ppermute | solution.py:73
  115.6 2.2 %fusion.13 = (f32[256]{0:T(256)S(1)}, bf16[256,1024]{1,0:T(8,128)(2,1)S(1)}) fusion(bf16[256,1024]{1,0:T(8,128)(2,1)S(1)} %collective-permute-done.8, bf16[256,1024]{1,0:T(8,128)(2,1)} %collective-permute-done.7, bf16[256,1024]{1,0:T(8,128)(2,1)} %collective-permute-done.6, bf16[256,1024]{1,0:T(8,128)(2,1)} %param.22, ...), kind=kOutput, calls=%fused_computation.17 | convolution fusion | flops 550764288 | bytes 3671040 | tf_op jit(solution)/shard_map/dot_general | solution.py:273
  117.9 1.0 fusion.15.normed_ref
  118.9 21.9 %all-gather.5.cloned.1.call-done.weight_ref.down_ref = bf16[3,16,1024,128]{3,2,1,0:T(8,128)(2,1)} async-done(((bf16[3,2,1024,128]{3,2,1,0:T(8,128)(2,1)}), bf16[3,16,1024,128]{3,2,1,0:T(8,128)(2,1)}) %all-gather.5.cloned.1.call-update) | async-done | bytes 12582928 | tf_op jit(solution)/shard_map/all_gather | solution.py:287
  140.8 15.3 %shard_map.150 = f32[8,256,128]{2,1,0:T(8,128)} custom-call(bf16[256,1024]{1,0:T(8,128)(2,1)} %fusion.15.normed_ref, f32[16,256,1]{2,1,0:T(8,128)} %copy.68.combine_ref, bf16[3,16,1024,128]{3,2,1,0:T(8,128)(2,1)} %all-gather.5.cloned.1.call-done.weight_ref.down_ref, bf16[3,16,1024,128]{3,2,1,0:T(8,128)(2,1)} %all-gather.5.cloned.1.call-done.weight_ref.down_ref), custom_call_target="tpu_custom_call" | custom-call | tf_op jit(solution)/shard_map/pallas_call | solution.py:206
  156.1 1.3 convert_bitcast_fusion
  157.5 1.0 copy.69
  158.5 4.6 %all-to-all-start = ((bf16[256,4,256]{0,2,1:T(8,128)(2,1)}), bf16[256,4,256]{0,2,1:T(8,128)(2,1)S(1)}, u32[]{:S(2)}, u32[]{:S(2)}) async-start(bf16[256,4,256]{0,2,1:T(8,128)(2,1)} %bitcast.27), calls=%async_computation | async-start | bytes 1048576 | tf_op jit(solution)/shard_map/all_to_all | solution.py:300
  163.1 0.1 pad_maximum_fusion.3
  163.3 0.6 scatter_fusion
  163.9 0.8 copy.72
  164.7 13.3 %all-to-all-done = bf16[256,4,256]{0,2,1:T(8,128)(2,1)S(1)} async-done(((bf16[256,4,256]{0,2,1:T(8,128)(2,1)}), bf16[256,4,256]{0,2,1:T(8,128)(2,1)S(1)}, u32[]{:S(2)}, u32[]{:S(2)}) %all-to-all-start) | async-done | bytes 524320 | tf_op jit(solution)/shard_map/all_to_all | solution.py:300
  178.0 0.1 copy.70
  178.2 0.7 add_convert_fusion.1
  (55 shorter events, 0.8 us)
Async XLA Ops:
  7.2 21.9 %copy-start = (bf16[2,128,1024]{2,1,0:T(8,128)(2,1)S(1)}, bf16[2,128,1024]{2,1,0:T(8,128)(2,1)}, u32[]{:S(2)}) copy-start(bf16[2,128,1024]{2,1,0:T(8,128)(2,1)} %param.27) | copy-start | bytes 1572868
  7.2 2.6 %copy-start.3 = (bf16[256,256]{1,0:T(8,128)(2,1)S(1)}, bf16[256,256]{1,0:T(8,128)(2,1)}, u32[]{:S(2)}) copy-start(bf16[256,256]{1,0:T(8,128)(2,1)} %param.14) | copy-start | bytes 393220
  7.2 8.7 %copy-start.4 = (s32[1,256]{1,0:T(1,128)S(1)}, s32[1,256]{1,0:T(1,128)}, u32[]{:S(2)}) copy-start(s32[1,256]{1,0:T(1,128)} %segk_ref.1) | copy-start | bytes 3076
  7.2 59.7 %all-gather.3.cloned.1.call-start = ((), (), s32[]{:S(2)}) async-start(), calls=%async_computation.1 | async-start | bytes 9437184 | tf_op jit(solution)/shard_map/all_gather | solution.py:265
  9.7 17.5 %copy-start.8 = (bf16[1024,256]{1,0:T(8,128)(2,1)S(1)}, bf16[1024,256]{1,0:T(8,128)(2,1)}, u32[]{:S(2)}) copy-start(bf16[1024,256]{1,0:T(8,128)(2,1)} %param.20) | copy-start | bytes 1572868
  9.7 17.5 %copy-start.10 = (f32[1024]{0:T(1024)S(1)}, f32[1024]{0:T(1024)}, u32[]{:S(2)}) copy-start(f32[1024]{0:T(1024)} %param.19) | copy-start | bytes 12292
  9.7 131.1 %all-gather.5.cloned.1.call-start = ((), (), s32[]{:S(2)}) async-start(), calls=%async_computation.2 | async-start | bytes 14155776 | tf_op jit(solution)/shard_map/all_gather | solution.py:287
  9.8 9.0 %collective-permute-start.2 = (bf16[256,256]{1,0:T(8,128)(2,1)S(1)}, bf16[256,256]{1,0:T(8,128)(2,1)S(1)}, u32[]{:S(2)}, u32[]{:S(2)}) collective-permute-start(bf16[256,256]{1,0:T(8,128)(2,1)S(1)} %copy-done.3), channel_id=1, source_target_pairs={{0,3},{1,0},{2,1},{3,2},{4,7},{5,4},{6,5},{7,6},{8,11},{9,8},{10,9... | collective-permute-start | bytes 393224 | tf_op jit(solution)/shard_map/ppermute | solution.py:73
  14.9 11.2 %collective-permute-start.1 = (bf16[256,256]{1,0:T(8,128)(2,1)S(1)}, bf16[256,256]{1,0:T(8,128)(2,1)S(1)}, u32[]{:S(2)}, u32[]{:S(2)}) collective-permute-start(bf16[256,256]{1,0:T(8,128)(2,1)S(1)} %copy-done.3), channel_id=1, source_target_pairs={{0,2},{1,3},{2,0},{3,1},{4,6},{5,7},{6,4},{7,5},{8,10},{9,11},{10,... | collective-permute-start | bytes 393224 | tf_op jit(solution)/shard_map/ppermute | solution.py:73
  14.9 11.2 %collective-permute-start = (bf16[256,256]{1,0:T(8,128)(2,1)S(1)}, bf16[256,256]{1,0:T(8,128)(2,1)S(1)}, u32[]{:S(2)}, u32[]{:S(2)}) collective-permute-start(bf16[256,256]{1,0:T(8,128)(2,1)S(1)} %copy-done.3), channel_id=1, source_target_pairs={{0,1},{1,2},{2,3},{3,0},{4,5},{5,6},{6,7},{7,4},{8,9},{9,10},{10,1... | collective-permute-start | bytes 393224 | tf_op jit(solution)/shard_map/ppermute | solution.py:73
  27.6 1.6 copy-start.2
  29.1 7.8 %copy-start.9 = (bf16[1024,256]{1,0:T(8,128)(2,1)S(1)}, bf16[1024,256]{1,0:T(8,128)(2,1)}, u32[]{:S(2)}) copy-start(bf16[1024,256]{1,0:T(8,128)(2,1)} %param.21) | copy-start | bytes 1572868
  30.6 75.1 %collective-permute-start.8 = (bf16[256,1024]{1,0:T(8,128)(2,1)}, bf16[256,1024]{1,0:T(8,128)(2,1)S(1)}, u32[]{:S(2)}, u32[]{:S(2)}) collective-permute-start(bf16[256,1024]{1,0:T(8,128)(2,1)} %param.22), channel_id=1, source_target_pairs={{0,3},{1,0},{2,1},{3,2},{4,7},{5,4},{6,5},{7,6},{8,11},{9,8},{10,9... | collective-permute-start | bytes 1572872 | tf_op jit(solution)/shard_map/ppermute | solution.py:73
  32.1 76.7 %collective-permute-start.7 = (bf16[256,1024]{1,0:T(8,128)(2,1)}, bf16[256,1024]{1,0:T(8,128)(2,1)}, u32[]{:S(2)}, u32[]{:S(2)}) collective-permute-start(bf16[256,1024]{1,0:T(8,128)(2,1)} %param.22), channel_id=1, source_target_pairs={{0,2},{1,3},{2,0},{3,1},{4,6},{5,7},{6,4},{7,5},{8,10},{9,11},{10,... | collective-permute-start | bytes 1572872 | tf_op jit(solution)/shard_map/ppermute | solution.py:73
  33.3 75.5 %collective-permute-start.6 = (bf16[256,1024]{1,0:T(8,128)(2,1)}, bf16[256,1024]{1,0:T(8,128)(2,1)}, u32[]{:S(2)}, u32[]{:S(2)}) collective-permute-start(bf16[256,1024]{1,0:T(8,128)(2,1)} %param.22), channel_id=1, source_target_pairs={{0,1},{1,2},{2,3},{3,0},{4,5},{5,6},{6,7},{7,4},{8,9},{9,10},{10,1... | collective-permute-start | bytes 1572872 | tf_op jit(solution)/shard_map/ppermute | solution.py:73
  66.9 39.9 %copy-start.5 = (f32[256,8]{0,1:T(8,128)S(1)}, f32[256,8]{0,1:T(8,128)}, u32[]{:S(2)}) copy-start(f32[256,8]{0,1:T(8,128)} %param.25) | copy-start | bytes 24580
  66.9 39.9 %copy-start.6 = (s32[256,8]{0,1:T(8,128)S(1)}, s32[256,8]{0,1:T(8,128)}, u32[]{:S(2)}) copy-start(s32[256,8]{0,1:T(8,128)} %param.24) | copy-start | bytes 24580
  102.3 6.8 %collective-permute-start.5 = (bf16[256,256]{0,1:T(8,128)(2,1)S(1)}, bf16[256,256]{0,1:T(8,128)(2,1)S(1)}, u32[]{:S(2)}, u32[]{:S(2)}) collective-permute-start(bf16[256,256]{0,1:T(8,128)(2,1)S(1)} %bitcast.60), channel_id=1, source_target_pairs={{0,3},{1,0},{2,1},{3,2},{4,7},{5,4},{6,5},{7,6},{8,11},{9,8},{10,9... | collective-permute-start | bytes 393224 | tf_op jit(solution)/shard_map/ppermute | solution.py:73
  105.7 9.9 %collective-permute-start.4 = (bf16[256,256]{0,1:T(8,128)(2,1)S(1)}, bf16[256,256]{0,1:T(8,128)(2,1)S(1)}, u32[]{:S(2)}, u32[]{:S(2)}) collective-permute-start(bf16[256,256]{0,1:T(8,128)(2,1)S(1)} %bitcast.61), channel_id=1, source_target_pairs={{0,2},{1,3},{2,0},{3,1},{4,6},{5,7},{6,4},{7,5},{8,10},{9,11},{10,... | collective-permute-start | bytes 393224 | tf_op jit(solution)/shard_map/ppermute | solution.py:73
  105.7 9.9 %collective-permute-start.3 = (bf16[256,256]{0,1:T(8,128)(2,1)S(1)}, bf16[256,256]{0,1:T(8,128)(2,1)S(1)}, u32[]{:S(2)}, u32[]{:S(2)}) collective-permute-start(bf16[256,256]{0,1:T(8,128)(2,1)S(1)} %bitcast.62), channel_id=1, source_target_pairs={{0,1},{1,2},{2,3},{3,0},{4,5},{5,6},{6,7},{7,4},{8,9},{9,10},{10,1... | collective-permute-start | bytes 393224 | tf_op jit(solution)/shard_map/ppermute | solution.py:73
  108.8 9.1 %copy-start.7 = (f32[1024]{0:T(1024)S(1)}, f32[1024]{0:T(1024)}, u32[]{:S(2)}) copy-start(f32[1024]{0:T(1024)} %param.23) | copy-start | bytes 12292
  156.1 7.0 %copy-start.11 = (s32[1,2]{1,0:T(1,128)S(1)}, s32[1,2]{1,0:T(1,128)}, u32[]{:S(2)}) copy-start(s32[1,2]{1,0:T(1,128)} %param.18) | copy-start | bytes 28
  156.1 7.0 %copy-start.1 = (bf16[256,2,64]{2,0,1:T(8,128)(2,1)S(1)}, bf16[256,2,64]{2,0,1:T(8,128)(2,1)}, u32[]{:S(2)}) copy-start(bf16[256,2,64]{2,0,1:T(8,128)(2,1)} %copy.77) | copy-start | bytes 196612
  158.5 19.5 %all-to-all-start = ((bf16[256,4,256]{0,2,1:T(8,128)(2,1)}), bf16[256,4,256]{0,2,1:T(8,128)(2,1)S(1)}, u32[]{:S(2)}, u32[]{:S(2)}) async-start(bf16[256,4,256]{0,2,1:T(8,128)(2,1)} %bitcast.27), calls=%async_computation | async-start | bytes 1048576 | tf_op jit(solution)/shard_map/all_to_all | solution.py:300
Sparse Core Ops, SparseCore 0:
  9.9 56.9 all-gather.2
  68.8 71.9 all-gather.4

commit v13 on v10

--- a/solution.py
+++ b/solution.py
@@ -190,12 +190,16 @@
             activated = gate_proj / (1.0 + jnp.exp(-gate_proj))
             hidden_ref[expert] = (activated * up_proj * combine_ref[expert]).astype(jnp.bfloat16)
 
-    total = jnp.zeros(out_ref.shape[1:], jnp.float32)
-    for expert in range(experts):
-        total = total + jnp.dot(
-            hidden_ref[expert], down_ref[0, expert], preferred_element_type=jnp.float32
-        )
-    out_ref[0] = total
+    units = hidden_ref.shape[2]
+    for col in range(out_ref.shape[0]):
+        total = jnp.zeros(out_ref.shape[1:], jnp.float32)
+        for expert in range(experts):
+            total = total + jnp.dot(
+                hidden_ref[expert],
+                down_ref[0, expert, col * units : (col + 1) * units, :],
+                preferred_element_type=jnp.float32,
+            )
+        out_ref[col] = total
 
 
 def expert_project(normed_moe, combine, packed):
@@ -203,16 +207,17 @@
     experts, lanes = packed.shape[1], packed.shape[3]
     units = lanes
     col_blocks = packed.shape[2] // units
+    per_step = 4 if col_blocks % 4 == 0 else 1
     return pl.pallas_call(
         expert_body,
-        grid=(col_blocks,),
+        grid=(col_blocks // per_step,),
         in_specs=[
             pl.BlockSpec((tok_count, model_width), lambda c: (0, 0)),
             pl.BlockSpec((experts, tok_count, 1), lambda c: (0, 0, 0)),
             pl.BlockSpec((2, experts, model_width, lanes), lambda c: (0, 0, 0, 0)),
-            pl.BlockSpec((1, experts, units, lanes), lambda c: (2, 0, c, 0)),
+            pl.BlockSpec((1, experts, per_step * units, lanes), lambda c: (2, 0, c, 0)),
         ],
-        out_specs=pl.BlockSpec((1, tok_count, lanes), lambda c: (c, 0, 0)),
+        out_specs=pl.BlockSpec((per_step, tok_count, lanes), lambda c: (c, 0, 0)),
         out_shape=jax.ShapeDtypeStruct((col_blocks, tok_count, lanes), jnp.float32),
         scratch_shapes=[pltpu.VMEM((experts, tok_count, units), jnp.bfloat16)],
         compiler_params=pltpu.CompilerParams(dimension_semantics=("arbitrary",)),

time: 181 us -> 178 us (0.983)
  Pallas kernels: 49.1 us -> 43.8 us
  waiting for transfers between devices: 75.3 us -> 78 us
    all_gather x1, waiting for transfers between devices: 19.9 us -> 22.8 us  [shards(): packed = lax.all_gather(packed, 'req', axis=1, tiled=True)]
    pallas_call x1, Pallas kernels: 33.8 us -> 31.1 us  [attend(): pl.pallas_call(attention_body, grid_spec=grid_spec, out_shape=jax.ShapeDt...]
    pallas_call x1, Pallas kernels: 15.2 us -> 12.6 us  [expert_project(): pl.pallas_call(expert_body, grid=(col_blocks // per_step,), in_specs=[pl....]
  transfers between devices with their start and end apart: 14 -> 14, of which waited for: 8 -> 8; matrix products, arithmetic and copies ran while one was open for 10% -> 10% of each run, Pallas kernels for 19% -> 18%
where the time goes in v13:
time: 178 us
  waiting for transfers between devices  78 us (44%)
  Pallas kernels  43.8 us (25%)
  starting transfers between devices  19.9 us (11%)
  between operations  14.3 us (8%)
  local copies, waits for them, and re-layouts  10.4 us (6%)
  other arithmetic  8.1 us (5%)
  matrix products  3.26 us (2%)
    pallas_call x1, Pallas kernels, attend(): pl.pallas_call(attention_body, grid_spec=grid_spec, out_shape=jax.ShapeDt...  31.1 us
    all_gather x1, waiting for transfers between devices, shards(): gathered = lax.all_gather(prefix_cache, 'req', axis=0, tiled=True)  27.7 us
    all_gather x1, waiting for transfers between devices, shards(): packed = lax.all_gather(packed, 'req', axis=1, tiled=True)  22.8 us
    ppermute x9, waiting for transfers between devices, shifted_copies(): copies.append(lax.ppermute(block, axis_name, pairs))  18.3 us
    ppermute x9, starting transfers between devices, shifted_copies(): copies.append(lax.ppermute(block, axis_name, pairs))  15.3 us
    pallas_call x1, Pallas kernels, expert_project(): pl.pallas_call(expert_body, grid=(col_blocks // per_step,), in_specs=[pl....  12.6 us
    ppermute x3, waiting for transfers between devices, shards(): incoming = lax.ppermute(outgoing.astype(jnp.bfloat16), 'hid', pairs)  9.14 us
    unnamed x31, local copies, waits for them, and re-layouts  4.68 us
  transfers between devices with their start and end apart: 14, of which 8 were waited for; matrix products, arithmetic and copies ran while one was open for 10% of the time, Pallas kernels for 18%

profile of v13, /device:TPU:0, one launch (start us, length us, event | category | flops | bytes accessed | tf_op | source)
XLA Modules:
  0.0 177.8 jit_solution(16787847629534294897)
XLA Ops:
  7.2 2.4 %copy.63 = bf16[2,1024,2,128]{3,1,2,0:T(8,128)(2,1)} copy(bf16[2,1024,2,128]{3,2,1,0:T(2,128)(2,1)} %param.17) | data formatting | bytes 2097152 | tf_op args[3]
  9.7 5.1 %collective-permute-start.2 = (bf16[256,256]{1,0:T(8,128)(2,1)S(1)}, bf16[256,256]{1,0:T(8,128)(2,1)S(1)}, u32[]{:S(2)}, u32[]{:S(2)}) collective-permute-start(bf16[256,256]{1,0:T(8,128)(2,1)S(1)} %copy-done.3), channel_id=1, source_target_pairs={{0,3},{1,0},{2,1},{3,2},{4,7},{5,4},{6,5},{7,6},{8,11},{9,8},{10,9... | collective-permute-start | bytes 393224 | tf_op jit(solution)/shard_map/ppermute | solution.py:73
  14.9 1.0 collective-permute-start
  15.9 0.2 convert_reduce_fusion
  16.1 0.5 multiply_cosine_fusion
  16.7 2.1 %collective-permute-done.2 = bf16[256,256]{1,0:T(8,128)(2,1)S(1)} collective-permute-done((bf16[256,256]{1,0:T(8,128)(2,1)S(1)}, bf16[256,256]{1,0:T(8,128)(2,1)S(1)}, u32[]{:S(2)}, u32[]{:S(2)}) %collective-permute-start.2) | collective-permute-done | bytes 131104 | tf_op jit(solution)/shard_map/ppermute | solution.py:73
  18.8 7.3 %collective-permute-done.1 = bf16[256,256]{1,0:T(8,128)(2,1)S(1)} collective-permute-done((bf16[256,256]{1,0:T(8,128)(2,1)S(1)}, bf16[256,256]{1,0:T(8,128)(2,1)S(1)}, u32[]{:S(2)}, u32[]{:S(2)}) %collective-permute-start.1) | collective-permute-done | bytes 131104 | tf_op jit(solution)/shard_map/ppermute | solution.py:73
  26.2 0.6 gather_fusion
  26.9 0.2 fusion.16
  27.1 0.5 fusion.28
  27.6 0.2 copy.73
  27.8 0.2 copy.72
  28.0 0.1 subtract_convert_fusion
  28.2 0.9 pad_maximum_fusion.2
  29.2 1.3 maximum_bitcast_fusion
  30.6 1.6 collective-permute-start.8
  32.1 1.2 collective-permute-start.7
  33.3 1.9 %collective-permute-start.6 = (bf16[256,1024]{1,0:T(8,128)(2,1)}, bf16[256,1024]{1,0:T(8,128)(2,1)}, u32[]{:S(2)}, u32[]{:S(2)}) collective-permute-start(bf16[256,1024]{1,0:T(8,128)(2,1)} %param.22), channel_id=1, source_target_pairs={{0,1},{1,2},{2,3},{3,0},{4,5},{5,6},{6,7},{7,4},{8,9},{9,10},{10,1... | collective-permute-start | bytes 1572872 | tf_op jit(solution)/shard_map/ppermute | solution.py:73
  35.3 0.8 copy.64.segq_ref
  36.0 0.2 convert_reduce_fusion.2
  36.2 0.6 pad_add_fusion.bound_ref
  36.8 0.4 fusion.26
  37.3 0.1 copy.75
  37.4 0.1 copy.74
  37.7 0.8 copy.76
  38.4 0.8 maximum_bitcast_fusion.1.k_ref
  39.2 27.7 %all-gather.3.cloned.1.call-done = bf16[16,1024,2,128]{3,1,2,0:T(8,128)(2,1)} async-done(((bf16[2,1024,2,128]{3,1,2,0:T(8,128)(2,1)}), bf16[16,1024,2,128]{3,1,2,0:T(8,128)(2,1)}) %all-gather.3.cloned.1.call-update) | async-done | bytes 8388624 | tf_op jit(solution)/shard_map/all_gather | solution.py:270
  66.9 31.1 %shard_map.149 = f32[2,2,256,64]{3,2,1,0:T(8,128)} custom-call(s32[8]{0:T(128)} %bitcast.75, s32[16]{0:T(128)} %pad_add_fusion.bound_ref, bf16[2,2,256,64]{3,2,1,0:T(8,128)(2,1)} %bitcast.58, bf16[2,256,64]{2,1,0:T(8,128)(2,1)} %maximum_bitcast_fusion.1.k_ref, bf16[2,256,64]{2,1,0:T(8,128)(2,1)} %bitcast.57, s32[256,1]{1,0:T(8,128)} %copy.64.segq_ref, ...), custom_call_target="tpu_custom_call" | custom-call | tf_op jit(solution)/shard_map/pallas_call | solution.py:169
  98.0 1.1 convert_bitcast_fusion
  99.1 0.1 copy.65
  99.3 3.4 %collective-permute-start.5 = (bf16[256,256]{0,1:T(8,128)(2,1)S(1)}, bf16[256,256]{0,1:T(8,128)(2,1)S(1)}, u32[]{:S(2)}, u32[]{:S(2)}) collective-permute-start(bf16[256,256]{0,1:T(8,128)(2,1)S(1)} %bitcast.63), channel_id=1, source_target_pairs={{0,3},{1,0},{2,1},{3,2},{4,7},{5,4},{6,5},{7,6},{8,11},{9,8},{10,9... | collective-permute-start | bytes 393224 | tf_op jit(solution)/shard_map/ppermute | solution.py:73
  102.7 1.1 collective-permute-start.3
  103.8 2.0 %copy.68.combine_ref = f32[16,256,1]{2,1,0:T(8,128)} copy(f32[16,256,1]{1,0,2:T(8,128)S(1)} %bitcast.71) | data formatting | bytes 32768 | tf_op jit(solution)/shard_map/broadcast_in_dim | solution.py:299
  105.8 0.8 collective-permute-done.5
  106.6 8.1 %collective-permute-done.4 = bf16[256,256]{0,1:T(8,128)(2,1)S(1)} collective-permute-done((bf16[256,256]{0,1:T(8,128)(2,1)S(1)}, bf16[256,256]{0,1:T(8,128)(2,1)S(1)}, u32[]{:S(2)}, u32[]{:S(2)}) %collective-permute-start.4) | collective-permute-done | bytes 131104 | tf_op jit(solution)/shard_map/ppermute | solution.py:73
  114.7 2.4 %fusion.13 = (f32[256]{0:T(256)S(1)}, bf16[256,1024]{1,0:T(8,128)(2,1)S(1)}) fusion(bf16[256,1024]{1,0:T(8,128)(2,1)} %collective-permute-done.8, bf16[256,1024]{1,0:T(8,128)(2,1)} %collective-permute-done.7, bf16[256,1024]{1,0:T(8,128)(2,1)} %collective-permute-done.6, bf16[256,1024]{1,0:T(8,128)(2,1)} %param.22, ...), kind=kOutput, calls=%fused_computation.17 | convolution fusion | flops 550764288 | bytes 3671040 | tf_op jit(solution)/shard_map/dot_general | solution.py:278
  117.1 1.0 fusion.15.normed_ref
  118.1 22.8 %all-gather.5.cloned.1.call-done.weight_ref.down_ref = bf16[3,16,1024,128]{3,2,1,0:T(8,128)(2,1)} async-done(((bf16[3,2,1024,128]{3,2,1,0:T(8,128)(2,1)}), bf16[3,16,1024,128]{3,2,1,0:T(8,128)(2,1)}) %all-gather.5.cloned.1.call-update) | async-done | bytes 12582928 | tf_op jit(solution)/shard_map/all_gather | solution.py:292
  140.9 12.6 %shard_map.150 = f32[8,256,128]{2,1,0:T(8,128)} custom-call(bf16[256,1024]{1,0:T(8,128)(2,1)} %fusion.15.normed_ref, f32[16,256,1]{2,1,0:T(8,128)} %copy.68.combine_ref, bf16[3,16,1024,128]{3,2,1,0:T(8,128)(2,1)} %all-gather.5.cloned.1.call-done.weight_ref.down_ref, bf16[3,16,1024,128]{3,2,1,0:T(8,128)(2,1)} %all-gather.5.cloned.1.call-done.weight_ref.down_ref), custom_call_target="tpu_custom_call" | custom-call | tf_op jit(solution)/shard_map/pallas_call | solution.py:211
  153.5 1.3 copy_bitcast_fusion
  154.9 3.4 %collective-permute-start.11 = (bf16[256,256]{1,0:T(8,128)(2,1)S(1)}, bf16[256,256]{1,0:T(8,128)(2,1)S(1)}, u32[]{:S(2)}, u32[]{:S(2)}) collective-permute-start(bf16[256,256]{1,0:T(8,128)(2,1)S(1)} %get-tuple-element.21), channel_id=1, source_target_pairs={{0,3},{1,0},{2,1},{3,2},{4,7},{5,4},{6,5},{7,6},{8,11},{9,8},{10,9... | collective-permute-start | bytes 393224 | tf_op jit(solution)/shard_map/ppermute | solution.py:310
  158.3 1.1 collective-permute-start.9
  159.4 0.1 pad_maximum_fusion.3
  159.6 0.6 scatter_fusion
  160.3 0.8 copy.71
  161.1 1.2 collective-permute-done.11
  162.3 7.9 %collective-permute-done.10 = bf16[256,256]{1,0:T(8,128)(2,1)S(1)} collective-permute-done((bf16[256,256]{1,0:T(8,128)(2,1)S(1)}, bf16[256,256]{1,0:T(8,128)(2,1)S(1)}, u32[]{:S(2)}, u32[]{:S(2)}) %collective-permute-start.10) | collective-permute-done | bytes 131104 | tf_op jit(solution)/shard_map/ppermute | solution.py:310
  170.2 0.7 add_convert_fusion.1
  (57 shorter events, 0.8 us)
Async XLA Ops:
  7.2 21.9 %copy-start = (bf16[2,128,1024]{2,1,0:T(8,128)(2,1)S(1)}, bf16[2,128,1024]{2,1,0:T(8,128)(2,1)}, u32[]{:S(2)}) copy-start(bf16[2,128,1024]{2,1,0:T(8,128)(2,1)} %param.27) | copy-start | bytes 1572868
  7.2 2.6 %copy-start.3 = (bf16[256,256]{1,0:T(8,128)(2,1)S(1)}, bf16[256,256]{1,0:T(8,128)(2,1)}, u32[]{:S(2)}) copy-start(bf16[256,256]{1,0:T(8,128)(2,1)} %param.14) | copy-start | bytes 393220
  7.2 8.7 %copy-start.4 = (s32[1,256]{1,0:T(1,128)S(1)}, s32[1,256]{1,0:T(1,128)}, u32[]{:S(2)}) copy-start(s32[1,256]{1,0:T(1,128)} %segk_ref.1) | copy-start | bytes 3076
  7.2 59.7 %all-gather.3.cloned.1.call-start = ((), (), s32[]{:S(2)}) async-start(), calls=%async_computation | async-start | bytes 9437184 | tf_op jit(solution)/shard_map/all_gather | solution.py:270
  9.7 17.5 %copy-start.8 = (bf16[1024,256]{1,0:T(8,128)(2,1)S(1)}, bf16[1024,256]{1,0:T(8,128)(2,1)}, u32[]{:S(2)}) copy-start(bf16[1024,256]{1,0:T(8,128)(2,1)} %param.20) | copy-start | bytes 1572868
  9.7 17.5 %copy-start.10 = (f32[1024]{0:T(1024)S(1)}, f32[1024]{0:T(1024)}, u32[]{:S(2)}) copy-start(f32[1024]{0:T(1024)} %param.19) | copy-start | bytes 12292
  9.7 131.2 %all-gather.5.cloned.1.call-start = ((), (), s32[]{:S(2)}) async-start(), calls=%async_computation.1 | async-start | bytes 14155776 | tf_op jit(solution)/shard_map/all_gather | solution.py:292
  9.7 9.0 %collective-permute-start.2 = (bf16[256,256]{1,0:T(8,128)(2,1)S(1)}, bf16[256,256]{1,0:T(8,128)(2,1)S(1)}, u32[]{:S(2)}, u32[]{:S(2)}) collective-permute-start(bf16[256,256]{1,0:T(8,128)(2,1)S(1)} %copy-done.3), channel_id=1, source_target_pairs={{0,3},{1,0},{2,1},{3,2},{4,7},{5,4},{6,5},{7,6},{8,11},{9,8},{10,9... | collective-permute-start | bytes 393224 | tf_op jit(solution)/shard_map/ppermute | solution.py:73
  14.9 11.2 %collective-permute-start.1 = (bf16[256,256]{1,0:T(8,128)(2,1)S(1)}, bf16[256,256]{1,0:T(8,128)(2,1)S(1)}, u32[]{:S(2)}, u32[]{:S(2)}) collective-permute-start(bf16[256,256]{1,0:T(8,128)(2,1)S(1)} %copy-done.3), channel_id=1, source_target_pairs={{0,2},{1,3},{2,0},{3,1},{4,6},{5,7},{6,4},{7,5},{8,10},{9,11},{10,... | collective-permute-start | bytes 393224 | tf_op jit(solution)/shard_map/ppermute | solution.py:73
  14.9 11.2 %collective-permute-start = (bf16[256,256]{1,0:T(8,128)(2,1)S(1)}, bf16[256,256]{1,0:T(8,128)(2,1)S(1)}, u32[]{:S(2)}, u32[]{:S(2)}) collective-permute-start(bf16[256,256]{1,0:T(8,128)(2,1)S(1)} %copy-done.3), channel_id=1, source_target_pairs={{0,1},{1,2},{2,3},{3,0},{4,5},{5,6},{6,7},{7,4},{8,9},{9,10},{10,1... | collective-permute-start | bytes 393224 | tf_op jit(solution)/shard_map/ppermute | solution.py:73
  27.6 1.6 copy-start.2
  29.1 7.8 %copy-start.9 = (bf16[1024,256]{1,0:T(8,128)(2,1)S(1)}, bf16[1024,256]{1,0:T(8,128)(2,1)}, u32[]{:S(2)}) copy-start(bf16[1024,256]{1,0:T(8,128)(2,1)} %param.21) | copy-start | bytes 1572868
  30.6 72.1 %collective-permute-start.8 = (bf16[256,1024]{1,0:T(8,128)(2,1)}, bf16[256,1024]{1,0:T(8,128)(2,1)}, u32[]{:S(2)}, u32[]{:S(2)}) collective-permute-start(bf16[256,1024]{1,0:T(8,128)(2,1)} %param.22), channel_id=1, source_target_pairs={{0,3},{1,0},{2,1},{3,2},{4,7},{5,4},{6,5},{7,6},{8,11},{9,8},{10,9... | collective-permute-start | bytes 1572872 | tf_op jit(solution)/shard_map/ppermute | solution.py:73
  32.1 73.7 %collective-permute-start.7 = (bf16[256,1024]{1,0:T(8,128)(2,1)}, bf16[256,1024]{1,0:T(8,128)(2,1)}, u32[]{:S(2)}, u32[]{:S(2)}) collective-permute-start(bf16[256,1024]{1,0:T(8,128)(2,1)} %param.22), channel_id=1, source_target_pairs={{0,2},{1,3},{2,0},{3,1},{4,6},{5,7},{6,4},{7,5},{8,10},{9,11},{10,... | collective-permute-start | bytes 1572872 | tf_op jit(solution)/shard_map/ppermute | solution.py:73
  33.3 72.5 %collective-permute-start.6 = (bf16[256,1024]{1,0:T(8,128)(2,1)}, bf16[256,1024]{1,0:T(8,128)(2,1)}, u32[]{:S(2)}, u32[]{:S(2)}) collective-permute-start(bf16[256,1024]{1,0:T(8,128)(2,1)} %param.22), channel_id=1, source_target_pairs={{0,1},{1,2},{2,3},{3,0},{4,5},{5,6},{6,7},{7,4},{8,9},{9,10},{10,1... | collective-permute-start | bytes 1572872 | tf_op jit(solution)/shard_map/ppermute | solution.py:73
  66.9 36.8 %copy-start.5 = (f32[256,8]{0,1:T(8,128)S(1)}, f32[256,8]{0,1:T(8,128)}, u32[]{:S(2)}) copy-start(f32[256,8]{0,1:T(8,128)} %param.25) | copy-start | bytes 24580
  66.9 36.8 %copy-start.6 = (s32[256,8]{0,1:T(8,128)S(1)}, s32[256,8]{0,1:T(8,128)}, u32[]{:S(2)}) copy-start(s32[256,8]{0,1:T(8,128)} %param.24) | copy-start | bytes 24580
  99.3 7.4 %collective-permute-start.5 = (bf16[256,256]{0,1:T(8,128)(2,1)S(1)}, bf16[256,256]{0,1:T(8,128)(2,1)S(1)}, u32[]{:S(2)}, u32[]{:S(2)}) collective-permute-start(bf16[256,256]{0,1:T(8,128)(2,1)S(1)} %bitcast.63), channel_id=1, source_target_pairs={{0,3},{1,0},{2,1},{3,2},{4,7},{5,4},{6,5},{7,6},{8,11},{9,8},{10,9... | collective-permute-start | bytes 393224 | tf_op jit(solution)/shard_map/ppermute | solution.py:73
  102.6 12.1 %collective-permute-start.4 = (bf16[256,256]{0,1:T(8,128)(2,1)S(1)}, bf16[256,256]{0,1:T(8,128)(2,1)S(1)}, u32[]{:S(2)}, u32[]{:S(2)}) collective-permute-start(bf16[256,256]{0,1:T(8,128)(2,1)S(1)} %bitcast.64), channel_id=1, source_target_pairs={{0,2},{1,3},{2,0},{3,1},{4,6},{5,7},{6,4},{7,5},{8,10},{9,11},{10,... | collective-permute-start | bytes 393224 | tf_op jit(solution)/shard_map/ppermute | solution.py:73
  102.7 12.1 %collective-permute-start.3 = (bf16[256,256]{0,1:T(8,128)(2,1)S(1)}, bf16[256,256]{0,1:T(8,128)(2,1)S(1)}, u32[]{:S(2)}, u32[]{:S(2)}) collective-permute-start(bf16[256,256]{0,1:T(8,128)(2,1)S(1)} %bitcast.65), channel_id=1, source_target_pairs={{0,1},{1,2},{2,3},{3,0},{4,5},{5,6},{6,7},{7,4},{8,9},{9,10},{10,1... | collective-permute-start | bytes 393224 | tf_op jit(solution)/shard_map/ppermute | solution.py:73
  105.8 11.3 %copy-start.7 = (f32[1024]{0:T(1024)S(1)}, f32[1024]{0:T(1024)}, u32[]{:S(2)}) copy-start(f32[1024]{0:T(1024)} %param.23) | copy-start | bytes 12292
  118.1 41.3 %copy-start.11 = (s32[1,2]{1,0:T(1,128)S(1)}, s32[1,2]{1,0:T(1,128)}, u32[]{:S(2)}) copy-start(s32[1,2]{1,0:T(1,128)} %param.18) | copy-start | bytes 28
  118.1 41.3 %copy-start.1 = (bf16[256,2,64]{2,0,1:T(8,128)(2,1)S(1)}, bf16[256,2,64]{2,0,1:T(8,128)(2,1)}, u32[]{:S(2)}) copy-start(bf16[256,2,64]{2,0,1:T(8,128)(2,1)} %copy.76) | copy-start | bytes 196612
  154.9 7.4 %collective-permute-start.11 = (bf16[256,256]{1,0:T(8,128)(2,1)S(1)}, bf16[256,256]{1,0:T(8,128)(2,1)S(1)}, u32[]{:S(2)}, u32[]{:S(2)}) collective-permute-start(bf16[256,256]{1,0:T(8,128)(2,1)S(1)} %get-tuple-element.21), channel_id=1, source_target_pairs={{0,3},{1,0},{2,1},{3,2},{4,7},{5,4},{6,5},{7,6},{8,11},{9,8},{10,9... | collective-permute-start | bytes 393224 | tf_op jit(solution)/shard_map/ppermute | solution.py:310
  158.3 11.9 %collective-permute-start.10 = (bf16[256,256]{1,0:T(8,128)(2,1)S(1)}, bf16[256,256]{1,0:T(8,128)(2,1)S(1)}, u32[]{:S(2)}, u32[]{:S(2)}) collective-permute-start(bf16[256,256]{1,0:T(8,128)(2,1)S(1)} %get-tuple-element.22), channel_id=1, source_target_pairs={{0,2},{1,3},{2,0},{3,1},{4,6},{5,7},{6,4},{7,5},{8,10},{9,11},{10,... | collective-permute-start | bytes 393224 | tf_op jit(solution)/shard_map/ppermute | solution.py:310
  158.3 11.9 %collective-permute-start.9 = (bf16[256,256]{1,0:T(8,128)(2,1)S(1)}, bf16[256,256]{1,0:T(8,128)(2,1)S(1)}, u32[]{:S(2)}, u32[]{:S(2)}) collective-permute-start(bf16[256,256]{1,0:T(8,128)(2,1)S(1)} %get-tuple-element.20), channel_id=1, source_target_pairs={{0,1},{1,2},{2,3},{3,0},{4,5},{5,6},{6,7},{7,4},{8,9},{9,10},{10,1... | collective-permute-start | bytes 393224 | tf_op jit(solution)/shard_map/ppermute | solution.py:310
Sparse Core Ops, SparseCore 0:
  9.9 56.9 all-gather.2
  68.8 72.0 all-gather.4

commit v14 on v13

--- a/solution.py
+++ b/solution.py
@@ -207,7 +207,7 @@
     experts, lanes = packed.shape[1], packed.shape[3]
     units = lanes
     col_blocks = packed.shape[2] // units
-    per_step = 4 if col_blocks % 4 == 0 else 1
+    per_step = col_blocks
     return pl.pallas_call(
         expert_body,
         grid=(col_blocks // per_step,),

time: 178 us -> 179 us (level)
  Pallas kernels: 43.8 us -> 47.2 us
  waiting for transfers between devices: 78 us -> 74.9 us
    pallas_call x1, Pallas kernels: 31.1 us -> 34.2 us  [attend(): pl.pallas_call(attention_body, grid_spec=grid_spec, out_shape=jax.ShapeDt...]
    all_gather x1, waiting for transfers between devices: 22.8 us -> 20.4 us  [shards(): packed = lax.all_gather(packed, 'req', axis=1, tiled=True)]
  transfers between devices with their start and end apart: 14 -> 14, of which waited for: 8 -> 8; matrix products, arithmetic and copies ran while one was open for 10% -> 10% of each run, Pallas kernels for 18% -> 19%
where the time goes in v14:
time: 179 us; the launch traced here: 178 us
  waiting for transfers between devices  74.9 us (42%)
  Pallas kernels  47.2 us (26%)
  starting transfers between devices  19.9 us (11%)
  between operations  14.3 us (8%)
  local copies, waits for them, and re-layouts  10.4 us (6%)
  other arithmetic  8.1 us (5%)
  matrix products  3.26 us (2%)
    pallas_call x1, Pallas kernels, attend(): pl.pallas_call(attention_body, grid_spec=grid_spec, out_shape=jax.ShapeDt...  34.2 us
    all_gather x1, waiting for transfers between devices, shards(): gathered = lax.all_gather(prefix_cache, 'req', axis=0, tiled=True)  27.7 us
    all_gather x1, waiting for transfers between devices, shards(): packed = lax.all_gather(packed, 'req', axis=1, tiled=True)  20.4 us
    ppermute x9, waiting for transfers between devices, shifted_copies(): copies.append(lax.ppermute(block, axis_name, pairs))  17.6 us
    ppermute x9, starting transfers between devices, shifted_copies(): copies.append(lax.ppermute(block, axis_name, pairs))  15.4 us
    pallas_call x1, Pallas kernels, expert_project(): pl.pallas_call(expert_body, grid=(col_blocks // per_step,), in_specs=[pl....  13 us
    ppermute x3, waiting for transfers between devices, shards(): incoming = lax.ppermute(outgoing.astype(jnp.bfloat16), 'hid', pairs)  9.14 us
    unnamed x31, local copies, waits for them, and re-layouts  4.68 us
  transfers between devices with their start and end apart: 14, of which 8 were waited for; matrix products, arithmetic and copies ran while one was open for 10% of the time, Pallas kernels for 19%

profile of v14, /device:TPU:0, one launch (start us, length us, event | category | flops | bytes accessed | tf_op | source)
XLA Modules:
  0.0 178.2 jit_solution(6515357603424772839)
XLA Ops:
  7.2 2.4 %copy.63 = bf16[2,1024,2,128]{3,1,2,0:T(8,128)(2,1)} copy(bf16[2,1024,2,128]{3,2,1,0:T(2,128)(2,1)} %param.17) | data formatting | bytes 2097152 | tf_op args[3]
  9.7 5.1 %collective-permute-start.2 = (bf16[256,256]{1,0:T(8,128)(2,1)S(1)}, bf16[256,256]{1,0:T(8,128)(2,1)S(1)}, u32[]{:S(2)}, u32[]{:S(2)}) collective-permute-start(bf16[256,256]{1,0:T(8,128)(2,1)S(1)} %copy-done.3), channel_id=1, source_target_pairs={{0,3},{1,0},{2,1},{3,2},{4,7},{5,4},{6,5},{7,6},{8,11},{9,8},{10,9... | collective-permute-start | bytes 393224 | tf_op jit(solution)/shard_map/ppermute | solution.py:73
  14.9 1.0 collective-permute-start
  15.9 0.2 convert_reduce_fusion
  16.1 0.5 multiply_cosine_fusion
  16.7 2.1 %collective-permute-done.2 = bf16[256,256]{1,0:T(8,128)(2,1)S(1)} collective-permute-done((bf16[256,256]{1,0:T(8,128)(2,1)S(1)}, bf16[256,256]{1,0:T(8,128)(2,1)S(1)}, u32[]{:S(2)}, u32[]{:S(2)}) %collective-permute-start.2) | collective-permute-done | bytes 131104 | tf_op jit(solution)/shard_map/ppermute | solution.py:73
  18.8 7.3 %collective-permute-done.1 = bf16[256,256]{1,0:T(8,128)(2,1)S(1)} collective-permute-done((bf16[256,256]{1,0:T(8,128)(2,1)S(1)}, bf16[256,256]{1,0:T(8,128)(2,1)S(1)}, u32[]{:S(2)}, u32[]{:S(2)}) %collective-permute-start.1) | collective-permute-done | bytes 131104 | tf_op jit(solution)/shard_map/ppermute | solution.py:73
  26.2 0.6 gather_fusion
  26.9 0.2 fusion.16
  27.1 0.5 fusion.28
  27.6 0.2 copy.73
  27.8 0.2 copy.72
  28.0 0.1 subtract_convert_fusion
  28.2 0.9 pad_maximum_fusion.2
  29.2 1.3 maximum_bitcast_fusion
  30.6 1.6 collective-permute-start.8
  32.1 1.2 collective-permute-start.7
  33.3 1.9 %collective-permute-start.6 = (bf16[256,1024]{1,0:T(8,128)(2,1)}, bf16[256,1024]{1,0:T(8,128)(2,1)}, u32[]{:S(2)}, u32[]{:S(2)}) collective-permute-start(bf16[256,1024]{1,0:T(8,128)(2,1)} %param.22), channel_id=1, source_target_pairs={{0,1},{1,2},{2,3},{3,0},{4,5},{5,6},{6,7},{7,4},{8,9},{9,10},{10,1... | collective-permute-start | bytes 1572872 | tf_op jit(solution)/shard_map/ppermute | solution.py:73
  35.3 0.8 copy.64.segq_ref
  36.0 0.2 convert_reduce_fusion.2
  36.2 0.6 pad_add_fusion.bound_ref
  36.8 0.4 fusion.26
  37.3 0.1 copy.75
  37.4 0.1 copy.74
  37.7 0.8 copy.76
  38.4 0.8 maximum_bitcast_fusion.1.k_ref
  39.2 27.7 %all-gather.3.cloned.1.call-done = bf16[16,1024,2,128]{3,1,2,0:T(8,128)(2,1)} async-done(((bf16[2,1024,2,128]{3,1,2,0:T(8,128)(2,1)}), bf16[16,1024,2,128]{3,1,2,0:T(8,128)(2,1)}) %all-gather.3.cloned.1.call-update) | async-done | bytes 8388624 | tf_op jit(solution)/shard_map/all_gather | solution.py:270
  66.9 34.2 %shard_map.149 = f32[2,2,256,64]{3,2,1,0:T(8,128)} custom-call(s32[8]{0:T(128)} %bitcast.75, s32[16]{0:T(128)} %pad_add_fusion.bound_ref, bf16[2,2,256,64]{3,2,1,0:T(8,128)(2,1)} %bitcast.58, bf16[2,256,64]{2,1,0:T(8,128)(2,1)} %maximum_bitcast_fusion.1.k_ref, bf16[2,256,64]{2,1,0:T(8,128)(2,1)} %bitcast.57, s32[256,1]{1,0:T(8,128)} %copy.64.segq_ref, ...), custom_call_target="tpu_custom_call" | custom-call | tf_op jit(solution)/shard_map/pallas_call | solution.py:169
  101.1 1.1 convert_bitcast_fusion
  102.2 0.1 copy.65
  102.3 3.4 %collective-permute-start.5 = (bf16[256,256]{0,1:T(8,128)(2,1)S(1)}, bf16[256,256]{0,1:T(8,128)(2,1)S(1)}, u32[]{:S(2)}, u32[]{:S(2)}) collective-permute-start(bf16[256,256]{0,1:T(8,128)(2,1)S(1)} %bitcast.63), channel_id=1, source_target_pairs={{0,3},{1,0},{2,1},{3,2},{4,7},{5,4},{6,5},{7,6},{8,11},{9,8},{10,9... | collective-permute-start | bytes 393224 | tf_op jit(solution)/shard_map/ppermute | solution.py:73
  105.7 1.1 collective-permute-start.3
  106.9 2.0 %copy.68.combine_ref = f32[16,256,1]{2,1,0:T(8,128)} copy(f32[16,256,1]{1,0,2:T(8,128)S(1)} %bitcast.71) | data formatting | bytes 32768 | tf_op jit(solution)/shard_map/broadcast_in_dim | solution.py:299
  108.9 0.7 collective-permute-done.5
  109.6 7.5 %collective-permute-done.4 = bf16[256,256]{0,1:T(8,128)(2,1)S(1)} collective-permute-done((bf16[256,256]{0,1:T(8,128)(2,1)S(1)}, bf16[256,256]{0,1:T(8,128)(2,1)S(1)}, u32[]{:S(2)}, u32[]{:S(2)}) %collective-permute-start.4) | collective-permute-done | bytes 131104 | tf_op jit(solution)/shard_map/ppermute | solution.py:73
  117.1 2.4 %fusion.13 = (f32[256]{0:T(256)S(1)}, bf16[256,1024]{1,0:T(8,128)(2,1)S(1)}) fusion(bf16[256,1024]{1,0:T(8,128)(2,1)} %collective-permute-done.8, bf16[256,1024]{1,0:T(8,128)(2,1)} %collective-permute-done.7, bf16[256,1024]{1,0:T(8,128)(2,1)} %collective-permute-done.6, bf16[256,1024]{1,0:T(8,128)(2,1)} %param.22, ...), kind=kOutput, calls=%fused_computation.17 | convolution fusion | flops 550764288 | bytes 3671040 | tf_op jit(solution)/shard_map/dot_general | solution.py:278
  119.5 1.0 fusion.15.normed_ref
  120.5 20.4 %all-gather.5.cloned.1.call-done.weight_ref.down_ref = bf16[3,16,1024,128]{3,2,1,0:T(8,128)(2,1)} async-done(((bf16[3,2,1024,128]{3,2,1,0:T(8,128)(2,1)}), bf16[3,16,1024,128]{3,2,1,0:T(8,128)(2,1)}) %all-gather.5.cloned.1.call-update) | async-done | bytes 12582928 | tf_op jit(solution)/shard_map/all_gather | solution.py:292
  140.8 13.0 %shard_map.150 = f32[8,256,128]{2,1,0:T(8,128)} custom-call(bf16[256,1024]{1,0:T(8,128)(2,1)} %fusion.15.normed_ref, f32[16,256,1]{2,1,0:T(8,128)} %copy.68.combine_ref, bf16[3,16,1024,128]{3,2,1,0:T(8,128)(2,1)} %all-gather.5.cloned.1.call-done.weight_ref.down_ref, bf16[3,16,1024,128]{3,2,1,0:T(8,128)(2,1)} %all-gather.5.cloned.1.call-done.weight_ref.down_ref), custom_call_target="tpu_custom_call" | custom-call | tf_op jit(solution)/shard_map/pallas_call | solution.py:211
  153.9 1.3 copy_bitcast_fusion
  155.3 3.4 %collective-permute-start.11 = (bf16[256,256]{1,0:T(8,128)(2,1)S(1)}, bf16[256,256]{1,0:T(8,128)(2,1)S(1)}, u32[]{:S(2)}, u32[]{:S(2)}) collective-permute-start(bf16[256,256]{1,0:T(8,128)(2,1)S(1)} %get-tuple-element.21), channel_id=1, source_target_pairs={{0,3},{1,0},{2,1},{3,2},{4,7},{5,4},{6,5},{7,6},{8,11},{9,8},{10,9... | collective-permute-start | bytes 393224 | tf_op jit(solution)/shard_map/ppermute | solution.py:310
  158.7 1.1 collective-permute-start.9
  159.8 0.1 pad_maximum_fusion.3
  160.0 0.6 scatter_fusion
  160.6 0.8 copy.71
  161.4 1.2 collective-permute-done.11
  162.7 7.9 %collective-permute-done.10 = bf16[256,256]{1,0:T(8,128)(2,1)S(1)} collective-permute-done((bf16[256,256]{1,0:T(8,128)(2,1)S(1)}, bf16[256,256]{1,0:T(8,128)(2,1)S(1)}, u32[]{:S(2)}, u32[]{:S(2)}) %collective-permute-start.10) | collective-permute-done | bytes 131104 | tf_op jit(solution)/shard_map/ppermute | solution.py:310
  170.6 0.7 add_convert_fusion.1
  (57 shorter events, 0.8 us)
Async XLA Ops:
  7.2 21.9 %copy-start = (bf16[2,128,1024]{2,1,0:T(8,128)(2,1)S(1)}, bf16[2,128,1024]{2,1,0:T(8,128)(2,1)}, u32[]{:S(2)}) copy-start(bf16[2,128,1024]{2,1,0:T(8,128)(2,1)} %param.27) | copy-start | bytes 1572868
  7.2 2.6 %copy-start.3 = (bf16[256,256]{1,0:T(8,128)(2,1)S(1)}, bf16[256,256]{1,0:T(8,128)(2,1)}, u32[]{:S(2)}) copy-start(bf16[256,256]{1,0:T(8,128)(2,1)} %param.14) | copy-start | bytes 393220
  7.2 8.7 %copy-start.4 = (s32[1,256]{1,0:T(1,128)S(1)}, s32[1,256]{1,0:T(1,128)}, u32[]{:S(2)}) copy-start(s32[1,256]{1,0:T(1,128)} %segk_ref.1) | copy-start | bytes 3076
  7.2 59.7 %all-gather.3.cloned.1.call-start = ((), (), s32[]{:S(2)}) async-start(), calls=%async_computation | async-start | bytes 9437184 | tf_op jit(solution)/shard_map/all_gather | solution.py:270
  9.7 17.5 %copy-start.8 = (bf16[1024,256]{1,0:T(8,128)(2,1)S(1)}, bf16[1024,256]{1,0:T(8,128)(2,1)}, u32[]{:S(2)}) copy-start(bf16[1024,256]{1,0:T(8,128)(2,1)} %param.20) | copy-start | bytes 1572868
  9.7 17.5 %copy-start.10 = (f32[1024]{0:T(1024)S(1)}, f32[1024]{0:T(1024)}, u32[]{:S(2)}) copy-start(f32[1024]{0:T(1024)} %param.19) | copy-start | bytes 12292
  9.7 131.2 %all-gather.5.cloned.1.call-start = ((), (), s32[]{:S(2)}) async-start(), calls=%async_computation.1 | async-start | bytes 14155776 | tf_op jit(solution)/shard_map/all_gather | solution.py:292
  9.7 9.0 %collective-permute-start.2 = (bf16[256,256]{1,0:T(8,128)(2,1)S(1)}, bf16[256,256]{1,0:T(8,128)(2,1)S(1)}, u32[]{:S(2)}, u32[]{:S(2)}) collective-permute-start(bf16[256,256]{1,0:T(8,128)(2,1)S(1)} %copy-done.3), channel_id=1, source_target_pairs={{0,3},{1,0},{2,1},{3,2},{4,7},{5,4},{6,5},{7,6},{8,11},{9,8},{10,9... | collective-permute-start | bytes 393224 | tf_op jit(solution)/shard_map/ppermute | solution.py:73
  14.9 11.2 %collective-permute-start.1 = (bf16[256,256]{1,0:T(8,128)(2,1)S(1)}, bf16[256,256]{1,0:T(8,128)(2,1)S(1)}, u32[]{:S(2)}, u32[]{:S(2)}) collective-permute-start(bf16[256,256]{1,0:T(8,128)(2,1)S(1)} %copy-done.3), channel_id=1, source_target_pairs={{0,2},{1,3},{2,0},{3,1},{4,6},{5,7},{6,4},{7,5},{8,10},{9,11},{10,... | collective-permute-start | bytes 393224 | tf_op jit(solution)/shard_map/ppermute | solution.py:73
  14.9 11.2 %collective-permute-start = (bf16[256,256]{1,0:T(8,128)(2,1)S(1)}, bf16[256,256]{1,0:T(8,128)(2,1)S(1)}, u32[]{:S(2)}, u32[]{:S(2)}) collective-permute-start(bf16[256,256]{1,0:T(8,128)(2,1)S(1)} %copy-done.3), channel_id=1, source_target_pairs={{0,1},{1,2},{2,3},{3,0},{4,5},{5,6},{6,7},{7,4},{8,9},{9,10},{10,1... | collective-permute-start | bytes 393224 | tf_op jit(solution)/shard_map/ppermute | solution.py:73
  27.6 1.6 copy-start.2
  29.1 7.8 %copy-start.9 = (bf16[1024,256]{1,0:T(8,128)(2,1)S(1)}, bf16[1024,256]{1,0:T(8,128)(2,1)}, u32[]{:S(2)}) copy-start(bf16[1024,256]{1,0:T(8,128)(2,1)} %param.21) | copy-start | bytes 1572868
  30.6 75.2 %collective-permute-start.8 = (bf16[256,1024]{1,0:T(8,128)(2,1)}, bf16[256,1024]{1,0:T(8,128)(2,1)}, u32[]{:S(2)}, u32[]{:S(2)}) collective-permute-start(bf16[256,1024]{1,0:T(8,128)(2,1)} %param.22), channel_id=1, source_target_pairs={{0,3},{1,0},{2,1},{3,2},{4,7},{5,4},{6,5},{7,6},{8,11},{9,8},{10,9... | collective-permute-start | bytes 1572872 | tf_op jit(solution)/shard_map/ppermute | solution.py:73
  32.1 76.7 %collective-permute-start.7 = (bf16[256,1024]{1,0:T(8,128)(2,1)}, bf16[256,1024]{1,0:T(8,128)(2,1)}, u32[]{:S(2)}, u32[]{:S(2)}) collective-permute-start(bf16[256,1024]{1,0:T(8,128)(2,1)} %param.22), channel_id=1, source_target_pairs={{0,2},{1,3},{2,0},{3,1},{4,6},{5,7},{6,4},{7,5},{8,10},{9,11},{10,... | collective-permute-start | bytes 1572872 | tf_op jit(solution)/shard_map/ppermute | solution.py:73
  33.3 75.6 %collective-permute-start.6 = (bf16[256,1024]{1,0:T(8,128)(2,1)}, bf16[256,1024]{1,0:T(8,128)(2,1)}, u32[]{:S(2)}, u32[]{:S(2)}) collective-permute-start(bf16[256,1024]{1,0:T(8,128)(2,1)} %param.22), channel_id=1, source_target_pairs={{0,1},{1,2},{2,3},{3,0},{4,5},{5,6},{6,7},{7,4},{8,9},{9,10},{10,1... | collective-permute-start | bytes 1572872 | tf_op jit(solution)/shard_map/ppermute | solution.py:73
  66.9 39.9 %copy-start.5 = (f32[256,8]{0,1:T(8,128)S(1)}, f32[256,8]{0,1:T(8,128)}, u32[]{:S(2)}) copy-start(f32[256,8]{0,1:T(8,128)} %param.25) | copy-start | bytes 24580
  66.9 39.9 %copy-start.6 = (s32[256,8]{0,1:T(8,128)S(1)}, s32[256,8]{0,1:T(8,128)}, u32[]{:S(2)}) copy-start(s32[256,8]{0,1:T(8,128)} %param.24) | copy-start | bytes 24580
  102.3 7.3 %collective-permute-start.5 = (bf16[256,256]{0,1:T(8,128)(2,1)S(1)}, bf16[256,256]{0,1:T(8,128)(2,1)S(1)}, u32[]{:S(2)}, u32[]{:S(2)}) collective-permute-start(bf16[256,256]{0,1:T(8,128)(2,1)S(1)} %bitcast.63), channel_id=1, source_target_pairs={{0,3},{1,0},{2,1},{3,2},{4,7},{5,4},{6,5},{7,6},{8,11},{9,8},{10,9... | collective-permute-start | bytes 393224 | tf_op jit(solution)/shard_map/ppermute | solution.py:73
  105.7 11.3 %collective-permute-start.4 = (bf16[256,256]{0,1:T(8,128)(2,1)S(1)}, bf16[256,256]{0,1:T(8,128)(2,1)S(1)}, u32[]{:S(2)}, u32[]{:S(2)}) collective-permute-start(bf16[256,256]{0,1:T(8,128)(2,1)S(1)} %bitcast.64), channel_id=1, source_target_pairs={{0,2},{1,3},{2,0},{3,1},{4,6},{5,7},{6,4},{7,5},{8,10},{9,11},{10,... | collective-permute-start | bytes 393224 | tf_op jit(solution)/shard_map/ppermute | solution.py:73
  105.7 11.3 %collective-permute-start.3 = (bf16[256,256]{0,1:T(8,128)(2,1)S(1)}, bf16[256,256]{0,1:T(8,128)(2,1)S(1)}, u32[]{:S(2)}, u32[]{:S(2)}) collective-permute-start(bf16[256,256]{0,1:T(8,128)(2,1)S(1)} %bitcast.65), channel_id=1, source_target_pairs={{0,1},{1,2},{2,3},{3,0},{4,5},{5,6},{6,7},{7,4},{8,9},{9,10},{10,1... | collective-permute-start | bytes 393224 | tf_op jit(solution)/shard_map/ppermute | solution.py:73
  108.9 10.6 %copy-start.7 = (f32[1024]{0:T(1024)S(1)}, f32[1024]{0:T(1024)}, u32[]{:S(2)}) copy-start(f32[1024]{0:T(1024)} %param.23) | copy-start | bytes 12292
  120.5 39.3 %copy-start.11 = (s32[1,2]{1,0:T(1,128)S(1)}, s32[1,2]{1,0:T(1,128)}, u32[]{:S(2)}) copy-start(s32[1,2]{1,0:T(1,128)} %param.18) | copy-start | bytes 28
  120.5 39.3 %copy-start.1 = (bf16[256,2,64]{2,0,1:T(8,128)(2,1)S(1)}, bf16[256,2,64]{2,0,1:T(8,128)(2,1)}, u32[]{:S(2)}) copy-start(bf16[256,2,64]{2,0,1:T(8,128)(2,1)} %copy.76) | copy-start | bytes 196612
  155.3 7.4 %collective-permute-start.11 = (bf16[256,256]{1,0:T(8,128)(2,1)S(1)}, bf16[256,256]{1,0:T(8,128)(2,1)S(1)}, u32[]{:S(2)}, u32[]{:S(2)}) collective-permute-start(bf16[256,256]{1,0:T(8,128)(2,1)S(1)} %get-tuple-element.21), channel_id=1, source_target_pairs={{0,3},{1,0},{2,1},{3,2},{4,7},{5,4},{6,5},{7,6},{8,11},{9,8},{10,9... | collective-permute-start | bytes 393224 | tf_op jit(solution)/shard_map/ppermute | solution.py:310
  158.7 11.9 %collective-permute-start.10 = (bf16[256,256]{1,0:T(8,128)(2,1)S(1)}, bf16[256,256]{1,0:T(8,128)(2,1)S(1)}, u32[]{:S(2)}, u32[]{:S(2)}) collective-permute-start(bf16[256,256]{1,0:T(8,128)(2,1)S(1)} %get-tuple-element.22), channel_id=1, source_target_pairs={{0,2},{1,3},{2,0},{3,1},{4,6},{5,7},{6,4},{7,5},{8,10},{9,11},{10,... | collective-permute-start | bytes 393224 | tf_op jit(solution)/shard_map/ppermute | solution.py:310
  158.7 11.9 %collective-permute-start.9 = (bf16[256,256]{1,0:T(8,128)(2,1)S(1)}, bf16[256,256]{1,0:T(8,128)(2,1)S(1)}, u32[]{:S(2)}, u32[]{:S(2)}) collective-permute-start(bf16[256,256]{1,0:T(8,128)(2,1)S(1)} %get-tuple-element.20), channel_id=1, source_target_pairs={{0,1},{1,2},{2,3},{3,0},{4,5},{5,6},{6,7},{7,4},{8,9},{9,10},{10,1... | collective-permute-start | bytes 393224 | tf_op jit(solution)/shard_map/ppermute | solution.py:310
Sparse Core Ops, SparseCore 0:
  9.9 56.9 all-gather.2
  68.8 71.9 all-gather.4

commit v15 on v14

--- a/solution.py
+++ b/solution.py
@@ -191,15 +191,16 @@
             hidden_ref[expert] = (activated * up_proj * combine_ref[expert]).astype(jnp.bfloat16)
 
     units = hidden_ref.shape[2]
-    for col in range(out_ref.shape[0]):
-        total = jnp.zeros(out_ref.shape[1:], jnp.float32)
+    per_block = down_ref.shape[2] // units
+    for col in range(per_block):
+        total = jnp.zeros((out_ref.shape[0], out_ref.shape[1] // per_block), jnp.float32)
         for expert in range(experts):
             total = total + jnp.dot(
                 hidden_ref[expert],
                 down_ref[0, expert, col * units : (col + 1) * units, :],
                 preferred_element_type=jnp.float32,
             )
-        out_ref[col] = total
+        out_ref[:, col * out_ref.shape[1] // per_block : (col + 1) * out_ref.shape[1] // per_block] = total
 
 
 def expert_project(normed_moe, combine, packed):
@@ -207,7 +208,7 @@
     experts, lanes = packed.shape[1], packed.shape[3]
     units = lanes
     col_blocks = packed.shape[2] // units
-    per_step = col_blocks
+    per_step = 4 if col_blocks % 4 == 0 and (4 * lanes) % 128 == 0 else col_blocks
     return pl.pallas_call(
         expert_body,
         grid=(col_blocks // per_step,),
@@ -217,8 +218,8 @@
             pl.BlockSpec((2, experts, model_width, lanes), lambda c: (0, 0, 0, 0)),
             pl.BlockSpec((1, experts, per_step * units, lanes), lambda c: (2, 0, c, 0)),
         ],
-        out_specs=pl.BlockSpec((per_step, tok_count, lanes), lambda c: (c, 0, 0)),
-        out_shape=jax.ShapeDtypeStruct((col_blocks, tok_count, lanes), jnp.float32),
+        out_specs=pl.BlockSpec((tok_count, per_step * lanes), lambda c: (0, c)),
+        out_shape=jax.ShapeDtypeStruct((tok_count, col_blocks * lanes), jnp.float32),
         scratch_shapes=[pltpu.VMEM((experts, tok_count, units), jnp.bfloat16)],
         compiler_params=pltpu.CompilerParams(dimension_semantics=("arbitrary",)),
     )(normed_moe, combine, packed, packed)
@@ -295,11 +296,7 @@
     combine = jnp.sum(
         jnp.where(routes[:, :, None] == expert_ids[None, None, :], gates[:, :, None], 0.0), axis=1
     )
-    partial_out = (
-        expert_project(normed_moe, combine.T[:, :, None], packed)
-        .transpose(1, 0, 2)
-        .reshape(tok_count, model_width)
-    )
+    partial_out = expert_project(normed_moe, combine.T[:, :, None], packed)
     hid_count = lax.axis_size("hid")
     hid_index = lax.axis_index("hid")
     expert_sum = lax.dynamic_slice_in_dim(partial_out, hid_index * share_width, share_width, 1)

time: 179 us -> 179 us (level)
  transfers between devices with their start and end apart: 14 -> 14, of which waited for: 8 -> 8; matrix products, arithmetic and copies ran while one was open for 10% -> 9% of each run, Pallas kernels for 19% -> 19%
where the time goes in v15:
time: 179 us
  waiting for transfers between devices  75.4 us (42%)
  Pallas kernels  46.7 us (26%)
  starting transfers between devices  19.9 us (11%)
  between operations  14.3 us (8%)
  local copies, waits for them, and re-layouts  10.2 us (6%)
  other arithmetic  9.03 us (5%)
  matrix products  3.02 us (2%)
    pallas_call x1, Pallas kernels, attend(): pl.pallas_call(attention_body, grid_spec=grid_spec, out_shape=jax.ShapeDt...  34 us
    all_gather x1, waiting for transfers between devices, shards(): gathered = lax.all_gather(prefix_cache, 'req', axis=0, tiled=True)  27.7 us
    all_gather x1, waiting for transfers between devices, shards(): packed = lax.all_gather(packed, 'req', axis=1, tiled=True)  20.3 us
    ppermute x9, waiting for transfers between devices, shifted_copies(): copies.append(lax.ppermute(block, axis_name, pairs))  18.1 us
    ppermute x9, starting transfers between devices, shifted_copies(): copies.append(lax.ppermute(block, axis_name, pairs))  15.3 us
    pallas_call x1, Pallas kernels, expert_project(): pl.pallas_call(expert_body, grid=(col_blocks // per_step,), in_specs=[pl....  12.7 us
    ppermute x3, waiting for transfers between devices, shards(): incoming = lax.ppermute(outgoing.astype(jnp.bfloat16), 'hid', pairs)  9.14 us
    unnamed x31, local copies, waits for them, and re-layouts  4.68 us
  transfers between devices with their start and end apart: 14, of which 8 were waited for; matrix products, arithmetic and copies ran while one was open for 9% of the time, Pallas kernels for 19%

profile of v15, /device:TPU:0, one launch (start us, length us, event | category | flops | bytes accessed | tf_op | source)
XLA Modules:
  0.0 178.5 jit_solution(3912145578365289096)
XLA Ops:
  7.2 2.4 %copy.60 = bf16[2,1024,2,128]{3,1,2,0:T(8,128)(2,1)} copy(bf16[2,1024,2,128]{3,2,1,0:T(2,128)(2,1)} %param.17) | data formatting | bytes 2097152 | tf_op args[3]
  9.7 5.1 %collective-permute-start.2 = (bf16[256,256]{1,0:T(8,128)(2,1)S(1)}, bf16[256,256]{1,0:T(8,128)(2,1)S(1)}, u32[]{:S(2)}, u32[]{:S(2)}) collective-permute-start(bf16[256,256]{1,0:T(8,128)(2,1)S(1)} %copy-done.3), channel_id=1, source_target_pairs={{0,3},{1,0},{2,1},{3,2},{4,7},{5,4},{6,5},{7,6},{8,11},{9,8},{10,9... | collective-permute-start | bytes 393224 | tf_op jit(solution)/shard_map/ppermute | solution.py:73
  14.9 1.0 collective-permute-start
  15.9 0.2 convert_reduce_fusion
  16.1 0.5 multiply_cosine_fusion
  16.7 2.1 %collective-permute-done.2 = bf16[256,256]{1,0:T(8,128)(2,1)S(1)} collective-permute-done((bf16[256,256]{1,0:T(8,128)(2,1)S(1)}, bf16[256,256]{1,0:T(8,128)(2,1)S(1)}, u32[]{:S(2)}, u32[]{:S(2)}) %collective-permute-start.2) | collective-permute-done | bytes 131104 | tf_op jit(solution)/shard_map/ppermute | solution.py:73
  18.8 7.3 %collective-permute-done.1 = bf16[256,256]{1,0:T(8,128)(2,1)S(1)} collective-permute-done((bf16[256,256]{1,0:T(8,128)(2,1)S(1)}, bf16[256,256]{1,0:T(8,128)(2,1)S(1)}, u32[]{:S(2)}, u32[]{:S(2)}) %collective-permute-start.1) | collective-permute-done | bytes 131104 | tf_op jit(solution)/shard_map/ppermute | solution.py:73
  26.2 0.6 gather_fusion
  26.9 0.2 fusion.16
  27.1 0.5 fusion.28
  27.6 0.2 copy.69
  27.8 0.2 copy.68
  28.0 0.1 subtract_convert_fusion
  28.2 0.8 pad_maximum_fusion.2
  29.2 1.3 maximum_bitcast_fusion
  30.5 1.6 collective-permute-start.8
  32.1 1.2 collective-permute-start.7
  33.3 1.9 %collective-permute-start.6 = (bf16[256,1024]{1,0:T(8,128)(2,1)}, bf16[256,1024]{1,0:T(8,128)(2,1)}, u32[]{:S(2)}, u32[]{:S(2)}) collective-permute-start(bf16[256,1024]{1,0:T(8,128)(2,1)} %param.22), channel_id=1, source_target_pairs={{0,1},{1,2},{2,3},{3,0},{4,5},{5,6},{6,7},{7,4},{8,9},{9,10},{10,1... | collective-permute-start | bytes 1572872 | tf_op jit(solution)/shard_map/ppermute | solution.py:73
  35.2 0.8 copy.61.segq_ref
  36.0 0.2 convert_reduce_fusion.2
  36.2 0.6 pad_add_fusion.bound_ref
  36.8 0.4 fusion.26
  37.3 0.1 copy.71
  37.4 0.1 copy.70
  37.6 0.8 copy.72
  38.4 0.8 maximum_bitcast_fusion.1.k_ref
  39.2 27.7 %all-gather.3.cloned.1.call-done = bf16[16,1024,2,128]{3,1,2,0:T(8,128)(2,1)} async-done(((bf16[2,1024,2,128]{3,1,2,0:T(8,128)(2,1)}), bf16[16,1024,2,128]{3,1,2,0:T(8,128)(2,1)}) %all-gather.3.cloned.1.call-update) | async-done | bytes 8388624 | tf_op jit(solution)/shard_map/all_gather | solution.py:271
  66.9 34.0 %shard_map.149 = f32[2,2,256,64]{3,2,1,0:T(8,128)} custom-call(s32[8]{0:T(128)} %bitcast.69, s32[16]{0:T(128)} %pad_add_fusion.bound_ref, bf16[2,2,256,64]{3,2,1,0:T(8,128)(2,1)} %bitcast.52, bf16[2,256,64]{2,1,0:T(8,128)(2,1)} %maximum_bitcast_fusion.1.k_ref, bf16[2,256,64]{2,1,0:T(8,128)(2,1)} %bitcast.51, s32[256,1]{1,0:T(8,128)} %copy.61.segq_ref, ...), custom_call_target="tpu_custom_call" | custom-call | tf_op jit(solution)/shard_map/pallas_call | solution.py:169
  100.9 1.1 convert_bitcast_fusion
  102.0 0.1 copy.62
  102.1 3.4 %collective-permute-start.5 = (bf16[256,256]{0,1:T(8,128)(2,1)S(1)}, bf16[256,256]{0,1:T(8,128)(2,1)S(1)}, u32[]{:S(2)}, u32[]{:S(2)}) collective-permute-start(bf16[256,256]{0,1:T(8,128)(2,1)S(1)} %bitcast.57), channel_id=1, source_target_pairs={{0,3},{1,0},{2,1},{3,2},{4,7},{5,4},{6,5},{7,6},{8,11},{9,8},{10,9... | collective-permute-start | bytes 393224 | tf_op jit(solution)/shard_map/ppermute | solution.py:73
  105.5 1.1 collective-permute-start.3
  106.6 2.0 %copy.65.combine_ref = f32[16,256,1]{2,1,0:T(8,128)} copy(f32[16,256,1]{1,0,2:T(8,128)S(1)} %bitcast.65) | data formatting | bytes 32768 | tf_op jit(solution)/shard_map/broadcast_in_dim | solution.py:299
  108.6 0.8 collective-permute-done.5
  109.5 7.9 %collective-permute-done.4 = bf16[256,256]{0,1:T(8,128)(2,1)S(1)} collective-permute-done((bf16[256,256]{0,1:T(8,128)(2,1)S(1)}, bf16[256,256]{0,1:T(8,128)(2,1)S(1)}, u32[]{:S(2)}, u32[]{:S(2)}) %collective-permute-start.4) | collective-permute-done | bytes 131104 | tf_op jit(solution)/shard_map/ppermute | solution.py:73
  117.4 2.1 %fusion.13 = (f32[256]{0:T(256)S(1)}, bf16[256,1024]{1,0:T(8,128)(2,1)S(1)}) fusion(bf16[256,1024]{1,0:T(8,128)(2,1)S(1)} %collective-permute-done.8, bf16[256,1024]{1,0:T(8,128)(2,1)S(1)} %collective-permute-done.7, bf16[256,1024]{1,0:T(8,128)(2,1)} %collective-permute-done.6, bf16[256,1024]{1,0:T(8,128)(2,1)} %param.22, ...), kind=kOutput, calls=%fused_computation.17 | convolution fusion | flops 550764288 | bytes 3671040 | tf_op jit(solution)/shard_map/dot_general | solution.py:279
  119.5 1.0 fusion.15.normed_ref
  120.5 20.3 %all-gather.5.cloned.1.call-done.weight_ref.down_ref = bf16[3,16,1024,128]{3,2,1,0:T(8,128)(2,1)} async-done(((bf16[3,2,1024,128]{3,2,1,0:T(8,128)(2,1)}), bf16[3,16,1024,128]{3,2,1,0:T(8,128)(2,1)}) %all-gather.5.cloned.1.call-update) | async-done | bytes 12582928 | tf_op jit(solution)/shard_map/all_gather | solution.py:293
  140.9 12.7 %shard_map.150 = f32[256,1024]{1,0:T(8,128)} custom-call(bf16[256,1024]{1,0:T(8,128)(2,1)} %fusion.15.normed_ref, f32[16,256,1]{2,1,0:T(8,128)} %copy.65.combine_ref, bf16[3,16,1024,128]{3,2,1,0:T(8,128)(2,1)} %all-gather.5.cloned.1.call-done.weight_ref.down_ref, bf16[3,16,1024,128]{3,2,1,0:T(8,128)(2,1)} %all-gather.5.cloned.1.call-done.weight_ref.down_ref), custom_call_target="tpu_custom_call" | custom-call | tf_op jit(solution)/shard_map/pallas_call | solution.py:212
  153.6 1.2 dynamic-slice_convert_fusion.2
  154.7 3.4 %collective-permute-start.11 = (bf16[256,256]{1,0:T(8,128)(2,1)S(1)}, bf16[256,256]{1,0:T(8,128)(2,1)S(1)}, u32[]{:S(2)}, u32[]{:S(2)}) collective-permute-start(bf16[256,256]{1,0:T(8,128)(2,1)S(1)} %get-tuple-element.21), channel_id=1, source_target_pairs={{0,3},{1,0},{2,1},{3,2},{4,7},{5,4},{6,5},{7,6},{8,11},{9,8},{10,9... | collective-permute-start | bytes 393224 | tf_op jit(solution)/shard_map/ppermute | solution.py:307
  158.1 1.1 collective-permute-start.9
  159.2 0.1 pad_maximum_fusion.3
  159.4 0.6 scatter_fusion
  160.0 0.8 copy.67
  160.8 1.2 collective-permute-done.11
  162.1 7.9 %collective-permute-done.10 = bf16[256,256]{1,0:T(8,128)(2,1)S(1)} collective-permute-done((bf16[256,256]{1,0:T(8,128)(2,1)S(1)}, bf16[256,256]{1,0:T(8,128)(2,1)S(1)}, u32[]{:S(2)}, u32[]{:S(2)}) %collective-permute-start.10) | collective-permute-done | bytes 131104 | tf_op jit(solution)/shard_map/ppermute | solution.py:307
  170.0 1.7 add_convert_fusion.1
  (56 shorter events, 0.8 us)
Async XLA Ops:
  7.2 21.9 %copy-start = (bf16[2,128,1024]{2,1,0:T(8,128)(2,1)S(1)}, bf16[2,128,1024]{2,1,0:T(8,128)(2,1)}, u32[]{:S(2)}) copy-start(bf16[2,128,1024]{2,1,0:T(8,128)(2,1)} %param.27) | copy-start | bytes 1572868
  7.2 2.6 %copy-start.3 = (bf16[256,256]{1,0:T(8,128)(2,1)S(1)}, bf16[256,256]{1,0:T(8,128)(2,1)}, u32[]{:S(2)}) copy-start(bf16[256,256]{1,0:T(8,128)(2,1)} %param.14) | copy-start | bytes 393220
  7.2 8.7 %copy-start.4 = (s32[1,256]{1,0:T(1,128)S(1)}, s32[1,256]{1,0:T(1,128)}, u32[]{:S(2)}) copy-start(s32[1,256]{1,0:T(1,128)} %segk_ref.1) | copy-start | bytes 3076
  7.2 59.7 %all-gather.3.cloned.1.call-start = ((), (), s32[]{:S(2)}) async-start(), calls=%async_computation | async-start | bytes 9437184 | tf_op jit(solution)/shard_map/all_gather | solution.py:271
  9.7 17.5 %copy-start.8 = (bf16[1024,256]{1,0:T(8,128)(2,1)S(1)}, bf16[1024,256]{1,0:T(8,128)(2,1)}, u32[]{:S(2)}) copy-start(bf16[1024,256]{1,0:T(8,128)(2,1)} %param.20) | copy-start | bytes 1572868
  9.7 17.5 %copy-start.10 = (f32[1024]{0:T(1024)S(1)}, f32[1024]{0:T(1024)}, u32[]{:S(2)}) copy-start(f32[1024]{0:T(1024)} %param.19) | copy-start | bytes 12292
  9.7 131.2 %all-gather.5.cloned.1.call-start = ((), (), s32[]{:S(2)}) async-start(), calls=%async_computation.1 | async-start | bytes 14155776 | tf_op jit(solution)/shard_map/all_gather | solution.py:293
  9.7 9.0 %collective-permute-start.2 = (bf16[256,256]{1,0:T(8,128)(2,1)S(1)}, bf16[256,256]{1,0:T(8,128)(2,1)S(1)}, u32[]{:S(2)}, u32[]{:S(2)}) collective-permute-start(bf16[256,256]{1,0:T(8,128)(2,1)S(1)} %copy-done.3), channel_id=1, source_target_pairs={{0,3},{1,0},{2,1},{3,2},{4,7},{5,4},{6,5},{7,6},{8,11},{9,8},{10,9... | collective-permute-start | bytes 393224 | tf_op jit(solution)/shard_map/ppermute | solution.py:73
  14.9 11.2 %collective-permute-start.1 = (bf16[256,256]{1,0:T(8,128)(2,1)S(1)}, bf16[256,256]{1,0:T(8,128)(2,1)S(1)}, u32[]{:S(2)}, u32[]{:S(2)}) collective-permute-start(bf16[256,256]{1,0:T(8,128)(2,1)S(1)} %copy-done.3), channel_id=1, source_target_pairs={{0,2},{1,3},{2,0},{3,1},{4,6},{5,7},{6,4},{7,5},{8,10},{9,11},{10,... | collective-permute-start | bytes 393224 | tf_op jit(solution)/shard_map/ppermute | solution.py:73
  14.9 11.2 %collective-permute-start = (bf16[256,256]{1,0:T(8,128)(2,1)S(1)}, bf16[256,256]{1,0:T(8,128)(2,1)S(1)}, u32[]{:S(2)}, u32[]{:S(2)}) collective-permute-start(bf16[256,256]{1,0:T(8,128)(2,1)S(1)} %copy-done.3), channel_id=1, source_target_pairs={{0,1},{1,2},{2,3},{3,0},{4,5},{5,6},{6,7},{7,4},{8,9},{9,10},{10,1... | collective-permute-start | bytes 393224 | tf_op jit(solution)/shard_map/ppermute | solution.py:73
  27.6 1.6 copy-start.2
  29.0 7.8 %copy-start.9 = (bf16[1024,256]{1,0:T(8,128)(2,1)S(1)}, bf16[1024,256]{1,0:T(8,128)(2,1)}, u32[]{:S(2)}) copy-start(bf16[1024,256]{1,0:T(8,128)(2,1)} %param.21) | copy-start | bytes 1572868
  30.5 74.9 %collective-permute-start.8 = (bf16[256,1024]{1,0:T(8,128)(2,1)}, bf16[256,1024]{1,0:T(8,128)(2,1)S(1)}, u32[]{:S(2)}, u32[]{:S(2)}) collective-permute-start(bf16[256,1024]{1,0:T(8,128)(2,1)} %param.22), channel_id=1, source_target_pairs={{0,3},{1,0},{2,1},{3,2},{4,7},{5,4},{6,5},{7,6},{8,11},{9,8},{10,9... | collective-permute-start | bytes 1572872 | tf_op jit(solution)/shard_map/ppermute | solution.py:73
  32.1 76.5 %collective-permute-start.7 = (bf16[256,1024]{1,0:T(8,128)(2,1)}, bf16[256,1024]{1,0:T(8,128)(2,1)S(1)}, u32[]{:S(2)}, u32[]{:S(2)}) collective-permute-start(bf16[256,1024]{1,0:T(8,128)(2,1)} %param.22), channel_id=1, source_target_pairs={{0,2},{1,3},{2,0},{3,1},{4,6},{5,7},{6,4},{7,5},{8,10},{9,11},{10,... | collective-permute-start | bytes 1572872 | tf_op jit(solution)/shard_map/ppermute | solution.py:73
  33.3 75.3 %collective-permute-start.6 = (bf16[256,1024]{1,0:T(8,128)(2,1)}, bf16[256,1024]{1,0:T(8,128)(2,1)}, u32[]{:S(2)}, u32[]{:S(2)}) collective-permute-start(bf16[256,1024]{1,0:T(8,128)(2,1)} %param.22), channel_id=1, source_target_pairs={{0,1},{1,2},{2,3},{3,0},{4,5},{5,6},{6,7},{7,4},{8,9},{9,10},{10,1... | collective-permute-start | bytes 1572872 | tf_op jit(solution)/shard_map/ppermute | solution.py:73
  66.9 39.7 %copy-start.5 = (f32[256,8]{0,1:T(8,128)S(1)}, f32[256,8]{0,1:T(8,128)}, u32[]{:S(2)}) copy-start(f32[256,8]{0,1:T(8,128)} %param.25) | copy-start | bytes 24580
  66.9 39.7 %copy-start.6 = (s32[256,8]{0,1:T(8,128)S(1)}, s32[256,8]{0,1:T(8,128)}, u32[]{:S(2)}) copy-start(s32[256,8]{0,1:T(8,128)} %param.24) | copy-start | bytes 24580
  102.1 7.4 %collective-permute-start.5 = (bf16[256,256]{0,1:T(8,128)(2,1)S(1)}, bf16[256,256]{0,1:T(8,128)(2,1)S(1)}, u32[]{:S(2)}, u32[]{:S(2)}) collective-permute-start(bf16[256,256]{0,1:T(8,128)(2,1)S(1)} %bitcast.57), channel_id=1, source_target_pairs={{0,3},{1,0},{2,1},{3,2},{4,7},{5,4},{6,5},{7,6},{8,11},{9,8},{10,9... | collective-permute-start | bytes 393224 | tf_op jit(solution)/shard_map/ppermute | solution.py:73
  105.5 11.9 %collective-permute-start.4 = (bf16[256,256]{0,1:T(8,128)(2,1)S(1)}, bf16[256,256]{0,1:T(8,128)(2,1)S(1)}, u32[]{:S(2)}, u32[]{:S(2)}) collective-permute-start(bf16[256,256]{0,1:T(8,128)(2,1)S(1)} %bitcast.58), channel_id=1, source_target_pairs={{0,2},{1,3},{2,0},{3,1},{4,6},{5,7},{6,4},{7,5},{8,10},{9,11},{10,... | collective-permute-start | bytes 393224 | tf_op jit(solution)/shard_map/ppermute | solution.py:73
  105.5 11.9 %collective-permute-start.3 = (bf16[256,256]{0,1:T(8,128)(2,1)S(1)}, bf16[256,256]{0,1:T(8,128)(2,1)}, u32[]{:S(2)}, u32[]{:S(2)}) collective-permute-start(bf16[256,256]{0,1:T(8,128)(2,1)S(1)} %bitcast.59), channel_id=1, source_target_pairs={{0,1},{1,2},{2,3},{3,0},{4,5},{5,6},{6,7},{7,4},{8,9},{9,10},{10,1... | collective-permute-start | bytes 393224 | tf_op jit(solution)/shard_map/ppermute | solution.py:73
  108.6 10.9 %copy-start.7 = (f32[1024]{0:T(1024)S(1)}, f32[1024]{0:T(1024)}, u32[]{:S(2)}) copy-start(f32[1024]{0:T(1024)} %param.23) | copy-start | bytes 12292
  120.5 38.7 %copy-start.11 = (s32[1,2]{1,0:T(1,128)S(1)}, s32[1,2]{1,0:T(1,128)}, u32[]{:S(2)}) copy-start(s32[1,2]{1,0:T(1,128)} %param.18) | copy-start | bytes 28
  120.5 38.7 %copy-start.1 = (bf16[256,2,64]{2,0,1:T(8,128)(2,1)S(1)}, bf16[256,2,64]{2,0,1:T(8,128)(2,1)}, u32[]{:S(2)}) copy-start(bf16[256,2,64]{2,0,1:T(8,128)(2,1)} %copy.72) | copy-start | bytes 196612
  154.7 7.4 %collective-permute-start.11 = (bf16[256,256]{1,0:T(8,128)(2,1)S(1)}, bf16[256,256]{1,0:T(8,128)(2,1)S(1)}, u32[]{:S(2)}, u32[]{:S(2)}) collective-permute-start(bf16[256,256]{1,0:T(8,128)(2,1)S(1)} %get-tuple-element.21), channel_id=1, source_target_pairs={{0,3},{1,0},{2,1},{3,2},{4,7},{5,4},{6,5},{7,6},{8,11},{9,8},{10,9... | collective-permute-start | bytes 393224 | tf_op jit(solution)/shard_map/ppermute | solution.py:307
  158.1 11.9 %collective-permute-start.10 = (bf16[256,256]{1,0:T(8,128)(2,1)S(1)}, bf16[256,256]{1,0:T(8,128)(2,1)S(1)}, u32[]{:S(2)}, u32[]{:S(2)}) collective-permute-start(bf16[256,256]{1,0:T(8,128)(2,1)S(1)} %get-tuple-element.22), channel_id=1, source_target_pairs={{0,2},{1,3},{2,0},{3,1},{4,6},{5,7},{6,4},{7,5},{8,10},{9,11},{10,... | collective-permute-start | bytes 393224 | tf_op jit(solution)/shard_map/ppermute | solution.py:307
  158.1 11.9 %collective-permute-start.9 = (bf16[256,256]{1,0:T(8,128)(2,1)S(1)}, bf16[256,256]{1,0:T(8,128)(2,1)S(1)}, u32[]{:S(2)}, u32[]{:S(2)}) collective-permute-start(bf16[256,256]{1,0:T(8,128)(2,1)S(1)} %get-tuple-element.20), channel_id=1, source_target_pairs={{0,1},{1,2},{2,3},{3,0},{4,5},{5,6},{6,7},{7,4},{8,9},{9,10},{10,1... | collective-permute-start | bytes 393224 | tf_op jit(solution)/shard_map/ppermute | solution.py:307
Sparse Core Ops, SparseCore 0:
  9.9 56.9 all-gather.2
  68.8 71.9 all-gather.4

commit v16 on v14

--- a/solution.py
+++ b/solution.py
@@ -207,7 +207,7 @@
     experts, lanes = packed.shape[1], packed.shape[3]
     units = lanes
     col_blocks = packed.shape[2] // units
-    per_step = col_blocks
+    per_step = 2 if col_blocks % 2 == 0 else 1
     return pl.pallas_call(
         expert_body,
         grid=(col_blocks // per_step,),

time: 179 us -> 179 us (level)
    ppermute x9, waiting for transfers between devices: 17.6 us -> 14.7 us  [shifted_copies(): copies.append(lax.ppermute(block, axis_name, pairs))]
    all_gather x1, waiting for transfers between devices: 20.4 us -> 23.2 us  [shards(): packed = lax.all_gather(packed, 'req', axis=1, tiled=True)]
where the time goes in v16:
time: 179 us; the launch traced here: 178 us
  waiting for transfers between devices  74.8 us (42%)
  Pallas kernels  47.4 us (26%)
  starting transfers between devices  19.9 us (11%)
  between operations  14.3 us (8%)
  local copies, waits for them, and re-layouts  10.4 us (6%)
  other arithmetic  8.1 us (5%)
  matrix products  3.4 us (2%)
    pallas_call x1, Pallas kernels, attend(): pl.pallas_call(attention_body, grid_spec=grid_spec, out_shape=jax.ShapeDt...  34.1 us
    all_gather x1, waiting for transfers between devices, shards(): gathered = lax.all_gather(prefix_cache, 'req', axis=0, tiled=True)  27.7 us
    all_gather x1, waiting for transfers between devices, shards(): packed = lax.all_gather(packed, 'req', axis=1, tiled=True)  23.2 us
    ppermute x9, starting transfers between devices, shifted_copies(): copies.append(lax.ppermute(block, axis_name, pairs))  15.4 us
    ppermute x9, waiting for transfers between devices, shifted_copies(): copies.append(lax.ppermute(block, axis_name, pairs))  14.7 us
    pallas_call x1, Pallas kernels, expert_project(): pl.pallas_call(expert_body, grid=(col_blocks // per_step,), in_specs=[pl....  13.3 us
    ppermute x3, waiting for transfers between devices, shards(): incoming = lax.ppermute(outgoing.astype(jnp.bfloat16), 'hid', pairs)  9.14 us
    unnamed x31, local copies, waits for them, and re-layouts  4.68 us
  transfers between devices with their start and end apart: 14, of which 8 were waited for; matrix products, arithmetic and copies ran while one was open for 10% of the time, Pallas kernels for 19%

profile of v16, /device:TPU:0, one launch (start us, length us, event | category | flops | bytes accessed | tf_op | source)
XLA Modules:
  0.0 178.4 jit_solution(7813018466093930542)
XLA Ops:
  7.2 2.4 %copy.63 = bf16[2,1024,2,128]{3,1,2,0:T(8,128)(2,1)} copy(bf16[2,1024,2,128]{3,2,1,0:T(2,128)(2,1)} %param.17) | data formatting | bytes 2097152 | tf_op args[3]
  9.7 5.1 %collective-permute-start.2 = (bf16[256,256]{1,0:T(8,128)(2,1)S(1)}, bf16[256,256]{1,0:T(8,128)(2,1)S(1)}, u32[]{:S(2)}, u32[]{:S(2)}) collective-permute-start(bf16[256,256]{1,0:T(8,128)(2,1)S(1)} %copy-done.3), channel_id=1, source_target_pairs={{0,3},{1,0},{2,1},{3,2},{4,7},{5,4},{6,5},{7,6},{8,11},{9,8},{10,9... | collective-permute-start | bytes 393224 | tf_op jit(solution)/shard_map/ppermute | solution.py:73
  14.9 1.0 collective-permute-start
  15.9 0.2 convert_reduce_fusion
  16.1 0.5 multiply_cosine_fusion
  16.7 2.1 %collective-permute-done.2 = bf16[256,256]{1,0:T(8,128)(2,1)S(1)} collective-permute-done((bf16[256,256]{1,0:T(8,128)(2,1)S(1)}, bf16[256,256]{1,0:T(8,128)(2,1)S(1)}, u32[]{:S(2)}, u32[]{:S(2)}) %collective-permute-start.2) | collective-permute-done | bytes 131104 | tf_op jit(solution)/shard_map/ppermute | solution.py:73
  18.8 7.3 %collective-permute-done.1 = bf16[256,256]{1,0:T(8,128)(2,1)S(1)} collective-permute-done((bf16[256,256]{1,0:T(8,128)(2,1)S(1)}, bf16[256,256]{1,0:T(8,128)(2,1)S(1)}, u32[]{:S(2)}, u32[]{:S(2)}) %collective-permute-start.1) | collective-permute-done | bytes 131104 | tf_op jit(solution)/shard_map/ppermute | solution.py:73
  26.2 0.6 gather_fusion
  26.9 0.2 fusion.16
  27.1 0.5 fusion.28
  27.6 0.2 copy.73
  27.8 0.2 copy.72
  28.0 0.1 subtract_convert_fusion
  28.2 0.9 pad_maximum_fusion.2
  29.2 1.3 maximum_bitcast_fusion
  30.6 1.6 collective-permute-start.8
  32.1 1.2 collective-permute-start.7
  33.3 1.9 %collective-permute-start.6 = (bf16[256,1024]{1,0:T(8,128)(2,1)}, bf16[256,1024]{1,0:T(8,128)(2,1)}, u32[]{:S(2)}, u32[]{:S(2)}) collective-permute-start(bf16[256,1024]{1,0:T(8,128)(2,1)} %param.22), channel_id=1, source_target_pairs={{0,1},{1,2},{2,3},{3,0},{4,5},{5,6},{6,7},{7,4},{8,9},{9,10},{10,1... | collective-permute-start | bytes 1572872 | tf_op jit(solution)/shard_map/ppermute | solution.py:73
  35.3 0.8 copy.64.segq_ref
  36.0 0.2 convert_reduce_fusion.2
  36.2 0.6 pad_add_fusion.bound_ref
  36.8 0.4 fusion.26
  37.3 0.1 copy.75
  37.4 0.1 copy.74
  37.7 0.8 copy.76
  38.4 0.8 maximum_bitcast_fusion.1.k_ref
  39.2 27.7 %all-gather.3.cloned.1.call-done = bf16[16,1024,2,128]{3,1,2,0:T(8,128)(2,1)} async-done(((bf16[2,1024,2,128]{3,1,2,0:T(8,128)(2,1)}), bf16[16,1024,2,128]{3,1,2,0:T(8,128)(2,1)}) %all-gather.3.cloned.1.call-update) | async-done | bytes 8388624 | tf_op jit(solution)/shard_map/all_gather | solution.py:270
  66.9 34.1 %shard_map.149 = f32[2,2,256,64]{3,2,1,0:T(8,128)} custom-call(s32[8]{0:T(128)} %bitcast.75, s32[16]{0:T(128)} %pad_add_fusion.bound_ref, bf16[2,2,256,64]{3,2,1,0:T(8,128)(2,1)} %bitcast.58, bf16[2,256,64]{2,1,0:T(8,128)(2,1)} %maximum_bitcast_fusion.1.k_ref, bf16[2,256,64]{2,1,0:T(8,128)(2,1)} %bitcast.57, s32[256,1]{1,0:T(8,128)} %copy.64.segq_ref, ...), custom_call_target="tpu_custom_call" | custom-call | tf_op jit(solution)/shard_map/pallas_call | solution.py:169
  101.0 1.1 convert_bitcast_fusion
  102.1 0.1 copy.65
  102.2 3.4 %collective-permute-start.5 = (bf16[256,256]{0,1:T(8,128)(2,1)S(1)}, bf16[256,256]{0,1:T(8,128)(2,1)S(1)}, u32[]{:S(2)}, u32[]{:S(2)}) collective-permute-start(bf16[256,256]{0,1:T(8,128)(2,1)S(1)} %bitcast.63), channel_id=1, source_target_pairs={{0,3},{1,0},{2,1},{3,2},{4,7},{5,4},{6,5},{7,6},{8,11},{9,8},{10,9... | collective-permute-start | bytes 393224 | tf_op jit(solution)/shard_map/ppermute | solution.py:73
  105.7 1.1 collective-permute-start.3
  106.8 2.0 %copy.68.combine_ref = f32[16,256,1]{2,1,0:T(8,128)} copy(f32[16,256,1]{1,0,2:T(8,128)S(1)} %bitcast.71) | data formatting | bytes 32768 | tf_op jit(solution)/shard_map/broadcast_in_dim | solution.py:299
  108.8 0.9 collective-permute-done.5
  109.7 4.4 %collective-permute-done.4 = bf16[256,256]{0,1:T(8,128)(2,1)S(1)} collective-permute-done((bf16[256,256]{0,1:T(8,128)(2,1)S(1)}, bf16[256,256]{0,1:T(8,128)(2,1)S(1)}, u32[]{:S(2)}, u32[]{:S(2)}) %collective-permute-start.4) | collective-permute-done | bytes 131104 | tf_op jit(solution)/shard_map/ppermute | solution.py:73
  114.1 2.5 %fusion.13 = (f32[256]{0:T(256)S(1)}, bf16[256,1024]{1,0:T(8,128)(2,1)S(1)}) fusion(bf16[256,1024]{1,0:T(8,128)(2,1)} %collective-permute-done.8, bf16[256,1024]{1,0:T(8,128)(2,1)} %collective-permute-done.7, bf16[256,1024]{1,0:T(8,128)(2,1)} %collective-permute-done.6, bf16[256,1024]{1,0:T(8,128)(2,1)} %param.22, ...), kind=kOutput, calls=%fused_computation.17 | convolution fusion | flops 550764288 | bytes 3671040 | tf_op jit(solution)/shard_map/dot_general | solution.py:278
  116.6 1.0 fusion.15.normed_ref
  117.6 23.2 %all-gather.5.cloned.1.call-done.weight_ref.down_ref = bf16[3,16,1024,128]{3,2,1,0:T(8,128)(2,1)} async-done(((bf16[3,2,1024,128]{3,2,1,0:T(8,128)(2,1)}), bf16[3,16,1024,128]{3,2,1,0:T(8,128)(2,1)}) %all-gather.5.cloned.1.call-update) | async-done | bytes 12582928 | tf_op jit(solution)/shard_map/all_gather | solution.py:292
  140.8 13.3 %shard_map.150 = f32[8,256,128]{2,1,0:T(8,128)} custom-call(bf16[256,1024]{1,0:T(8,128)(2,1)} %fusion.15.normed_ref, f32[16,256,1]{2,1,0:T(8,128)} %copy.68.combine_ref, bf16[3,16,1024,128]{3,2,1,0:T(8,128)(2,1)} %all-gather.5.cloned.1.call-done.weight_ref.down_ref, bf16[3,16,1024,128]{3,2,1,0:T(8,128)(2,1)} %all-gather.5.cloned.1.call-done.weight_ref.down_ref), custom_call_target="tpu_custom_call" | custom-call | tf_op jit(solution)/shard_map/pallas_call | solution.py:211
  154.1 1.3 copy_bitcast_fusion
  155.5 3.4 %collective-permute-start.11 = (bf16[256,256]{1,0:T(8,128)(2,1)S(1)}, bf16[256,256]{1,0:T(8,128)(2,1)S(1)}, u32[]{:S(2)}, u32[]{:S(2)}) collective-permute-start(bf16[256,256]{1,0:T(8,128)(2,1)S(1)} %get-tuple-element.21), channel_id=1, source_target_pairs={{0,3},{1,0},{2,1},{3,2},{4,7},{5,4},{6,5},{7,6},{8,11},{9,8},{10,9... | collective-permute-start | bytes 393224 | tf_op jit(solution)/shard_map/ppermute | solution.py:310
  158.9 1.1 collective-permute-start.9
  160.0 0.1 pad_maximum_fusion.3
  160.2 0.6 scatter_fusion
  160.8 0.8 copy.71
  161.6 1.2 collective-permute-done.11
  162.9 7.9 %collective-permute-done.10 = bf16[256,256]{1,0:T(8,128)(2,1)S(1)} collective-permute-done((bf16[256,256]{1,0:T(8,128)(2,1)S(1)}, bf16[256,256]{1,0:T(8,128)(2,1)S(1)}, u32[]{:S(2)}, u32[]{:S(2)}) %collective-permute-start.10) | collective-permute-done | bytes 131104 | tf_op jit(solution)/shard_map/ppermute | solution.py:310
  170.8 0.7 add_convert_fusion.1
  (57 shorter events, 0.8 us)
Async XLA Ops:
  7.2 21.9 %copy-start = (bf16[2,128,1024]{2,1,0:T(8,128)(2,1)S(1)}, bf16[2,128,1024]{2,1,0:T(8,128)(2,1)}, u32[]{:S(2)}) copy-start(bf16[2,128,1024]{2,1,0:T(8,128)(2,1)} %param.27) | copy-start | bytes 1572868
  7.2 2.6 %copy-start.3 = (bf16[256,256]{1,0:T(8,128)(2,1)S(1)}, bf16[256,256]{1,0:T(8,128)(2,1)}, u32[]{:S(2)}) copy-start(bf16[256,256]{1,0:T(8,128)(2,1)} %param.14) | copy-start | bytes 393220
  7.2 8.7 %copy-start.4 = (s32[1,256]{1,0:T(1,128)S(1)}, s32[1,256]{1,0:T(1,128)}, u32[]{:S(2)}) copy-start(s32[1,256]{1,0:T(1,128)} %segk_ref.1) | copy-start | bytes 3076
  7.2 59.7 %all-gather.3.cloned.1.call-start = ((), (), s32[]{:S(2)}) async-start(), calls=%async_computation | async-start | bytes 9437184 | tf_op jit(solution)/shard_map/all_gather | solution.py:270
  9.7 17.5 %copy-start.8 = (bf16[1024,256]{1,0:T(8,128)(2,1)S(1)}, bf16[1024,256]{1,0:T(8,128)(2,1)}, u32[]{:S(2)}) copy-start(bf16[1024,256]{1,0:T(8,128)(2,1)} %param.20) | copy-start | bytes 1572868
  9.7 17.5 %copy-start.10 = (f32[1024]{0:T(1024)S(1)}, f32[1024]{0:T(1024)}, u32[]{:S(2)}) copy-start(f32[1024]{0:T(1024)} %param.19) | copy-start | bytes 12292
  9.7 131.2 %all-gather.5.cloned.1.call-start = ((), (), s32[]{:S(2)}) async-start(), calls=%async_computation.1 | async-start | bytes 14155776 | tf_op jit(solution)/shard_map/all_gather | solution.py:292
  9.7 9.0 %collective-permute-start.2 = (bf16[256,256]{1,0:T(8,128)(2,1)S(1)}, bf16[256,256]{1,0:T(8,128)(2,1)S(1)}, u32[]{:S(2)}, u32[]{:S(2)}) collective-permute-start(bf16[256,256]{1,0:T(8,128)(2,1)S(1)} %copy-done.3), channel_id=1, source_target_pairs={{0,3},{1,0},{2,1},{3,2},{4,7},{5,4},{6,5},{7,6},{8,11},{9,8},{10,9... | collective-permute-start | bytes 393224 | tf_op jit(solution)/shard_map/ppermute | solution.py:73
  14.9 11.2 %collective-permute-start.1 = (bf16[256,256]{1,0:T(8,128)(2,1)S(1)}, bf16[256,256]{1,0:T(8,128)(2,1)S(1)}, u32[]{:S(2)}, u32[]{:S(2)}) collective-permute-start(bf16[256,256]{1,0:T(8,128)(2,1)S(1)} %copy-done.3), channel_id=1, source_target_pairs={{0,2},{1,3},{2,0},{3,1},{4,6},{5,7},{6,4},{7,5},{8,10},{9,11},{10,... | collective-permute-start | bytes 393224 | tf_op jit(solution)/shard_map/ppermute | solution.py:73
  14.9 11.2 %collective-permute-start = (bf16[256,256]{1,0:T(8,128)(2,1)S(1)}, bf16[256,256]{1,0:T(8,128)(2,1)S(1)}, u32[]{:S(2)}, u32[]{:S(2)}) collective-permute-start(bf16[256,256]{1,0:T(8,128)(2,1)S(1)} %copy-done.3), channel_id=1, source_target_pairs={{0,1},{1,2},{2,3},{3,0},{4,5},{5,6},{6,7},{7,4},{8,9},{9,10},{10,1... | collective-permute-start | bytes 393224 | tf_op jit(solution)/shard_map/ppermute | solution.py:73
  27.6 1.6 copy-start.2
  29.1 7.8 %copy-start.9 = (bf16[1024,256]{1,0:T(8,128)(2,1)S(1)}, bf16[1024,256]{1,0:T(8,128)(2,1)}, u32[]{:S(2)}) copy-start(bf16[1024,256]{1,0:T(8,128)(2,1)} %param.21) | copy-start | bytes 1572868
  30.6 75.1 %collective-permute-start.8 = (bf16[256,1024]{1,0:T(8,128)(2,1)}, bf16[256,1024]{1,0:T(8,128)(2,1)}, u32[]{:S(2)}, u32[]{:S(2)}) collective-permute-start(bf16[256,1024]{1,0:T(8,128)(2,1)} %param.22), channel_id=1, source_target_pairs={{0,3},{1,0},{2,1},{3,2},{4,7},{5,4},{6,5},{7,6},{8,11},{9,8},{10,9... | collective-permute-start | bytes 1572872 | tf_op jit(solution)/shard_map/ppermute | solution.py:73
  32.1 76.7 %collective-permute-start.7 = (bf16[256,1024]{1,0:T(8,128)(2,1)}, bf16[256,1024]{1,0:T(8,128)(2,1)}, u32[]{:S(2)}, u32[]{:S(2)}) collective-permute-start(bf16[256,1024]{1,0:T(8,128)(2,1)} %param.22), channel_id=1, source_target_pairs={{0,2},{1,3},{2,0},{3,1},{4,6},{5,7},{6,4},{7,5},{8,10},{9,11},{10,... | collective-permute-start | bytes 1572872 | tf_op jit(solution)/shard_map/ppermute | solution.py:73
  33.3 75.5 %collective-permute-start.6 = (bf16[256,1024]{1,0:T(8,128)(2,1)}, bf16[256,1024]{1,0:T(8,128)(2,1)}, u32[]{:S(2)}, u32[]{:S(2)}) collective-permute-start(bf16[256,1024]{1,0:T(8,128)(2,1)} %param.22), channel_id=1, source_target_pairs={{0,1},{1,2},{2,3},{3,0},{4,5},{5,6},{6,7},{7,4},{8,9},{9,10},{10,1... | collective-permute-start | bytes 1572872 | tf_op jit(solution)/shard_map/ppermute | solution.py:73
  66.9 39.9 %copy-start.5 = (f32[256,8]{0,1:T(8,128)S(1)}, f32[256,8]{0,1:T(8,128)}, u32[]{:S(2)}) copy-start(f32[256,8]{0,1:T(8,128)} %param.25) | copy-start | bytes 24580
  66.9 39.9 %copy-start.6 = (s32[256,8]{0,1:T(8,128)S(1)}, s32[256,8]{0,1:T(8,128)}, u32[]{:S(2)}) copy-start(s32[256,8]{0,1:T(8,128)} %param.24) | copy-start | bytes 24580
  102.2 7.4 %collective-permute-start.5 = (bf16[256,256]{0,1:T(8,128)(2,1)S(1)}, bf16[256,256]{0,1:T(8,128)(2,1)S(1)}, u32[]{:S(2)}, u32[]{:S(2)}) collective-permute-start(bf16[256,256]{0,1:T(8,128)(2,1)S(1)} %bitcast.63), channel_id=1, source_target_pairs={{0,3},{1,0},{2,1},{3,2},{4,7},{5,4},{6,5},{7,6},{8,11},{9,8},{10,9... | collective-permute-start | bytes 393224 | tf_op jit(solution)/shard_map/ppermute | solution.py:73
  105.7 8.4 %collective-permute-start.4 = (bf16[256,256]{0,1:T(8,128)(2,1)S(1)}, bf16[256,256]{0,1:T(8,128)(2,1)S(1)}, u32[]{:S(2)}, u32[]{:S(2)}) collective-permute-start(bf16[256,256]{0,1:T(8,128)(2,1)S(1)} %bitcast.64), channel_id=1, source_target_pairs={{0,2},{1,3},{2,0},{3,1},{4,6},{5,7},{6,4},{7,5},{8,10},{9,11},{10,... | collective-permute-start | bytes 393224 | tf_op jit(solution)/shard_map/ppermute | solution.py:73
  105.7 8.4 %collective-permute-start.3 = (bf16[256,256]{0,1:T(8,128)(2,1)S(1)}, bf16[256,256]{0,1:T(8,128)(2,1)S(1)}, u32[]{:S(2)}, u32[]{:S(2)}) collective-permute-start(bf16[256,256]{0,1:T(8,128)(2,1)S(1)} %bitcast.65), channel_id=1, source_target_pairs={{0,1},{1,2},{2,3},{3,0},{4,5},{5,6},{6,7},{7,4},{8,9},{9,10},{10,1... | collective-permute-start | bytes 393224 | tf_op jit(solution)/shard_map/ppermute | solution.py:73
  108.8 7.8 %copy-start.7 = (f32[1024]{0:T(1024)S(1)}, f32[1024]{0:T(1024)}, u32[]{:S(2)}) copy-start(f32[1024]{0:T(1024)} %param.23) | copy-start | bytes 12292
  117.6 42.4 %copy-start.11 = (s32[1,2]{1,0:T(1,128)S(1)}, s32[1,2]{1,0:T(1,128)}, u32[]{:S(2)}) copy-start(s32[1,2]{1,0:T(1,128)} %param.18) | copy-start | bytes 28
  117.6 42.4 %copy-start.1 = (bf16[256,2,64]{2,0,1:T(8,128)(2,1)S(1)}, bf16[256,2,64]{2,0,1:T(8,128)(2,1)}, u32[]{:S(2)}) copy-start(bf16[256,2,64]{2,0,1:T(8,128)(2,1)} %copy.76) | copy-start | bytes 196612
  155.5 7.4 %collective-permute-start.11 = (bf16[256,256]{1,0:T(8,128)(2,1)S(1)}, bf16[256,256]{1,0:T(8,128)(2,1)S(1)}, u32[]{:S(2)}, u32[]{:S(2)}) collective-permute-start(bf16[256,256]{1,0:T(8,128)(2,1)S(1)} %get-tuple-element.21), channel_id=1, source_target_pairs={{0,3},{1,0},{2,1},{3,2},{4,7},{5,4},{6,5},{7,6},{8,11},{9,8},{10,9... | collective-permute-start | bytes 393224 | tf_op jit(solution)/shard_map/ppermute | solution.py:310
  158.9 11.9 %collective-permute-start.10 = (bf16[256,256]{1,0:T(8,128)(2,1)S(1)}, bf16[256,256]{1,0:T(8,128)(2,1)S(1)}, u32[]{:S(2)}, u32[]{:S(2)}) collective-permute-start(bf16[256,256]{1,0:T(8,128)(2,1)S(1)} %get-tuple-element.22), channel_id=1, source_target_pairs={{0,2},{1,3},{2,0},{3,1},{4,6},{5,7},{6,4},{7,5},{8,10},{9,11},{10,... | collective-permute-start | bytes 393224 | tf_op jit(solution)/shard_map/ppermute | solution.py:310
  158.9 11.9 %collective-permute-start.9 = (bf16[256,256]{1,0:T(8,128)(2,1)S(1)}, bf16[256,256]{1,0:T(8,128)(2,1)S(1)}, u32[]{:S(2)}, u32[]{:S(2)}) collective-permute-start(bf16[256,256]{1,0:T(8,128)(2,1)S(1)} %get-tuple-element.20), channel_id=1, source_target_pairs={{0,1},{1,2},{2,3},{3,0},{4,5},{5,6},{6,7},{7,4},{8,9},{9,10},{10,1... | collective-permute-start | bytes 393224 | tf_op jit(solution)/shard_map/ppermute | solution.py:310
Sparse Core Ops, SparseCore 0:
  9.9 56.9 all-gather.2
  68.8 71.9 all-gather.4
